TPU v7x, 32 devices: a whole 2x2x4 slice. The times are simulated.
32 devices in a mesh: prow: 8 (over z, x), pcol: 4 (over y, core).
Axes of the slice: x: 2, y: 2, z: 4, core: 2. Of those that a mesh axis runs over, the one named last changes fastest.
Arguments:
- dof_values: float32 [9, 56, 4096], P(None, None, ('prow', 'pcol')), may hold values from -6 to 6
- grad_matrix: float32 [3, 56, 56], replicated, may hold values from -0.75 to 0.75
- stiff_matrix: float32 [3, 56, 56], replicated, may hold values from -0.1875 to 0.1875
- face_proj: float32 [4, 21, 56], replicated, may hold values from -0.75 to 0.75
- face_lift: float32 [4, 56, 21], replicated, may hold values from -0.3125 to 0.3125
- rotate: float32 [3, 21, 21], replicated, may hold values from -1.25 to 1.25
- material: float32 [16, 3], replicated, may hold values from 0.5 to 2
- material_id: int32 [4096], P(('prow', 'pcol')), may hold values from 0 to 15
- inv_jacobian: float32 [3, 3, 4096], P(None, None, ('prow', 'pcol')), may hold values from -3 to 3
- normals: float32 [4, 3, 4096], P(None, None, ('prow', 'pcol')), may hold values from -2 to 2
- orientation: int32 [4, 4096], P(None, ('prow', 'pcol')), may hold values from 0 to 2
- neighbour: int32 [4, 4096], P(None, ('prow', 'pcol')), may hold values from -1 to 127, as said below
- neighbour_face: int32 [4, 4096], P(None, ('prow', 'pcol')), may hold values from 0 to 3, as said below
- send_list: int32 [8, 4, 8, 24], P('prow', 'pcol'), may hold values from -1 to 511, as said below
- recv_list: int32 [8, 4, 8, 24], P('prow', 'pcol'), may hold values from -1 to 511, as said below
Outputs:
- new_dofs: float32 [9, 56, 4096], P(None, None, ('prow', 'pcol'))
Inputs may be any that keep to these rules, and one draw needn't show every extreme that they name: `neighbour`: -1 where the face has no neighbour in the same partition; otherwise faces are matched in pairs: the element neighbour[f, e] lists e back across its face neighbour_face[f, e]. `neighbour_face`: 0 where neighbour is -1. `send_list`: entry (r, c, d, m) is a local face id of partition (r, c) whose neighbour lies in the partition at offset d, or -1; live slots of a direction come first, each such face appears once, and the live count of (r, c, d) equals that of the partner's direction 7 - d; directions leaving the grid have none. Some partition has 24 live slots in all eight directions, and every live count is at most 24. `recv_list`: entry (r, c, d, m) is the local face id of partition (r, c) that meets the face in slot m of the send_list of the partner at offset d for direction 7 - d, or -1 where that slot is empty; its live slots hold the same faces as send_list of (r, c, d) in another order.
All inputs are finite; a program needn't handle non-finite values.
Results may differ from a plain program's by a relative error of at most 0.0003.
Values sent between devices are 32-bit elements; how exact they have to be, the bound alone decides.
No kernel may reach another device: no remote copies, remote signals or barrier semaphores. Data moves between devices by JAX's collectives and lax.ppermute only.
A program may use at most 64 MiB of HBM per device.

v0:
```python
import jax
import jax.numpy as jnp
from jax import lax
from jax.sharding import PartitionSpec as P

ORDER = 6
STEPS = 2


exact_mode = lax.Precision.HIGHEST
time_step = 0.8
OFFSETS = ((-1, -1), (-1, 0), (-1, 1), (0, -1), (0, 1), (1, -1), (1, 0), (1, 1))
ENTRIES = (
    (0, 0, 6, 0),
    (0, 1, 6, 1),
    (0, 2, 6, 1),
    (0, 3, 7, 2),
    (0, 5, 8, 2),
    (0, 6, 0, 3),
    (0, 7, 3, 3),
    (0, 8, 5, 3),
    (1, 0, 7, 1),
    (1, 1, 7, 0),
    (1, 2, 7, 1),
    (1, 3, 6, 2),
    (1, 4, 8, 2),
    (1, 6, 3, 3),
    (1, 7, 1, 3),
    (1, 8, 4, 3),
    (2, 0, 8, 1),
    (2, 1, 8, 1),
    (2, 2, 8, 0),
    (2, 4, 7, 2),
    (2, 5, 6, 2),
    (2, 6, 5, 3),
    (2, 7, 4, 3),
    (2, 8, 2, 3),
)


def shifted(x, axis, by):
    devices = lax.axis_size(axis)
    pairs = [(i, i + by) for i in range(devices) if 0 <= i + by < devices]
    return lax.ppermute(x, axis, pairs)


def element_params(material, material_id, normals):
    id_range = jnp.arange(material.shape[0], dtype=jnp.int32)
    onehot = (material_id[None, :] == id_range[:, None]).astype(material.dtype)
    params = jnp.dot(material.T, onehot, precision=exact_mode)
    density, lame_first, shear_modulus = (params[0], params[1], params[2])
    values = (-(lame_first + 2.0 * shear_modulus), -lame_first, -shear_modulus, -1.0 / density)
    wave_speed = jnp.sqrt((lame_first + 2.0 * shear_modulus) / density) * jnp.sum(
        jnp.abs(normals), axis=1
    )
    return (values, wave_speed)


def elastic_apply(parts, values):
    result = [None] * 9
    for comp_axis, row_index, col_index, kind_index in ENTRIES:
        term = values[kind_index] * parts[comp_axis][col_index]
        result[row_index] = term if result[row_index] is None else result[row_index] + term
    return jnp.stack(result, axis=0)


def star_apply(slopes, inv_jacobian, values):
    parts = [jnp.sum(inv_jacobian[:, k][:, None, None, :] * slopes, axis=0) for k in range(3)]
    return elastic_apply(parts, values)


def predict(current, inv_jacobian, values, grad_matrix):
    derivative = current
    integrated = time_step * current
    factor = time_step
    for power_level in range(1, ORDER):
        slopes = jnp.einsum("dab,qbe->dqae", grad_matrix, derivative, precision=exact_mode)
        derivative = -star_apply(slopes, inv_jacobian, values)
        factor = factor * time_step / (power_level + 1)
        integrated = integrated + factor * derivative
    return integrated


def local_part(current, inv_jacobian, values, grad_matrix, stiff_matrix, face_proj):
    integrated = predict(current, inv_jacobian, values, grad_matrix)
    slopes = jnp.einsum("dab,qbe->dqae", stiff_matrix, integrated, precision=exact_mode)
    volume = star_apply(slopes, inv_jacobian, values)
    face_data = jnp.einsum("fib,qbe->qife", face_proj, integrated, precision=exact_mode)
    return (volume, face_data)


def face_update(
    current,
    volume,
    face_data,
    neighbour_data,
    orientation,
    normals,
    values,
    wave_speed,
    rotate,
    face_lift,
):
    turned = jnp.einsum("hil,qlfe->hqife", rotate, neighbour_data, precision=exact_mode)
    chosen = (orientation[None] == jnp.arange(3, dtype=jnp.int32)[:, None, None]).astype(
        current.dtype
    )
    turned = jnp.sum(turned * chosen[:, None, None, :, :], axis=0)
    both = face_data + turned
    apart = face_data - turned
    parts = [normals[:, k, :][None, None] * both for k in range(3)]
    flux_total = 0.5 * (elastic_apply(parts, values) + wave_speed[None, None] * apart)
    lifted = jnp.einsum("fai,pife->pae", face_lift, flux_total, precision=exact_mode)
    return current + volume - lifted


def deliver(outgoing):
    forwarded = {}
    for col_step in (-1, 1):
        bundle = jnp.stack(
            [outgoing[:, :, OFFSETS.index((row_step, col_step))] for row_step in (-1, 0, 1)], axis=2
        )
        forwarded[col_step] = shifted(bundle, "pcol", col_step)
    pieces = {}
    for col_step in (-1, 1):
        pieces[OFFSETS.index((0, -col_step))] = forwarded[col_step][:, :, 1]
    for row_step in (-1, 1):
        bundle = jnp.stack(
            [
                outgoing[:, :, OFFSETS.index((row_step, 0))],
                forwarded[1][:, :, row_step + 1],
                forwarded[-1][:, :, row_step + 1],
            ],
            axis=2,
        )
        arrived_rows = shifted(bundle, "prow", row_step)
        pieces[OFFSETS.index((-row_step, 0))] = arrived_rows[:, :, 0]
        pieces[OFFSETS.index((-row_step, -1))] = arrived_rows[:, :, 1]
        pieces[OFFSETS.index((-row_step, 1))] = arrived_rows[:, :, 2]
    return jnp.stack([pieces[direction] for direction in range(8)], axis=2)


def per_device(
    dof_values,
    grad_matrix,
    stiff_matrix,
    face_proj,
    face_lift,
    rotate,
    material,
    material_id,
    inv_jacobian,
    normals,
    orientation,
    neighbour,
    neighbour_face,
    send_list,
    recv_list,
):
    elem_count = dof_values.shape[2]
    face_width = face_proj.shape[1]
    values, wave_speed = element_params(material, material_id, normals)
    inside = (neighbour >= 0).reshape(-1)
    local_index = (neighbour_face * elem_count + jnp.maximum(neighbour, 0)).reshape(-1)
    source_ids = send_list[0, 0]
    slot_total = source_ids.shape[1]
    source_index = jnp.maximum(source_ids, 0).reshape(-1)
    source_mask = (source_ids >= 0).reshape(-1).astype(dof_values.dtype)
    targets = jnp.where(recv_list[0, 0] >= 0, recv_list[0, 0], 4 * elem_count).reshape(-1)
    current = dof_values
    for time_index in range(STEPS):
        volume, face_data = local_part(
            current, inv_jacobian, values, grad_matrix, stiff_matrix, face_proj
        )
        flat_faces = face_data.reshape(9, face_width, 4 * elem_count)
        outgoing = (jnp.take(flat_faces, source_index, axis=2) * source_mask).reshape(
            9, face_width, 8, slot_total
        )
        received = deliver(outgoing).reshape(9, face_width, 8 * slot_total)
        arrived = jnp.zeros_like(flat_faces).at[:, :, targets].set(received, mode="drop")
        local_data = jnp.take(flat_faces, local_index, axis=2)
        neighbour_data = jnp.where(inside, local_data, arrived).reshape(
            9, face_width, 4, elem_count
        )
        current = face_update(
            current,
            volume,
            face_data,
            neighbour_data,
            orientation,
            normals,
            values,
            wave_speed,
            rotate,
            face_lift,
        )
    return current


def solution(mesh):
    return jax.shard_map(
        per_device,
        mesh=mesh,
        in_specs=(
            P(None, None, ("prow", "pcol")),
            P(),
            P(),
            P(),
            P(),
            P(),
            P(),
            P(("prow", "pcol")),
            P(None, None, ("prow", "pcol")),
            P(None, None, ("prow", "pcol")),
            P(None, ("prow", "pcol")),
            P(None, ("prow", "pcol")),
            P(None, ("prow", "pcol")),
            P("prow", "pcol", None, None),
            P("prow", "pcol", None, None),
        ),
        out_specs=P(None, None, ("prow", "pcol")),
        check_vma=False,
    )
```

profile of v0, /device:TPU:25, one launch (start us, length us, event | category | flops | bytes accessed | tf_op | source)
XLA Modules:
  0.0 175.4 jit_solution(67717169791084251)
XLA Ops:
  10.7 2.9 %copy.103 = f32[9,21,4,128]{1,0,3,2:T(8,128)} copy(f32[9,21,4,128]{3,1,2,0:T(8,128)S(1)} %convolution_bitcast_fusion.13) | data formatting | bytes 774144 | tf_op jit(solution)/shard_map/reshape | solution.py:175
  15.3 2.9 %gather_fusion.1 = f32[192,9,21]{2,1,0:T(8,128)S(1)} fusion(f32[9,21,512]{1,0,2:T(8,128)} %bitcast.279, s32[1024]{0:T(1024)S(1)} %get-tuple-element.104), kind=kCustom, calls=%fused_computation.1.clone | custom fusion | bytes 291072 | tf_op jit(solution)/shard_map/jit(_take)/gather | solution.py:176
  20.1 3.7 %collective-permute-start = (f32[9,21,3,24]{3,1,2,0:T(8,128)S(1)}, f32[9,21,3,24]{3,1,2,0:T(8,128)S(1)}, u32[]{:S(2)}, u32[]{:S(2)}) collective-permute-start(f32[9,21,3,24]{3,1,2,0:T(8,128)S(1)} %pad_maximum_fusion), channel_id=1, source_target_pairs={{0,1},{1,2},{2,3},{4,5},{5,6},{6,7},{8,9},{9,10},{10,11},{12,13},{... | collective-permute-start | bytes 163304 | tf_op jit(solution)/shard_map/ppermute | solution.py:44
  30.3 5.1 %gather_fusion = f32[512,9,21]{2,1,0:T(8,128)} fusion(f32[9,21,512]{1,0,2:T(8,128)} %bitcast.280, s32[1024]{0:T(1024)S(1)} %copy-done.19), kind=kCustom, calls=%fused_computation.clone | custom fusion | bytes 776192 | tf_op jit(solution)/shard_map/jit(_take)/gather | solution.py:181
  36.9 3.1 %collective-permute-start.2 = (f32[9,21,3,24]{3,1,2,0:T(8,128)S(1)}, f32[9,21,3,24]{3,1,2,0:T(8,128)S(1)}, u32[]{:S(2)}, u32[]{:S(2)}) collective-permute-start(f32[9,21,3,24]{3,1,2,0:T(8,128)S(1)} %pad_maximum_fusion.2), channel_id=1, source_target_pairs={{0,4},{4,8},{8,12},{12,16},{16,20},{20,24},{24,28},{1,5},{5,9},{9,... | collective-permute-start | bytes 163304 | tf_op jit(solution)/shard_map/ppermute | solution.py:44
  40.3 3.2 %collective-permute-start.3 = (f32[9,21,3,24]{3,1,2,0:T(8,128)S(1)}, f32[9,21,3,24]{3,1,2,0:T(8,128)S(1)}, u32[]{:S(2)}, u32[]{:S(2)}) collective-permute-start(f32[9,21,3,24]{3,1,2,0:T(8,128)S(1)} %pad_maximum_fusion.3), channel_id=1, source_target_pairs={{4,0},{8,4},{12,8},{16,12},{20,16},{24,20},{28,24},{5,1},{9,5},{13... | collective-permute-start | bytes 163304 | tf_op jit(solution)/shard_map/ppermute | solution.py:44
  43.5 4.3 %collective-permute-done.2 = f32[9,21,3,24]{3,1,2,0:T(8,128)S(1)} collective-permute-done((f32[9,21,3,24]{3,1,2,0:T(8,128)S(1)}, f32[9,21,3,24]{3,1,2,0:T(8,128)S(1)}, u32[]{:S(2)}, u32[]{:S(2)}) %collective-permute-start.2) | collective-permute-done | bytes 54464 | tf_op jit(solution)/shard_map/ppermute | solution.py:44
  48.2 6.8 %collective-permute-done.3 = f32[9,21,3,24]{3,1,2,0:T(8,128)S(1)} collective-permute-done((f32[9,21,3,24]{3,1,2,0:T(8,128)S(1)}, f32[9,21,3,24]{3,1,2,0:T(8,128)S(1)}, u32[]{:S(2)}, u32[]{:S(2)}) %collective-permute-start.3) | collective-permute-done | bytes 54464 | tf_op jit(solution)/shard_map/ppermute | solution.py:44
  57.5 2.2 %broadcast.1324.clone = f32[9,21,512]{1,0,2:T(8,128)} broadcast(f32[]{:T(128)} %constant.31.clone.1), dimensions={} | broadcast | bytes 387076 | tf_op jit(solution)/shard_map/broadcast.16
  59.7 20.7 %scatter_fusion = f32[9,21,512]{1,0,2:T(8,128)} fusion(f32[9,21,512]{1,0,2:T(8,128)} %broadcast.1324.clone, s32[192]{0:T(256)} %bitcast.297, f32[192,9,21]{2,1,0:T(8,128)S(1)} %bitcast.284), kind=kCustom, calls=%fused_computation.4 | custom fusion | bytes 436224 | tf_op jit(solution)/shard_map/scatter | solution.py:180
  80.4 5.7 %bitcast_select_fusion.1 = f32[9,21,512]{1,0,2:T(8,128)S(1)} fusion(f32[9,21,512]{1,0,2:T(8,128)} %scatter_fusion, f32[512,9,21]{2,1,0:T(8,128)} %gather_fusion, pred[512]{0:T(512)(128)(4,1)} %get-tuple-element.43, pred[512]{0:T(512)(128)(4,1)} %compare_bitcast_fusion), kind=kLoop, calls=%fused_computation.7 | loop fusion | flops 193536 | bytes 1162240 | tf_op jit(solution)/shard_map/jit(_where)/select_n | solution.py:182
  86.2 3.4 %fusion.19 = f32[9,21,4,128]{3,1,2,0:T(8,128)S(1)} fusion(f32[9,21,4,128,1]{1,0,3,2,4:T(8,128)S(1)} %bitcast.276, f32[3,4,128]{2,0,1:T(4,128)S(1)} %fusion.164, f32[3,21,21]{2,1,0:T(8,128)S(1)} %copy-done.6), kind=kOutput, calls=%fused_computation.19 | convolution fusion | flops 73640448 | bytes 785580 | tf_op jit(solution)/shard_map/hil,qlfe->hqife/dot_general | solution.py:104
  97.4 2.9 %copy.105 = f32[9,21,4,128]{1,0,3,2:T(8,128)} copy(f32[9,21,4,128]{3,1,2,0:T(8,128)S(1)} %convolution_bitcast_fusion.12) | data formatting | bytes 774144 | tf_op jit(solution)/shard_map/reshape | solution.py:175
  100.3 3.0 %gather_fusion.3 = f32[192,9,21]{2,1,0:T(8,128)S(1)} fusion(f32[9,21,512]{1,0,2:T(8,128)} %bitcast.281, s32[1024]{0:T(1024)} %copy-done.24), kind=kCustom, calls=%fused_computation.3.clone | custom fusion | bytes 291072 | tf_op jit(solution)/shard_map/jit(_take)/gather | solution.py:176
  105.6 4.6 %collective-permute-start.4 = (f32[9,21,3,24]{3,1,2,0:T(8,128)S(1)}, f32[9,21,3,24]{3,1,2,0:T(8,128)S(1)}, u32[]{:S(2)}, u32[]{:S(2)}) collective-permute-start(f32[9,21,3,24]{3,1,2,0:T(8,128)S(1)} %pad_maximum_fusion.4), channel_id=1, source_target_pairs={{0,1},{1,2},{2,3},{4,5},{5,6},{6,7},{8,9},{9,10},{10,11},{12,13},{... | collective-permute-start | bytes 163304 | tf_op jit(solution)/shard_map/ppermute | solution.py:44
  110.3 5.1 %gather_fusion.2 = f32[512,9,21]{2,1,0:T(8,128)} fusion(f32[9,21,512]{1,0,2:T(8,128)} %bitcast.282, s32[1024]{0:T(1024)S(1)} %copy-done.20), kind=kCustom, calls=%fused_computation.2.clone | custom fusion | bytes 776192 | tf_op jit(solution)/shard_map/jit(_take)/gather | solution.py:181
  117.6 6.5 %collective-permute-done.5 = f32[9,21,3,24]{3,1,2,0:T(8,128)S(1)} collective-permute-done((f32[9,21,3,24]{3,1,2,0:T(8,128)S(1)}, f32[9,21,3,24]{3,1,2,0:T(8,128)S(1)}, u32[]{:S(2)}, u32[]{:S(2)}) %collective-permute-start.5) | collective-permute-done | bytes 54464 | tf_op jit(solution)/shard_map/ppermute | solution.py:44
  126.3 4.3 %collective-permute-start.7 = (f32[9,21,3,24]{3,1,2,0:T(8,128)S(1)}, f32[9,21,3,24]{3,1,2,0:T(8,128)S(1)}, u32[]{:S(2)}, u32[]{:S(2)}) collective-permute-start(f32[9,21,3,24]{3,1,2,0:T(8,128)S(1)} %pad_maximum_fusion.7), channel_id=1, source_target_pairs={{4,0},{8,4},{12,8},{16,12},{20,16},{24,20},{28,24},{5,1},{9,5},{13... | collective-permute-start | bytes 163304 | tf_op jit(solution)/shard_map/ppermute | solution.py:44
  130.6 2.4 %collective-permute-done.6 = f32[9,21,3,24]{3,1,2,0:T(8,128)S(1)} collective-permute-done((f32[9,21,3,24]{3,1,2,0:T(8,128)S(1)}, f32[9,21,3,24]{3,1,2,0:T(8,128)S(1)}, u32[]{:S(2)}, u32[]{:S(2)}) %collective-permute-start.6) | collective-permute-done | bytes 54464 | tf_op jit(solution)/shard_map/ppermute | solution.py:44
  133.4 5.8 %collective-permute-done.7 = f32[9,21,3,24]{3,1,2,0:T(8,128)S(1)} collective-permute-done((f32[9,21,3,24]{3,1,2,0:T(8,128)S(1)}, f32[9,21,3,24]{3,1,2,0:T(8,128)S(1)}, u32[]{:S(2)}, u32[]{:S(2)}) %collective-permute-start.7) | collective-permute-done | bytes 54464 | tf_op jit(solution)/shard_map/ppermute | solution.py:44
  141.6 2.2 %broadcast.1324 = f32[9,21,512]{1,0,2:T(8,128)} broadcast(f32[]{:T(128)} %constant.31.clone.1), dimensions={} | broadcast | bytes 387076 | tf_op jit(solution)/shard_map/broadcast.16
  143.8 20.6 %scatter_fusion.1 = f32[9,21,512]{1,0,2:T(8,128)} fusion(f32[9,21,512]{1,0,2:T(8,128)} %broadcast.1324, s32[192]{0:T(256)S(1)} %bitcast.298, f32[192,9,21]{2,1,0:T(8,128)S(1)} %bitcast.283), kind=kCustom, calls=%fused_computation.5 | custom fusion | bytes 436224 | tf_op jit(solution)/shard_map/scatter | solution.py:180
  164.5 5.8 %bitcast_select_fusion = f32[9,21,512]{1,0,2:T(8,128)S(1)} fusion(f32[9,21,512]{1,0,2:T(8,128)} %scatter_fusion.1, f32[512,9,21]{2,1,0:T(8,128)} %gather_fusion.2, pred[512]{0:T(512)(128)(4,1)S(1)} %copy-done.27, pred[512]{0:T(512)(128)(4,1)S(1)} %copy-done.26), kind=kLoop, calls=%fused_computation.6 | loop fusion | flops 193536 | bytes 1162240 | tf_op jit(solution)/shard_map/jit(_where)/select_n | solution.py:182
  170.4 3.4 %fusion.16 = f32[9,21,4,128]{3,1,2,0:T(8,128)S(1)} fusion(f32[9,21,4,128,1]{1,0,3,2,4:T(8,128)S(1)} %bitcast.275, f32[3,4,128]{2,0,1:T(4,128)S(1)} %fusion.164, f32[3,21,21]{2,1,0:T(8,128)S(1)} %copy-done.7), kind=kOutput, calls=%fused_computation.18 | convolution fusion | flops 73640448 | bytes 785580 | tf_op jit(solution)/shard_map/hil,qlfe->hqife/dot_general | solution.py:104
  (296 shorter events, 42.8 us)
Async XLA Ops:
  1.5 16.7 %copy-start.29 = (pred[192]{0:T(512)(128)(4,1)}, pred[192]{0:T(512)(128)(4,1)S(1)}, u32[]{:S(2)}) copy-start(pred[192]{0:T(512)(128)(4,1)S(1)} %compare_and_fusion) | copy-start | bytes 580
  2.9 15.3 %copy-start.21 = (f32[192]{0:T(256)}, f32[192]{0:T(256)S(1)}, u32[]{:S(2)}) copy-start(f32[192]{0:T(256)S(1)} %reshape.1889) | copy-start | bytes 2308
  3.8 24.4 %copy-start.8 = (f32[3,128]{1,0:T(4,128)}, f32[3,128]{1,0:T(4,128)S(1)}, u32[]{:S(2)}) copy-start(f32[3,128]{1,0:T(4,128)S(1)} %get-tuple-element.103) | copy-start | bytes 4612
  18.3 9.8 %copy-start.28 = (s32[1,1,8,24]{3,2,1,0:T(8,128)S(1)}, s32[1,1,8,24]{3,2,1,0:T(8,128)}, u32[]{:S(2)}) copy-start(s32[1,1,8,24]{3,2,1,0:T(8,128)} %param.33) | copy-start | bytes 2308
  18.3 9.9 %copy-start.31 = (s32[4,128]{1,0:T(4,128)S(1)}, s32[4,128]{1,0:T(4,128)}, u32[]{:S(2)}) copy-start(s32[4,128]{1,0:T(4,128)} %param.29) | copy-start | bytes 6148
  18.3 9.9 %copy-start.2 = (f32[3,56,56]{2,1,0:T(8,128)S(1)}, f32[3,56,56]{2,1,0:T(8,128)}, u32[]{:S(2)}) copy-start(f32[3,56,56]{2,1,0:T(8,128)} %param.21) | copy-start | bytes 112900
  19.5 9.7 %copy-start.33 = (f32[128]{0:T(128)S(1)}, f32[128]{0:T(128)}, u32[]{:S(2)}) copy-start(f32[128]{0:T(128)} %get-tuple-element.97) | copy-start | bytes 1540
  19.5 10.8 %copy-start.19 = (s32[1024]{0:T(1024)S(1)}, s32[1024]{0:T(1024)}, u32[]{:S(2)}) copy-start(s32[1024]{0:T(1024)} %get-tuple-element.105) | copy-start | bytes 12292
  20.1 15.7 %collective-permute-start = (f32[9,21,3,24]{3,1,2,0:T(8,128)S(1)}, f32[9,21,3,24]{3,1,2,0:T(8,128)S(1)}, u32[]{:S(2)}, u32[]{:S(2)}) collective-permute-start(f32[9,21,3,24]{3,1,2,0:T(8,128)S(1)} %pad_maximum_fusion), channel_id=1, source_target_pairs={{0,1},{1,2},{2,3},{4,5},{5,6},{6,7},{8,9},{9,10},{10,11},{12,13},{... | collective-permute-start | bytes 163304 | tf_op jit(solution)/shard_map/ppermute | solution.py:44
  25.0 10.8 %collective-permute-start.1 = (f32[9,21,3,24]{3,1,2,0:T(8,128)}, f32[9,21,3,24]{3,1,2,0:T(8,128)}, u32[]{:S(2)}, u32[]{:S(2)}) collective-permute-start(f32[9,21,3,24]{3,1,2,0:T(8,128)} %pad_maximum_fusion.1), channel_id=1, source_target_pairs={{1,0},{2,1},{3,2},{5,4},{6,5},{7,6},{9,8},{10,9},{11,10},{13,12},{... | collective-permute-start | bytes 163304 | tf_op jit(solution)/shard_map/ppermute | solution.py:44
  36.9 11.0 %collective-permute-start.2 = (f32[9,21,3,24]{3,1,2,0:T(8,128)S(1)}, f32[9,21,3,24]{3,1,2,0:T(8,128)S(1)}, u32[]{:S(2)}, u32[]{:S(2)}) collective-permute-start(f32[9,21,3,24]{3,1,2,0:T(8,128)S(1)} %pad_maximum_fusion.2), channel_id=1, source_target_pairs={{0,4},{4,8},{8,12},{12,16},{16,20},{20,24},{24,28},{1,5},{5,9},{9,... | collective-permute-start | bytes 163304 | tf_op jit(solution)/shard_map/ppermute | solution.py:44
  40.3 14.8 %collective-permute-start.3 = (f32[9,21,3,24]{3,1,2,0:T(8,128)S(1)}, f32[9,21,3,24]{3,1,2,0:T(8,128)S(1)}, u32[]{:S(2)}, u32[]{:S(2)}) collective-permute-start(f32[9,21,3,24]{3,1,2,0:T(8,128)S(1)} %pad_maximum_fusion.3), channel_id=1, source_target_pairs={{4,0},{8,4},{12,8},{16,12},{20,16},{24,20},{28,24},{5,1},{9,5},{13... | collective-permute-start | bytes 163304 | tf_op jit(solution)/shard_map/ppermute | solution.py:44
  80.4 9.2 %copy-start.13 = (f32[4,128]{1,0:T(4,128)S(1)}, f32[4,128]{1,0:T(4,128)}, u32[]{:S(2)}) copy-start(f32[4,128]{1,0:T(4,128)} %get-tuple-element.91) | copy-start | bytes 6148
  80.4 9.2 %copy-start.15 = (f32[4,128]{1,0:T(4,128)S(1)}, f32[4,128]{1,0:T(4,128)}, u32[]{:S(2)}) copy-start(f32[4,128]{1,0:T(4,128)} %get-tuple-element.92) | copy-start | bytes 6148
  80.4 9.2 %copy-start.17 = (f32[4,128]{1,0:T(4,128)S(1)}, f32[4,128]{1,0:T(4,128)}, u32[]{:S(2)}) copy-start(f32[4,128]{1,0:T(4,128)} %get-tuple-element.93) | copy-start | bytes 6148
  105.6 12.0 %collective-permute-start.4 = (f32[9,21,3,24]{3,1,2,0:T(8,128)S(1)}, f32[9,21,3,24]{3,1,2,0:T(8,128)S(1)}, u32[]{:S(2)}, u32[]{:S(2)}) collective-permute-start(f32[9,21,3,24]{3,1,2,0:T(8,128)S(1)} %pad_maximum_fusion.4), channel_id=1, source_target_pairs={{0,1},{1,2},{2,3},{4,5},{5,6},{6,7},{8,9},{9,10},{10,11},{12,13},{... | collective-permute-start | bytes 163304 | tf_op jit(solution)/shard_map/ppermute | solution.py:44
  115.7 8.4 %collective-permute-start.5 = (f32[9,21,3,24]{3,1,2,0:T(8,128)S(1)}, f32[9,21,3,24]{3,1,2,0:T(8,128)S(1)}, u32[]{:S(2)}, u32[]{:S(2)}) collective-permute-start(f32[9,21,3,24]{3,1,2,0:T(8,128)S(1)} %pad_maximum_fusion.5), channel_id=1, source_target_pairs={{1,0},{2,1},{3,2},{5,4},{6,5},{7,6},{9,8},{10,9},{11,10},{13,12},{... | collective-permute-start | bytes 163304 | tf_op jit(solution)/shard_map/ppermute | solution.py:44
  124.2 8.9 %collective-permute-start.6 = (f32[9,21,3,24]{3,1,2,0:T(8,128)S(1)}, f32[9,21,3,24]{3,1,2,0:T(8,128)S(1)}, u32[]{:S(2)}, u32[]{:S(2)}) collective-permute-start(f32[9,21,3,24]{3,1,2,0:T(8,128)S(1)} %pad_maximum_fusion.6), channel_id=1, source_target_pairs={{0,4},{4,8},{8,12},{12,16},{16,20},{20,24},{24,28},{1,5},{5,9},{9,... | collective-permute-start | bytes 163304 | tf_op jit(solution)/shard_map/ppermute | solution.py:44
  126.3 12.8 %collective-permute-start.7 = (f32[9,21,3,24]{3,1,2,0:T(8,128)S(1)}, f32[9,21,3,24]{3,1,2,0:T(8,128)S(1)}, u32[]{:S(2)}, u32[]{:S(2)}) collective-permute-start(f32[9,21,3,24]{3,1,2,0:T(8,128)S(1)} %pad_maximum_fusion.7), channel_id=1, source_target_pairs={{4,0},{8,4},{12,8},{16,12},{20,16},{24,20},{28,24},{5,1},{9,5},{13... | collective-permute-start | bytes 163304 | tf_op jit(solution)/shard_map/ppermute | solution.py:44
  139.5 24.9 %copy-start.26 = (pred[512]{0:T(512)(128)(4,1)S(1)}, pred[512]{0:T(512)(128)(4,1)}, u32[]{:S(2)}) copy-start(pred[512]{0:T(512)(128)(4,1)} %compare_bitcast_fusion) | copy-start | bytes 1540
  139.5 24.9 %copy-start.27 = (pred[512]{0:T(512)(128)(4,1)S(1)}, pred[512]{0:T(512)(128)(4,1)}, u32[]{:S(2)}) copy-start(pred[512]{0:T(512)(128)(4,1)} %get-tuple-element.43) | copy-start | bytes 1540
  164.5 9.3 %copy-start.14 = (f32[4,128]{1,0:T(4,128)S(1)}, f32[4,128]{1,0:T(4,128)}, u32[]{:S(2)}) copy-start(f32[4,128]{1,0:T(4,128)} %get-tuple-element.91) | copy-start | bytes 6148
  164.5 9.3 %copy-start.16 = (f32[4,128]{1,0:T(4,128)S(1)}, f32[4,128]{1,0:T(4,128)}, u32[]{:S(2)}) copy-start(f32[4,128]{1,0:T(4,128)} %get-tuple-element.92) | copy-start | bytes 6148
  164.5 9.3 %copy-start.18 = (f32[4,128]{1,0:T(4,128)S(1)}, f32[4,128]{1,0:T(4,128)}, u32[]{:S(2)}) copy-start(f32[4,128]{1,0:T(4,128)} %get-tuple-element.93) | copy-start | bytes 6148
  (18 other events, 86.4 us)
where the time goes:
time: 179 us; the launch traced here: 175 us
  local copies, waits for them, and re-layouts  79.5 us (44%)
  waiting for transfers between devices  25.9 us (14%)
  starting transfers between devices  24.7 us (14%)
  matrix products  21.9 us (12%)
  other arithmetic  21.7 us (12%)
    scatter x2, local copies, waits for them, and re-layouts, per_device(): jnp.zeros_like(flat_faces).at[:, :, targets].set(received, mode='drop')  41.3 us
    ppermute x8, waiting for transfers between devices, shifted(): return lax.ppermute(x, axis, pairs)  25.9 us
    ppermute x8, starting transfers between devices, shifted(): return lax.ppermute(x, axis, pairs)  24.7 us
    select_n x2, other arithmetic, per_device(): jnp.where(inside, local_data, arrived).reshape(9, face_width, 4, elem_count)  11.5 us
    gather x2, local copies, waits for them, and re-layouts, per_device(): local_data = jnp.take(flat_faces, local_index, axis=2)  10.2 us
    dot_general x10, matrix products, predict(): jnp.einsum('dab,qbe->dqae', grad_matrix, derivative, precision=exact_mode)  9.65 us
    dot_general x2, matrix products, face_update(): jnp.einsum('hil,qlfe->hqife', rotate, neighbour_data, precision=exact_mode)  6.89 us
    gather x2, local copies, waits for them, and re-layouts, per_device(): jnp.take(flat_faces, source_index, axis=2) * source_mask  5.91 us
  transfers between devices with their start and end apart: 8, of which 5 were waited for; matrix products, arithmetic and copies ran while one was open for 9% of the time, Pallas kernels for 0%

commit v1 on v0

--- a/solution.py
+++ b/solution.py
@@ -115,29 +115,18 @@
 
 
 def deliver(outgoing):
-    forwarded = {}
-    for col_step in (-1, 1):
-        bundle = jnp.stack(
-            [outgoing[:, :, OFFSETS.index((row_step, col_step))] for row_step in (-1, 0, 1)], axis=2
-        )
-        forwarded[col_step] = shifted(bundle, "pcol", col_step)
-    pieces = {}
-    for col_step in (-1, 1):
-        pieces[OFFSETS.index((0, -col_step))] = forwarded[col_step][:, :, 1]
-    for row_step in (-1, 1):
-        bundle = jnp.stack(
-            [
-                outgoing[:, :, OFFSETS.index((row_step, 0))],
-                forwarded[1][:, :, row_step + 1],
-                forwarded[-1][:, :, row_step + 1],
-            ],
-            axis=2,
-        )
-        arrived_rows = shifted(bundle, "prow", row_step)
-        pieces[OFFSETS.index((-row_step, 0))] = arrived_rows[:, :, 0]
-        pieces[OFFSETS.index((-row_step, -1))] = arrived_rows[:, :, 1]
-        pieces[OFFSETS.index((-row_step, 1))] = arrived_rows[:, :, 2]
-    return jnp.stack([pieces[direction] for direction in range(8)], axis=2)
+    rows = lax.axis_size("prow")
+    cols = lax.axis_size("pcol")
+    pieces = [None] * 8
+    for direction, (row_step, col_step) in enumerate(OFFSETS):
+        pairs = [
+            (r * cols + c, (r + row_step) * cols + (c + col_step))
+            for r in range(rows)
+            for c in range(cols)
+            if 0 <= r + row_step < rows and 0 <= c + col_step < cols
+        ]
+        pieces[7 - direction] = lax.ppermute(outgoing[:, direction], ("prow", "pcol"), pairs)
+    return jnp.stack(pieces, axis=1)
 
 
 def per_device(
@@ -159,29 +148,32 @@
 ):
     elem_count = dof_values.shape[2]
     face_width = face_proj.shape[1]
+    face_total = 4 * elem_count
+    dtype = dof_values.dtype
     values, wave_speed = element_params(material, material_id, normals)
+    face_ids = jnp.arange(face_total, dtype=jnp.int32)
     inside = (neighbour >= 0).reshape(-1)
     local_index = (neighbour_face * elem_count + jnp.maximum(neighbour, 0)).reshape(-1)
+    gather_local = ((local_index[None, :] == face_ids[:, None]) & inside[None, :]).astype(dtype)
     source_ids = send_list[0, 0]
     slot_total = source_ids.shape[1]
-    source_index = jnp.maximum(source_ids, 0).reshape(-1)
-    source_mask = (source_ids >= 0).reshape(-1).astype(dof_values.dtype)
-    targets = jnp.where(recv_list[0, 0] >= 0, recv_list[0, 0], 4 * elem_count).reshape(-1)
+    gather_out = (source_ids.reshape(-1)[None, :] == face_ids[:, None]).astype(dtype)
+    targets = recv_list[0, 0].reshape(-1)
+    scatter_in = ((targets[:, None] == face_ids[None, :]) & ~inside[None, :]).astype(dtype)
     current = dof_values
     for time_index in range(STEPS):
         volume, face_data = local_part(
             current, inv_jacobian, values, grad_matrix, stiff_matrix, face_proj
         )
-        flat_faces = face_data.reshape(9, face_width, 4 * elem_count)
-        outgoing = (jnp.take(flat_faces, source_index, axis=2) * source_mask).reshape(
-            9, face_width, 8, slot_total
-        )
-        received = deliver(outgoing).reshape(9, face_width, 8 * slot_total)
-        arrived = jnp.zeros_like(flat_faces).at[:, :, targets].set(received, mode="drop")
-        local_data = jnp.take(flat_faces, local_index, axis=2)
-        neighbour_data = jnp.where(inside, local_data, arrived).reshape(
-            9, face_width, 4, elem_count
-        )
+        flat_faces = face_data.reshape(9 * face_width, face_total)
+        outgoing = jnp.dot(flat_faces, gather_out, precision=exact_mode).reshape(
+            9 * face_width, 8, slot_total
+        )
+        received = deliver(outgoing).reshape(9 * face_width, 8 * slot_total)
+        neighbour_data = jnp.dot(flat_faces, gather_local, precision=exact_mode) + jnp.dot(
+            received, scatter_in, precision=exact_mode
+        )
+        neighbour_data = neighbour_data.reshape(9, face_width, 4, elem_count)
         current = face_update(
             current,
             volume,

time: 179 us -> 99.6 us (0.56); the launches traced: 175 us -> 98.2 us
  local copies, waits for them, and re-layouts: 79.5 us -> 6.16 us
  starting transfers between devices: 24.7 us -> 47.6 us
  other arithmetic: 21.7 us -> 2.16 us
  waiting for transfers between devices: 25.9 us -> 20.4 us
    scatter x2 -> x0, local copies, waits for them, and re-layouts: 41.3 us -> none  [per_device(): jnp.zeros_like(flat_faces).at[:, :, targets].set(received, mode='drop')]
    ppermute x8 -> x16, starting transfers between devices: 24.7 us -> 47.6 us  [deliver(): lax.ppermute(outgoing[:, direction], ('prow', 'pcol'), pairs)]
    gather x4 -> x0, local copies, waits for them, and re-layouts: 16.1 us -> none  [the longest x2 10.2 us: per_device(): local_data = jnp.take(flat_faces, local_index, axis=2)]
    select_n x4 -> x0, other arithmetic: 12.1 us -> none  [the longest x2 11.5 us: per_device(): jnp.where(inside, local_data, arrived).reshape(9, face_width, 4, elem_count)]
    reshape x4, local copies, waits for them, and re-layouts: 7.47 us -> 0.58 us  [the longest x2 0.31 us: per_device(): flat_faces = face_data.reshape(9 * face_width, face_total)]
    another operation x4 -> x2, local copies, waits for them, and re-layouts: 6.86 us -> 0.01 us  [deliver(): return jnp.stack(pieces, axis=1)]
    ppermute x8 -> x16, waiting for transfers between devices: 25.9 us -> 20.4 us  [deliver(): lax.ppermute(outgoing[:, direction], ('prow', 'pcol'), pairs)]
    dot_general x2, matrix products: 6.89 us -> 2.38 us  [face_update(): jnp.einsum('hil,qlfe->hqife', rotate, neighbour_data, precision=exact_mode)]
  transfers between devices with their start and end apart: 8 -> 16, of which waited for: 5 -> 7; matrix products, arithmetic and copies ran while one was open for 9% -> 2% of each run, Pallas kernels for 0% -> 0%
where the time goes in v1:
time: 99.6 us; the launch traced here: 98.2 us
  starting transfers between devices  47.6 us (48%)
  matrix products  20.4 us (20%)
  waiting for transfers between devices  20.4 us (20%)
  local copies, waits for them, and re-layouts  6.16 us (6%)
  other arithmetic  2.16 us (2%)
  between operations  1.47 us (1%)
    ppermute x16, starting transfers between devices, deliver(): lax.ppermute(outgoing[:, direction], ('prow', 'pcol'), pairs)  47.6 us
    ppermute x16, waiting for transfers between devices, deliver(): lax.ppermute(outgoing[:, direction], ('prow', 'pcol'), pairs)  20.4 us
    dot_general x10, matrix products, predict(): jnp.einsum('dab,qbe->dqae', grad_matrix, derivative, precision=exact_mode)  9.65 us
    unnamed x44, local copies, waits for them, and re-layouts  4.43 us
    dot_general x2, matrix products, face_update(): jnp.einsum('hil,qlfe->hqife', rotate, neighbour_data, precision=exact_mode)  2.38 us
  transfers between devices with their start and end apart: 16, of which 7 were waited for; matrix products, arithmetic and copies ran while one was open for 2% of the time, Pallas kernels for 0%

profile of v1, /device:TPU:25, one launch (start us, length us, event | category | flops | bytes accessed | tf_op | source)
XLA Modules:
  0.0 98.2 jit_solution(5193432116477915806)
XLA Ops:
  1.7 1.9 %multiply_reduce_fusion.33 = (f32[9,56,128]{2,1,0:T(8,128)S(1)}, f32[9,56,128]{2,1,0:T(8,128)S(1)}, f32[9,56,128]{2,1,0:T(8,128)S(1)}) fusion(f32[3,128]{1,0:T(4,128)S(1)} %get-tuple-element.76, f32[3,128]{1,0:T(4,128)S(1)} %get-tuple-element.77, f32[3,128]{1,0:T(4,128)S(1)} %bitcast.341, f32[3,56,56]{2,1,0:T(8,128)S(1)} %copy-done, f32[9,56,128]{2,1,0:T(8,128)} %param.15), kind=kOutput, calls=%fused_computation.64 | convolution fusion | flops 131023872 | bytes 1074432 | tf_op jit(solution)/shard_map/dab,qbe->dqae/dot_general | solution.py:77
  11.2 3.6 %collective-permute-start.7 = (f32[189,24]{0,1:T(8,128)S(1)}, f32[189,24]{0,1:T(8,128)S(1)}, u32[]{:S(2)}, u32[]{:S(2)}) collective-permute-start(f32[189,24]{0,1:T(8,128)S(1)} %get-tuple-element.57), channel_id=1, source_target_pairs={{5,0},{6,1},{7,2},{9,4},{10,5},{11,6},{13,8},{14,9},{15,10},{17,12... | collective-permute-start | bytes 54440 | tf_op jit(solution)/shard_map/ppermute | solution.py:128
  14.8 2.2 %collective-permute-start.6 = (f32[189,24]{0,1:T(8,128)S(1)}, f32[189,24]{0,1:T(8,128)S(1)}, u32[]{:S(2)}, u32[]{:S(2)}) collective-permute-start(f32[189,24]{0,1:T(8,128)S(1)} %get-tuple-element.58), channel_id=1, source_target_pairs={{4,0},{5,1},{6,2},{7,3},{8,4},{9,5},{10,6},{11,7},{12,8},{13,9},{1... | collective-permute-start | bytes 54440 | tf_op jit(solution)/shard_map/ppermute | solution.py:128
  17.0 3.9 %collective-permute-start.5 = (f32[189,24]{0,1:T(8,128)S(1)}, f32[189,24]{0,1:T(8,128)S(1)}, u32[]{:S(2)}, u32[]{:S(2)}) collective-permute-start(f32[189,24]{0,1:T(8,128)S(1)} %get-tuple-element.59), channel_id=1, source_target_pairs={{4,1},{5,2},{6,3},{8,5},{9,6},{10,7},{12,9},{13,10},{14,11},{16,13... | collective-permute-start | bytes 54440 | tf_op jit(solution)/shard_map/ppermute | solution.py:128
  20.9 1.9 %collective-permute-start.4 = (f32[189,24]{0,1:T(8,128)S(1)}, f32[189,24]{0,1:T(8,128)S(1)}, u32[]{:S(2)}, u32[]{:S(2)}) collective-permute-start(f32[189,24]{0,1:T(8,128)S(1)} %get-tuple-element.60), channel_id=1, source_target_pairs={{1,0},{2,1},{3,2},{5,4},{6,5},{7,6},{9,8},{10,9},{11,10},{13,12},{... | collective-permute-start | bytes 54440 | tf_op jit(solution)/shard_map/ppermute | solution.py:128
  22.8 3.8 %collective-permute-start = (f32[189,24]{0,1:T(8,128)S(1)}, f32[189,24]{0,1:T(8,128)S(1)}, u32[]{:S(2)}, u32[]{:S(2)}) collective-permute-start(f32[189,24]{0,1:T(8,128)S(1)} %get-tuple-element.64), channel_id=1, source_target_pairs={{0,5},{1,6},{2,7},{4,9},{5,10},{6,11},{8,13},{9,14},{10,15},{12,17... | collective-permute-start | bytes 54440 | tf_op jit(solution)/shard_map/ppermute | solution.py:128
  29.5 1.9 %collective-permute-start.1 = (f32[189,24]{0,1:T(8,128)S(1)}, f32[189,24]{0,1:T(8,128)S(1)}, u32[]{:S(2)}, u32[]{:S(2)}) collective-permute-start(f32[189,24]{0,1:T(8,128)S(1)} %get-tuple-element.63), channel_id=1, source_target_pairs={{0,4},{1,5},{2,6},{3,7},{4,8},{5,9},{6,10},{7,11},{8,12},{9,13},{1... | collective-permute-start | bytes 54440 | tf_op jit(solution)/shard_map/ppermute | solution.py:128
  31.4 3.5 %collective-permute-done.1 = f32[189,24]{0,1:T(8,128)S(1)} collective-permute-done((f32[189,24]{0,1:T(8,128)S(1)}, f32[189,24]{0,1:T(8,128)S(1)}, u32[]{:S(2)}, u32[]{:S(2)}) %collective-permute-start.1) | collective-permute-done | bytes 18176 | tf_op jit(solution)/shard_map/ppermute | solution.py:128
  35.0 1.9 %collective-permute-start.2 = (f32[189,24]{0,1:T(8,128)S(1)}, f32[189,24]{0,1:T(8,128)S(1)}, u32[]{:S(2)}, u32[]{:S(2)}) collective-permute-start(f32[189,24]{0,1:T(8,128)S(1)} %get-tuple-element.62), channel_id=1, source_target_pairs={{1,4},{2,5},{3,6},{5,8},{6,9},{7,10},{9,12},{10,13},{11,14},{13,16... | collective-permute-start | bytes 54440 | tf_op jit(solution)/shard_map/ppermute | solution.py:128
  36.9 5.0 %collective-permute-done.2 = f32[189,24]{0,1:T(8,128)S(1)} collective-permute-done((f32[189,24]{0,1:T(8,128)S(1)}, f32[189,24]{0,1:T(8,128)S(1)}, u32[]{:S(2)}, u32[]{:S(2)}) %collective-permute-start.2) | collective-permute-done | bytes 18176 | tf_op jit(solution)/shard_map/ppermute | solution.py:128
  41.9 4.3 %collective-permute-start.3 = (f32[189,24]{0,1:T(8,128)S(1)}, f32[189,24]{0,1:T(8,128)S(1)}, u32[]{:S(2)}, u32[]{:S(2)}) collective-permute-start(f32[189,24]{0,1:T(8,128)S(1)} %get-tuple-element.61), channel_id=1, source_target_pairs={{0,1},{1,2},{2,3},{4,5},{5,6},{6,7},{8,9},{9,10},{10,11},{12,13},{... | collective-permute-start | bytes 54440 | tf_op jit(solution)/shard_map/ppermute | solution.py:128
  59.2 1.9 %collective-permute-start.15 = (f32[189,24]{0,1:T(8,128)S(1)}, f32[189,24]{0,1:T(8,128)S(1)}, u32[]{:S(2)}, u32[]{:S(2)}) collective-permute-start(f32[189,24]{0,1:T(8,128)S(1)} %get-tuple-element.49), channel_id=1, source_target_pairs={{5,0},{6,1},{7,2},{9,4},{10,5},{11,6},{13,8},{14,9},{15,10},{17,12... | collective-permute-start | bytes 54440 | tf_op jit(solution)/shard_map/ppermute | solution.py:128
  61.1 1.9 %collective-permute-start.14 = (f32[189,24]{0,1:T(8,128)S(1)}, f32[189,24]{0,1:T(8,128)S(1)}, u32[]{:S(2)}, u32[]{:S(2)}) collective-permute-start(f32[189,24]{0,1:T(8,128)S(1)} %get-tuple-element.50), channel_id=1, source_target_pairs={{4,0},{5,1},{6,2},{7,3},{8,4},{9,5},{10,6},{11,7},{12,8},{13,9},{1... | collective-permute-start | bytes 54440 | tf_op jit(solution)/shard_map/ppermute | solution.py:128
  63.0 5.6 %collective-permute-start.13 = (f32[189,24]{0,1:T(8,128)S(1)}, f32[189,24]{0,1:T(8,128)S(1)}, u32[]{:S(2)}, u32[]{:S(2)}) collective-permute-start(f32[189,24]{0,1:T(8,128)S(1)} %get-tuple-element.51), channel_id=1, source_target_pairs={{4,1},{5,2},{6,3},{8,5},{9,6},{10,7},{12,9},{13,10},{14,11},{16,13... | collective-permute-start | bytes 54440 | tf_op jit(solution)/shard_map/ppermute | solution.py:128
  68.6 1.9 %collective-permute-start.12 = (f32[189,24]{0,1:T(8,128)S(1)}, f32[189,24]{0,1:T(8,128)S(1)}, u32[]{:S(2)}, u32[]{:S(2)}) collective-permute-start(f32[189,24]{0,1:T(8,128)S(1)} %get-tuple-element.52), channel_id=1, source_target_pairs={{1,0},{2,1},{3,2},{5,4},{6,5},{7,6},{9,8},{10,9},{11,10},{13,12},{... | collective-permute-start | bytes 54440 | tf_op jit(solution)/shard_map/ppermute | solution.py:128
  70.5 4.0 %collective-permute-start.8 = (f32[189,24]{0,1:T(8,128)S(1)}, f32[189,24]{0,1:T(8,128)S(1)}, u32[]{:S(2)}, u32[]{:S(2)}) collective-permute-start(f32[189,24]{0,1:T(8,128)S(1)} %get-tuple-element.56), channel_id=1, source_target_pairs={{0,5},{1,6},{2,7},{4,9},{5,10},{6,11},{8,13},{9,14},{10,15},{12,17... | collective-permute-start | bytes 54440 | tf_op jit(solution)/shard_map/ppermute | solution.py:128
  74.7 1.9 %collective-permute-done.8 = f32[189,24]{0,1:T(8,128)S(1)} collective-permute-done((f32[189,24]{0,1:T(8,128)S(1)}, f32[189,24]{0,1:T(8,128)S(1)}, u32[]{:S(2)}, u32[]{:S(2)}) %collective-permute-start.8) | collective-permute-done | bytes 18176 | tf_op jit(solution)/shard_map/ppermute | solution.py:128
  76.6 1.9 %collective-permute-start.9 = (f32[189,24]{0,1:T(8,128)S(1)}, f32[189,24]{0,1:T(8,128)S(1)}, u32[]{:S(2)}, u32[]{:S(2)}) collective-permute-start(f32[189,24]{0,1:T(8,128)S(1)} %get-tuple-element.55), channel_id=1, source_target_pairs={{0,4},{1,5},{2,6},{3,7},{4,8},{5,9},{6,10},{7,11},{8,12},{9,13},{1... | collective-permute-start | bytes 54440 | tf_op jit(solution)/shard_map/ppermute | solution.py:128
  78.5 3.5 %collective-permute-done.9 = f32[189,24]{0,1:T(8,128)S(1)} collective-permute-done((f32[189,24]{0,1:T(8,128)S(1)}, f32[189,24]{0,1:T(8,128)S(1)}, u32[]{:S(2)}, u32[]{:S(2)}) %collective-permute-start.9) | collective-permute-done | bytes 18176 | tf_op jit(solution)/shard_map/ppermute | solution.py:128
  82.0 1.9 %collective-permute-start.10 = (f32[189,24]{0,1:T(8,128)S(1)}, f32[189,24]{0,1:T(8,128)S(1)}, u32[]{:S(2)}, u32[]{:S(2)}) collective-permute-start(f32[189,24]{0,1:T(8,128)S(1)} %get-tuple-element.54), channel_id=1, source_target_pairs={{1,4},{2,5},{3,6},{5,8},{6,9},{7,10},{9,12},{10,13},{11,14},{13,16... | collective-permute-start | bytes 54440 | tf_op jit(solution)/shard_map/ppermute | solution.py:128
  84.0 5.0 %collective-permute-done.10 = f32[189,24]{0,1:T(8,128)S(1)} collective-permute-done((f32[189,24]{0,1:T(8,128)S(1)}, f32[189,24]{0,1:T(8,128)S(1)}, u32[]{:S(2)}, u32[]{:S(2)}) %collective-permute-start.10) | collective-permute-done | bytes 18176 | tf_op jit(solution)/shard_map/ppermute | solution.py:128
  89.0 5.0 %collective-permute-start.11 = (f32[189,24]{0,1:T(8,128)S(1)}, f32[189,24]{0,1:T(8,128)S(1)}, u32[]{:S(2)}, u32[]{:S(2)}) collective-permute-start(f32[189,24]{0,1:T(8,128)S(1)} %get-tuple-element.53), channel_id=1, source_target_pairs={{0,1},{1,2},{2,3},{4,5},{5,6},{6,7},{8,9},{9,10},{10,11},{12,13},{... | collective-permute-start | bytes 54440 | tf_op jit(solution)/shard_map/ppermute | solution.py:128
  95.4 1.2 %fusion.3 = f32[9,21,4,128]{3,1,2,0:T(8,128)S(1)} fusion(f32[3,4,128]{2,0,1:T(4,128)S(1)} %fusion.171, f32[9,21,4,128,1]{3,2,1,0,4:T(4,128)S(1)} %bitcast.333, f32[3,21,21]{2,1,0:T(8,128)S(1)} %copy-done.5), kind=kOutput, calls=%fused_computation.5 | convolution fusion | flops 73640448 | bytes 785580 | tf_op jit(solution)/shard_map/hil,qlfe->hqife/dot_general | solution.py:104
  97.0 1.2 %fusion.5 = f32[9,56,128]{2,1,0:T(8,128)} fusion(f32[9,21,4,128]{3,1,2,0:T(8,128)S(1)} %constant_dynamic-update-slice_fusion.133, f32[9,21,4,128]{3,1,2,0:T(8,128)S(1)} %convolution_bitcast_fusion.14, f32[9,21,4,128]{3,1,2,0:T(8,128)S(1)} %fusion.3, f32[9,56,128]{2,1,0:T(8,128)S(1)} %fusion.4, f32[9,56,128]{2,1,0:T(8,128)S(1)} %constant_dynamic-update-slice_fusion.116, ...), kind=kOutput, calls=%fused_computation.25 | convolution fusion | flops 65544192 | bytes 1956224 | tf_op jit(solution)/shard_map/fai,pife->pae/dot_general | solution.py:113
  (226 shorter events, 25.8 us)
Async XLA Ops:
  0.0 1.7 %copy-start = (f32[3,56,56]{2,1,0:T(8,128)S(1)}, f32[3,56,56]{2,1,0:T(8,128)}, u32[]{:S(2)}) copy-start(f32[3,56,56]{2,1,0:T(8,128)} %param.16) | copy-start | bytes 112900
  7.7 1.0 copy-start.1
  10.8 15.9 %copy-start.6 = (f32[4,3,128]{2,0,1:T(4,128)S(1)}, f32[4,3,128]{2,0,1:T(4,128)}, u32[]{:S(2)}) copy-start(f32[4,3,128]{2,0,1:T(4,128)} %param.24) | copy-start | bytes 18436
  10.8 15.9 %copy-start.8 = (s32[4,128]{1,0:T(4,128)S(1)}, s32[4,128]{1,0:T(4,128)}, u32[]{:S(2)}) copy-start(s32[4,128]{1,0:T(4,128)} %param.26) | copy-start | bytes 6148
  10.8 15.9 %copy-start.10 = (s32[4,128]{1,0:T(4,128)S(1)}, s32[4,128]{1,0:T(4,128)}, u32[]{:S(2)}) copy-start(s32[4,128]{1,0:T(4,128)} %param.27) | copy-start | bytes 6148
  10.8 15.9 %copy-start.11 = (s32[4,128]{1,0:T(4,128)S(1)}, s32[4,128]{1,0:T(4,128)}, u32[]{:S(2)}) copy-start(s32[4,128]{1,0:T(4,128)} %param.25) | copy-start | bytes 6148
  11.2 35.8 %collective-permute-start.7 = (f32[189,24]{0,1:T(8,128)S(1)}, f32[189,24]{0,1:T(8,128)S(1)}, u32[]{:S(2)}, u32[]{:S(2)}) collective-permute-start(f32[189,24]{0,1:T(8,128)S(1)} %get-tuple-element.57), channel_id=1, source_target_pairs={{5,0},{6,1},{7,2},{9,4},{10,5},{11,6},{13,8},{14,9},{15,10},{17,12... | collective-permute-start | bytes 54440 | tf_op jit(solution)/shard_map/ppermute | solution.py:128
  14.8 32.2 %collective-permute-start.6 = (f32[189,24]{0,1:T(8,128)S(1)}, f32[189,24]{0,1:T(8,128)S(1)}, u32[]{:S(2)}, u32[]{:S(2)}) collective-permute-start(f32[189,24]{0,1:T(8,128)S(1)} %get-tuple-element.58), channel_id=1, source_target_pairs={{4,0},{5,1},{6,2},{7,3},{8,4},{9,5},{10,6},{11,7},{12,8},{13,9},{1... | collective-permute-start | bytes 54440 | tf_op jit(solution)/shard_map/ppermute | solution.py:128
  17.0 30.0 %collective-permute-start.5 = (f32[189,24]{0,1:T(8,128)S(1)}, f32[189,24]{0,1:T(8,128)S(1)}, u32[]{:S(2)}, u32[]{:S(2)}) collective-permute-start(f32[189,24]{0,1:T(8,128)S(1)} %get-tuple-element.59), channel_id=1, source_target_pairs={{4,1},{5,2},{6,3},{8,5},{9,6},{10,7},{12,9},{13,10},{14,11},{16,13... | collective-permute-start | bytes 54440 | tf_op jit(solution)/shard_map/ppermute | solution.py:128
  20.9 26.1 %collective-permute-start.4 = (f32[189,24]{0,1:T(8,128)S(1)}, f32[189,24]{0,1:T(8,128)S(1)}, u32[]{:S(2)}, u32[]{:S(2)}) collective-permute-start(f32[189,24]{0,1:T(8,128)S(1)} %get-tuple-element.60), channel_id=1, source_target_pairs={{1,0},{2,1},{3,2},{5,4},{6,5},{7,6},{9,8},{10,9},{11,10},{13,12},{... | collective-permute-start | bytes 54440 | tf_op jit(solution)/shard_map/ppermute | solution.py:128
  22.8 6.7 %collective-permute-start = (f32[189,24]{0,1:T(8,128)S(1)}, f32[189,24]{0,1:T(8,128)S(1)}, u32[]{:S(2)}, u32[]{:S(2)}) collective-permute-start(f32[189,24]{0,1:T(8,128)S(1)} %get-tuple-element.64), channel_id=1, source_target_pairs={{0,5},{1,6},{2,7},{4,9},{5,10},{6,11},{8,13},{9,14},{10,15},{12,17... | collective-permute-start | bytes 54440 | tf_op jit(solution)/shard_map/ppermute | solution.py:128
  26.8 0.9 copy-start.2
  29.5 5.5 %collective-permute-start.1 = (f32[189,24]{0,1:T(8,128)S(1)}, f32[189,24]{0,1:T(8,128)S(1)}, u32[]{:S(2)}, u32[]{:S(2)}) collective-permute-start(f32[189,24]{0,1:T(8,128)S(1)} %get-tuple-element.63), channel_id=1, source_target_pairs={{0,4},{1,5},{2,6},{3,7},{4,8},{5,9},{6,10},{7,11},{8,12},{9,13},{1... | collective-permute-start | bytes 54440 | tf_op jit(solution)/shard_map/ppermute | solution.py:128
  35.0 6.9 %collective-permute-start.2 = (f32[189,24]{0,1:T(8,128)S(1)}, f32[189,24]{0,1:T(8,128)S(1)}, u32[]{:S(2)}, u32[]{:S(2)}) collective-permute-start(f32[189,24]{0,1:T(8,128)S(1)} %get-tuple-element.62), channel_id=1, source_target_pairs={{1,4},{2,5},{3,6},{5,8},{6,9},{7,10},{9,12},{10,13},{11,14},{13,16... | collective-permute-start | bytes 54440 | tf_op jit(solution)/shard_map/ppermute | solution.py:128
  41.9 5.1 %collective-permute-start.3 = (f32[189,24]{0,1:T(8,128)S(1)}, f32[189,24]{0,1:T(8,128)S(1)}, u32[]{:S(2)}, u32[]{:S(2)}) collective-permute-start(f32[189,24]{0,1:T(8,128)S(1)} %get-tuple-element.61), channel_id=1, source_target_pairs={{0,1},{1,2},{2,3},{4,5},{5,6},{6,7},{8,9},{9,10},{10,11},{12,13},{... | collective-permute-start | bytes 54440 | tf_op jit(solution)/shard_map/ppermute | solution.py:128
  49.8 0.8 copy-start.4
  59.2 35.6 %collective-permute-start.15 = (f32[189,24]{0,1:T(8,128)S(1)}, f32[189,24]{0,1:T(8,128)S(1)}, u32[]{:S(2)}, u32[]{:S(2)}) collective-permute-start(f32[189,24]{0,1:T(8,128)S(1)} %get-tuple-element.49), channel_id=1, source_target_pairs={{5,0},{6,1},{7,2},{9,4},{10,5},{11,6},{13,8},{14,9},{15,10},{17,12... | collective-permute-start | bytes 54440 | tf_op jit(solution)/shard_map/ppermute | solution.py:128
  61.1 33.6 %collective-permute-start.14 = (f32[189,24]{0,1:T(8,128)S(1)}, f32[189,24]{0,1:T(8,128)S(1)}, u32[]{:S(2)}, u32[]{:S(2)}) collective-permute-start(f32[189,24]{0,1:T(8,128)S(1)} %get-tuple-element.50), channel_id=1, source_target_pairs={{4,0},{5,1},{6,2},{7,3},{8,4},{9,5},{10,6},{11,7},{12,8},{13,9},{1... | collective-permute-start | bytes 54440 | tf_op jit(solution)/shard_map/ppermute | solution.py:128
  63.0 31.7 %collective-permute-start.13 = (f32[189,24]{0,1:T(8,128)S(1)}, f32[189,24]{0,1:T(8,128)S(1)}, u32[]{:S(2)}, u32[]{:S(2)}) collective-permute-start(f32[189,24]{0,1:T(8,128)S(1)} %get-tuple-element.51), channel_id=1, source_target_pairs={{4,1},{5,2},{6,3},{8,5},{9,6},{10,7},{12,9},{13,10},{14,11},{16,13... | collective-permute-start | bytes 54440 | tf_op jit(solution)/shard_map/ppermute | solution.py:128
  68.6 26.1 %collective-permute-start.12 = (f32[189,24]{0,1:T(8,128)S(1)}, f32[189,24]{0,1:T(8,128)S(1)}, u32[]{:S(2)}, u32[]{:S(2)}) collective-permute-start(f32[189,24]{0,1:T(8,128)S(1)} %get-tuple-element.52), channel_id=1, source_target_pairs={{1,0},{2,1},{3,2},{5,4},{6,5},{7,6},{9,8},{10,9},{11,10},{13,12},{... | collective-permute-start | bytes 54440 | tf_op jit(solution)/shard_map/ppermute | solution.py:128
  70.5 6.0 %collective-permute-start.8 = (f32[189,24]{0,1:T(8,128)S(1)}, f32[189,24]{0,1:T(8,128)S(1)}, u32[]{:S(2)}, u32[]{:S(2)}) collective-permute-start(f32[189,24]{0,1:T(8,128)S(1)} %get-tuple-element.56), channel_id=1, source_target_pairs={{0,5},{1,6},{2,7},{4,9},{5,10},{6,11},{8,13},{9,14},{10,15},{12,17... | collective-permute-start | bytes 54440 | tf_op jit(solution)/shard_map/ppermute | solution.py:128
  76.6 5.5 %collective-permute-start.9 = (f32[189,24]{0,1:T(8,128)S(1)}, f32[189,24]{0,1:T(8,128)S(1)}, u32[]{:S(2)}, u32[]{:S(2)}) collective-permute-start(f32[189,24]{0,1:T(8,128)S(1)} %get-tuple-element.55), channel_id=1, source_target_pairs={{0,4},{1,5},{2,6},{3,7},{4,8},{5,9},{6,10},{7,11},{8,12},{9,13},{1... | collective-permute-start | bytes 54440 | tf_op jit(solution)/shard_map/ppermute | solution.py:128
  82.0 6.9 %collective-permute-start.10 = (f32[189,24]{0,1:T(8,128)S(1)}, f32[189,24]{0,1:T(8,128)S(1)}, u32[]{:S(2)}, u32[]{:S(2)}) collective-permute-start(f32[189,24]{0,1:T(8,128)S(1)} %get-tuple-element.54), channel_id=1, source_target_pairs={{1,4},{2,5},{3,6},{5,8},{6,9},{7,10},{9,12},{10,13},{11,14},{13,16... | collective-permute-start | bytes 54440 | tf_op jit(solution)/shard_map/ppermute | solution.py:128
  89.0 5.7 %collective-permute-start.11 = (f32[189,24]{0,1:T(8,128)S(1)}, f32[189,24]{0,1:T(8,128)S(1)}, u32[]{:S(2)}, u32[]{:S(2)}) collective-permute-start(f32[189,24]{0,1:T(8,128)S(1)} %get-tuple-element.53), channel_id=1, source_target_pairs={{0,1},{1,2},{2,3},{4,5},{5,6},{6,7},{8,9},{9,10},{10,11},{12,13},{... | collective-permute-start | bytes 54440 | tf_op jit(solution)/shard_map/ppermute | solution.py:128
  (4 other events, 2.9 us)

commit v2 on v1

--- a/solution.py
+++ b/solution.py
@@ -114,19 +114,25 @@
     return current + volume - lifted
 
 
-def deliver(outgoing):
-    rows = lax.axis_size("prow")
-    cols = lax.axis_size("pcol")
-    pieces = [None] * 8
-    for direction, (row_step, col_step) in enumerate(OFFSETS):
-        pairs = [
-            (r * cols + c, (r + row_step) * cols + (c + col_step))
-            for r in range(rows)
-            for c in range(cols)
-            if 0 <= r + row_step < rows and 0 <= c + col_step < cols
-        ]
-        pieces[7 - direction] = lax.ppermute(outgoing[:, direction], ("prow", "pcol"), pairs)
-    return jnp.stack(pieces, axis=1)
+SEND_ORDER = (0, 3, 5, 2, 4, 7, 1, 6)
+RECV_ORDER = (4, 3, 6, 5, 7, 1, 0, 2)
+
+
+def deliver(outgoing, slot_total):
+    group = 3 * slot_total
+    left = shifted(outgoing[:group], "pcol", -1)
+    right = shifted(outgoing[group : 2 * group], "pcol", 1)
+    up_bundle = jnp.concatenate(
+        [outgoing[2 * group : 2 * group + slot_total], right[:slot_total], left[:slot_total]], axis=0
+    )
+    down_bundle = jnp.concatenate(
+        [outgoing[2 * group + slot_total :], right[2 * slot_total :], left[2 * slot_total :]], axis=0
+    )
+    up = shifted(up_bundle, "prow", -1)
+    down = shifted(down_bundle, "prow", 1)
+    return jnp.concatenate(
+        [left[slot_total : 2 * slot_total], right[slot_total : 2 * slot_total], up, down], axis=0
+    )
 
 
 def per_device(
@@ -155,10 +161,10 @@
     inside = (neighbour >= 0).reshape(-1)
     local_index = (neighbour_face * elem_count + jnp.maximum(neighbour, 0)).reshape(-1)
     gather_local = ((local_index[None, :] == face_ids[:, None]) & inside[None, :]).astype(dtype)
-    source_ids = send_list[0, 0]
+    source_ids = send_list[0, 0][jnp.array(SEND_ORDER)]
     slot_total = source_ids.shape[1]
-    gather_out = (source_ids.reshape(-1)[None, :] == face_ids[:, None]).astype(dtype)
-    targets = recv_list[0, 0].reshape(-1)
+    gather_out = (source_ids.reshape(-1)[:, None] == face_ids[None, :]).astype(dtype)
+    targets = recv_list[0, 0][jnp.array(RECV_ORDER)].reshape(-1)
     scatter_in = ((targets[:, None] == face_ids[None, :]) & ~inside[None, :]).astype(dtype)
     current = dof_values
     for time_index in range(STEPS):
@@ -166,12 +172,12 @@
             current, inv_jacobian, values, grad_matrix, stiff_matrix, face_proj
         )
         flat_faces = face_data.reshape(9 * face_width, face_total)
-        outgoing = jnp.dot(flat_faces, gather_out, precision=exact_mode).reshape(
-            9 * face_width, 8, slot_total
-        )
-        received = deliver(outgoing).reshape(9 * face_width, 8 * slot_total)
-        neighbour_data = jnp.dot(flat_faces, gather_local, precision=exact_mode) + jnp.dot(
-            received, scatter_in, precision=exact_mode
+        outgoing = lax.dot_general(
+            gather_out, flat_faces, (((1,), (1,)), ((), ())), precision=exact_mode
+        )
+        received = deliver(outgoing, slot_total)
+        neighbour_data = jnp.dot(flat_faces, gather_local, precision=exact_mode) + lax.dot_general(
+            received, scatter_in, (((0,), (0,)), ((), ())), precision=exact_mode
         )
         neighbour_data = neighbour_data.reshape(9, face_width, 4, elem_count)
         current = face_update(

time: 99.6 us -> 64.3 us (0.65)
  starting transfers between devices: 47.6 us -> 21.6 us
  waiting for transfers between devices: 20.4 us -> 11.1 us
    ppermute x16 -> x8, starting transfers between devices: 47.6 us -> 21.6 us  [shifted(): return lax.ppermute(x, axis, pairs)]
    ppermute x16 -> x8, waiting for transfers between devices: 20.4 us -> 11.1 us  [shifted(): return lax.ppermute(x, axis, pairs)]
    gather x0 -> x2, local copies, waits for them, and re-layouts: none -> 1.8 us  [the longest x1 1.24 us: per_device(): source_ids = send_list[0, 0][jnp.array(SEND_ORDER)]]
    unnamed x44 -> x28, local copies, waits for them, and re-layouts: 4.43 us -> 2.98 us
  transfers between devices with their start and end apart: 16 -> 8, of which waited for: 7 -> 4; matrix products, arithmetic and copies ran while one was open for 2% -> 4% of each run, Pallas kernels for 0% -> 0%
where the time goes in v2:
time: 64.3 us; the launch traced here: 63.6 us
  starting transfers between devices  21.6 us (34%)
  matrix products  20.4 us (32%)
  waiting for transfers between devices  11.1 us (17%)
  local copies, waits for them, and re-layouts  6.29 us (10%)
  other arithmetic  2.87 us (4%)
  between operations  1.38 us (2%)
    ppermute x8, starting transfers between devices, shifted(): return lax.ppermute(x, axis, pairs)  21.6 us
    ppermute x8, waiting for transfers between devices, shifted(): return lax.ppermute(x, axis, pairs)  11.1 us
    dot_general x10, matrix products, predict(): jnp.einsum('dab,qbe->dqae', grad_matrix, derivative, precision=exact_mode)  9.65 us
    unnamed x28, local copies, waits for them, and re-layouts  2.98 us
    dot_general x2, matrix products, face_update(): jnp.einsum('hil,qlfe->hqife', rotate, neighbour_data, precision=exact_mode)  2.39 us
    dot_general x2, matrix products, face_update(): jnp.einsum('fai,pife->pae', face_lift, flux_total, precision=exact_mode)  1.78 us
    dot_general x2, matrix products, local_part(): jnp.einsum('dab,qbe->dqae', stiff_matrix, integrated, precision=exact_mode)  1.72 us
    unnamed x112, other arithmetic  1.32 us
  transfers between devices with their start and end apart: 8, of which 4 were waited for; matrix products, arithmetic and copies ran while one was open for 4% of the time, Pallas kernels for 0%

profile of v2, /device:TPU:25, one launch (start us, length us, event | category | flops | bytes accessed | tf_op | source)
XLA Modules:
  0.0 63.6 jit_solution(16912375733532458780)
XLA Ops:
  2.4 1.2 %gather_fusion = s32[8,24]{1,0:T(8,128)S(1)} fusion(s32[8,24]{1,0:T(8,128)} %bitcast.268, s32[1024]{0:T(1024)S(1)} %get-tuple-element.83), kind=kCustom, calls=%fused_computation | custom fusion | bytes 1568 | tf_op jit(solution)/shard_map/gather | solution.py:164
  3.7 1.9 %multiply_reduce_fusion.33 = (f32[9,56,128]{2,1,0:T(8,128)S(1)}, f32[9,56,128]{2,1,0:T(8,128)S(1)}, f32[9,56,128]{2,1,0:T(8,128)S(1)}) fusion(f32[3,128]{1,0:T(4,128)S(1)} %get-tuple-element.80, f32[3,128]{1,0:T(4,128)S(1)} %get-tuple-element.81, f32[3,128]{1,0:T(4,128)S(1)} %bitcast.270, f32[3,56,56]{2,1,0:T(8,128)S(1)} %copy-done, f32[9,56,128]{2,1,0:T(8,128)} %param.17), kind=kOutput, calls=%fused_computation.66 | convolution fusion | flops 131023872 | bytes 1074432 | tf_op jit(solution)/shard_map/dab,qbe->dqae/dot_general | solution.py:77
  5.8 0.9 %multiply_reduce_fusion.30 = (f32[9,56,128]{2,1,0:T(8,128)S(1)}, f32[9,56,128]{2,1,0:T(8,128)S(1)}, f32[9,56,128]{2,1,0:T(8,128)S(1)}) fusion(f32[3,128]{1,0:T(4,128)S(1)} %get-tuple-element.80, f32[3,128]{1,0:T(4,128)S(1)} %get-tuple-element.81, f32[3,128]{1,0:T(4,128)S(1)} %bitcast.271, f32[3,56,56]{2,1,0:T(8,128)S(1)} %copy-done, ...), kind=kOutput, calls=%fused_computation.63 | convolution fusion | flops 131088384 | bytes 1074432 | tf_op jit(solution)/shard_map/dab,qbe->dqae/dot_general | solution.py:77
  6.8 0.9 %multiply_reduce_fusion.27 = (f32[9,56,128]{2,1,0:T(8,128)S(1)}, f32[9,56,128]{2,1,0:T(8,128)S(1)}, f32[9,56,128]{2,1,0:T(8,128)S(1)}) fusion(f32[3,128]{1,0:T(4,128)S(1)} %get-tuple-element.80, f32[3,128]{1,0:T(4,128)S(1)} %get-tuple-element.81, f32[3,128]{1,0:T(4,128)S(1)} %bitcast.272, f32[3,56,56]{2,1,0:T(8,128)S(1)} %copy-done, ...), kind=kOutput, calls=%fused_computation.60 | convolution fusion | flops 131088384 | bytes 1074432 | tf_op jit(solution)/shard_map/dab,qbe->dqae/dot_general | solution.py:77
  7.8 0.9 %multiply_reduce_fusion.24 = (f32[9,56,128]{2,1,0:T(8,128)S(1)}, f32[9,56,128]{2,1,0:T(8,128)S(1)}, f32[9,56,128]{2,1,0:T(8,128)S(1)}) fusion(f32[3,128]{1,0:T(4,128)S(1)} %get-tuple-element.80, f32[3,128]{1,0:T(4,128)S(1)} %get-tuple-element.81, f32[3,128]{1,0:T(4,128)S(1)} %bitcast.273, f32[3,56,56]{2,1,0:T(8,128)S(1)} %copy-done, ...), kind=kOutput, calls=%fused_computation.57 | convolution fusion | flops 131088384 | bytes 1074432 | tf_op jit(solution)/shard_map/dab,qbe->dqae/dot_general | solution.py:77
  8.9 0.9 %multiply_reduce_fusion.21 = (f32[9,56,128]{2,1,0:T(8,128)S(1)}, f32[9,56,128]{2,1,0:T(8,128)S(1)}, f32[9,56,128]{2,1,0:T(8,128)S(1)}) fusion(f32[3,128]{1,0:T(4,128)S(1)} %get-tuple-element.80, f32[3,128]{1,0:T(4,128)S(1)} %get-tuple-element.81, f32[3,128]{1,0:T(4,128)S(1)} %bitcast.274, f32[3,56,56]{2,1,0:T(8,128)S(1)} %copy-done, ...), kind=kOutput, calls=%fused_computation.54 | convolution fusion | flops 131088384 | bytes 1074432 | tf_op jit(solution)/shard_map/dab,qbe->dqae/dot_general | solution.py:77
  12.7 3.7 %collective-permute-start.1 = (f32[72,189]{1,0:T(8,128)S(1)}, f32[72,189]{1,0:T(8,128)S(1)}, u32[]{:S(2)}, u32[]{:S(2)}) collective-permute-start(f32[72,189]{1,0:T(8,128)S(1)} %get-tuple-element.55), channel_id=1, source_target_pairs={{0,1},{1,2},{2,3},{4,5},{5,6},{6,7},{8,9},{9,10},{10,11},{12,13},{... | collective-permute-start | bytes 163304 | tf_op jit(solution)/shard_map/ppermute | solution.py:44
  16.4 1.9 %collective-permute-start = (f32[72,189]{1,0:T(8,128)S(1)}, f32[72,189]{1,0:T(8,128)S(1)}, u32[]{:S(2)}, u32[]{:S(2)}) collective-permute-start(f32[72,189]{1,0:T(8,128)S(1)} %get-tuple-element.56), channel_id=1, source_target_pairs={{1,0},{2,1},{3,2},{5,4},{6,5},{7,6},{9,8},{10,9},{11,10},{13,12},{... | collective-permute-start | bytes 163304 | tf_op jit(solution)/shard_map/ppermute | solution.py:44
  20.1 1.9 %collective-permute-done = f32[72,189]{1,0:T(8,128)S(1)} collective-permute-done((f32[72,189]{1,0:T(8,128)S(1)}, f32[72,189]{1,0:T(8,128)S(1)}, u32[]{:S(2)}, u32[]{:S(2)}) %collective-permute-start) | collective-permute-done | bytes 54464 | tf_op jit(solution)/shard_map/ppermute | solution.py:44
  22.1 3.0 %collective-permute-start.2 = (f32[72,189]{1,0:T(8,128)S(1)}, f32[72,189]{1,0:T(8,128)S(1)}, u32[]{:S(2)}, u32[]{:S(2)}) collective-permute-start(f32[72,189]{1,0:T(8,128)S(1)} %pad_maximum_fusion), channel_id=1, source_target_pairs={{4,0},{8,4},{12,8},{16,12},{20,16},{24,20},{28,24},{5,1},{9,5},{13... | collective-permute-start | bytes 163304 | tf_op jit(solution)/shard_map/ppermute | solution.py:44
  25.1 2.5 %collective-permute-start.3 = (f32[72,189]{1,0:T(8,128)S(1)}, f32[72,189]{1,0:T(8,128)S(1)}, u32[]{:S(2)}, u32[]{:S(2)}) collective-permute-start(f32[72,189]{1,0:T(8,128)S(1)} %pad_maximum_fusion.1), channel_id=1, source_target_pairs={{0,4},{4,8},{8,12},{12,16},{16,20},{20,24},{24,28},{1,5},{5,9},{9,... | collective-permute-start | bytes 163304 | tf_op jit(solution)/shard_map/ppermute | solution.py:44
  28.3 2.9 %collective-permute-done.3 = f32[72,189]{1,0:T(8,128)S(1)} collective-permute-done((f32[72,189]{1,0:T(8,128)S(1)}, f32[72,189]{1,0:T(8,128)S(1)}, u32[]{:S(2)}, u32[]{:S(2)}) %collective-permute-start.3) | collective-permute-done | bytes 54464 | tf_op jit(solution)/shard_map/ppermute | solution.py:44
  32.4 1.2 %fusion.2 = f32[9,21,4,128]{3,1,2,0:T(8,128)S(1)} fusion(f32[3,4,128]{2,0,1:T(4,128)S(1)} %fusion.182, f32[9,21,4,128,1]{3,2,1,0,4:T(4,128)S(1)} %bitcast.263, f32[3,21,21]{2,1,0:T(8,128)S(1)} %copy-done.6), kind=kOutput, calls=%fused_computation.6 | convolution fusion | flops 73640448 | bytes 785580 | tf_op jit(solution)/shard_map/hil,qlfe->hqife/dot_general | solution.py:104
  36.2 0.9 %multiply_reduce_fusion.12 = (f32[9,56,128]{2,1,0:T(8,128)S(1)}, f32[9,56,128]{2,1,0:T(8,128)S(1)}, f32[9,56,128]{2,1,0:T(8,128)S(1)}) fusion(f32[3,128]{1,0:T(4,128)S(1)} %get-tuple-element.80, f32[3,128]{1,0:T(4,128)S(1)} %get-tuple-element.81, f32[3,128]{1,0:T(4,128)S(1)} %bitcast.277, f32[3,56,56]{2,1,0:T(8,128)S(1)} %copy-done, ...), kind=kOutput, calls=%fused_computation.45 | convolution fusion | flops 131088384 | bytes 1074432 | tf_op jit(solution)/shard_map/dab,qbe->dqae/dot_general | solution.py:77
  37.2 0.9 %multiply_reduce_fusion.9 = (f32[9,56,128]{2,1,0:T(8,128)S(1)}, f32[9,56,128]{2,1,0:T(8,128)S(1)}, f32[9,56,128]{2,1,0:T(8,128)S(1)}) fusion(f32[3,128]{1,0:T(4,128)S(1)} %get-tuple-element.80, f32[3,128]{1,0:T(4,128)S(1)} %get-tuple-element.81, f32[3,128]{1,0:T(4,128)S(1)} %bitcast.278, f32[3,56,56]{2,1,0:T(8,128)S(1)} %copy-done, ...), kind=kOutput, calls=%fused_computation.42 | convolution fusion | flops 131088384 | bytes 1074432 | tf_op jit(solution)/shard_map/dab,qbe->dqae/dot_general | solution.py:77
  39.3 0.9 %multiply_reduce_fusion.3 = (f32[9,56,128]{2,1,0:T(8,128)S(1)}, f32[9,56,128]{2,1,0:T(8,128)S(1)}, f32[9,56,128]{2,1,0:T(8,128)S(1)}) fusion(f32[3,128]{1,0:T(4,128)S(1)} %get-tuple-element.80, f32[3,128]{1,0:T(4,128)S(1)} %get-tuple-element.81, f32[3,128]{1,0:T(4,128)S(1)} %bitcast.280, f32[3,56,56]{2,1,0:T(8,128)S(1)} %copy-done, ...), kind=kOutput, calls=%fused_computation.36 | convolution fusion | flops 131088384 | bytes 1074432 | tf_op jit(solution)/shard_map/dab,qbe->dqae/dot_general | solution.py:77
  43.1 3.3 %collective-permute-start.5 = (f32[72,189]{1,0:T(8,128)S(1)}, f32[72,189]{1,0:T(8,128)S(1)}, u32[]{:S(2)}, u32[]{:S(2)}) collective-permute-start(f32[72,189]{1,0:T(8,128)S(1)} %get-tuple-element.51), channel_id=1, source_target_pairs={{0,1},{1,2},{2,3},{4,5},{5,6},{6,7},{8,9},{9,10},{10,11},{12,13},{... | collective-permute-start | bytes 163304 | tf_op jit(solution)/shard_map/ppermute | solution.py:44
  46.6 1.9 %collective-permute-start.4 = (f32[72,189]{1,0:T(8,128)S(1)}, f32[72,189]{1,0:T(8,128)S(1)}, u32[]{:S(2)}, u32[]{:S(2)}) collective-permute-start(f32[72,189]{1,0:T(8,128)S(1)} %get-tuple-element.52), channel_id=1, source_target_pairs={{1,0},{2,1},{3,2},{5,4},{6,5},{7,6},{9,8},{10,9},{11,10},{13,12},{... | collective-permute-start | bytes 163304 | tf_op jit(solution)/shard_map/ppermute | solution.py:44
  48.5 3.7 %collective-permute-done.4 = f32[72,189]{1,0:T(8,128)S(1)} collective-permute-done((f32[72,189]{1,0:T(8,128)S(1)}, f32[72,189]{1,0:T(8,128)S(1)}, u32[]{:S(2)}, u32[]{:S(2)}) %collective-permute-start.4) | collective-permute-done | bytes 54464 | tf_op jit(solution)/shard_map/ppermute | solution.py:44
  52.2 1.9 %collective-permute-start.6 = (f32[72,189]{1,0:T(8,128)S(1)}, f32[72,189]{1,0:T(8,128)S(1)}, u32[]{:S(2)}, u32[]{:S(2)}) collective-permute-start(f32[72,189]{1,0:T(8,128)S(1)} %pad_maximum_fusion.2), channel_id=1, source_target_pairs={{4,0},{8,4},{12,8},{16,12},{20,16},{24,20},{28,24},{5,1},{9,5},{13... | collective-permute-start | bytes 163304 | tf_op jit(solution)/shard_map/ppermute | solution.py:44
  54.2 3.4 %collective-permute-start.7 = (f32[72,189]{1,0:T(8,128)S(1)}, f32[72,189]{1,0:T(8,128)S(1)}, u32[]{:S(2)}, u32[]{:S(2)}) collective-permute-start(f32[72,189]{1,0:T(8,128)S(1)} %pad_maximum_fusion.3), channel_id=1, source_target_pairs={{0,4},{4,8},{8,12},{12,16},{16,20},{20,24},{24,28},{1,5},{5,9},{9,... | collective-permute-start | bytes 163304 | tf_op jit(solution)/shard_map/ppermute | solution.py:44
  57.6 2.6 %collective-permute-done.7 = f32[72,189]{1,0:T(8,128)S(1)} collective-permute-done((f32[72,189]{1,0:T(8,128)S(1)}, f32[72,189]{1,0:T(8,128)S(1)}, u32[]{:S(2)}, u32[]{:S(2)}) %collective-permute-start.7) | collective-permute-done | bytes 54464 | tf_op jit(solution)/shard_map/ppermute | solution.py:44
  60.8 1.2 %fusion.3 = f32[9,21,4,128]{3,1,2,0:T(8,128)S(1)} fusion(f32[3,4,128]{2,0,1:T(4,128)S(1)} %fusion.182, f32[9,21,4,128,1]{3,2,1,0,4:T(4,128)S(1)} %bitcast.262, f32[3,21,21]{2,1,0:T(8,128)S(1)} %copy-done.6), kind=kOutput, calls=%fused_computation.7 | convolution fusion | flops 73640448 | bytes 785580 | tf_op jit(solution)/shard_map/hil,qlfe->hqife/dot_general | solution.py:104
  62.4 1.2 %fusion.5 = f32[9,56,128]{2,1,0:T(8,128)} fusion(f32[9,21,4,128]{3,1,2,0:T(8,128)S(1)} %constant_dynamic-update-slice_fusion.117, f32[9,21,4,128]{3,1,2,0:T(8,128)S(1)} %convolution_bitcast_fusion.14, f32[9,21,4,128]{3,1,2,0:T(8,128)S(1)} %fusion.3, f32[9,56,128]{2,1,0:T(8,128)S(1)} %fusion.4, f32[9,56,128]{2,1,0:T(8,128)S(1)} %constant_dynamic-update-slice_fusion.108, ...), kind=kOutput, calls=%fused_computation.27 | convolution fusion | flops 65544192 | bytes 1956224 | tf_op jit(solution)/shard_map/fai,pife->pae/dot_general | solution.py:113
  (204 shorter events, 16.8 us)
Async XLA Ops:
  0.0 3.7 %copy-start = (f32[3,56,56]{2,1,0:T(8,128)S(1)}, f32[3,56,56]{2,1,0:T(8,128)}, u32[]{:S(2)}) copy-start(f32[3,56,56]{2,1,0:T(8,128)} %param.18) | copy-start | bytes 112900
  9.7 1.0 %copy-start.1 = (f32[9,56,128]{2,1,0:T(8,128)S(1)}, f32[9,56,128]{2,1,0:T(8,128)}, u32[]{:S(2)}) copy-start(f32[9,56,128]{2,1,0:T(8,128)} %param.17) | copy-start | bytes 774148
  10.7 0.8 %copy-start.4 = (f32[4,21,56]{2,0,1:T(4,128)S(1)}, f32[4,21,56]{2,0,1:T(4,128)}, u32[]{:S(2)}) copy-start(f32[4,21,56]{2,0,1:T(4,128)} %param.20) | copy-start | bytes 56452
  12.2 6.1 %copy-start.8 = (s32[4,128]{1,0:T(4,128)S(1)}, s32[4,128]{1,0:T(4,128)}, u32[]{:S(2)}) copy-start(s32[4,128]{1,0:T(4,128)} %param.28) | copy-start | bytes 6148
  12.2 6.1 %copy-start.9 = (s32[4,128]{1,0:T(4,128)S(1)}, s32[4,128]{1,0:T(4,128)}, u32[]{:S(2)}) copy-start(s32[4,128]{1,0:T(4,128)} %param.29) | copy-start | bytes 6148
  12.2 6.2 %copy-start.7 = (f32[4,3,128]{2,0,1:T(4,128)S(1)}, f32[4,3,128]{2,0,1:T(4,128)}, u32[]{:S(2)}) copy-start(f32[4,3,128]{2,0,1:T(4,128)} %param.26) | copy-start | bytes 18436
  12.3 6.2 %copy-start.10 = (s32[4,128]{1,0:T(4,128)S(1)}, s32[4,128]{1,0:T(4,128)}, u32[]{:S(2)}) copy-start(s32[4,128]{1,0:T(4,128)} %param.27) | copy-start | bytes 6148
  12.3 6.2 %copy-start.2 = (f32[3,56,56]{2,1,0:T(8,128)S(1)}, f32[3,56,56]{2,1,0:T(8,128)}, u32[]{:S(2)}) copy-start(f32[3,56,56]{2,1,0:T(8,128)} %param.19) | copy-start | bytes 112900
  12.7 7.4 %collective-permute-start.1 = (f32[72,189]{1,0:T(8,128)S(1)}, f32[72,189]{1,0:T(8,128)S(1)}, u32[]{:S(2)}, u32[]{:S(2)}) collective-permute-start(f32[72,189]{1,0:T(8,128)S(1)} %get-tuple-element.55), channel_id=1, source_target_pairs={{0,1},{1,2},{2,3},{4,5},{5,6},{6,7},{8,9},{9,10},{10,11},{12,13},{... | collective-permute-start | bytes 163304 | tf_op jit(solution)/shard_map/ppermute | solution.py:44
  16.4 5.7 %collective-permute-start = (f32[72,189]{1,0:T(8,128)S(1)}, f32[72,189]{1,0:T(8,128)S(1)}, u32[]{:S(2)}, u32[]{:S(2)}) collective-permute-start(f32[72,189]{1,0:T(8,128)S(1)} %get-tuple-element.56), channel_id=1, source_target_pairs={{1,0},{2,1},{3,2},{5,4},{6,5},{7,6},{9,8},{10,9},{11,10},{13,12},{... | collective-permute-start | bytes 163304 | tf_op jit(solution)/shard_map/ppermute | solution.py:44
  20.1 7.5 %copy-start.3 = (s32[1,1,8,24]{3,2,1,0:T(8,128)S(1)}, s32[1,1,8,24]{3,2,1,0:T(8,128)}, u32[]{:S(2)}) copy-start(s32[1,1,8,24]{3,2,1,0:T(8,128)} %param.31) | copy-start | bytes 2308
  22.1 6.2 %collective-permute-start.2 = (f32[72,189]{1,0:T(8,128)S(1)}, f32[72,189]{1,0:T(8,128)S(1)}, u32[]{:S(2)}, u32[]{:S(2)}) collective-permute-start(f32[72,189]{1,0:T(8,128)S(1)} %pad_maximum_fusion), channel_id=1, source_target_pairs={{4,0},{8,4},{12,8},{16,12},{20,16},{24,20},{28,24},{5,1},{9,5},{13... | collective-permute-start | bytes 163304 | tf_op jit(solution)/shard_map/ppermute | solution.py:44
  25.1 6.0 %collective-permute-start.3 = (f32[72,189]{1,0:T(8,128)S(1)}, f32[72,189]{1,0:T(8,128)S(1)}, u32[]{:S(2)}, u32[]{:S(2)}) collective-permute-start(f32[72,189]{1,0:T(8,128)S(1)} %pad_maximum_fusion.1), channel_id=1, source_target_pairs={{0,4},{4,8},{8,12},{12,16},{16,20},{20,24},{24,28},{1,5},{5,9},{9,... | collective-permute-start | bytes 163304 | tf_op jit(solution)/shard_map/ppermute | solution.py:44
  31.6 0.8 %copy-start.6 = (f32[3,21,21]{2,1,0:T(8,128)S(1)}, f32[3,21,21]{2,1,0:T(8,128)}, u32[]{:S(2)}) copy-start(f32[3,21,21]{2,1,0:T(8,128)} %param.22) | copy-start | bytes 15880
  33.9 0.8 %copy-start.5 = (f32[4,56,21]{1,0,2:T(4,128)S(1)}, f32[4,56,21]{1,0,2:T(4,128)}, u32[]{:S(2)}) copy-start(f32[4,56,21]{1,0,2:T(4,128)} %param.21) | copy-start | bytes 56452
  43.1 5.4 %collective-permute-start.5 = (f32[72,189]{1,0:T(8,128)S(1)}, f32[72,189]{1,0:T(8,128)S(1)}, u32[]{:S(2)}, u32[]{:S(2)}) collective-permute-start(f32[72,189]{1,0:T(8,128)S(1)} %get-tuple-element.51), channel_id=1, source_target_pairs={{0,1},{1,2},{2,3},{4,5},{5,6},{6,7},{8,9},{9,10},{10,11},{12,13},{... | collective-permute-start | bytes 163304 | tf_op jit(solution)/shard_map/ppermute | solution.py:44
  46.6 5.7 %collective-permute-start.4 = (f32[72,189]{1,0:T(8,128)S(1)}, f32[72,189]{1,0:T(8,128)S(1)}, u32[]{:S(2)}, u32[]{:S(2)}) collective-permute-start(f32[72,189]{1,0:T(8,128)S(1)} %get-tuple-element.52), channel_id=1, source_target_pairs={{1,0},{2,1},{3,2},{5,4},{6,5},{7,6},{9,8},{10,9},{11,10},{13,12},{... | collective-permute-start | bytes 163304 | tf_op jit(solution)/shard_map/ppermute | solution.py:44
  52.2 5.3 %collective-permute-start.6 = (f32[72,189]{1,0:T(8,128)S(1)}, f32[72,189]{1,0:T(8,128)S(1)}, u32[]{:S(2)}, u32[]{:S(2)}) collective-permute-start(f32[72,189]{1,0:T(8,128)S(1)} %pad_maximum_fusion.2), channel_id=1, source_target_pairs={{4,0},{8,4},{12,8},{16,12},{20,16},{24,20},{28,24},{5,1},{9,5},{13... | collective-permute-start | bytes 163304 | tf_op jit(solution)/shard_map/ppermute | solution.py:44
  54.2 6.0 %collective-permute-start.7 = (f32[72,189]{1,0:T(8,128)S(1)}, f32[72,189]{1,0:T(8,128)S(1)}, u32[]{:S(2)}, u32[]{:S(2)}) collective-permute-start(f32[72,189]{1,0:T(8,128)S(1)} %pad_maximum_fusion.3), channel_id=1, source_target_pairs={{0,4},{4,8},{8,12},{12,16},{16,20},{20,24},{24,28},{1,5},{5,9},{9,... | collective-permute-start | bytes 163304 | tf_op jit(solution)/shard_map/ppermute | solution.py:44

commit v3 on v2

--- a/solution.py
+++ b/solution.py
@@ -8,6 +8,7 @@
 
 
 exact_mode = lax.Precision.HIGHEST
+fast_mode = lax.Precision.HIGH
 time_step = 0.8
 OFFSETS = ((-1, -1), (-1, 0), (-1, 1), (0, -1), (0, 1), (1, -1), (1, 0), (1, 1))
 ENTRIES = (
@@ -74,7 +75,7 @@
     integrated = time_step * current
     factor = time_step
     for power_level in range(1, ORDER):
-        slopes = jnp.einsum("dab,qbe->dqae", grad_matrix, derivative, precision=exact_mode)
+        slopes = jnp.einsum("dab,qbe->dqae", grad_matrix, derivative, precision=fast_mode)
         derivative = -star_apply(slopes, inv_jacobian, values)
         factor = factor * time_step / (power_level + 1)
         integrated = integrated + factor * derivative
@@ -83,9 +84,9 @@
 
 def local_part(current, inv_jacobian, values, grad_matrix, stiff_matrix, face_proj):
     integrated = predict(current, inv_jacobian, values, grad_matrix)
-    slopes = jnp.einsum("dab,qbe->dqae", stiff_matrix, integrated, precision=exact_mode)
+    slopes = jnp.einsum("dab,qbe->dqae", stiff_matrix, integrated, precision=fast_mode)
     volume = star_apply(slopes, inv_jacobian, values)
-    face_data = jnp.einsum("fib,qbe->qife", face_proj, integrated, precision=exact_mode)
+    face_data = jnp.einsum("fib,qbe->qife", face_proj, integrated, precision=fast_mode)
     return (volume, face_data)
 
 
@@ -101,7 +102,7 @@
     rotate,
     face_lift,
 ):
-    turned = jnp.einsum("hil,qlfe->hqife", rotate, neighbour_data, precision=exact_mode)
+    turned = jnp.einsum("hil,qlfe->hqife", rotate, neighbour_data, precision=fast_mode)
     chosen = (orientation[None] == jnp.arange(3, dtype=jnp.int32)[:, None, None]).astype(
         current.dtype
     )
@@ -110,7 +111,7 @@
     apart = face_data - turned
     parts = [normals[:, k, :][None, None] * both for k in range(3)]
     flux_total = 0.5 * (elastic_apply(parts, values) + wave_speed[None, None] * apart)
-    lifted = jnp.einsum("fai,pife->pae", face_lift, flux_total, precision=exact_mode)
+    lifted = jnp.einsum("fai,pife->pae", face_lift, flux_total, precision=fast_mode)
     return current + volume - lifted
 
 

time: 64.3 us -> 59 us (0.918)
  matrix products: 20.4 us -> 14.8 us
    dot_general x18, matrix products: 16.6 us -> 11 us  [the longest x10 6.45 us: predict(): jnp.einsum('dab,qbe->dqae', grad_matrix, derivative, precision=fast_mode)]
where the time goes in v3:
time: 59 us; the launch traced here: 58.4 us
  starting transfers between devices  21.6 us (37%)
  matrix products  14.8 us (25%)
  waiting for transfers between devices  11.4 us (19%)
  local copies, waits for them, and re-layouts  6.29 us (11%)
  other arithmetic  2.87 us (5%)
  between operations  1.38 us (2%)
    ppermute x8, starting transfers between devices, shifted(): return lax.ppermute(x, axis, pairs)  21.6 us
    ppermute x8, waiting for transfers between devices, shifted(): return lax.ppermute(x, axis, pairs)  11.4 us
    dot_general x10, matrix products, predict(): jnp.einsum('dab,qbe->dqae', grad_matrix, derivative, precision=fast_mode)  6.45 us
    unnamed x28, local copies, waits for them, and re-layouts  2.98 us
    dot_general x2, matrix products, face_update(): jnp.einsum('fai,pife->pae', face_lift, flux_total, precision=fast_mode)  1.46 us
    dot_general x2, matrix products, face_update(): jnp.einsum('hil,qlfe->hqife', rotate, neighbour_data, precision=fast_mode)  1.36 us
    unnamed x112, other arithmetic  1.32 us
    gather x1, local copies, waits for them, and re-layouts, per_device(): source_ids = send_list[0, 0][jnp.array(SEND_ORDER)]  1.24 us
  transfers between devices with their start and end apart: 8, of which 4 were waited for; matrix products, arithmetic and copies ran while one was open for 4% of the time, Pallas kernels for 0%

profile of v3, /device:TPU:25, one launch (start us, length us, event | category | flops | bytes accessed | tf_op | source)
XLA Modules:
  0.0 58.4 jit_solution(17046783329300900923)
XLA Ops:
  0.0 0.8 %convolution_bitcast_fusion.18 = f32[3,128]{1,0:T(4,128)S(1)} fusion(f32[16,3]{0,1:T(4,128)} %param.23, s32[128]{0:T(128)} %param.24), kind=kOutput, calls=%fused_computation.28 | convolution fusion | flops 75776 | bytes 2240 | tf_op jit(solution)/shard_map/dot_general | solution.py:51
  0.9 0.8 %fusion.197 = (f32[3,1,128]{2,1,0:T(1,128)S(1)}, f32[3,1,128]{2,1,0:T(1,128)S(1)}, f32[3,1,128]{2,1,0:T(1,128)S(1)}) fusion(f32[3,3,128]{2,1,0:T(4,128)} %param.25), kind=kLoop, calls=%fused_computation.581 | loop fusion | bytes 9216 | tf_op jit(solution)/shard_map/slice | solution.py:69
  1.7 0.7 %pad_clamp_fusion = (s32[1024]{0:T(1024)S(1)}, s32[1024]{0:T(1024)S(1)}) fusion(s32[8]{0:T(128)} %constant.44, s32[8]{0:T(128)} %constant.43), kind=kLoop, calls=%fused_computation.550 | loop fusion | flops 2048 | bytes 8256 | tf_op jit(solution)/shard_map/gather | solution.py:168
  2.4 1.2 %gather_fusion = s32[8,24]{1,0:T(8,128)S(1)} fusion(s32[8,24]{1,0:T(8,128)} %bitcast.268, s32[1024]{0:T(1024)S(1)} %get-tuple-element.83), kind=kCustom, calls=%fused_computation | custom fusion | bytes 1568 | tf_op jit(solution)/shard_map/gather | solution.py:165
  3.7 1.6 %multiply_reduce_fusion.33 = (f32[9,56,128]{2,1,0:T(8,128)S(1)}, f32[9,56,128]{2,1,0:T(8,128)S(1)}, f32[9,56,128]{2,1,0:T(8,128)S(1)}) fusion(f32[3,128]{1,0:T(4,128)S(1)} %get-tuple-element.80, f32[3,128]{1,0:T(4,128)S(1)} %get-tuple-element.81, f32[3,128]{1,0:T(4,128)S(1)} %bitcast.270, f32[3,56,56]{2,1,0:T(8,128)S(1)} %copy-done, f32[9,56,128]{2,1,0:T(8,128)} %param.17), kind=kOutput, calls=%fused_computation.66 | convolution fusion | flops 65995776 | bytes 1074432 | tf_op jit(solution)/shard_map/dab,qbe->dqae/dot_general | solution.py:78
  8.3 0.8 %copy-done.1 = f32[9,56,128]{2,1,0:T(8,128)S(1)} copy-done((f32[9,56,128]{2,1,0:T(8,128)S(1)}, f32[9,56,128]{2,1,0:T(8,128)}, u32[]{:S(2)}) %copy-start.1) | copy-done | bytes 258072
  9.2 0.6 %copy-done.4 = f32[4,21,56]{2,0,1:T(4,128)S(1)} copy-done((f32[4,21,56]{2,0,1:T(4,128)S(1)}, f32[4,21,56]{2,0,1:T(4,128)}, u32[]{:S(2)}) %copy-start.4) | copy-done | bytes 18840
  10.9 3.7 %collective-permute-start.1 = (f32[72,189]{1,0:T(8,128)S(1)}, f32[72,189]{1,0:T(8,128)S(1)}, u32[]{:S(2)}, u32[]{:S(2)}) collective-permute-start(f32[72,189]{1,0:T(8,128)S(1)} %get-tuple-element.55), channel_id=1, source_target_pairs={{0,1},{1,2},{2,3},{4,5},{5,6},{6,7},{8,9},{9,10},{10,11},{12,13},{... | collective-permute-start | bytes 163304 | tf_op jit(solution)/shard_map/ppermute | solution.py:45
  14.6 1.9 %collective-permute-start = (f32[72,189]{1,0:T(8,128)S(1)}, f32[72,189]{1,0:T(8,128)S(1)}, u32[]{:S(2)}, u32[]{:S(2)}) collective-permute-start(f32[72,189]{1,0:T(8,128)S(1)} %get-tuple-element.56), channel_id=1, source_target_pairs={{1,0},{2,1},{3,2},{5,4},{6,5},{7,6},{9,8},{10,9},{11,10},{13,12},{... | collective-permute-start | bytes 163304 | tf_op jit(solution)/shard_map/ppermute | solution.py:45
  18.1 2.2 %collective-permute-done = f32[72,189]{1,0:T(8,128)S(1)} collective-permute-done((f32[72,189]{1,0:T(8,128)S(1)}, f32[72,189]{1,0:T(8,128)S(1)}, u32[]{:S(2)}, u32[]{:S(2)}) %collective-permute-start) | collective-permute-done | bytes 54464 | tf_op jit(solution)/shard_map/ppermute | solution.py:45
  20.3 3.0 %collective-permute-start.2 = (f32[72,189]{1,0:T(8,128)S(1)}, f32[72,189]{1,0:T(8,128)S(1)}, u32[]{:S(2)}, u32[]{:S(2)}) collective-permute-start(f32[72,189]{1,0:T(8,128)S(1)} %pad_maximum_fusion), channel_id=1, source_target_pairs={{4,0},{8,4},{12,8},{16,12},{20,16},{24,20},{28,24},{5,1},{9,5},{13... | collective-permute-start | bytes 163304 | tf_op jit(solution)/shard_map/ppermute | solution.py:45
  23.3 2.5 %collective-permute-start.3 = (f32[72,189]{1,0:T(8,128)S(1)}, f32[72,189]{1,0:T(8,128)S(1)}, u32[]{:S(2)}, u32[]{:S(2)}) collective-permute-start(f32[72,189]{1,0:T(8,128)S(1)} %pad_maximum_fusion.1), channel_id=1, source_target_pairs={{0,4},{4,8},{8,12},{12,16},{16,20},{20,24},{24,28},{1,5},{5,9},{9,... | collective-permute-start | bytes 163304 | tf_op jit(solution)/shard_map/ppermute | solution.py:45
  26.5 2.9 %collective-permute-done.3 = f32[72,189]{1,0:T(8,128)S(1)} collective-permute-done((f32[72,189]{1,0:T(8,128)S(1)}, f32[72,189]{1,0:T(8,128)S(1)}, u32[]{:S(2)}, u32[]{:S(2)}) %collective-permute-start.3) | collective-permute-done | bytes 54464 | tf_op jit(solution)/shard_map/ppermute | solution.py:45
  30.0 0.6 %copy-done.6 = f32[3,21,21]{2,1,0:T(8,128)S(1)} copy-done((f32[3,21,21]{2,1,0:T(8,128)S(1)}, f32[3,21,21]{2,1,0:T(8,128)}, u32[]{:S(2)}) %copy-start.6) | copy-done | bytes 5316
  30.6 0.7 %fusion.2 = f32[9,21,4,128]{3,1,2,0:T(8,128)S(1)} fusion(f32[3,4,128]{2,0,1:T(4,128)S(1)} %fusion.182, f32[9,21,4,128,1]{3,2,1,0,4:T(4,128)S(1)} %bitcast.263, f32[3,21,21]{2,1,0:T(8,128)S(1)} %copy-done.6), kind=kOutput, calls=%fused_computation.6 | convolution fusion | flops 37062144 | bytes 785580 | tf_op jit(solution)/shard_map/hil,qlfe->hqife/dot_general | solution.py:105
  31.7 0.7 %copy-done.5 = f32[4,56,21]{1,0,2:T(4,128)S(1)} copy-done((f32[4,56,21]{1,0,2:T(4,128)S(1)}, f32[4,56,21]{1,0,2:T(4,128)}, u32[]{:S(2)}) %copy-start.5) | copy-done | bytes 18840
  38.5 3.3 %collective-permute-start.5 = (f32[72,189]{1,0:T(8,128)S(1)}, f32[72,189]{1,0:T(8,128)S(1)}, u32[]{:S(2)}, u32[]{:S(2)}) collective-permute-start(f32[72,189]{1,0:T(8,128)S(1)} %get-tuple-element.51), channel_id=1, source_target_pairs={{0,1},{1,2},{2,3},{4,5},{5,6},{6,7},{8,9},{9,10},{10,11},{12,13},{... | collective-permute-start | bytes 163304 | tf_op jit(solution)/shard_map/ppermute | solution.py:45
  42.0 1.9 %collective-permute-start.4 = (f32[72,189]{1,0:T(8,128)S(1)}, f32[72,189]{1,0:T(8,128)S(1)}, u32[]{:S(2)}, u32[]{:S(2)}) collective-permute-start(f32[72,189]{1,0:T(8,128)S(1)} %get-tuple-element.52), channel_id=1, source_target_pairs={{1,0},{2,1},{3,2},{5,4},{6,5},{7,6},{9,8},{10,9},{11,10},{13,12},{... | collective-permute-start | bytes 163304 | tf_op jit(solution)/shard_map/ppermute | solution.py:45
  43.9 3.7 %collective-permute-done.4 = f32[72,189]{1,0:T(8,128)S(1)} collective-permute-done((f32[72,189]{1,0:T(8,128)S(1)}, f32[72,189]{1,0:T(8,128)S(1)}, u32[]{:S(2)}, u32[]{:S(2)}) %collective-permute-start.4) | collective-permute-done | bytes 54464 | tf_op jit(solution)/shard_map/ppermute | solution.py:45
  47.7 1.9 %collective-permute-start.6 = (f32[72,189]{1,0:T(8,128)S(1)}, f32[72,189]{1,0:T(8,128)S(1)}, u32[]{:S(2)}, u32[]{:S(2)}) collective-permute-start(f32[72,189]{1,0:T(8,128)S(1)} %pad_maximum_fusion.2), channel_id=1, source_target_pairs={{4,0},{8,4},{12,8},{16,12},{20,16},{24,20},{28,24},{5,1},{9,5},{13... | collective-permute-start | bytes 163304 | tf_op jit(solution)/shard_map/ppermute | solution.py:45
  49.6 3.4 %collective-permute-start.7 = (f32[72,189]{1,0:T(8,128)S(1)}, f32[72,189]{1,0:T(8,128)S(1)}, u32[]{:S(2)}, u32[]{:S(2)}) collective-permute-start(f32[72,189]{1,0:T(8,128)S(1)} %pad_maximum_fusion.3), channel_id=1, source_target_pairs={{0,4},{4,8},{8,12},{12,16},{16,20},{20,24},{24,28},{1,5},{5,9},{9,... | collective-permute-start | bytes 163304 | tf_op jit(solution)/shard_map/ppermute | solution.py:45
  53.0 2.6 %collective-permute-done.7 = f32[72,189]{1,0:T(8,128)S(1)} collective-permute-done((f32[72,189]{1,0:T(8,128)S(1)}, f32[72,189]{1,0:T(8,128)S(1)}, u32[]{:S(2)}, u32[]{:S(2)}) %collective-permute-start.7) | collective-permute-done | bytes 54464 | tf_op jit(solution)/shard_map/ppermute | solution.py:45
  56.2 0.7 %fusion.3 = f32[9,21,4,128]{3,1,2,0:T(8,128)S(1)} fusion(f32[3,4,128]{2,0,1:T(4,128)S(1)} %fusion.182, f32[9,21,4,128,1]{3,2,1,0,4:T(4,128)S(1)} %bitcast.262, f32[3,21,21]{2,1,0:T(8,128)S(1)} %copy-done.6), kind=kOutput, calls=%fused_computation.7 | convolution fusion | flops 37062144 | bytes 785580 | tf_op jit(solution)/shard_map/hil,qlfe->hqife/dot_general | solution.py:105
  57.3 1.1 %fusion.5 = f32[9,56,128]{2,1,0:T(8,128)} fusion(f32[9,21,4,128]{3,1,2,0:T(8,128)S(1)} %constant_dynamic-update-slice_fusion.117, f32[9,21,4,128]{3,1,2,0:T(8,128)S(1)} %convolution_bitcast_fusion.14, f32[9,21,4,128]{3,1,2,0:T(8,128)S(1)} %fusion.3, f32[9,56,128]{2,1,0:T(8,128)S(1)} %fusion.4, f32[9,56,128]{2,1,0:T(8,128)S(1)} %constant_dynamic-update-slice_fusion.108, ...), kind=kOutput, calls=%fused_computation.27 | convolution fusion | flops 33030144 | bytes 1956224 | tf_op jit(solution)/shard_map/fai,pife->pae/dot_general | solution.py:114
  (204 shorter events, 13.7 us)
Async XLA Ops:
  0.0 3.7 %copy-start = (f32[3,56,56]{2,1,0:T(8,128)S(1)}, f32[3,56,56]{2,1,0:T(8,128)}, u32[]{:S(2)}) copy-start(f32[3,56,56]{2,1,0:T(8,128)} %param.18) | copy-start | bytes 112900
  8.1 1.0 %copy-start.1 = (f32[9,56,128]{2,1,0:T(8,128)S(1)}, f32[9,56,128]{2,1,0:T(8,128)}, u32[]{:S(2)}) copy-start(f32[9,56,128]{2,1,0:T(8,128)} %param.17) | copy-start | bytes 774148
  9.1 0.8 %copy-start.4 = (f32[4,21,56]{2,0,1:T(4,128)S(1)}, f32[4,21,56]{2,0,1:T(4,128)}, u32[]{:S(2)}) copy-start(f32[4,21,56]{2,0,1:T(4,128)} %param.20) | copy-start | bytes 56452
  10.4 6.1 %copy-start.8 = (s32[4,128]{1,0:T(4,128)S(1)}, s32[4,128]{1,0:T(4,128)}, u32[]{:S(2)}) copy-start(s32[4,128]{1,0:T(4,128)} %param.28) | copy-start | bytes 6148
  10.4 6.2 %copy-start.9 = (s32[4,128]{1,0:T(4,128)S(1)}, s32[4,128]{1,0:T(4,128)}, u32[]{:S(2)}) copy-start(s32[4,128]{1,0:T(4,128)} %param.29) | copy-start | bytes 6148
  10.5 6.2 %copy-start.7 = (f32[4,3,128]{2,0,1:T(4,128)S(1)}, f32[4,3,128]{2,0,1:T(4,128)}, u32[]{:S(2)}) copy-start(f32[4,3,128]{2,0,1:T(4,128)} %param.26) | copy-start | bytes 18436
  10.5 6.2 %copy-start.10 = (s32[4,128]{1,0:T(4,128)S(1)}, s32[4,128]{1,0:T(4,128)}, u32[]{:S(2)}) copy-start(s32[4,128]{1,0:T(4,128)} %param.27) | copy-start | bytes 6148
  10.5 6.2 %copy-start.2 = (f32[3,56,56]{2,1,0:T(8,128)S(1)}, f32[3,56,56]{2,1,0:T(8,128)}, u32[]{:S(2)}) copy-start(f32[3,56,56]{2,1,0:T(8,128)} %param.19) | copy-start | bytes 112900
  10.9 7.1 %collective-permute-start.1 = (f32[72,189]{1,0:T(8,128)S(1)}, f32[72,189]{1,0:T(8,128)S(1)}, u32[]{:S(2)}, u32[]{:S(2)}) collective-permute-start(f32[72,189]{1,0:T(8,128)S(1)} %get-tuple-element.55), channel_id=1, source_target_pairs={{0,1},{1,2},{2,3},{4,5},{5,6},{6,7},{8,9},{9,10},{10,11},{12,13},{... | collective-permute-start | bytes 163304 | tf_op jit(solution)/shard_map/ppermute | solution.py:45
  14.6 5.7 %collective-permute-start = (f32[72,189]{1,0:T(8,128)S(1)}, f32[72,189]{1,0:T(8,128)S(1)}, u32[]{:S(2)}, u32[]{:S(2)}) collective-permute-start(f32[72,189]{1,0:T(8,128)S(1)} %get-tuple-element.56), channel_id=1, source_target_pairs={{1,0},{2,1},{3,2},{5,4},{6,5},{7,6},{9,8},{10,9},{11,10},{13,12},{... | collective-permute-start | bytes 163304 | tf_op jit(solution)/shard_map/ppermute | solution.py:45
  18.0 7.8 %copy-start.3 = (s32[1,1,8,24]{3,2,1,0:T(8,128)S(1)}, s32[1,1,8,24]{3,2,1,0:T(8,128)}, u32[]{:S(2)}) copy-start(s32[1,1,8,24]{3,2,1,0:T(8,128)} %param.31) | copy-start | bytes 2308
  20.3 6.2 %collective-permute-start.2 = (f32[72,189]{1,0:T(8,128)S(1)}, f32[72,189]{1,0:T(8,128)S(1)}, u32[]{:S(2)}, u32[]{:S(2)}) collective-permute-start(f32[72,189]{1,0:T(8,128)S(1)} %pad_maximum_fusion), channel_id=1, source_target_pairs={{4,0},{8,4},{12,8},{16,12},{20,16},{24,20},{28,24},{5,1},{9,5},{13... | collective-permute-start | bytes 163304 | tf_op jit(solution)/shard_map/ppermute | solution.py:45
  23.3 6.0 %collective-permute-start.3 = (f32[72,189]{1,0:T(8,128)S(1)}, f32[72,189]{1,0:T(8,128)S(1)}, u32[]{:S(2)}, u32[]{:S(2)}) collective-permute-start(f32[72,189]{1,0:T(8,128)S(1)} %pad_maximum_fusion.1), channel_id=1, source_target_pairs={{0,4},{4,8},{8,12},{12,16},{16,20},{20,24},{24,28},{1,5},{5,9},{9,... | collective-permute-start | bytes 163304 | tf_op jit(solution)/shard_map/ppermute | solution.py:45
  29.8 0.8 %copy-start.6 = (f32[3,21,21]{2,1,0:T(8,128)S(1)}, f32[3,21,21]{2,1,0:T(8,128)}, u32[]{:S(2)}) copy-start(f32[3,21,21]{2,1,0:T(8,128)} %param.22) | copy-start | bytes 15880
  31.6 0.8 %copy-start.5 = (f32[4,56,21]{1,0,2:T(4,128)S(1)}, f32[4,56,21]{1,0,2:T(4,128)}, u32[]{:S(2)}) copy-start(f32[4,56,21]{1,0,2:T(4,128)} %param.21) | copy-start | bytes 56452
  38.5 5.4 %collective-permute-start.5 = (f32[72,189]{1,0:T(8,128)S(1)}, f32[72,189]{1,0:T(8,128)S(1)}, u32[]{:S(2)}, u32[]{:S(2)}) collective-permute-start(f32[72,189]{1,0:T(8,128)S(1)} %get-tuple-element.51), channel_id=1, source_target_pairs={{0,1},{1,2},{2,3},{4,5},{5,6},{6,7},{8,9},{9,10},{10,11},{12,13},{... | collective-permute-start | bytes 163304 | tf_op jit(solution)/shard_map/ppermute | solution.py:45
  42.0 5.7 %collective-permute-start.4 = (f32[72,189]{1,0:T(8,128)S(1)}, f32[72,189]{1,0:T(8,128)S(1)}, u32[]{:S(2)}, u32[]{:S(2)}) collective-permute-start(f32[72,189]{1,0:T(8,128)S(1)} %get-tuple-element.52), channel_id=1, source_target_pairs={{1,0},{2,1},{3,2},{5,4},{6,5},{7,6},{9,8},{10,9},{11,10},{13,12},{... | collective-permute-start | bytes 163304 | tf_op jit(solution)/shard_map/ppermute | solution.py:45
  47.7 5.3 %collective-permute-start.6 = (f32[72,189]{1,0:T(8,128)S(1)}, f32[72,189]{1,0:T(8,128)S(1)}, u32[]{:S(2)}, u32[]{:S(2)}) collective-permute-start(f32[72,189]{1,0:T(8,128)S(1)} %pad_maximum_fusion.2), channel_id=1, source_target_pairs={{4,0},{8,4},{12,8},{16,12},{20,16},{24,20},{28,24},{5,1},{9,5},{13... | collective-permute-start | bytes 163304 | tf_op jit(solution)/shard_map/ppermute | solution.py:45
  49.6 6.0 %collective-permute-start.7 = (f32[72,189]{1,0:T(8,128)S(1)}, f32[72,189]{1,0:T(8,128)S(1)}, u32[]{:S(2)}, u32[]{:S(2)}) collective-permute-start(f32[72,189]{1,0:T(8,128)S(1)} %pad_maximum_fusion.3), channel_id=1, source_target_pairs={{0,4},{4,8},{8,12},{12,16},{16,20},{20,24},{24,28},{1,5},{5,9},{9,... | collective-permute-start | bytes 163304 | tf_op jit(solution)/shard_map/ppermute | solution.py:45

commit v4 on v3

--- a/solution.py
+++ b/solution.py
@@ -47,8 +47,8 @@
 
 def element_params(material, material_id, normals):
     id_range = jnp.arange(material.shape[0], dtype=jnp.int32)
-    onehot = (material_id[None, :] == id_range[:, None]).astype(material.dtype)
-    params = jnp.dot(material.T, onehot, precision=exact_mode)
+    chosen = material_id[None, None, :] == id_range[:, None, None]
+    params = jnp.sum(jnp.where(chosen, material[:, :, None], 0.0), axis=0)
     density, lame_first, shear_modulus = (params[0], params[1], params[2])
     values = (-(lame_first + 2.0 * shear_modulus), -lame_first, -shear_modulus, -1.0 / density)
     wave_speed = jnp.sqrt((lame_first + 2.0 * shear_modulus) / density) * jnp.sum(
@@ -162,10 +162,10 @@
     inside = (neighbour >= 0).reshape(-1)
     local_index = (neighbour_face * elem_count + jnp.maximum(neighbour, 0)).reshape(-1)
     gather_local = ((local_index[None, :] == face_ids[:, None]) & inside[None, :]).astype(dtype)
-    source_ids = send_list[0, 0][jnp.array(SEND_ORDER)]
+    source_ids = jnp.concatenate([send_list[0, 0, d : d + 1] for d in SEND_ORDER], axis=0)
     slot_total = source_ids.shape[1]
     gather_out = (source_ids.reshape(-1)[:, None] == face_ids[None, :]).astype(dtype)
-    targets = recv_list[0, 0][jnp.array(RECV_ORDER)].reshape(-1)
+    targets = jnp.concatenate([recv_list[0, 0, d] for d in RECV_ORDER], axis=0)
     scatter_in = ((targets[:, None] == face_ids[None, :]) & ~inside[None, :]).astype(dtype)
     current = dof_values
     for time_index in range(STEPS):

time: 59 us -> 58.8 us (level)
  matrix products: 14.8 us -> 14 us
  other arithmetic: 2.87 us -> 3.65 us
  local copies, waits for them, and re-layouts: 6.29 us -> 5.52 us
  waiting for transfers between devices: 11.4 us -> 12 us
    gather x2 -> x0, local copies, waits for them, and re-layouts: 1.8 us -> none  [the longest x1 1.24 us: per_device(): source_ids = send_list[0, 0][jnp.array(SEND_ORDER)]]
    squeeze x0 -> x2, local copies, waits for them, and re-layouts: none -> 1 us  [the longest x1 0.99 us: per_device(): send_list[0, 0, d:d + 1]]
    dot_general x1 -> x0, matrix products: 0.85 us -> none  [element_params(): params = jnp.dot(material.T, onehot, precision=exact_mode)]
    reduce_sum x0 -> x1, other arithmetic: none -> 0.77 us  [element_params(): params = jnp.sum(jnp.where(chosen, material[:, :, None], 0.0), axis=0)]
    eq x0 -> x1, other arithmetic: none -> 0.69 us  [element_params(): chosen = material_id[None, None, :] == id_range[:, None, None]]
    gather x1 -> x0, other arithmetic: 0.68 us -> none  [per_device(): targets = recv_list[0, 0][jnp.array(RECV_ORDER)].reshape(-1)]
  transfers between devices with their start and end apart: 8 -> 8, of which waited for: 4 -> 4; matrix products, arithmetic and copies ran while one was open for 4% -> 3% of each run, Pallas kernels for 0% -> 0%
where the time goes in v4:
time: 58.8 us; the launch traced here: 58.1 us
  starting transfers between devices  21.6 us (37%)
  matrix products  14 us (24%)
  waiting for transfers between devices  12 us (20%)
  local copies, waits for them, and re-layouts  5.52 us (9%)
  other arithmetic  3.65 us (6%)
  between operations  1.38 us (2%)
    ppermute x8, starting transfers between devices, shifted(): return lax.ppermute(x, axis, pairs)  21.6 us
    ppermute x8, waiting for transfers between devices, shifted(): return lax.ppermute(x, axis, pairs)  12 us
    dot_general x10, matrix products, predict(): jnp.einsum('dab,qbe->dqae', grad_matrix, derivative, precision=fast_mode)  6.45 us
    unnamed x28, local copies, waits for them, and re-layouts  2.98 us
    dot_general x2, matrix products, face_update(): jnp.einsum('fai,pife->pae', face_lift, flux_total, precision=fast_mode)  1.46 us
    dot_general x2, matrix products, face_update(): jnp.einsum('hil,qlfe->hqife', rotate, neighbour_data, precision=fast_mode)  1.36 us
    unnamed x112, other arithmetic  1.32 us
    dot_general x2, matrix products, per_device(): jnp.dot(flat_faces, gather_local, precision=exact_mode)  1.22 us
  transfers between devices with their start and end apart: 8, of which 4 were waited for; matrix products, arithmetic and copies ran while one was open for 3% of the time, Pallas kernels for 0%

profile of v4, /device:TPU:25, one launch (start us, length us, event | category | flops | bytes accessed | tf_op | source)
XLA Modules:
  0.0 58.1 jit_solution(2296093758803014782)
XLA Ops:
  0.0 0.7 %iota_compare_fusion.6 = pred[16,128]{1,0:T(8,128)(4,1)S(1)} fusion(s32[128]{0:T(128)} %param.22), kind=kLoop, calls=%fused_computation.545 | loop fusion | flops 2048 | bytes 2560 | tf_op jit(solution)/shard_map/eq | solution.py:50
  0.7 0.8 %select_reduce_fusion = f32[3,128]{1,0:T(4,128)S(1)} fusion(f32[16,3]{0,1:T(4,128)} %param.21, pred[16,128]{1,0:T(8,128)(4,1)S(1)} %iota_compare_fusion.6), kind=kLoop, calls=%fused_computation.543 | loop fusion | flops 11904 | bytes 3776 | tf_op jit(solution)/shard_map/reduce_sum | solution.py:51
  1.5 1.0 %slice_bitcast_fusion.11 = (s32[1,24]{1,0:T(1,128)S(1)}, s32[1,24]{1,0:T(1,128)S(1)}, s32[1,24]{1,0:T(1,128)S(1)}, s32[1,24]{1,0:T(1,128)S(1)}, s32[1,24]{1,0:T(...) fusion(s32[1,1,8,24]{3,2,1,0:T(8,128)} %param.28), kind=kLoop, calls=%fused_computation.566 | loop fusion | bytes 1536 | tf_op jit(solution)/shard_map/squeeze | solution.py:165
  2.6 0.8 %fusion.196 = (f32[3,1,128]{2,1,0:T(1,128)S(1)}, f32[3,1,128]{2,1,0:T(1,128)S(1)}, f32[3,1,128]{2,1,0:T(1,128)S(1)}) fusion(f32[3,3,128]{2,1,0:T(4,128)} %param.23), kind=kLoop, calls=%fused_computation.592 | loop fusion | bytes 9216 | tf_op jit(solution)/shard_map/slice | solution.py:69
  3.4 1.6 %multiply_reduce_fusion.33 = (f32[9,56,128]{2,1,0:T(8,128)S(1)}, f32[9,56,128]{2,1,0:T(8,128)S(1)}, f32[9,56,128]{2,1,0:T(8,128)S(1)}) fusion(f32[3,128]{1,0:T(4,128)S(1)} %get-tuple-element.96, f32[3,128]{1,0:T(4,128)S(1)} %get-tuple-element.97, f32[3,128]{1,0:T(4,128)S(1)} %bitcast.295, f32[3,56,56]{2,1,0:T(8,128)S(1)} %copy-done, f32[9,56,128]{2,1,0:T(8,128)} %param.15), kind=kOutput, calls=%fused_computation.63 | convolution fusion | flops 65995776 | bytes 1074432 | tf_op jit(solution)/shard_map/dab,qbe->dqae/dot_general | solution.py:78
  8.0 0.8 %copy-done.1 = f32[9,56,128]{2,1,0:T(8,128)S(1)} copy-done((f32[9,56,128]{2,1,0:T(8,128)S(1)}, f32[9,56,128]{2,1,0:T(8,128)}, u32[]{:S(2)}) %copy-start.1) | copy-done | bytes 258072
  9.0 0.6 %copy-done.3 = f32[4,21,56]{2,0,1:T(4,128)S(1)} copy-done((f32[4,21,56]{2,0,1:T(4,128)S(1)}, f32[4,21,56]{2,0,1:T(4,128)}, u32[]{:S(2)}) %copy-start.3) | copy-done | bytes 18840
  10.6 3.7 %collective-permute-start.1 = (f32[72,189]{1,0:T(8,128)S(1)}, f32[72,189]{1,0:T(8,128)S(1)}, u32[]{:S(2)}, u32[]{:S(2)}) collective-permute-start(f32[72,189]{1,0:T(8,128)S(1)} %get-tuple-element.55), channel_id=1, source_target_pairs={{0,1},{1,2},{2,3},{4,5},{5,6},{6,7},{8,9},{9,10},{10,11},{12,13},{... | collective-permute-start | bytes 163304 | tf_op jit(solution)/shard_map/ppermute | solution.py:45
  14.3 1.9 %collective-permute-start = (f32[72,189]{1,0:T(8,128)S(1)}, f32[72,189]{1,0:T(8,128)S(1)}, u32[]{:S(2)}, u32[]{:S(2)}) collective-permute-start(f32[72,189]{1,0:T(8,128)S(1)} %get-tuple-element.56), channel_id=1, source_target_pairs={{1,0},{2,1},{3,2},{5,4},{6,5},{7,6},{9,8},{10,9},{11,10},{13,12},{... | collective-permute-start | bytes 163304 | tf_op jit(solution)/shard_map/ppermute | solution.py:45
  17.8 2.2 %collective-permute-done = f32[72,189]{1,0:T(8,128)S(1)} collective-permute-done((f32[72,189]{1,0:T(8,128)S(1)}, f32[72,189]{1,0:T(8,128)S(1)}, u32[]{:S(2)}, u32[]{:S(2)}) %collective-permute-start) | collective-permute-done | bytes 54464 | tf_op jit(solution)/shard_map/ppermute | solution.py:45
  20.0 3.0 %collective-permute-start.2 = (f32[72,189]{1,0:T(8,128)S(1)}, f32[72,189]{1,0:T(8,128)S(1)}, u32[]{:S(2)}, u32[]{:S(2)}) collective-permute-start(f32[72,189]{1,0:T(8,128)S(1)} %pad_maximum_fusion), channel_id=1, source_target_pairs={{4,0},{8,4},{12,8},{16,12},{20,16},{24,20},{28,24},{5,1},{9,5},{13... | collective-permute-start | bytes 163304 | tf_op jit(solution)/shard_map/ppermute | solution.py:45
  23.1 2.5 %collective-permute-start.3 = (f32[72,189]{1,0:T(8,128)S(1)}, f32[72,189]{1,0:T(8,128)S(1)}, u32[]{:S(2)}, u32[]{:S(2)}) collective-permute-start(f32[72,189]{1,0:T(8,128)S(1)} %pad_maximum_fusion.1), channel_id=1, source_target_pairs={{0,4},{4,8},{8,12},{12,16},{16,20},{20,24},{24,28},{1,5},{5,9},{9,... | collective-permute-start | bytes 163304 | tf_op jit(solution)/shard_map/ppermute | solution.py:45
  25.6 3.4 %collective-permute-done.3 = f32[72,189]{1,0:T(8,128)S(1)} collective-permute-done((f32[72,189]{1,0:T(8,128)S(1)}, f32[72,189]{1,0:T(8,128)S(1)}, u32[]{:S(2)}, u32[]{:S(2)}) %collective-permute-start.3) | collective-permute-done | bytes 54464 | tf_op jit(solution)/shard_map/ppermute | solution.py:45
  29.7 0.6 %copy-done.5 = f32[3,21,21]{2,1,0:T(8,128)S(1)} copy-done((f32[3,21,21]{2,1,0:T(8,128)S(1)}, f32[3,21,21]{2,1,0:T(8,128)}, u32[]{:S(2)}) %copy-start.5) | copy-done | bytes 5316
  30.3 0.7 %fusion.2 = f32[9,21,4,128]{3,1,2,0:T(8,128)S(1)} fusion(f32[3,4,128]{2,0,1:T(4,128)S(1)} %fusion.182, f32[9,21,4,128,1]{3,2,1,0,4:T(4,128)S(1)} %bitcast.290, f32[3,21,21]{2,1,0:T(8,128)S(1)} %copy-done.5), kind=kOutput, calls=%fused_computation.4 | convolution fusion | flops 37062144 | bytes 785580 | tf_op jit(solution)/shard_map/hil,qlfe->hqife/dot_general | solution.py:105
  31.4 0.7 %copy-done.4 = f32[4,56,21]{1,0,2:T(4,128)S(1)} copy-done((f32[4,56,21]{1,0,2:T(4,128)S(1)}, f32[4,56,21]{1,0,2:T(4,128)}, u32[]{:S(2)}) %copy-start.4) | copy-done | bytes 18840
  38.2 3.3 %collective-permute-start.5 = (f32[72,189]{1,0:T(8,128)S(1)}, f32[72,189]{1,0:T(8,128)S(1)}, u32[]{:S(2)}, u32[]{:S(2)}) collective-permute-start(f32[72,189]{1,0:T(8,128)S(1)} %get-tuple-element.51), channel_id=1, source_target_pairs={{0,1},{1,2},{2,3},{4,5},{5,6},{6,7},{8,9},{9,10},{10,11},{12,13},{... | collective-permute-start | bytes 163304 | tf_op jit(solution)/shard_map/ppermute | solution.py:45
  41.7 1.9 %collective-permute-start.4 = (f32[72,189]{1,0:T(8,128)S(1)}, f32[72,189]{1,0:T(8,128)S(1)}, u32[]{:S(2)}, u32[]{:S(2)}) collective-permute-start(f32[72,189]{1,0:T(8,128)S(1)} %get-tuple-element.52), channel_id=1, source_target_pairs={{1,0},{2,1},{3,2},{5,4},{6,5},{7,6},{9,8},{10,9},{11,10},{13,12},{... | collective-permute-start | bytes 163304 | tf_op jit(solution)/shard_map/ppermute | solution.py:45
  43.7 3.7 %collective-permute-done.4 = f32[72,189]{1,0:T(8,128)S(1)} collective-permute-done((f32[72,189]{1,0:T(8,128)S(1)}, f32[72,189]{1,0:T(8,128)S(1)}, u32[]{:S(2)}, u32[]{:S(2)}) %collective-permute-start.4) | collective-permute-done | bytes 54464 | tf_op jit(solution)/shard_map/ppermute | solution.py:45
  47.4 1.9 %collective-permute-start.6 = (f32[72,189]{1,0:T(8,128)S(1)}, f32[72,189]{1,0:T(8,128)S(1)}, u32[]{:S(2)}, u32[]{:S(2)}) collective-permute-start(f32[72,189]{1,0:T(8,128)S(1)} %pad_maximum_fusion.2), channel_id=1, source_target_pairs={{4,0},{8,4},{12,8},{16,12},{20,16},{24,20},{28,24},{5,1},{9,5},{13... | collective-permute-start | bytes 163304 | tf_op jit(solution)/shard_map/ppermute | solution.py:45
  49.3 3.4 %collective-permute-start.7 = (f32[72,189]{1,0:T(8,128)S(1)}, f32[72,189]{1,0:T(8,128)S(1)}, u32[]{:S(2)}, u32[]{:S(2)}) collective-permute-start(f32[72,189]{1,0:T(8,128)S(1)} %pad_maximum_fusion.3), channel_id=1, source_target_pairs={{0,4},{4,8},{8,12},{12,16},{16,20},{20,24},{24,28},{1,5},{5,9},{9,... | collective-permute-start | bytes 163304 | tf_op jit(solution)/shard_map/ppermute | solution.py:45
  52.7 2.6 %collective-permute-done.7 = f32[72,189]{1,0:T(8,128)S(1)} collective-permute-done((f32[72,189]{1,0:T(8,128)S(1)}, f32[72,189]{1,0:T(8,128)S(1)}, u32[]{:S(2)}, u32[]{:S(2)}) %collective-permute-start.7) | collective-permute-done | bytes 54464 | tf_op jit(solution)/shard_map/ppermute | solution.py:45
  56.0 0.7 %fusion.3 = f32[9,21,4,128]{3,1,2,0:T(8,128)S(1)} fusion(f32[3,4,128]{2,0,1:T(4,128)S(1)} %fusion.182, f32[9,21,4,128,1]{3,2,1,0,4:T(4,128)S(1)} %bitcast.289, f32[3,21,21]{2,1,0:T(8,128)S(1)} %copy-done.5), kind=kOutput, calls=%fused_computation.5 | convolution fusion | flops 37062144 | bytes 785580 | tf_op jit(solution)/shard_map/hil,qlfe->hqife/dot_general | solution.py:105
  57.0 1.1 %fusion.5 = f32[9,56,128]{2,1,0:T(8,128)} fusion(f32[9,21,4,128]{3,1,2,0:T(8,128)S(1)} %constant_dynamic-update-slice_fusion.117, f32[9,21,4,128]{3,1,2,0:T(8,128)S(1)} %convolution_bitcast_fusion.14, f32[9,21,4,128]{3,1,2,0:T(8,128)S(1)} %fusion.3, f32[9,56,128]{2,1,0:T(8,128)S(1)} %fusion.4, f32[9,56,128]{2,1,0:T(8,128)S(1)} %constant_dynamic-update-slice_fusion.108, ...), kind=kOutput, calls=%fused_computation.25 | convolution fusion | flops 33030144 | bytes 1956224 | tf_op jit(solution)/shard_map/fai,pife->pae/dot_general | solution.py:114
  (205 shorter events, 13.1 us)
Async XLA Ops:
  0.0 3.4 %copy-start = (f32[3,56,56]{2,1,0:T(8,128)S(1)}, f32[3,56,56]{2,1,0:T(8,128)}, u32[]{:S(2)}) copy-start(f32[3,56,56]{2,1,0:T(8,128)} %param.16) | copy-start | bytes 112900
  7.9 1.0 %copy-start.1 = (f32[9,56,128]{2,1,0:T(8,128)S(1)}, f32[9,56,128]{2,1,0:T(8,128)}, u32[]{:S(2)}) copy-start(f32[9,56,128]{2,1,0:T(8,128)} %param.15) | copy-start | bytes 774148
  8.8 0.8 %copy-start.3 = (f32[4,21,56]{2,0,1:T(4,128)S(1)}, f32[4,21,56]{2,0,1:T(4,128)}, u32[]{:S(2)}) copy-start(f32[4,21,56]{2,0,1:T(4,128)} %param.18) | copy-start | bytes 56452
  10.1 6.1 %copy-start.7 = (s32[4,128]{1,0:T(4,128)S(1)}, s32[4,128]{1,0:T(4,128)}, u32[]{:S(2)}) copy-start(s32[4,128]{1,0:T(4,128)} %param.26) | copy-start | bytes 6148
  10.2 6.1 %copy-start.9 = (s32[4,128]{1,0:T(4,128)S(1)}, s32[4,128]{1,0:T(4,128)}, u32[]{:S(2)}) copy-start(s32[4,128]{1,0:T(4,128)} %param.27) | copy-start | bytes 6148
  10.2 6.2 %copy-start.8 = (s32[1,1,8,24]{3,2,1,0:T(8,128)S(1)}, s32[1,1,8,24]{3,2,1,0:T(8,128)}, u32[]{:S(2)}) copy-start(s32[1,1,8,24]{3,2,1,0:T(8,128)} %param.29) | copy-start | bytes 2308
  10.2 6.2 %copy-start.6 = (f32[4,3,128]{2,0,1:T(4,128)S(1)}, f32[4,3,128]{2,0,1:T(4,128)}, u32[]{:S(2)}) copy-start(f32[4,3,128]{2,0,1:T(4,128)} %param.24) | copy-start | bytes 18436
  10.2 6.2 %copy-start.10 = (s32[4,128]{1,0:T(4,128)S(1)}, s32[4,128]{1,0:T(4,128)}, u32[]{:S(2)}) copy-start(s32[4,128]{1,0:T(4,128)} %param.25) | copy-start | bytes 6148
  10.2 6.2 %copy-start.2 = (f32[3,56,56]{2,1,0:T(8,128)S(1)}, f32[3,56,56]{2,1,0:T(8,128)}, u32[]{:S(2)}) copy-start(f32[3,56,56]{2,1,0:T(8,128)} %param.17) | copy-start | bytes 112900
  10.6 7.1 %collective-permute-start.1 = (f32[72,189]{1,0:T(8,128)S(1)}, f32[72,189]{1,0:T(8,128)S(1)}, u32[]{:S(2)}, u32[]{:S(2)}) collective-permute-start(f32[72,189]{1,0:T(8,128)S(1)} %get-tuple-element.55), channel_id=1, source_target_pairs={{0,1},{1,2},{2,3},{4,5},{5,6},{6,7},{8,9},{9,10},{10,11},{12,13},{... | collective-permute-start | bytes 163304 | tf_op jit(solution)/shard_map/ppermute | solution.py:45
  14.3 5.7 %collective-permute-start = (f32[72,189]{1,0:T(8,128)S(1)}, f32[72,189]{1,0:T(8,128)S(1)}, u32[]{:S(2)}, u32[]{:S(2)}) collective-permute-start(f32[72,189]{1,0:T(8,128)S(1)} %get-tuple-element.56), channel_id=1, source_target_pairs={{1,0},{2,1},{3,2},{5,4},{6,5},{7,6},{9,8},{10,9},{11,10},{13,12},{... | collective-permute-start | bytes 163304 | tf_op jit(solution)/shard_map/ppermute | solution.py:45
  20.0 5.6 %collective-permute-start.2 = (f32[72,189]{1,0:T(8,128)S(1)}, f32[72,189]{1,0:T(8,128)S(1)}, u32[]{:S(2)}, u32[]{:S(2)}) collective-permute-start(f32[72,189]{1,0:T(8,128)S(1)} %pad_maximum_fusion), channel_id=1, source_target_pairs={{4,0},{8,4},{12,8},{16,12},{20,16},{24,20},{28,24},{5,1},{9,5},{13... | collective-permute-start | bytes 163304 | tf_op jit(solution)/shard_map/ppermute | solution.py:45
  23.1 6.0 %collective-permute-start.3 = (f32[72,189]{1,0:T(8,128)S(1)}, f32[72,189]{1,0:T(8,128)S(1)}, u32[]{:S(2)}, u32[]{:S(2)}) collective-permute-start(f32[72,189]{1,0:T(8,128)S(1)} %pad_maximum_fusion.1), channel_id=1, source_target_pairs={{0,4},{4,8},{8,12},{12,16},{16,20},{20,24},{24,28},{1,5},{5,9},{9,... | collective-permute-start | bytes 163304 | tf_op jit(solution)/shard_map/ppermute | solution.py:45
  29.5 0.8 %copy-start.5 = (f32[3,21,21]{2,1,0:T(8,128)S(1)}, f32[3,21,21]{2,1,0:T(8,128)}, u32[]{:S(2)}) copy-start(f32[3,21,21]{2,1,0:T(8,128)} %param.20) | copy-start | bytes 15880
  31.3 0.8 %copy-start.4 = (f32[4,56,21]{1,0,2:T(4,128)S(1)}, f32[4,56,21]{1,0,2:T(4,128)}, u32[]{:S(2)}) copy-start(f32[4,56,21]{1,0,2:T(4,128)} %param.19) | copy-start | bytes 56452
  38.2 5.4 %collective-permute-start.5 = (f32[72,189]{1,0:T(8,128)S(1)}, f32[72,189]{1,0:T(8,128)S(1)}, u32[]{:S(2)}, u32[]{:S(2)}) collective-permute-start(f32[72,189]{1,0:T(8,128)S(1)} %get-tuple-element.51), channel_id=1, source_target_pairs={{0,1},{1,2},{2,3},{4,5},{5,6},{6,7},{8,9},{9,10},{10,11},{12,13},{... | collective-permute-start | bytes 163304 | tf_op jit(solution)/shard_map/ppermute | solution.py:45
  41.7 5.7 %collective-permute-start.4 = (f32[72,189]{1,0:T(8,128)S(1)}, f32[72,189]{1,0:T(8,128)S(1)}, u32[]{:S(2)}, u32[]{:S(2)}) collective-permute-start(f32[72,189]{1,0:T(8,128)S(1)} %get-tuple-element.52), channel_id=1, source_target_pairs={{1,0},{2,1},{3,2},{5,4},{6,5},{7,6},{9,8},{10,9},{11,10},{13,12},{... | collective-permute-start | bytes 163304 | tf_op jit(solution)/shard_map/ppermute | solution.py:45
  47.4 5.3 %collective-permute-start.6 = (f32[72,189]{1,0:T(8,128)S(1)}, f32[72,189]{1,0:T(8,128)S(1)}, u32[]{:S(2)}, u32[]{:S(2)}) collective-permute-start(f32[72,189]{1,0:T(8,128)S(1)} %pad_maximum_fusion.2), channel_id=1, source_target_pairs={{4,0},{8,4},{12,8},{16,12},{20,16},{24,20},{28,24},{5,1},{9,5},{13... | collective-permute-start | bytes 163304 | tf_op jit(solution)/shard_map/ppermute | solution.py:45
  49.3 6.0 %collective-permute-start.7 = (f32[72,189]{1,0:T(8,128)S(1)}, f32[72,189]{1,0:T(8,128)S(1)}, u32[]{:S(2)}, u32[]{:S(2)}) collective-permute-start(f32[72,189]{1,0:T(8,128)S(1)} %pad_maximum_fusion.3), channel_id=1, source_target_pairs={{0,4},{4,8},{8,12},{12,16},{16,20},{20,24},{24,28},{1,5},{5,9},{9,... | collective-permute-start | bytes 163304 | tf_op jit(solution)/shard_map/ppermute | solution.py:45

commit v5 on v4

--- a/solution.py
+++ b/solution.py
@@ -65,27 +65,38 @@
     return jnp.stack(result, axis=0)
 
 
-def star_apply(slopes, inv_jacobian, values):
-    parts = [jnp.sum(inv_jacobian[:, k][:, None, None, :] * slopes, axis=0) for k in range(3)]
-    return elastic_apply(parts, values)
-
-
-def predict(current, inv_jacobian, values, grad_matrix):
+def star_coefficients(inv_jacobian, values):
+    return {
+        (d, row_index, col_index): inv_jacobian[d, comp_axis] * values[kind_index]
+        for d in range(3)
+        for comp_axis, row_index, col_index, kind_index in ENTRIES
+    }
+
+
+def star_apply(slopes, coefficients):
+    result = [None] * 9
+    for (d, row_index, col_index), coefficient in coefficients.items():
+        term = coefficient[None, :] * slopes[d, col_index]
+        result[row_index] = term if result[row_index] is None else result[row_index] + term
+    return jnp.stack(result, axis=0)
+
+
+def predict(current, coefficients, grad_matrix):
     derivative = current
     integrated = time_step * current
     factor = time_step
     for power_level in range(1, ORDER):
         slopes = jnp.einsum("dab,qbe->dqae", grad_matrix, derivative, precision=fast_mode)
-        derivative = -star_apply(slopes, inv_jacobian, values)
+        derivative = -star_apply(slopes, coefficients)
         factor = factor * time_step / (power_level + 1)
         integrated = integrated + factor * derivative
     return integrated
 
 
-def local_part(current, inv_jacobian, values, grad_matrix, stiff_matrix, face_proj):
-    integrated = predict(current, inv_jacobian, values, grad_matrix)
+def local_part(current, coefficients, grad_matrix, stiff_matrix, face_proj):
+    integrated = predict(current, coefficients, grad_matrix)
     slopes = jnp.einsum("dab,qbe->dqae", stiff_matrix, integrated, precision=fast_mode)
-    volume = star_apply(slopes, inv_jacobian, values)
+    volume = star_apply(slopes, coefficients)
     face_data = jnp.einsum("fib,qbe->qife", face_proj, integrated, precision=fast_mode)
     return (volume, face_data)
 
@@ -158,6 +169,7 @@
     face_total = 4 * elem_count
     dtype = dof_values.dtype
     values, wave_speed = element_params(material, material_id, normals)
+    coefficients = star_coefficients(inv_jacobian, values)
     face_ids = jnp.arange(face_total, dtype=jnp.int32)
     inside = (neighbour >= 0).reshape(-1)
     local_index = (neighbour_face * elem_count + jnp.maximum(neighbour, 0)).reshape(-1)
@@ -170,7 +182,7 @@
     current = dof_values
     for time_index in range(STEPS):
         volume, face_data = local_part(
-            current, inv_jacobian, values, grad_matrix, stiff_matrix, face_proj
+            current, coefficients, grad_matrix, stiff_matrix, face_proj
         )
         flat_faces = face_data.reshape(9 * face_width, face_total)
         outgoing = lax.dot_general(

time: 58.8 us -> 61 us (1.037)
  other arithmetic: 3.65 us -> 8.52 us
  local copies, waits for them, and re-layouts: 5.52 us -> 4.06 us
  matrix products: 14 us -> 13.1 us
    mul x0 -> x3, other arithmetic: none -> 2.47 us  [star_apply(): term = coefficient[None, :] * slopes[d, col_index]]
    unnamed x112, other arithmetic: 1.32 us -> 2.74 us
    slice x1 -> x0, local copies, waits for them, and re-layouts: 0.81 us -> none  [star_apply(): inv_jacobian[:, k][:, None, None, :] * slopes]
    sqrt x1, other arithmetic: 0.02 us -> 0.77 us  [element_params(): jnp.sqrt((lame_first + 2.0 * shear_modulus) / density)]
    dot_general x10, matrix products: 6.45 us -> 5.73 us  [predict(): jnp.einsum('dab,qbe->dqae', grad_matrix, derivative, precision=fast_mode)]
    unnamed x28 -> x26, local copies, waits for them, and re-layouts: 2.98 us -> 2.34 us
where the time goes in v5:
time: 61 us; the launch traced here: 60.2 us
  starting transfers between devices  21.6 us (35%)
  matrix products  13.1 us (21%)
  waiting for transfers between devices  11.7 us (19%)
  other arithmetic  8.52 us (14%)
  local copies, waits for them, and re-layouts  4.06 us (7%)
  between operations  1.24 us (2%)
    ppermute x8, starting transfers between devices, shifted(): return lax.ppermute(x, axis, pairs)  21.6 us
    ppermute x8, waiting for transfers between devices, shifted(): return lax.ppermute(x, axis, pairs)  11.7 us
    dot_general x10, matrix products, predict(): jnp.einsum('dab,qbe->dqae', grad_matrix, derivative, precision=fast_mode)  5.73 us
    unnamed x112, other arithmetic  2.74 us
    mul x3, other arithmetic, star_apply(): term = coefficient[None, :] * slopes[d, col_index]  2.47 us
    unnamed x26, local copies, waits for them, and re-layouts  2.34 us
    dot_general x2, matrix products, face_update(): jnp.einsum('fai,pife->pae', face_lift, flux_total, precision=fast_mode)  1.46 us
    dot_general x2, matrix products, face_update(): jnp.einsum('hil,qlfe->hqife', rotate, neighbour_data, precision=fast_mode)  1.36 us
  transfers between devices with their start and end apart: 8, of which 4 were waited for; matrix products, arithmetic and copies ran while one was open for 3% of the time, Pallas kernels for 0%

profile of v5, /device:TPU:25, one launch (start us, length us, event | category | flops | bytes accessed | tf_op | source)
XLA Modules:
  0.0 60.2 jit_solution(6332386629781413746)
XLA Ops:
  0.0 0.7 %iota_compare_fusion.6 = pred[16,128]{1,0:T(8,128)(4,1)S(1)} fusion(s32[128]{0:T(128)} %param.22), kind=kLoop, calls=%fused_computation.1001 | loop fusion | flops 2048 | bytes 2560 | tf_op jit(solution)/shard_map/eq | solution.py:50
  0.7 0.8 %select_reduce_fusion = f32[3,128]{1,0:T(4,128)S(1)} fusion(f32[16,3]{0,1:T(4,128)} %param.21, pred[16,128]{1,0:T(8,128)(4,1)S(1)} %iota_compare_fusion.6), kind=kLoop, calls=%fused_computation.999 | loop fusion | flops 11904 | bytes 3776 | tf_op jit(solution)/shard_map/reduce_sum | solution.py:51
  1.5 0.8 %sqrt_bitcast_fusion = (f32[128]{0:T(128)S(1)}, f32[128]{0:T(128)S(1)}, f32[128]{0:T(128)S(1)}, f32[128]{0:T(128)S(1)}, f32[128]{0:T(128)S(1)}) fusion(f32[3,128]{1,0:T(4,128)S(1)} %select_reduce_fusion, f32[3,3,128]{2,1,0:T(4,128)} %param.23), kind=kLoop, calls=%fused_computation.1082 | loop fusion | flops 896 | bytes 5120 | tf_op jit(solution)/shard_map/sqrt | solution.py:54
  2.2 0.8 %fusion.509 = (f32[128]{0:T(128)S(1)}, f32[128]{0:T(128)S(1)}, f32[128]{0:T(128)S(1)}, f32[128]{0:T(128)S(1)}, f32[128]{0:T(128)S(1)}, /*index=5*/f32[128]{0:T(1...) fusion(f32[3,3,128]{2,1,0:T(4,128)} %param.23, f32[3,128]{1,0:T(4,128)S(1)} %select_reduce_fusion), kind=kLoop, calls=%fused_computation.1040 | loop fusion | flops 1408 | bytes 9216 | tf_op jit(solution)/shard_map/mul | solution.py:79
  3.0 0.8 %fusion.530 = (f32[128]{0:T(128)S(1)}, f32[1,128]{1,0:T(1,128)S(1)}, f32[128]{0:T(128)S(1)}, f32[128]{0:T(128)S(1)}, f32[128]{0:T(128)S(1)}, /*index=5*/f32[128]...) fusion(f32[3,3,128]{2,1,0:T(4,128)} %param.23, ...), kind=kLoop, calls=%fused_computation.1081 | loop fusion | flops 1920 | bytes 9728 | tf_op jit(solution)/shard_map/mul | solution.py:79
  3.9 1.0 %slice_bitcast_fusion.335 = (s32[1,24]{1,0:T(1,128)S(1)}, s32[1,24]{1,0:T(1,128)S(1)}, s32[1,24]{1,0:T(1,128)S(1)}, s32[1,24]{1,0:T(1,128)S(1)}, s32[1,24]{1,0:T...) fusion(s32[1,1,8,24]{3,2,1,0:T(8,128)} %param.28), kind=kLoop, calls=%fused_computation.1091 | loop fusion | bytes 1536 | tf_op jit(solution)/shard_map/squeeze | solution.py:177
  5.0 0.8 %fusion.526 = (f32[128]{0:T(128)S(1)}, f32[128]{0:T(128)S(1)}, f32[128]{0:T(128)S(1)}, f32[128]{0:T(128)S(1)}, f32[128]{0:T(128)S(1)}, /*index=5*/f32[128]{0:T(1...) fusion(f32[1,128]{1,0:T(1,128)S(1)} %get-tuple-element.8, ...), kind=kLoop, calls=%fused_computation.1073 | loop fusion | flops 2048 | bytes 13824 | tf_op jit(solution)/shard_map/mul | solution.py:79
  5.8 1.4 %convolution_bitcast_fusion.13 = f32[3,9,56,128]{3,2,0,1:T(8,128)S(1)} fusion(f32[9,56,128]{2,1,0:T(8,128)} %param.15, f32[3,56,56]{2,1,0:T(8,128)S(1)} %copy-done), kind=kOutput, calls=%fused_computation.17 | convolution fusion | flops 65028096 | bytes 1069824 | tf_op jit(solution)/shard_map/dab,qbe->dqae/dot_general | solution.py:89
  10.6 0.8 %copy-done.1 = f32[9,56,128]{2,1,0:T(8,128)S(1)} copy-done((f32[9,56,128]{2,1,0:T(8,128)S(1)}, f32[9,56,128]{2,1,0:T(8,128)}, u32[]{:S(2)}) %copy-start.1) | copy-done | bytes 258072
  13.2 3.7 %collective-permute-start.1 = (f32[72,189]{1,0:T(8,128)S(1)}, f32[72,189]{1,0:T(8,128)S(1)}, u32[]{:S(2)}, u32[]{:S(2)}) collective-permute-start(f32[72,189]{1,0:T(8,128)S(1)} %get-tuple-element.23), channel_id=1, source_target_pairs={{0,1},{1,2},{2,3},{4,5},{5,6},{6,7},{8,9},{9,10},{10,11},{12,13},{... | collective-permute-start | bytes 163304 | tf_op jit(solution)/shard_map/ppermute | solution.py:45
  16.9 1.9 %collective-permute-start = (f32[72,189]{1,0:T(8,128)S(1)}, f32[72,189]{1,0:T(8,128)S(1)}, u32[]{:S(2)}, u32[]{:S(2)}) collective-permute-start(f32[72,189]{1,0:T(8,128)S(1)} %get-tuple-element.24), channel_id=1, source_target_pairs={{1,0},{2,1},{3,2},{5,4},{6,5},{7,6},{9,8},{10,9},{11,10},{13,12},{... | collective-permute-start | bytes 163304 | tf_op jit(solution)/shard_map/ppermute | solution.py:45
  20.4 2.2 %collective-permute-done = f32[72,189]{1,0:T(8,128)S(1)} collective-permute-done((f32[72,189]{1,0:T(8,128)S(1)}, f32[72,189]{1,0:T(8,128)S(1)}, u32[]{:S(2)}, u32[]{:S(2)}) %collective-permute-start) | collective-permute-done | bytes 54464 | tf_op jit(solution)/shard_map/ppermute | solution.py:45
  22.6 3.0 %collective-permute-start.2 = (f32[72,189]{1,0:T(8,128)S(1)}, f32[72,189]{1,0:T(8,128)S(1)}, u32[]{:S(2)}, u32[]{:S(2)}) collective-permute-start(f32[72,189]{1,0:T(8,128)S(1)} %pad_maximum_fusion), channel_id=1, source_target_pairs={{4,0},{8,4},{12,8},{16,12},{20,16},{24,20},{28,24},{5,1},{9,5},{13... | collective-permute-start | bytes 163304 | tf_op jit(solution)/shard_map/ppermute | solution.py:45
  25.6 2.5 %collective-permute-start.3 = (f32[72,189]{1,0:T(8,128)S(1)}, f32[72,189]{1,0:T(8,128)S(1)}, u32[]{:S(2)}, u32[]{:S(2)}) collective-permute-start(f32[72,189]{1,0:T(8,128)S(1)} %pad_maximum_fusion.1), channel_id=1, source_target_pairs={{0,4},{4,8},{8,12},{12,16},{16,20},{20,24},{24,28},{1,5},{5,9},{9,... | collective-permute-start | bytes 163304 | tf_op jit(solution)/shard_map/ppermute | solution.py:45
  28.2 3.4 %collective-permute-done.3 = f32[72,189]{1,0:T(8,128)S(1)} collective-permute-done((f32[72,189]{1,0:T(8,128)S(1)}, f32[72,189]{1,0:T(8,128)S(1)}, u32[]{:S(2)}, u32[]{:S(2)}) %collective-permute-start.3) | collective-permute-done | bytes 54464 | tf_op jit(solution)/shard_map/ppermute | solution.py:45
  32.4 0.7 %fusion.2 = f32[9,21,4,128]{3,1,2,0:T(8,128)S(1)} fusion(f32[3,4,128]{2,0,1:T(4,128)S(1)} %fusion.494, f32[9,21,4,128,1]{3,2,1,0,4:T(4,128)S(1)} %bitcast.3604, f32[3,21,21]{2,1,0:T(8,128)S(1)} %copy-done.5), kind=kOutput, calls=%fused_computation.4 | convolution fusion | flops 37062144 | bytes 785580 | tf_op jit(solution)/shard_map/hil,qlfe->hqife/dot_general | solution.py:116
  40.5 3.3 %collective-permute-start.5 = (f32[72,189]{1,0:T(8,128)S(1)}, f32[72,189]{1,0:T(8,128)S(1)}, u32[]{:S(2)}, u32[]{:S(2)}) collective-permute-start(f32[72,189]{1,0:T(8,128)S(1)} %get-tuple-element.19), channel_id=1, source_target_pairs={{0,1},{1,2},{2,3},{4,5},{5,6},{6,7},{8,9},{9,10},{10,11},{12,13},{... | collective-permute-start | bytes 163304 | tf_op jit(solution)/shard_map/ppermute | solution.py:45
  43.8 1.9 %collective-permute-start.4 = (f32[72,189]{1,0:T(8,128)S(1)}, f32[72,189]{1,0:T(8,128)S(1)}, u32[]{:S(2)}, u32[]{:S(2)}) collective-permute-start(f32[72,189]{1,0:T(8,128)S(1)} %get-tuple-element.20), channel_id=1, source_target_pairs={{1,0},{2,1},{3,2},{5,4},{6,5},{7,6},{9,8},{10,9},{11,10},{13,12},{... | collective-permute-start | bytes 163304 | tf_op jit(solution)/shard_map/ppermute | solution.py:45
  46.0 3.5 %collective-permute-done.4 = f32[72,189]{1,0:T(8,128)S(1)} collective-permute-done((f32[72,189]{1,0:T(8,128)S(1)}, f32[72,189]{1,0:T(8,128)S(1)}, u32[]{:S(2)}, u32[]{:S(2)}) %collective-permute-start.4) | collective-permute-done | bytes 54464 | tf_op jit(solution)/shard_map/ppermute | solution.py:45
  49.5 1.9 %collective-permute-start.6 = (f32[72,189]{1,0:T(8,128)S(1)}, f32[72,189]{1,0:T(8,128)S(1)}, u32[]{:S(2)}, u32[]{:S(2)}) collective-permute-start(f32[72,189]{1,0:T(8,128)S(1)} %pad_maximum_fusion.2), channel_id=1, source_target_pairs={{4,0},{8,4},{12,8},{16,12},{20,16},{24,20},{28,24},{5,1},{9,5},{13... | collective-permute-start | bytes 163304 | tf_op jit(solution)/shard_map/ppermute | solution.py:45
  51.4 3.4 %collective-permute-start.7 = (f32[72,189]{1,0:T(8,128)S(1)}, f32[72,189]{1,0:T(8,128)S(1)}, u32[]{:S(2)}, u32[]{:S(2)}) collective-permute-start(f32[72,189]{1,0:T(8,128)S(1)} %pad_maximum_fusion.3), channel_id=1, source_target_pairs={{0,4},{4,8},{8,12},{12,16},{16,20},{20,24},{24,28},{1,5},{5,9},{9,... | collective-permute-start | bytes 163304 | tf_op jit(solution)/shard_map/ppermute | solution.py:45
  54.8 2.6 %collective-permute-done.7 = f32[72,189]{1,0:T(8,128)S(1)} collective-permute-done((f32[72,189]{1,0:T(8,128)S(1)}, f32[72,189]{1,0:T(8,128)S(1)}, u32[]{:S(2)}, u32[]{:S(2)}) %collective-permute-start.7) | collective-permute-done | bytes 54464 | tf_op jit(solution)/shard_map/ppermute | solution.py:45
  58.0 0.7 %fusion.3 = f32[9,21,4,128]{3,1,2,0:T(8,128)S(1)} fusion(f32[3,4,128]{2,0,1:T(4,128)S(1)} %fusion.494, f32[9,21,4,128,1]{3,2,1,0,4:T(4,128)S(1)} %bitcast.3603, f32[3,21,21]{2,1,0:T(8,128)S(1)} %copy-done.5), kind=kOutput, calls=%fused_computation.5 | convolution fusion | flops 37062144 | bytes 785580 | tf_op jit(solution)/shard_map/hil,qlfe->hqife/dot_general | solution.py:116
  59.1 1.1 %fusion.5 = f32[9,56,128]{2,1,0:T(8,128)} fusion(f32[9,21,4,128]{3,1,2,0:T(8,128)S(1)} %constant_dynamic-update-slice_fusion.117, f32[9,21,4,128]{3,1,2,0:T(8,128)S(1)} %convolution_bitcast_fusion.14, f32[9,21,4,128]{3,1,2,0:T(8,128)S(1)} %fusion.3, f32[9,56,128]{2,1,0:T(8,128)S(1)} %fusion.4, f32[9,56,128]{2,1,0:T(8,128)S(1)} %constant_dynamic-update-slice_fusion.108, ...), kind=kOutput, calls=%fused_computation.25 | convolution fusion | flops 33030144 | bytes 1956224 | tf_op jit(solution)/shard_map/fai,pife->pae/dot_general | solution.py:125
  (205 shorter events, 15.4 us)
Async XLA Ops:
  0.0 5.8 %copy-start = (f32[3,56,56]{2,1,0:T(8,128)S(1)}, f32[3,56,56]{2,1,0:T(8,128)}, u32[]{:S(2)}) copy-start(f32[3,56,56]{2,1,0:T(8,128)} %param.16) | copy-start | bytes 112900
  10.4 1.0 %copy-start.1 = (f32[9,56,128]{2,1,0:T(8,128)S(1)}, f32[9,56,128]{2,1,0:T(8,128)}, u32[]{:S(2)}) copy-start(f32[9,56,128]{2,1,0:T(8,128)} %param.15) | copy-start | bytes 774148
  11.4 0.8 %copy-start.3 = (f32[4,21,56]{2,0,1:T(4,128)S(1)}, f32[4,21,56]{2,0,1:T(4,128)}, u32[]{:S(2)}) copy-start(f32[4,21,56]{2,0,1:T(4,128)} %param.18) | copy-start | bytes 56452
  12.7 6.2 %copy-start.7 = (s32[4,128]{1,0:T(4,128)S(1)}, s32[4,128]{1,0:T(4,128)}, u32[]{:S(2)}) copy-start(s32[4,128]{1,0:T(4,128)} %param.26) | copy-start | bytes 6148
  12.7 6.2 %copy-start.9 = (s32[4,128]{1,0:T(4,128)S(1)}, s32[4,128]{1,0:T(4,128)}, u32[]{:S(2)}) copy-start(s32[4,128]{1,0:T(4,128)} %param.27) | copy-start | bytes 6148
  12.7 6.2 %copy-start.8 = (s32[1,1,8,24]{3,2,1,0:T(8,128)S(1)}, s32[1,1,8,24]{3,2,1,0:T(8,128)}, u32[]{:S(2)}) copy-start(s32[1,1,8,24]{3,2,1,0:T(8,128)} %param.29) | copy-start | bytes 2308
  12.7 6.2 %copy-start.6 = (f32[4,3,128]{2,0,1:T(4,128)S(1)}, f32[4,3,128]{2,0,1:T(4,128)}, u32[]{:S(2)}) copy-start(f32[4,3,128]{2,0,1:T(4,128)} %param.24) | copy-start | bytes 18436
  12.7 6.2 %copy-start.10 = (s32[4,128]{1,0:T(4,128)S(1)}, s32[4,128]{1,0:T(4,128)}, u32[]{:S(2)}) copy-start(s32[4,128]{1,0:T(4,128)} %param.25) | copy-start | bytes 6148
  12.8 6.2 %copy-start.2 = (f32[3,56,56]{2,1,0:T(8,128)S(1)}, f32[3,56,56]{2,1,0:T(8,128)}, u32[]{:S(2)}) copy-start(f32[3,56,56]{2,1,0:T(8,128)} %param.17) | copy-start | bytes 112900
  13.2 7.2 %collective-permute-start.1 = (f32[72,189]{1,0:T(8,128)S(1)}, f32[72,189]{1,0:T(8,128)S(1)}, u32[]{:S(2)}, u32[]{:S(2)}) collective-permute-start(f32[72,189]{1,0:T(8,128)S(1)} %get-tuple-element.23), channel_id=1, source_target_pairs={{0,1},{1,2},{2,3},{4,5},{5,6},{6,7},{8,9},{9,10},{10,11},{12,13},{... | collective-permute-start | bytes 163304 | tf_op jit(solution)/shard_map/ppermute | solution.py:45
  16.9 5.7 %collective-permute-start = (f32[72,189]{1,0:T(8,128)S(1)}, f32[72,189]{1,0:T(8,128)S(1)}, u32[]{:S(2)}, u32[]{:S(2)}) collective-permute-start(f32[72,189]{1,0:T(8,128)S(1)} %get-tuple-element.24), channel_id=1, source_target_pairs={{1,0},{2,1},{3,2},{5,4},{6,5},{7,6},{9,8},{10,9},{11,10},{13,12},{... | collective-permute-start | bytes 163304 | tf_op jit(solution)/shard_map/ppermute | solution.py:45
  22.6 5.6 %collective-permute-start.2 = (f32[72,189]{1,0:T(8,128)S(1)}, f32[72,189]{1,0:T(8,128)S(1)}, u32[]{:S(2)}, u32[]{:S(2)}) collective-permute-start(f32[72,189]{1,0:T(8,128)S(1)} %pad_maximum_fusion), channel_id=1, source_target_pairs={{4,0},{8,4},{12,8},{16,12},{20,16},{24,20},{28,24},{5,1},{9,5},{13... | collective-permute-start | bytes 163304 | tf_op jit(solution)/shard_map/ppermute | solution.py:45
  25.6 6.0 %collective-permute-start.3 = (f32[72,189]{1,0:T(8,128)S(1)}, f32[72,189]{1,0:T(8,128)S(1)}, u32[]{:S(2)}, u32[]{:S(2)}) collective-permute-start(f32[72,189]{1,0:T(8,128)S(1)} %pad_maximum_fusion.1), channel_id=1, source_target_pairs={{0,4},{4,8},{8,12},{12,16},{16,20},{20,24},{24,28},{1,5},{5,9},{9,... | collective-permute-start | bytes 163304 | tf_op jit(solution)/shard_map/ppermute | solution.py:45
  31.6 0.8 %copy-start.5 = (f32[3,21,21]{2,1,0:T(8,128)S(1)}, f32[3,21,21]{2,1,0:T(8,128)}, u32[]{:S(2)}) copy-start(f32[3,21,21]{2,1,0:T(8,128)} %param.20) | copy-start | bytes 15880
  33.3 0.8 %copy-start.4 = (f32[4,56,21]{1,0,2:T(4,128)S(1)}, f32[4,56,21]{1,0,2:T(4,128)}, u32[]{:S(2)}) copy-start(f32[4,56,21]{1,0,2:T(4,128)} %param.19) | copy-start | bytes 56452
  40.5 5.5 %collective-permute-start.5 = (f32[72,189]{1,0:T(8,128)S(1)}, f32[72,189]{1,0:T(8,128)S(1)}, u32[]{:S(2)}, u32[]{:S(2)}) collective-permute-start(f32[72,189]{1,0:T(8,128)S(1)} %get-tuple-element.19), channel_id=1, source_target_pairs={{0,1},{1,2},{2,3},{4,5},{5,6},{6,7},{8,9},{9,10},{10,11},{12,13},{... | collective-permute-start | bytes 163304 | tf_op jit(solution)/shard_map/ppermute | solution.py:45
  43.8 5.7 %collective-permute-start.4 = (f32[72,189]{1,0:T(8,128)S(1)}, f32[72,189]{1,0:T(8,128)S(1)}, u32[]{:S(2)}, u32[]{:S(2)}) collective-permute-start(f32[72,189]{1,0:T(8,128)S(1)} %get-tuple-element.20), channel_id=1, source_target_pairs={{1,0},{2,1},{3,2},{5,4},{6,5},{7,6},{9,8},{10,9},{11,10},{13,12},{... | collective-permute-start | bytes 163304 | tf_op jit(solution)/shard_map/ppermute | solution.py:45
  49.5 5.4 %collective-permute-start.6 = (f32[72,189]{1,0:T(8,128)S(1)}, f32[72,189]{1,0:T(8,128)S(1)}, u32[]{:S(2)}, u32[]{:S(2)}) collective-permute-start(f32[72,189]{1,0:T(8,128)S(1)} %pad_maximum_fusion.2), channel_id=1, source_target_pairs={{4,0},{8,4},{12,8},{16,12},{20,16},{24,20},{28,24},{5,1},{9,5},{13... | collective-permute-start | bytes 163304 | tf_op jit(solution)/shard_map/ppermute | solution.py:45
  51.4 6.0 %collective-permute-start.7 = (f32[72,189]{1,0:T(8,128)S(1)}, f32[72,189]{1,0:T(8,128)S(1)}, u32[]{:S(2)}, u32[]{:S(2)}) collective-permute-start(f32[72,189]{1,0:T(8,128)S(1)} %pad_maximum_fusion.3), channel_id=1, source_target_pairs={{0,4},{4,8},{8,12},{12,16},{16,20},{20,24},{24,28},{1,5},{5,9},{9,... | collective-permute-start | bytes 163304 | tf_op jit(solution)/shard_map/ppermute | solution.py:45

commit v6 on v4

--- a/solution.py
+++ b/solution.py
@@ -2,6 +2,7 @@
 import jax.numpy as jnp
 from jax import lax
 from jax.sharding import PartitionSpec as P
+from jax.experimental import pallas as pl
 
 ORDER = 6
 STEPS = 2
@@ -82,17 +83,54 @@
     return integrated
 
 
-def local_part(current, inv_jacobian, values, grad_matrix, stiff_matrix, face_proj):
-    integrated = predict(current, inv_jacobian, values, grad_matrix)
-    slopes = jnp.einsum("dab,qbe->dqae", stiff_matrix, integrated, precision=fast_mode)
-    volume = star_apply(slopes, inv_jacobian, values)
+def predict_kernel(q_ref, jac_ref, val_ref, grad_ref, stiff_ref, integ_ref, qvol_ref):
+    basis = q_ref.shape[1]
+    lanes = q_ref.shape[2]
+    jac = [[jac_ref[pl.ds(d * 3 + k, 1), :] for k in range(3)] for d in range(3)]
+    vals = [val_ref[pl.ds(i, 1), :] for i in range(4)]
+    coef = {}
+    for d in range(3):
+        for comp_axis, row_index, col_index, kind_index in ENTRIES:
+            coef[(d, row_index, col_index)] = jac[d][comp_axis] * vals[kind_index]
+
+    def apply(op, parts):
+        stacked = jnp.concatenate(parts, axis=1)
+        slopes = jnp.dot(op, stacked, precision=lax.Precision.HIGHEST, preferred_element_type=jnp.float32)
+        out = [None] * 9
+        for (d, row_index, col_index), c in coef.items():
+            t = c * slopes[d * basis:(d + 1) * basis, col_index * lanes:(col_index + 1) * lanes]
+            out[row_index] = t if out[row_index] is None else out[row_index] + t
+        return out
+
+    grad = grad_ref[...]
+    derivative = [q_ref[q] for q in range(9)]
+    integrated = [time_step * x for x in derivative]
+    factor = time_step
+    for level in range(1, ORDER):
+        derivative = [-x for x in apply(grad, derivative)]
+        factor = factor * time_step / (level + 1)
+        integrated = [a + factor * b for a, b in zip(integrated, derivative)]
+    for q in range(9):
+        integ_ref[q] = integrated[q]
+    volume = apply(stiff_ref[...], integrated)
+    for q in range(9):
+        qvol_ref[q] = q_ref[q] + volume[q]
+
+def predict_call(current, jacobian_rows, value_rows, grad_rows, stiff_rows):
+    shape = jax.ShapeDtypeStruct(current.shape, current.dtype)
+    return pl.pallas_call(predict_kernel, out_shape=(shape, shape))(
+        current, jacobian_rows, value_rows, grad_rows, stiff_rows
+    )
+
+
+def local_part(current, jacobian_rows, value_rows, grad_rows, stiff_rows, face_proj):
+    integrated, advanced = predict_call(current, jacobian_rows, value_rows, grad_rows, stiff_rows)
     face_data = jnp.einsum("fib,qbe->qife", face_proj, integrated, precision=fast_mode)
-    return (volume, face_data)
+    return (advanced, face_data)
 
 
 def face_update(
-    current,
-    volume,
+    advanced,
     face_data,
     neighbour_data,
     orientation,
@@ -104,7 +142,7 @@
 ):
     turned = jnp.einsum("hil,qlfe->hqife", rotate, neighbour_data, precision=fast_mode)
     chosen = (orientation[None] == jnp.arange(3, dtype=jnp.int32)[:, None, None]).astype(
-        current.dtype
+        advanced.dtype
     )
     turned = jnp.sum(turned * chosen[:, None, None, :, :], axis=0)
     both = face_data + turned
@@ -112,7 +150,7 @@
     parts = [normals[:, k, :][None, None] * both for k in range(3)]
     flux_total = 0.5 * (elastic_apply(parts, values) + wave_speed[None, None] * apart)
     lifted = jnp.einsum("fai,pife->pae", face_lift, flux_total, precision=fast_mode)
-    return current + volume - lifted
+    return advanced - lifted
 
 
 SEND_ORDER = (0, 3, 5, 2, 4, 7, 1, 6)
@@ -158,6 +196,10 @@
     face_total = 4 * elem_count
     dtype = dof_values.dtype
     values, wave_speed = element_params(material, material_id, normals)
+    jacobian_rows = inv_jacobian.reshape(9, elem_count)
+    value_rows = jnp.stack(values, axis=0)
+    grad_rows = grad_matrix.reshape(-1, grad_matrix.shape[2])
+    stiff_rows = stiff_matrix.reshape(-1, stiff_matrix.shape[2])
     face_ids = jnp.arange(face_total, dtype=jnp.int32)
     inside = (neighbour >= 0).reshape(-1)
     local_index = (neighbour_face * elem_count + jnp.maximum(neighbour, 0)).reshape(-1)
@@ -169,8 +211,8 @@
     scatter_in = ((targets[:, None] == face_ids[None, :]) & ~inside[None, :]).astype(dtype)
     current = dof_values
     for time_index in range(STEPS):
-        volume, face_data = local_part(
-            current, inv_jacobian, values, grad_matrix, stiff_matrix, face_proj
+        advanced, face_data = local_part(
+            current, jacobian_rows, value_rows, grad_rows, stiff_rows, face_proj
         )
         flat_faces = face_data.reshape(9 * face_width, face_total)
         outgoing = lax.dot_general(
@@ -182,8 +224,7 @@
         )
         neighbour_data = neighbour_data.reshape(9, face_width, 4, elem_count)
         current = face_update(
-            current,
-            volume,
+            advanced,
             face_data,
             neighbour_data,
             orientation,

time: 58.8 us -> 67.3 us (1.14)
  Pallas kernels: 0 us -> 15 us
  matrix products: 14 us -> 9.04 us
  between operations: 1.38 us -> 0.62 us
    pallas_call x0 -> x2, Pallas kernels: none -> 15 us  [predict_call(): pl.pallas_call(predict_kernel, out_shape=(shape, shape))]
    dot_general x12 -> x0, matrix products: 7.54 us -> none  [the longest x10 6.45 us: predict(): jnp.einsum('dab,qbe->dqae', grad_matrix, derivative, precision=fast_mode)]
    dot_general x2, matrix products: 0.64 us -> 2.53 us  [local_part(): jnp.einsum('fib,qbe->qife', face_proj, integrated, precision=fast_mode)]
    reshape x0 -> x1, local copies, waits for them, and re-layouts: none -> 1.3 us  [per_device(): jacobian_rows = inv_jacobian.reshape(9, elem_count)]
    unnamed x112 -> x16, other arithmetic: 1.32 us -> 0.21 us
    unnamed x28 -> x24, local copies, waits for them, and re-layouts: 2.98 us -> 1.91 us
    slice x1 -> x0, local copies, waits for them, and re-layouts: 0.81 us -> none  [star_apply(): inv_jacobian[:, k][:, None, None, :] * slopes]
    dot_general x2, matrix products: 1.46 us -> 2.16 us  [face_update(): jnp.einsum('fai,pife->pae', face_lift, flux_total, precision=fast_mode)]
  transfers between devices with their start and end apart: 8 -> 8, of which waited for: 4 -> 4; matrix products, arithmetic and copies ran while one was open for 3% -> 2% of each run, Pallas kernels for 0% -> 0%
where the time goes in v6:
time: 67.3 us; the launch traced here: 66.6 us
  starting transfers between devices  21.6 us (32%)
  Pallas kernels  15 us (22%)
  waiting for transfers between devices  12.1 us (18%)
  matrix products  9.04 us (13%)
  local copies, waits for them, and re-layouts  4.93 us (7%)
  other arithmetic  3.34 us (5%)
    ppermute x8, starting transfers between devices, shifted(): return lax.ppermute(x, axis, pairs)  21.6 us
    pallas_call x2, Pallas kernels, predict_call(): pl.pallas_call(predict_kernel, out_shape=(shape, shape))  15 us
    ppermute x8, waiting for transfers between devices, shifted(): return lax.ppermute(x, axis, pairs)  12.1 us
    dot_general x2, matrix products, local_part(): jnp.einsum('fib,qbe->qife', face_proj, integrated, precision=fast_mode)  2.53 us
    dot_general x2, matrix products, face_update(): jnp.einsum('fai,pife->pae', face_lift, flux_total, precision=fast_mode)  2.16 us
    unnamed x24, local copies, waits for them, and re-layouts  1.91 us
    dot_general x2, matrix products, face_update(): jnp.einsum('hil,qlfe->hqife', rotate, neighbour_data, precision=fast_mode)  1.36 us
  transfers between devices with their start and end apart: 8, of which 4 were waited for; matrix products, arithmetic and copies ran while one was open for 2% of the time, Pallas kernels for 0%

profile of v6, /device:TPU:25, one launch (start us, length us, event | category | flops | bytes accessed | tf_op | source)
XLA Modules:
  0.0 66.6 jit_solution(15110097619286622116)
XLA Ops:
  0.7 0.8 %select_reduce_fusion = f32[3,128]{1,0:T(4,128)S(1)} fusion(f32[16,3]{0,1:T(4,128)} %param.21, pred[16,128]{1,0:T(8,128)(4,1)S(1)} %iota_compare_fusion.6), kind=kLoop, calls=%fused_computation.137 | loop fusion | flops 11904 | bytes 3776 | tf_op jit(solution)/shard_map/reduce_sum | solution.py:52
  1.5 0.7 %abs_reduce_fusion = f32[4,128]{1,0:T(4,128)S(1)} fusion(f32[4,3,128]{2,0,1:T(4,128)} %param.24), kind=kLoop, calls=%fused_computation.141 | loop fusion | flops 2560 | bytes 8192 | tf_op jit(solution)/shard_map/reduce_sum | solution.py:55
  2.2 1.0 %slice_bitcast_fusion.11 = (s32[1,24]{1,0:T(1,128)S(1)}, s32[1,24]{1,0:T(1,128)S(1)}, s32[1,24]{1,0:T(1,128)S(1)}, s32[1,24]{1,0:T(1,128)S(1)}, s32[1,24]{1,0:T(...) fusion(s32[1,1,8,24]{3,2,1,0:T(8,128)} %param.28), kind=kLoop, calls=%fused_computation.158 | loop fusion | bytes 1536 | tf_op jit(solution)/shard_map/squeeze | solution.py:207
  3.3 1.3 %reshape.115.jac_ref = f32[9,128]{1,0:T(8,128)} reshape(f32[3,3,128]{2,1,0:T(4,128)} %param.23) | data formatting | bytes 9216 | tf_op jit(solution)/shard_map/reshape | solution.py:199
  5.1 7.5 %shard_map.145 = (f32[9,56,128]{2,1,0:T(8,128)}, f32[9,56,128]{2,1,0:T(8,128)}) custom-call(f32[9,56,128]{2,1,0:T(8,128)} %q_ref.1, f32[9,128]{1,0:T(8,128)} %reshape.115.jac_ref, f32[4,128]{1,0:T(4,128)} %get-tuple-element.71.val_ref, f32[168,56]{1,0:T(8,128)} %bitcast.137, f32[168,56]{1,0:T(8,128)} %bitcast.139), custom_call_target="tpu_custom_call" | custom-call | tf_op jit(solution)/shard_map/pallas_call | solution.py:121
  12.6 1.3 %convolution_bitcast_fusion.3 = f32[9,21,4,128]{3,1,2,0:T(8,128)S(1)} fusion(f32[9,56,128]{2,1,0:T(8,128)} %get-tuple-element.10, f32[4,21,56]{2,0,1:T(4,128)S(1)} %copy-done.3), kind=kOutput, calls=%fused_computation.7 | convolution fusion | flops 32514048 | bytes 663936 | tf_op jit(solution)/shard_map/fib,qbe->qife/dot_general | solution.py:128
  14.6 3.7 %collective-permute-start.1 = (f32[72,189]{1,0:T(8,128)S(1)}, f32[72,189]{1,0:T(8,128)S(1)}, u32[]{:S(2)}, u32[]{:S(2)}) collective-permute-start(f32[72,189]{1,0:T(8,128)S(1)} %get-tuple-element.29), channel_id=1, source_target_pairs={{0,1},{1,2},{2,3},{4,5},{5,6},{6,7},{8,9},{9,10},{10,11},{12,13},{... | collective-permute-start | bytes 163304 | tf_op jit(solution)/shard_map/ppermute | solution.py:46
  18.3 1.9 %collective-permute-start = (f32[72,189]{1,0:T(8,128)S(1)}, f32[72,189]{1,0:T(8,128)S(1)}, u32[]{:S(2)}, u32[]{:S(2)}) collective-permute-start(f32[72,189]{1,0:T(8,128)S(1)} %get-tuple-element.30), channel_id=1, source_target_pairs={{1,0},{2,1},{3,2},{5,4},{6,5},{7,6},{9,8},{10,9},{11,10},{13,12},{... | collective-permute-start | bytes 163304 | tf_op jit(solution)/shard_map/ppermute | solution.py:46
  21.0 3.0 %collective-permute-done = f32[72,189]{1,0:T(8,128)S(1)} collective-permute-done((f32[72,189]{1,0:T(8,128)S(1)}, f32[72,189]{1,0:T(8,128)S(1)}, u32[]{:S(2)}, u32[]{:S(2)}) %collective-permute-start) | collective-permute-done | bytes 54464 | tf_op jit(solution)/shard_map/ppermute | solution.py:46
  24.0 3.0 %collective-permute-start.2 = (f32[72,189]{1,0:T(8,128)S(1)}, f32[72,189]{1,0:T(8,128)S(1)}, u32[]{:S(2)}, u32[]{:S(2)}) collective-permute-start(f32[72,189]{1,0:T(8,128)S(1)} %pad_maximum_fusion), channel_id=1, source_target_pairs={{4,0},{8,4},{12,8},{16,12},{20,16},{24,20},{28,24},{5,1},{9,5},{13... | collective-permute-start | bytes 163304 | tf_op jit(solution)/shard_map/ppermute | solution.py:46
  27.0 2.5 %collective-permute-start.3 = (f32[72,189]{1,0:T(8,128)S(1)}, f32[72,189]{1,0:T(8,128)S(1)}, u32[]{:S(2)}, u32[]{:S(2)}) collective-permute-start(f32[72,189]{1,0:T(8,128)S(1)} %pad_maximum_fusion.1), channel_id=1, source_target_pairs={{0,4},{4,8},{8,12},{12,16},{16,20},{20,24},{24,28},{1,5},{5,9},{9,... | collective-permute-start | bytes 163304 | tf_op jit(solution)/shard_map/ppermute | solution.py:46
  29.6 3.4 %collective-permute-done.3 = f32[72,189]{1,0:T(8,128)S(1)} collective-permute-done((f32[72,189]{1,0:T(8,128)S(1)}, f32[72,189]{1,0:T(8,128)S(1)}, u32[]{:S(2)}, u32[]{:S(2)}) %collective-permute-start.3) | collective-permute-done | bytes 54464 | tf_op jit(solution)/shard_map/ppermute | solution.py:46
  34.7 0.8 %copy-done.1 = f32[9,56,128]{2,1,0:T(8,128)S(1)} copy-done((f32[9,56,128]{2,1,0:T(8,128)S(1)}, f32[9,56,128]{2,1,0:T(8,128)}, u32[]{:S(2)}) %copy-start.1) | copy-done | bytes 258072
  35.6 1.1 %fusion.4.q_ref = f32[9,56,128]{2,1,0:T(8,128)} fusion(f32[9,56,128]{2,1,0:T(8,128)S(1)} %copy-done.1, f32[9,21,4,128]{3,1,2,0:T(8,128)S(1)} %fusion.69, f32[9,21,4,128]{3,1,2,0:T(8,128)S(1)} %convolution_bitcast_fusion.3, f32[9,21,4,128]{3,1,2,0:T(8,128)S(1)} %fusion.2, f32[4,128]{1,0:T(4,128)S(1)} %get-tuple-element.72, f32[4,56,21]{1,0,2:T(4,128)S(1)} %copy-done.4), kind=kOutput, calls=%fused_computation.12 | convolution fusion | flops 32965632 | bytes 1698176 | tf_op jit(solution)/shard_map/fai,pife->pae/dot_general | solution.py:152
  36.6 7.5 %shard_map.146 = (f32[9,56,128]{2,1,0:T(8,128)}, f32[9,56,128]{2,1,0:T(8,128)}) custom-call(f32[9,56,128]{2,1,0:T(8,128)} %fusion.4.q_ref, f32[9,128]{1,0:T(8,128)} %reshape.115.jac_ref, f32[4,128]{1,0:T(4,128)} %get-tuple-element.71.val_ref, f32[168,56]{1,0:T(8,128)} %bitcast.138, f32[168,56]{1,0:T(8,128)} %bitcast.140), custom_call_target="tpu_custom_call" | custom-call | tf_op jit(solution)/shard_map/pallas_call | solution.py:121
  44.1 1.3 %convolution_bitcast_fusion.2 = f32[9,21,4,128]{3,1,2,0:T(8,128)S(1)} fusion(f32[9,56,128]{2,1,0:T(8,128)} %get-tuple-element.12, f32[4,21,56]{2,0,1:T(4,128)S(1)} %copy-done.3), kind=kOutput, calls=%fused_computation.6 | convolution fusion | flops 32514048 | bytes 663936 | tf_op jit(solution)/shard_map/fib,qbe->qife/dot_general | solution.py:128
  46.0 3.3 %collective-permute-start.5 = (f32[72,189]{1,0:T(8,128)S(1)}, f32[72,189]{1,0:T(8,128)S(1)}, u32[]{:S(2)}, u32[]{:S(2)}) collective-permute-start(f32[72,189]{1,0:T(8,128)S(1)} %get-tuple-element.25), channel_id=1, source_target_pairs={{0,1},{1,2},{2,3},{4,5},{5,6},{6,7},{8,9},{9,10},{10,11},{12,13},{... | collective-permute-start | bytes 163304 | tf_op jit(solution)/shard_map/ppermute | solution.py:46
  49.3 1.9 %collective-permute-start.4 = (f32[72,189]{1,0:T(8,128)S(1)}, f32[72,189]{1,0:T(8,128)S(1)}, u32[]{:S(2)}, u32[]{:S(2)}) collective-permute-start(f32[72,189]{1,0:T(8,128)S(1)} %get-tuple-element.26), channel_id=1, source_target_pairs={{1,0},{2,1},{3,2},{5,4},{6,5},{7,6},{9,8},{10,9},{11,10},{13,12},{... | collective-permute-start | bytes 163304 | tf_op jit(solution)/shard_map/ppermute | solution.py:46
  51.3 3.7 %collective-permute-done.4 = f32[72,189]{1,0:T(8,128)S(1)} collective-permute-done((f32[72,189]{1,0:T(8,128)S(1)}, f32[72,189]{1,0:T(8,128)S(1)}, u32[]{:S(2)}, u32[]{:S(2)}) %collective-permute-start.4) | collective-permute-done | bytes 54464 | tf_op jit(solution)/shard_map/ppermute | solution.py:46
  55.0 1.9 %collective-permute-start.6 = (f32[72,189]{1,0:T(8,128)S(1)}, f32[72,189]{1,0:T(8,128)S(1)}, u32[]{:S(2)}, u32[]{:S(2)}) collective-permute-start(f32[72,189]{1,0:T(8,128)S(1)} %pad_maximum_fusion.2), channel_id=1, source_target_pairs={{4,0},{8,4},{12,8},{16,12},{20,16},{24,20},{28,24},{5,1},{9,5},{13... | collective-permute-start | bytes 163304 | tf_op jit(solution)/shard_map/ppermute | solution.py:46
  57.0 3.4 %collective-permute-start.7 = (f32[72,189]{1,0:T(8,128)S(1)}, f32[72,189]{1,0:T(8,128)S(1)}, u32[]{:S(2)}, u32[]{:S(2)}) collective-permute-start(f32[72,189]{1,0:T(8,128)S(1)} %pad_maximum_fusion.3), channel_id=1, source_target_pairs={{0,4},{4,8},{8,12},{12,16},{16,20},{20,24},{24,28},{1,5},{5,9},{9,... | collective-permute-start | bytes 163304 | tf_op jit(solution)/shard_map/ppermute | solution.py:46
  61.0 2.0 %collective-permute-done.7 = f32[72,189]{1,0:T(8,128)S(1)} collective-permute-done((f32[72,189]{1,0:T(8,128)S(1)}, f32[72,189]{1,0:T(8,128)S(1)}, u32[]{:S(2)}, u32[]{:S(2)}) %collective-permute-start.7) | collective-permute-done | bytes 54464 | tf_op jit(solution)/shard_map/ppermute | solution.py:46
  64.7 0.8 %copy-done.2 = f32[9,56,128]{2,1,0:T(8,128)S(1)} copy-done((f32[9,56,128]{2,1,0:T(8,128)S(1)}, f32[9,56,128]{2,1,0:T(8,128)}, u32[]{:S(2)}) %copy-start.2) | copy-done | bytes 258072
  65.5 1.1 %fusion.5 = f32[9,56,128]{2,1,0:T(8,128)} fusion(f32[9,56,128]{2,1,0:T(8,128)S(1)} %copy-done.2, f32[9,21,4,128]{3,1,2,0:T(8,128)S(1)} %fusion.57, f32[9,21,4,128]{3,1,2,0:T(8,128)S(1)} %convolution_bitcast_fusion.2, f32[9,21,4,128]{3,1,2,0:T(8,128)S(1)} %fusion.3, f32[4,128]{1,0:T(4,128)S(1)} %get-tuple-element.72, f32[4,56,21]{1,0,2:T(4,128)S(1)} %copy-done.4), kind=kOutput, calls=%fused_computation.13 | convolution fusion | flops 32965632 | bytes 1698176 | tf_op jit(solution)/shard_map/fai,pife->pae/dot_general | solution.py:152
  (82 shorter events, 7.2 us)
Async XLA Ops:
  0.0 33.7 %copy-start = (f32[3,21,21]{2,1,0:T(8,128)S(1)}, f32[3,21,21]{2,1,0:T(8,128)}, u32[]{:S(2)}) copy-start(f32[3,21,21]{2,1,0:T(8,128)} %param.20) | copy-start | bytes 15880
  0.0 12.6 %copy-start.3 = (f32[4,21,56]{2,0,1:T(4,128)S(1)}, f32[4,21,56]{2,0,1:T(4,128)}, u32[]{:S(2)}) copy-start(f32[4,21,56]{2,0,1:T(4,128)} %param.18) | copy-start | bytes 56452
  14.1 6.1 %copy-start.6 = (s32[4,128]{1,0:T(4,128)S(1)}, s32[4,128]{1,0:T(4,128)}, u32[]{:S(2)}) copy-start(s32[4,128]{1,0:T(4,128)} %param.26) | copy-start | bytes 6148
  14.1 6.1 %copy-start.8 = (s32[4,128]{1,0:T(4,128)S(1)}, s32[4,128]{1,0:T(4,128)}, u32[]{:S(2)}) copy-start(s32[4,128]{1,0:T(4,128)} %param.27) | copy-start | bytes 6148
  14.1 6.2 %copy-start.9 = (s32[4,128]{1,0:T(4,128)S(1)}, s32[4,128]{1,0:T(4,128)}, u32[]{:S(2)}) copy-start(s32[4,128]{1,0:T(4,128)} %param.25) | copy-start | bytes 6148
  14.6 6.4 %collective-permute-start.1 = (f32[72,189]{1,0:T(8,128)S(1)}, f32[72,189]{1,0:T(8,128)S(1)}, u32[]{:S(2)}, u32[]{:S(2)}) collective-permute-start(f32[72,189]{1,0:T(8,128)S(1)} %get-tuple-element.29), channel_id=1, source_target_pairs={{0,1},{1,2},{2,3},{4,5},{5,6},{6,7},{8,9},{9,10},{10,11},{12,13},{... | collective-permute-start | bytes 163304 | tf_op jit(solution)/shard_map/ppermute | solution.py:46
  18.3 2.6 %copy-start.5 = (f32[4,3,128]{2,0,1:T(4,128)S(1)}, f32[4,3,128]{2,0,1:T(4,128)}, u32[]{:S(2)}) copy-start(f32[4,3,128]{2,0,1:T(4,128)} %param.24) | copy-start | bytes 18436
  18.3 5.7 %collective-permute-start = (f32[72,189]{1,0:T(8,128)S(1)}, f32[72,189]{1,0:T(8,128)S(1)}, u32[]{:S(2)}, u32[]{:S(2)}) collective-permute-start(f32[72,189]{1,0:T(8,128)S(1)} %get-tuple-element.30), channel_id=1, source_target_pairs={{1,0},{2,1},{3,2},{5,4},{6,5},{7,6},{9,8},{10,9},{11,10},{13,12},{... | collective-permute-start | bytes 163304 | tf_op jit(solution)/shard_map/ppermute | solution.py:46
  20.9 8.5 %copy-start.7 = (s32[1,1,8,24]{3,2,1,0:T(8,128)S(1)}, s32[1,1,8,24]{3,2,1,0:T(8,128)}, u32[]{:S(2)}) copy-start(s32[1,1,8,24]{3,2,1,0:T(8,128)} %param.29) | copy-start | bytes 2308
  24.0 5.6 %collective-permute-start.2 = (f32[72,189]{1,0:T(8,128)S(1)}, f32[72,189]{1,0:T(8,128)S(1)}, u32[]{:S(2)}, u32[]{:S(2)}) collective-permute-start(f32[72,189]{1,0:T(8,128)S(1)} %pad_maximum_fusion), channel_id=1, source_target_pairs={{4,0},{8,4},{12,8},{16,12},{20,16},{24,20},{28,24},{5,1},{9,5},{13... | collective-permute-start | bytes 163304 | tf_op jit(solution)/shard_map/ppermute | solution.py:46
  27.0 6.0 %collective-permute-start.3 = (f32[72,189]{1,0:T(8,128)S(1)}, f32[72,189]{1,0:T(8,128)S(1)}, u32[]{:S(2)}, u32[]{:S(2)}) collective-permute-start(f32[72,189]{1,0:T(8,128)S(1)} %pad_maximum_fusion.1), channel_id=1, source_target_pairs={{0,4},{4,8},{8,12},{12,16},{16,20},{20,24},{24,28},{1,5},{5,9},{9,... | collective-permute-start | bytes 163304 | tf_op jit(solution)/shard_map/ppermute | solution.py:46
  34.6 0.9 %copy-start.1 = (f32[9,56,128]{2,1,0:T(8,128)S(1)}, f32[9,56,128]{2,1,0:T(8,128)}, u32[]{:S(2)}) copy-start(f32[9,56,128]{2,1,0:T(8,128)} %get-tuple-element.9) | copy-start | bytes 774148
  34.6 0.9 %copy-start.4 = (f32[4,56,21]{1,0,2:T(4,128)S(1)}, f32[4,56,21]{1,0,2:T(4,128)}, u32[]{:S(2)}) copy-start(f32[4,56,21]{1,0,2:T(4,128)} %param.19) | copy-start | bytes 56452
  46.0 5.2 %collective-permute-start.5 = (f32[72,189]{1,0:T(8,128)S(1)}, f32[72,189]{1,0:T(8,128)S(1)}, u32[]{:S(2)}, u32[]{:S(2)}) collective-permute-start(f32[72,189]{1,0:T(8,128)S(1)} %get-tuple-element.25), channel_id=1, source_target_pairs={{0,1},{1,2},{2,3},{4,5},{5,6},{6,7},{8,9},{9,10},{10,11},{12,13},{... | collective-permute-start | bytes 163304 | tf_op jit(solution)/shard_map/ppermute | solution.py:46
  49.3 5.7 %collective-permute-start.4 = (f32[72,189]{1,0:T(8,128)S(1)}, f32[72,189]{1,0:T(8,128)S(1)}, u32[]{:S(2)}, u32[]{:S(2)}) collective-permute-start(f32[72,189]{1,0:T(8,128)S(1)} %get-tuple-element.26), channel_id=1, source_target_pairs={{1,0},{2,1},{3,2},{5,4},{6,5},{7,6},{9,8},{10,9},{11,10},{13,12},{... | collective-permute-start | bytes 163304 | tf_op jit(solution)/shard_map/ppermute | solution.py:46
  55.0 5.9 %collective-permute-start.6 = (f32[72,189]{1,0:T(8,128)S(1)}, f32[72,189]{1,0:T(8,128)S(1)}, u32[]{:S(2)}, u32[]{:S(2)}) collective-permute-start(f32[72,189]{1,0:T(8,128)S(1)} %pad_maximum_fusion.2), channel_id=1, source_target_pairs={{4,0},{8,4},{12,8},{16,12},{20,16},{24,20},{28,24},{5,1},{9,5},{13... | collective-permute-start | bytes 163304 | tf_op jit(solution)/shard_map/ppermute | solution.py:46
  57.0 6.0 %collective-permute-start.7 = (f32[72,189]{1,0:T(8,128)S(1)}, f32[72,189]{1,0:T(8,128)S(1)}, u32[]{:S(2)}, u32[]{:S(2)}) collective-permute-start(f32[72,189]{1,0:T(8,128)S(1)} %pad_maximum_fusion.3), channel_id=1, source_target_pairs={{0,4},{4,8},{8,12},{12,16},{16,20},{20,24},{24,28},{1,5},{5,9},{9,... | collective-permute-start | bytes 163304 | tf_op jit(solution)/shard_map/ppermute | solution.py:46
  64.6 0.9 %copy-start.2 = (f32[9,56,128]{2,1,0:T(8,128)S(1)}, f32[9,56,128]{2,1,0:T(8,128)}, u32[]{:S(2)}) copy-start(f32[9,56,128]{2,1,0:T(8,128)} %get-tuple-element.11) | copy-start | bytes 774148

commit v7 on v4

--- a/solution.py
+++ b/solution.py
@@ -90,29 +90,18 @@
     return (volume, face_data)
 
 
-def face_update(
-    current,
-    volume,
-    face_data,
-    neighbour_data,
-    orientation,
-    normals,
-    values,
-    wave_speed,
-    rotate,
-    face_lift,
-):
+def rotated(neighbour_data, orientation, rotate):
     turned = jnp.einsum("hil,qlfe->hqife", rotate, neighbour_data, precision=fast_mode)
     chosen = (orientation[None] == jnp.arange(3, dtype=jnp.int32)[:, None, None]).astype(
-        current.dtype
-    )
-    turned = jnp.sum(turned * chosen[:, None, None, :, :], axis=0)
-    both = face_data + turned
-    apart = face_data - turned
+        neighbour_data.dtype
+    )
+    return jnp.sum(turned * chosen[:, None, None, :, :], axis=0)
+
+
+def lifted_flux(both, apart, normals, values, wave_speed, face_lift):
     parts = [normals[:, k, :][None, None] * both for k in range(3)]
     flux_total = 0.5 * (elastic_apply(parts, values) + wave_speed[None, None] * apart)
-    lifted = jnp.einsum("fai,pife->pae", face_lift, flux_total, precision=fast_mode)
-    return current + volume - lifted
+    return jnp.einsum("fai,pife->pae", face_lift, flux_total, precision=fast_mode)
 
 
 SEND_ORDER = (0, 3, 5, 2, 4, 7, 1, 6)
@@ -176,22 +165,32 @@
         outgoing = lax.dot_general(
             gather_out, flat_faces, (((1,), (1,)), ((), ())), precision=exact_mode
         )
-        received = deliver(outgoing, slot_total)
-        neighbour_data = jnp.dot(flat_faces, gather_local, precision=exact_mode) + lax.dot_general(
-            received, scatter_in, (((0,), (0,)), ((), ())), precision=exact_mode
-        )
-        neighbour_data = neighbour_data.reshape(9, face_width, 4, elem_count)
-        current = face_update(
-            current,
-            volume,
-            face_data,
-            neighbour_data,
+        local_turned = rotated(
+            jnp.dot(flat_faces, gather_local, precision=exact_mode).reshape(
+                9, face_width, 4, elem_count
+            ),
             orientation,
+            rotate,
+        )
+        advanced = current + volume - lifted_flux(
+            face_data + local_turned,
+            face_data - local_turned,
             normals,
             values,
             wave_speed,
+            face_lift,
+        )
+        received = deliver(outgoing, slot_total)
+        received, advanced = lax.optimization_barrier((received, advanced))
+        remote_turned = rotated(
+            lax.dot_general(
+                received, scatter_in, (((0,), (0,)), ((), ())), precision=exact_mode
+            ).reshape(9, face_width, 4, elem_count),
+            orientation,
             rotate,
-            face_lift,
+        )
+        current = advanced - lifted_flux(
+            remote_turned, -remote_turned, normals, values, wave_speed, face_lift
         )
     return current
 

time: 58.8 us -> 61.1 us (1.039)
  waiting for transfers between devices: 12 us -> 9.37 us
  starting transfers between devices: 21.6 us -> 23.5 us
  matrix products: 14 us -> 15.8 us
  other arithmetic: 3.65 us -> 4.99 us
    ppermute x8, waiting for transfers between devices: 12 us -> 9.37 us  [shifted(): return lax.ppermute(x, axis, pairs)]
    ppermute x8, starting transfers between devices: 21.6 us -> 23.5 us  [shifted(): return lax.ppermute(x, axis, pairs)]
    dot_general x4 -> x8, matrix products: 2.82 us -> 4.19 us  [the longest x4 2.7 us: rotated(): jnp.einsum('hil,qlfe->hqife', rotate, neighbour_data, precision=fast_mode)]
    sub x0 -> x2, other arithmetic: none -> 0.76 us  [per_device(): advanced - lifted_flux(remote_turned, -remote_turned, normals, values, wa...]
    unnamed x28, local copies, waits for them, and re-layouts: 2.98 us -> 2.36 us
    unnamed x112 -> x128, other arithmetic: 1.32 us -> 1.55 us
  transfers between devices with their start and end apart: 8 -> 8, of which waited for: 4 -> 3; matrix products, arithmetic and copies ran while one was open for 3% -> 9% of each run, Pallas kernels for 0% -> 0%
where the time goes in v7:
time: 61.1 us; the launch traced here: 60.4 us
  starting transfers between devices  23.5 us (38%)
  matrix products  15.8 us (26%)
  waiting for transfers between devices  9.37 us (15%)
  local copies, waits for them, and re-layouts  5.21 us (9%)
  other arithmetic  4.99 us (8%)
  between operations  1.59 us (3%)
    ppermute x8, starting transfers between devices, shifted(): return lax.ppermute(x, axis, pairs)  23.5 us
    ppermute x8, waiting for transfers between devices, shifted(): return lax.ppermute(x, axis, pairs)  9.37 us
    dot_general x10, matrix products, predict(): jnp.einsum('dab,qbe->dqae', grad_matrix, derivative, precision=fast_mode)  6.45 us
    dot_general x4, matrix products, rotated(): jnp.einsum('hil,qlfe->hqife', rotate, neighbour_data, precision=fast_mode)  2.7 us
    unnamed x28, local copies, waits for them, and re-layouts  2.36 us
    dot_general x2, matrix products, per_device(): jnp.dot(flat_faces, gather_local, precision=exact_mode)  1.66 us
    unnamed x128, other arithmetic  1.55 us
    dot_general x4, matrix products, lifted_flux(): jnp.einsum('fai,pife->pae', face_lift, flux_total, precision=fast_mode)  1.49 us
  transfers between devices with their start and end apart: 8, of which 3 were waited for; matrix products, arithmetic and copies ran while one was open for 9% of the time, Pallas kernels for 0%

profile of v7, /device:TPU:25, one launch (start us, length us, event | category | flops | bytes accessed | tf_op | source)
XLA Modules:
  0.0 60.4 jit_solution(13124637423480018135)
XLA Ops:
  0.0 0.7 %iota_compare_fusion.6 = pred[16,128]{1,0:T(8,128)(4,1)S(1)} fusion(s32[128]{0:T(128)} %param.22), kind=kLoop, calls=%fused_computation.622 | loop fusion | flops 2048 | bytes 2560 | tf_op jit(solution)/shard_map/eq | solution.py:50
  0.7 0.8 %select_reduce_fusion = f32[3,128]{1,0:T(4,128)S(1)} fusion(f32[16,3]{0,1:T(4,128)} %param.21, pred[16,128]{1,0:T(8,128)(4,1)S(1)} %iota_compare_fusion.6), kind=kLoop, calls=%fused_computation.620 | loop fusion | flops 11904 | bytes 3776 | tf_op jit(solution)/shard_map/reduce_sum | solution.py:51
  1.5 1.0 %slice_bitcast_fusion.11 = (s32[1,24]{1,0:T(1,128)S(1)}, s32[1,24]{1,0:T(1,128)S(1)}, s32[1,24]{1,0:T(1,128)S(1)}, s32[1,24]{1,0:T(1,128)S(1)}, s32[1,24]{1,0:T(...) fusion(s32[1,1,8,24]{3,2,1,0:T(8,128)} %param.28), kind=kLoop, calls=%fused_computation.649 | loop fusion | bytes 1536 | tf_op jit(solution)/shard_map/squeeze | solution.py:154
  2.6 0.8 %fusion.218 = (f32[3,1,128]{2,1,0:T(1,128)S(1)}, f32[3,1,128]{2,1,0:T(1,128)S(1)}, f32[3,1,128]{2,1,0:T(1,128)S(1)}) fusion(f32[3,3,128]{2,1,0:T(4,128)} %param.23), kind=kLoop, calls=%fused_computation.669 | loop fusion | bytes 9216 | tf_op jit(solution)/shard_map/slice | solution.py:69
  3.4 1.6 %multiply_reduce_fusion.33 = (f32[9,56,128]{2,1,0:T(8,128)S(1)}, f32[9,56,128]{2,1,0:T(8,128)S(1)}, f32[9,56,128]{2,1,0:T(8,128)S(1)}) fusion(f32[3,128]{1,0:T(4,128)S(1)} %get-tuple-element.110, f32[3,128]{1,0:T(4,128)S(1)} %get-tuple-element.111, f32[3,128]{1,0:T(4,128)S(1)} %bitcast.343, f32[3,56,56]{2,1,0:T(8,128)S(1)} %copy-done, f32[9,56,128]{2,1,0:T(8,128)} %param.15), kind=kOutput, calls=%fused_computation.70 | convolution fusion | flops 65995776 | bytes 1074432 | tf_op jit(solution)/shard_map/dab,qbe->dqae/dot_general | solution.py:78
  8.0 0.8 %copy-done.1 = f32[9,56,128]{2,1,0:T(8,128)S(1)} copy-done((f32[9,56,128]{2,1,0:T(8,128)S(1)}, f32[9,56,128]{2,1,0:T(8,128)}, u32[]{:S(2)}) %copy-start.1) | copy-done | bytes 258072
  10.6 3.8 %collective-permute-start.1 = (f32[72,189]{1,0:T(8,128)S(1)}, f32[72,189]{1,0:T(8,128)S(1)}, u32[]{:S(2)}, u32[]{:S(2)}) collective-permute-start(f32[72,189]{1,0:T(8,128)S(1)} %get-tuple-element.69), channel_id=1, source_target_pairs={{0,1},{1,2},{2,3},{4,5},{5,6},{6,7},{8,9},{9,10},{10,11},{12,13},{... | collective-permute-start | bytes 163304 | tf_op jit(solution)/shard_map/ppermute | solution.py:45
  14.5 1.9 %collective-permute-start = (f32[72,189]{1,0:T(8,128)S(1)}, f32[72,189]{1,0:T(8,128)S(1)}, u32[]{:S(2)}, u32[]{:S(2)}) collective-permute-start(f32[72,189]{1,0:T(8,128)S(1)} %get-tuple-element.70), channel_id=1, source_target_pairs={{1,0},{2,1},{3,2},{5,4},{6,5},{7,6},{9,8},{10,9},{11,10},{13,12},{... | collective-permute-start | bytes 163304 | tf_op jit(solution)/shard_map/ppermute | solution.py:45
  17.4 0.8 %convolution_bitcast_fusion.18 = f32[9,21,4,128,1]{3,1,4,2,0:T(8,128)S(1)} fusion(s32[4,128]{1,0:T(4,128)S(1)} %maximum_add_fusion, pred[4,128]{1,0:T(4,128)(4,1)S(1)} %get-tuple-element.50, f32[9,21,512,1]{2,1,0,3:T(8,128)S(1)} %reshape.1884), kind=kOutput, calls=%fused_computation.26 | convolution fusion | flops 595066880 | bytes 776704 | tf_op jit(solution)/shard_map/dot_general | solution.py:169
  18.2 0.7 %fusion.4 = f32[9,21,4,128]{3,1,2,0:T(8,128)S(1)} fusion(f32[9,21,4,128,1]{3,1,4,2,0:T(8,128)S(1)} %convolution_bitcast_fusion.18, f32[3,4,128]{2,0,1:T(4,128)S(1)} %fusion.205, f32[3,21,21]{2,1,0:T(8,128)S(1)} %copy-done.3), kind=kOutput, calls=%fused_computation.8 | convolution fusion | flops 37062144 | bytes 785580 | tf_op jit(solution)/shard_map/hil,qlfe->hqife/dot_general | solution.py:94
  20.4 3.0 %collective-permute-start.2 = (f32[72,189]{1,0:T(8,128)S(1)}, f32[72,189]{1,0:T(8,128)S(1)}, u32[]{:S(2)}, u32[]{:S(2)}) collective-permute-start(f32[72,189]{1,0:T(8,128)S(1)} %pad_maximum_fusion.2), channel_id=1, source_target_pairs={{4,0},{8,4},{12,8},{16,12},{20,16},{24,20},{28,24},{5,1},{9,5},{13... | collective-permute-start | bytes 163304 | tf_op jit(solution)/shard_map/ppermute | solution.py:45
  23.5 2.5 %collective-permute-start.3 = (f32[72,189]{1,0:T(8,128)S(1)}, f32[72,189]{1,0:T(8,128)S(1)}, u32[]{:S(2)}, u32[]{:S(2)}) collective-permute-start(f32[72,189]{1,0:T(8,128)S(1)} %pad_maximum_fusion.3), channel_id=1, source_target_pairs={{0,4},{4,8},{8,12},{12,16},{16,20},{20,24},{24,28},{1,5},{5,9},{9,... | collective-permute-start | bytes 163304 | tf_op jit(solution)/shard_map/ppermute | solution.py:45
  26.1 3.4 %collective-permute-done.3 = f32[72,189]{1,0:T(8,128)S(1)} collective-permute-done((f32[72,189]{1,0:T(8,128)S(1)}, f32[72,189]{1,0:T(8,128)S(1)}, u32[]{:S(2)}, u32[]{:S(2)}) %collective-permute-start.3) | collective-permute-done | bytes 54464 | tf_op jit(solution)/shard_map/ppermute | solution.py:45
  30.1 0.7 %fusion.5 = f32[9,21,4,128]{3,1,2,0:T(8,128)S(1)} fusion(f32[3,4,128]{2,0,1:T(4,128)S(1)} %fusion.205, f32[9,21,4,128,1]{3,2,1,0,4:T(4,128)S(1)} %bitcast.338, f32[3,21,21]{2,1,0:T(8,128)S(1)} %copy-done.3), kind=kOutput, calls=%fused_computation.9 | convolution fusion | flops 37062144 | bytes 785580 | tf_op jit(solution)/shard_map/hil,qlfe->hqife/dot_general | solution.py:94
  36.9 5.1 %collective-permute-start.5 = (f32[72,189]{1,0:T(8,128)S(1)}, f32[72,189]{1,0:T(8,128)S(1)}, u32[]{:S(2)}, u32[]{:S(2)}) collective-permute-start(f32[72,189]{1,0:T(8,128)S(1)} %get-tuple-element.65), channel_id=1, source_target_pairs={{0,1},{1,2},{2,3},{4,5},{5,6},{6,7},{8,9},{9,10},{10,11},{12,13},{... | collective-permute-start | bytes 163304 | tf_op jit(solution)/shard_map/ppermute | solution.py:45
  42.0 0.8 %convolution_bitcast_fusion.16 = f32[9,21,4,128,1]{3,1,4,2,0:T(8,128)S(1)} fusion(s32[4,128]{1,0:T(4,128)S(1)} %maximum_add_fusion, pred[4,128]{1,0:T(4,128)(4,1)S(1)} %get-tuple-element.50, f32[9,21,512,1]{2,1,0,3:T(8,128)S(1)} %reshape.1900), kind=kOutput, calls=%fused_computation.24 | convolution fusion | flops 595066880 | bytes 776704 | tf_op jit(solution)/shard_map/dot_general | solution.py:169
  42.8 0.7 %fusion.6 = f32[9,21,4,128]{3,1,2,0:T(8,128)S(1)} fusion(f32[9,21,4,128,1]{3,1,4,2,0:T(8,128)S(1)} %convolution_bitcast_fusion.16, f32[3,4,128]{2,0,1:T(4,128)S(1)} %fusion.205, f32[3,21,21]{2,1,0:T(8,128)S(1)} %copy-done.3), kind=kOutput, calls=%fused_computation.10 | convolution fusion | flops 37062144 | bytes 785580 | tf_op jit(solution)/shard_map/hil,qlfe->hqife/dot_general | solution.py:94
  44.0 1.9 %collective-permute-start.4 = (f32[72,189]{1,0:T(8,128)S(1)}, f32[72,189]{1,0:T(8,128)S(1)}, u32[]{:S(2)}, u32[]{:S(2)}) collective-permute-start(f32[72,189]{1,0:T(8,128)S(1)} %get-tuple-element.66), channel_id=1, source_target_pairs={{1,0},{2,1},{3,2},{5,4},{6,5},{7,6},{9,8},{10,9},{11,10},{13,12},{... | collective-permute-start | bytes 163304 | tf_op jit(solution)/shard_map/ppermute | solution.py:45
  46.0 3.7 %collective-permute-done.4 = f32[72,189]{1,0:T(8,128)S(1)} collective-permute-done((f32[72,189]{1,0:T(8,128)S(1)}, f32[72,189]{1,0:T(8,128)S(1)}, u32[]{:S(2)}, u32[]{:S(2)}) %collective-permute-start.4) | collective-permute-done | bytes 54464 | tf_op jit(solution)/shard_map/ppermute | solution.py:45
  49.7 1.9 %collective-permute-start.6 = (f32[72,189]{1,0:T(8,128)S(1)}, f32[72,189]{1,0:T(8,128)S(1)}, u32[]{:S(2)}, u32[]{:S(2)}) collective-permute-start(f32[72,189]{1,0:T(8,128)S(1)} %pad_maximum_fusion.4), channel_id=1, source_target_pairs={{4,0},{8,4},{12,8},{16,12},{20,16},{24,20},{28,24},{5,1},{9,5},{13... | collective-permute-start | bytes 163304 | tf_op jit(solution)/shard_map/ppermute | solution.py:45
  51.6 3.4 %collective-permute-start.7 = (f32[72,189]{1,0:T(8,128)S(1)}, f32[72,189]{1,0:T(8,128)S(1)}, u32[]{:S(2)}, u32[]{:S(2)}) collective-permute-start(f32[72,189]{1,0:T(8,128)S(1)} %pad_maximum_fusion.5), channel_id=1, source_target_pairs={{0,4},{4,8},{8,12},{12,16},{16,20},{20,24},{24,28},{1,5},{5,9},{9,... | collective-permute-start | bytes 163304 | tf_op jit(solution)/shard_map/ppermute | solution.py:45
  55.4 2.2 %collective-permute-done.7 = f32[72,189]{1,0:T(8,128)S(1)} collective-permute-done((f32[72,189]{1,0:T(8,128)S(1)}, f32[72,189]{1,0:T(8,128)S(1)}, u32[]{:S(2)}, u32[]{:S(2)}) %collective-permute-start.7) | collective-permute-done | bytes 54464 | tf_op jit(solution)/shard_map/ppermute | solution.py:45
  58.3 0.7 %fusion.7 = f32[9,21,4,128]{3,1,2,0:T(8,128)S(1)} fusion(f32[3,4,128]{2,0,1:T(4,128)S(1)} %fusion.205, f32[9,21,4,128,1]{3,2,1,0,4:T(4,128)S(1)} %bitcast.337, f32[3,21,21]{2,1,0:T(8,128)S(1)} %copy-done.3), kind=kOutput, calls=%fused_computation.11 | convolution fusion | flops 37062144 | bytes 785580 | tf_op jit(solution)/shard_map/hil,qlfe->hqife/dot_general | solution.py:94
  59.7 0.7 %sub.23 = f32[9,56,128]{2,1,0:T(8,128)} subtract(f32[9,56,128]{2,1,0:T(8,128)S(1)} %fusion.9, f32[9,56,128]{2,1,0:T(8,128)S(1)} %convolution_bitcast_fusion.20) | non-fusion elementwise | flops 64512 | bytes 774144 | tf_op jit(solution)/shard_map/sub | solution.py:192
  (235 shorter events, 15.2 us)
Async XLA Ops:
  0.0 3.4 %copy-start = (f32[3,56,56]{2,1,0:T(8,128)S(1)}, f32[3,56,56]{2,1,0:T(8,128)}, u32[]{:S(2)}) copy-start(f32[3,56,56]{2,1,0:T(8,128)} %param.16) | copy-start | bytes 112900
  7.9 1.0 %copy-start.1 = (f32[9,56,128]{2,1,0:T(8,128)S(1)}, f32[9,56,128]{2,1,0:T(8,128)}, u32[]{:S(2)}) copy-start(f32[9,56,128]{2,1,0:T(8,128)} %param.15) | copy-start | bytes 774148
  8.8 0.8 %copy-start.5 = (f32[4,21,56]{2,0,1:T(4,128)S(1)}, f32[4,21,56]{2,0,1:T(4,128)}, u32[]{:S(2)}) copy-start(f32[4,21,56]{2,0,1:T(4,128)} %param.18) | copy-start | bytes 56452
  10.1 6.2 %copy-start.6 = (f32[4,3,128]{2,0,1:T(4,128)S(1)}, f32[4,3,128]{2,0,1:T(4,128)}, u32[]{:S(2)}) copy-start(f32[4,3,128]{2,0,1:T(4,128)} %param.24) | copy-start | bytes 18436
  10.6 6.0 %copy-start.7 = (s32[4,128]{1,0:T(4,128)S(1)}, s32[4,128]{1,0:T(4,128)}, u32[]{:S(2)}) copy-start(s32[4,128]{1,0:T(4,128)} %param.26) | copy-start | bytes 6148
  10.6 6.0 %copy-start.9 = (s32[4,128]{1,0:T(4,128)S(1)}, s32[4,128]{1,0:T(4,128)}, u32[]{:S(2)}) copy-start(s32[4,128]{1,0:T(4,128)} %param.27) | copy-start | bytes 6148
  10.6 6.0 %copy-start.10 = (s32[4,128]{1,0:T(4,128)S(1)}, s32[4,128]{1,0:T(4,128)}, u32[]{:S(2)}) copy-start(s32[4,128]{1,0:T(4,128)} %param.25) | copy-start | bytes 6148
  10.6 6.1 %copy-start.4 = (f32[3,56,56]{2,1,0:T(8,128)S(1)}, f32[3,56,56]{2,1,0:T(8,128)}, u32[]{:S(2)}) copy-start(f32[3,56,56]{2,1,0:T(8,128)} %param.17) | copy-start | bytes 112900
  10.6 9.8 %collective-permute-start.1 = (f32[72,189]{1,0:T(8,128)S(1)}, f32[72,189]{1,0:T(8,128)S(1)}, u32[]{:S(2)}, u32[]{:S(2)}) collective-permute-start(f32[72,189]{1,0:T(8,128)S(1)} %get-tuple-element.69), channel_id=1, source_target_pairs={{0,1},{1,2},{2,3},{4,5},{5,6},{6,7},{8,9},{9,10},{10,11},{12,13},{... | collective-permute-start | bytes 163304 | tf_op jit(solution)/shard_map/ppermute | solution.py:45
  14.5 5.9 %collective-permute-start = (f32[72,189]{1,0:T(8,128)S(1)}, f32[72,189]{1,0:T(8,128)S(1)}, u32[]{:S(2)}, u32[]{:S(2)}) collective-permute-start(f32[72,189]{1,0:T(8,128)S(1)} %get-tuple-element.70), channel_id=1, source_target_pairs={{1,0},{2,1},{3,2},{5,4},{6,5},{7,6},{9,8},{10,9},{11,10},{13,12},{... | collective-permute-start | bytes 163304 | tf_op jit(solution)/shard_map/ppermute | solution.py:45
  17.4 0.8 %copy-start.3 = (f32[3,21,21]{2,1,0:T(8,128)S(1)}, f32[3,21,21]{2,1,0:T(8,128)}, u32[]{:S(2)}) copy-start(f32[3,21,21]{2,1,0:T(8,128)} %param.20) | copy-start | bytes 15880
  19.2 0.8 %copy-start.2 = (f32[4,56,21]{1,0,2:T(4,128)S(1)}, f32[4,56,21]{1,0,2:T(4,128)}, u32[]{:S(2)}) copy-start(f32[4,56,21]{1,0,2:T(4,128)} %param.19) | copy-start | bytes 56452
  20.4 5.6 %copy-start.8 = (s32[1,1,8,24]{3,2,1,0:T(8,128)S(1)}, s32[1,1,8,24]{3,2,1,0:T(8,128)}, u32[]{:S(2)}) copy-start(s32[1,1,8,24]{3,2,1,0:T(8,128)} %param.29) | copy-start | bytes 2308
  20.4 5.6 %collective-permute-start.2 = (f32[72,189]{1,0:T(8,128)S(1)}, f32[72,189]{1,0:T(8,128)S(1)}, u32[]{:S(2)}, u32[]{:S(2)}) collective-permute-start(f32[72,189]{1,0:T(8,128)S(1)} %pad_maximum_fusion.2), channel_id=1, source_target_pairs={{4,0},{8,4},{12,8},{16,12},{20,16},{24,20},{28,24},{5,1},{9,5},{13... | collective-permute-start | bytes 163304 | tf_op jit(solution)/shard_map/ppermute | solution.py:45
  23.5 6.0 %collective-permute-start.3 = (f32[72,189]{1,0:T(8,128)S(1)}, f32[72,189]{1,0:T(8,128)S(1)}, u32[]{:S(2)}, u32[]{:S(2)}) collective-permute-start(f32[72,189]{1,0:T(8,128)S(1)} %pad_maximum_fusion.3), channel_id=1, source_target_pairs={{0,4},{4,8},{8,12},{12,16},{16,20},{20,24},{24,28},{1,5},{5,9},{9,... | collective-permute-start | bytes 163304 | tf_op jit(solution)/shard_map/ppermute | solution.py:45
  36.9 9.1 %collective-permute-start.5 = (f32[72,189]{1,0:T(8,128)S(1)}, f32[72,189]{1,0:T(8,128)S(1)}, u32[]{:S(2)}, u32[]{:S(2)}) collective-permute-start(f32[72,189]{1,0:T(8,128)S(1)} %get-tuple-element.65), channel_id=1, source_target_pairs={{0,1},{1,2},{2,3},{4,5},{5,6},{6,7},{8,9},{9,10},{10,11},{12,13},{... | collective-permute-start | bytes 163304 | tf_op jit(solution)/shard_map/ppermute | solution.py:45
  44.0 5.7 %collective-permute-start.4 = (f32[72,189]{1,0:T(8,128)S(1)}, f32[72,189]{1,0:T(8,128)S(1)}, u32[]{:S(2)}, u32[]{:S(2)}) collective-permute-start(f32[72,189]{1,0:T(8,128)S(1)} %get-tuple-element.66), channel_id=1, source_target_pairs={{1,0},{2,1},{3,2},{5,4},{6,5},{7,6},{9,8},{10,9},{11,10},{13,12},{... | collective-permute-start | bytes 163304 | tf_op jit(solution)/shard_map/ppermute | solution.py:45
  49.7 5.7 %collective-permute-start.6 = (f32[72,189]{1,0:T(8,128)S(1)}, f32[72,189]{1,0:T(8,128)S(1)}, u32[]{:S(2)}, u32[]{:S(2)}) collective-permute-start(f32[72,189]{1,0:T(8,128)S(1)} %pad_maximum_fusion.4), channel_id=1, source_target_pairs={{4,0},{8,4},{12,8},{16,12},{20,16},{24,20},{28,24},{5,1},{9,5},{13... | collective-permute-start | bytes 163304 | tf_op jit(solution)/shard_map/ppermute | solution.py:45
  51.6 6.0 %collective-permute-start.7 = (f32[72,189]{1,0:T(8,128)S(1)}, f32[72,189]{1,0:T(8,128)S(1)}, u32[]{:S(2)}, u32[]{:S(2)}) collective-permute-start(f32[72,189]{1,0:T(8,128)S(1)} %pad_maximum_fusion.5), channel_id=1, source_target_pairs={{0,4},{4,8},{8,12},{12,16},{16,20},{20,24},{24,28},{1,5},{5,9},{9,... | collective-permute-start | bytes 163304 | tf_op jit(solution)/shard_map/ppermute | solution.py:45

commit v8 on v4

--- a/solution.py
+++ b/solution.py
@@ -116,7 +116,6 @@
 
 
 SEND_ORDER = (0, 3, 5, 2, 4, 7, 1, 6)
-RECV_ORDER = (4, 3, 6, 5, 7, 1, 0, 2)
 
 
 def deliver(outgoing, slot_total):
@@ -124,15 +123,15 @@
     left = shifted(outgoing[:group], "pcol", -1)
     right = shifted(outgoing[group : 2 * group], "pcol", 1)
     up_bundle = jnp.concatenate(
-        [outgoing[2 * group : 2 * group + slot_total], right[:slot_total], left[:slot_total]], axis=0
+        [right[:slot_total], outgoing[2 * group : 2 * group + slot_total], left[:slot_total]], axis=0
     )
     down_bundle = jnp.concatenate(
-        [outgoing[2 * group + slot_total :], right[2 * slot_total :], left[2 * slot_total :]], axis=0
+        [right[2 * slot_total :], outgoing[2 * group + slot_total :], left[2 * slot_total :]], axis=0
     )
     up = shifted(up_bundle, "prow", -1)
     down = shifted(down_bundle, "prow", 1)
     return jnp.concatenate(
-        [left[slot_total : 2 * slot_total], right[slot_total : 2 * slot_total], up, down], axis=0
+        [down, right[slot_total : 2 * slot_total], left[slot_total : 2 * slot_total], up], axis=0
     )
 
 
@@ -165,7 +164,7 @@
     source_ids = jnp.concatenate([send_list[0, 0, d : d + 1] for d in SEND_ORDER], axis=0)
     slot_total = source_ids.shape[1]
     gather_out = (source_ids.reshape(-1)[:, None] == face_ids[None, :]).astype(dtype)
-    targets = jnp.concatenate([recv_list[0, 0, d] for d in RECV_ORDER], axis=0)
+    targets = recv_list[0, 0].reshape(-1)
     scatter_in = ((targets[:, None] == face_ids[None, :]) & ~inside[None, :]).astype(dtype)
     current = dof_values
     for time_index in range(STEPS):

time: 58.8 us -> 58.8 us (level)
  no operation moved by 1% of the time
where the time goes in v8:
time: 58.8 us; the launch traced here: 58.1 us
  starting transfers between devices  21.6 us (37%)
  matrix products  14 us (24%)
  waiting for transfers between devices  12 us (20%)
  local copies, waits for them, and re-layouts  5.5 us (9%)
  other arithmetic  3.65 us (6%)
  between operations  1.38 us (2%)
    ppermute x8, starting transfers between devices, shifted(): return lax.ppermute(x, axis, pairs)  21.6 us
    ppermute x8, waiting for transfers between devices, shifted(): return lax.ppermute(x, axis, pairs)  12 us
    dot_general x10, matrix products, predict(): jnp.einsum('dab,qbe->dqae', grad_matrix, derivative, precision=fast_mode)  6.46 us
    unnamed x28, local copies, waits for them, and re-layouts  2.98 us
    dot_general x2, matrix products, face_update(): jnp.einsum('fai,pife->pae', face_lift, flux_total, precision=fast_mode)  1.46 us
    dot_general x2, matrix products, face_update(): jnp.einsum('hil,qlfe->hqife', rotate, neighbour_data, precision=fast_mode)  1.36 us
    unnamed x112, other arithmetic  1.32 us
    dot_general x2, matrix products, per_device(): jnp.dot(flat_faces, gather_local, precision=exact_mode)  1.22 us
  transfers between devices with their start and end apart: 8, of which 4 were waited for; matrix products, arithmetic and copies ran while one was open for 3% of the time, Pallas kernels for 0%

profile of v8, /device:TPU:25, one launch (start us, length us, event | category | flops | bytes accessed | tf_op | source)
XLA Modules:
  0.0 58.1 jit_solution(6352763660412387858)
XLA Ops:
  0.0 0.7 %iota_compare_fusion.6 = pred[16,128]{1,0:T(8,128)(4,1)S(1)} fusion(s32[128]{0:T(128)} %param.22), kind=kLoop, calls=%fused_computation.545 | loop fusion | flops 2048 | bytes 2560 | tf_op jit(solution)/shard_map/eq | solution.py:50
  0.7 0.8 %select_reduce_fusion = f32[3,128]{1,0:T(4,128)S(1)} fusion(f32[16,3]{0,1:T(4,128)} %param.21, pred[16,128]{1,0:T(8,128)(4,1)S(1)} %iota_compare_fusion.6), kind=kLoop, calls=%fused_computation.543 | loop fusion | flops 11904 | bytes 3776 | tf_op jit(solution)/shard_map/reduce_sum | solution.py:51
  1.5 1.0 %slice_bitcast_fusion.3 = (s32[1,24]{1,0:T(1,128)S(1)}, s32[1,24]{1,0:T(1,128)S(1)}, s32[1,24]{1,0:T(1,128)S(1)}, s32[1,24]{1,0:T(1,128)S(1)}, s32[1,24]{1,0:T(1...) fusion(s32[1,1,8,24]{3,2,1,0:T(8,128)} %param.28), kind=kLoop, calls=%fused_computation.558 | loop fusion | bytes 1536 | tf_op jit(solution)/shard_map/squeeze | solution.py:164
  2.6 0.8 %fusion.196 = (f32[3,1,128]{2,1,0:T(1,128)S(1)}, f32[3,1,128]{2,1,0:T(1,128)S(1)}, f32[3,1,128]{2,1,0:T(1,128)S(1)}) fusion(f32[3,3,128]{2,1,0:T(4,128)} %param.23), kind=kLoop, calls=%fused_computation.584 | loop fusion | bytes 9216 | tf_op jit(solution)/shard_map/slice | solution.py:69
  3.4 1.6 %multiply_reduce_fusion.33 = (f32[9,56,128]{2,1,0:T(8,128)S(1)}, f32[9,56,128]{2,1,0:T(8,128)S(1)}, f32[9,56,128]{2,1,0:T(8,128)S(1)}) fusion(f32[3,128]{1,0:T(4,128)S(1)} %get-tuple-element.88, f32[3,128]{1,0:T(4,128)S(1)} %get-tuple-element.89, f32[3,128]{1,0:T(4,128)S(1)} %bitcast.281, f32[3,56,56]{2,1,0:T(8,128)S(1)} %copy-done, f32[9,56,128]{2,1,0:T(8,128)} %param.15), kind=kOutput, calls=%fused_computation.63 | convolution fusion | flops 65995776 | bytes 1074432 | tf_op jit(solution)/shard_map/dab,qbe->dqae/dot_general | solution.py:78
  8.0 0.8 %copy-done.1 = f32[9,56,128]{2,1,0:T(8,128)S(1)} copy-done((f32[9,56,128]{2,1,0:T(8,128)S(1)}, f32[9,56,128]{2,1,0:T(8,128)}, u32[]{:S(2)}) %copy-start.1) | copy-done | bytes 258072
  9.0 0.6 %copy-done.3 = f32[4,21,56]{2,0,1:T(4,128)S(1)} copy-done((f32[4,21,56]{2,0,1:T(4,128)S(1)}, f32[4,21,56]{2,0,1:T(4,128)}, u32[]{:S(2)}) %copy-start.3) | copy-done | bytes 18840
  10.6 3.7 %collective-permute-start = (f32[72,189]{1,0:T(8,128)S(1)}, f32[72,189]{1,0:T(8,128)S(1)}, u32[]{:S(2)}, u32[]{:S(2)}) collective-permute-start(f32[72,189]{1,0:T(8,128)S(1)} %get-tuple-element.55), channel_id=1, source_target_pairs={{0,1},{1,2},{2,3},{4,5},{5,6},{6,7},{8,9},{9,10},{10,11},{12,13},{... | collective-permute-start | bytes 163304 | tf_op jit(solution)/shard_map/ppermute | solution.py:45
  14.3 1.9 %collective-permute-start.1 = (f32[72,189]{1,0:T(8,128)S(1)}, f32[72,189]{1,0:T(8,128)S(1)}, u32[]{:S(2)}, u32[]{:S(2)}) collective-permute-start(f32[72,189]{1,0:T(8,128)S(1)} %get-tuple-element.56), channel_id=1, source_target_pairs={{1,0},{2,1},{3,2},{5,4},{6,5},{7,6},{9,8},{10,9},{11,10},{13,12},{... | collective-permute-start | bytes 163304 | tf_op jit(solution)/shard_map/ppermute | solution.py:45
  17.8 2.2 %collective-permute-done.1 = f32[72,189]{1,0:T(8,128)S(1)} collective-permute-done((f32[72,189]{1,0:T(8,128)S(1)}, f32[72,189]{1,0:T(8,128)S(1)}, u32[]{:S(2)}, u32[]{:S(2)}) %collective-permute-start.1) | collective-permute-done | bytes 54464 | tf_op jit(solution)/shard_map/ppermute | solution.py:45
  20.0 3.0 %collective-permute-start.3 = (f32[72,189]{1,0:T(8,128)S(1)}, f32[72,189]{1,0:T(8,128)S(1)}, u32[]{:S(2)}, u32[]{:S(2)}) collective-permute-start(f32[72,189]{1,0:T(8,128)S(1)} %pad_maximum_fusion.1), channel_id=1, source_target_pairs={{4,0},{8,4},{12,8},{16,12},{20,16},{24,20},{28,24},{5,1},{9,5},{13... | collective-permute-start | bytes 163304 | tf_op jit(solution)/shard_map/ppermute | solution.py:45
  23.0 2.5 %collective-permute-start.2 = (f32[72,189]{1,0:T(8,128)S(1)}, f32[72,189]{1,0:T(8,128)S(1)}, u32[]{:S(2)}, u32[]{:S(2)}) collective-permute-start(f32[72,189]{1,0:T(8,128)S(1)} %pad_maximum_fusion), channel_id=1, source_target_pairs={{0,4},{4,8},{8,12},{12,16},{16,20},{20,24},{24,28},{1,5},{5,9},{9,... | collective-permute-start | bytes 163304 | tf_op jit(solution)/shard_map/ppermute | solution.py:45
  25.6 3.4 %collective-permute-done.2 = f32[72,189]{1,0:T(8,128)S(1)} collective-permute-done((f32[72,189]{1,0:T(8,128)S(1)}, f32[72,189]{1,0:T(8,128)S(1)}, u32[]{:S(2)}, u32[]{:S(2)}) %collective-permute-start.2) | collective-permute-done | bytes 54464 | tf_op jit(solution)/shard_map/ppermute | solution.py:45
  29.7 0.6 %copy-done.5 = f32[3,21,21]{2,1,0:T(8,128)S(1)} copy-done((f32[3,21,21]{2,1,0:T(8,128)S(1)}, f32[3,21,21]{2,1,0:T(8,128)}, u32[]{:S(2)}) %copy-start.5) | copy-done | bytes 5316
  30.3 0.7 %fusion.2 = f32[9,21,4,128]{3,1,2,0:T(8,128)S(1)} fusion(f32[3,4,128]{2,0,1:T(4,128)S(1)} %fusion.182, f32[9,21,4,128,1]{3,2,1,0,4:T(4,128)S(1)} %bitcast.276, f32[3,21,21]{2,1,0:T(8,128)S(1)} %copy-done.5), kind=kOutput, calls=%fused_computation.4 | convolution fusion | flops 37062144 | bytes 785580 | tf_op jit(solution)/shard_map/hil,qlfe->hqife/dot_general | solution.py:105
  31.4 0.7 %copy-done.4 = f32[4,56,21]{1,0,2:T(4,128)S(1)} copy-done((f32[4,56,21]{1,0,2:T(4,128)S(1)}, f32[4,56,21]{1,0,2:T(4,128)}, u32[]{:S(2)}) %copy-start.4) | copy-done | bytes 18840
  38.2 3.3 %collective-permute-start.4 = (f32[72,189]{1,0:T(8,128)S(1)}, f32[72,189]{1,0:T(8,128)S(1)}, u32[]{:S(2)}, u32[]{:S(2)}) collective-permute-start(f32[72,189]{1,0:T(8,128)S(1)} %get-tuple-element.51), channel_id=1, source_target_pairs={{0,1},{1,2},{2,3},{4,5},{5,6},{6,7},{8,9},{9,10},{10,11},{12,13},{... | collective-permute-start | bytes 163304 | tf_op jit(solution)/shard_map/ppermute | solution.py:45
  41.7 1.9 %collective-permute-start.5 = (f32[72,189]{1,0:T(8,128)S(1)}, f32[72,189]{1,0:T(8,128)S(1)}, u32[]{:S(2)}, u32[]{:S(2)}) collective-permute-start(f32[72,189]{1,0:T(8,128)S(1)} %get-tuple-element.52), channel_id=1, source_target_pairs={{1,0},{2,1},{3,2},{5,4},{6,5},{7,6},{9,8},{10,9},{11,10},{13,12},{... | collective-permute-start | bytes 163304 | tf_op jit(solution)/shard_map/ppermute | solution.py:45
  43.6 3.7 %collective-permute-done.5 = f32[72,189]{1,0:T(8,128)S(1)} collective-permute-done((f32[72,189]{1,0:T(8,128)S(1)}, f32[72,189]{1,0:T(8,128)S(1)}, u32[]{:S(2)}, u32[]{:S(2)}) %collective-permute-start.5) | collective-permute-done | bytes 54464 | tf_op jit(solution)/shard_map/ppermute | solution.py:45
  47.4 1.9 %collective-permute-start.7 = (f32[72,189]{1,0:T(8,128)S(1)}, f32[72,189]{1,0:T(8,128)S(1)}, u32[]{:S(2)}, u32[]{:S(2)}) collective-permute-start(f32[72,189]{1,0:T(8,128)S(1)} %pad_maximum_fusion.3), channel_id=1, source_target_pairs={{4,0},{8,4},{12,8},{16,12},{20,16},{24,20},{28,24},{5,1},{9,5},{13... | collective-permute-start | bytes 163304 | tf_op jit(solution)/shard_map/ppermute | solution.py:45
  49.3 3.4 %collective-permute-start.6 = (f32[72,189]{1,0:T(8,128)S(1)}, f32[72,189]{1,0:T(8,128)S(1)}, u32[]{:S(2)}, u32[]{:S(2)}) collective-permute-start(f32[72,189]{1,0:T(8,128)S(1)} %pad_maximum_fusion.2), channel_id=1, source_target_pairs={{0,4},{4,8},{8,12},{12,16},{16,20},{20,24},{24,28},{1,5},{5,9},{9,... | collective-permute-start | bytes 163304 | tf_op jit(solution)/shard_map/ppermute | solution.py:45
  52.7 2.6 %collective-permute-done.6 = f32[72,189]{1,0:T(8,128)S(1)} collective-permute-done((f32[72,189]{1,0:T(8,128)S(1)}, f32[72,189]{1,0:T(8,128)S(1)}, u32[]{:S(2)}, u32[]{:S(2)}) %collective-permute-start.6) | collective-permute-done | bytes 54464 | tf_op jit(solution)/shard_map/ppermute | solution.py:45
  56.0 0.7 %fusion.3 = f32[9,21,4,128]{3,1,2,0:T(8,128)S(1)} fusion(f32[3,4,128]{2,0,1:T(4,128)S(1)} %fusion.182, f32[9,21,4,128,1]{3,2,1,0,4:T(4,128)S(1)} %bitcast.275, f32[3,21,21]{2,1,0:T(8,128)S(1)} %copy-done.5), kind=kOutput, calls=%fused_computation.5 | convolution fusion | flops 37062144 | bytes 785580 | tf_op jit(solution)/shard_map/hil,qlfe->hqife/dot_general | solution.py:105
  57.0 1.1 %fusion.5 = f32[9,56,128]{2,1,0:T(8,128)} fusion(f32[9,21,4,128]{3,1,2,0:T(8,128)S(1)} %constant_dynamic-update-slice_fusion.117, f32[9,21,4,128]{3,1,2,0:T(8,128)S(1)} %convolution_bitcast_fusion.14, f32[9,21,4,128]{3,1,2,0:T(8,128)S(1)} %fusion.3, f32[9,56,128]{2,1,0:T(8,128)S(1)} %fusion.4, f32[9,56,128]{2,1,0:T(8,128)S(1)} %constant_dynamic-update-slice_fusion.108, ...), kind=kOutput, calls=%fused_computation.25 | convolution fusion | flops 33030144 | bytes 1956224 | tf_op jit(solution)/shard_map/fai,pife->pae/dot_general | solution.py:114
  (204 shorter events, 13.1 us)
Async XLA Ops:
  0.0 3.4 %copy-start = (f32[3,56,56]{2,1,0:T(8,128)S(1)}, f32[3,56,56]{2,1,0:T(8,128)}, u32[]{:S(2)}) copy-start(f32[3,56,56]{2,1,0:T(8,128)} %param.16) | copy-start | bytes 112900
  7.9 1.0 %copy-start.1 = (f32[9,56,128]{2,1,0:T(8,128)S(1)}, f32[9,56,128]{2,1,0:T(8,128)}, u32[]{:S(2)}) copy-start(f32[9,56,128]{2,1,0:T(8,128)} %param.15) | copy-start | bytes 774148
  8.8 0.8 %copy-start.3 = (f32[4,21,56]{2,0,1:T(4,128)S(1)}, f32[4,21,56]{2,0,1:T(4,128)}, u32[]{:S(2)}) copy-start(f32[4,21,56]{2,0,1:T(4,128)} %param.18) | copy-start | bytes 56452
  10.1 6.1 %copy-start.7 = (s32[4,128]{1,0:T(4,128)S(1)}, s32[4,128]{1,0:T(4,128)}, u32[]{:S(2)}) copy-start(s32[4,128]{1,0:T(4,128)} %param.26) | copy-start | bytes 6148
  10.2 6.1 %copy-start.9 = (s32[4,128]{1,0:T(4,128)S(1)}, s32[4,128]{1,0:T(4,128)}, u32[]{:S(2)}) copy-start(s32[4,128]{1,0:T(4,128)} %param.27) | copy-start | bytes 6148
  10.2 6.1 %copy-start.6 = (f32[4,3,128]{2,0,1:T(4,128)S(1)}, f32[4,3,128]{2,0,1:T(4,128)}, u32[]{:S(2)}) copy-start(f32[4,3,128]{2,0,1:T(4,128)} %param.24) | copy-start | bytes 18436
  10.2 6.2 %copy-start.10 = (s32[4,128]{1,0:T(4,128)S(1)}, s32[4,128]{1,0:T(4,128)}, u32[]{:S(2)}) copy-start(s32[4,128]{1,0:T(4,128)} %param.25) | copy-start | bytes 6148
  10.2 6.2 %copy-start.2 = (f32[3,56,56]{2,1,0:T(8,128)S(1)}, f32[3,56,56]{2,1,0:T(8,128)}, u32[]{:S(2)}) copy-start(f32[3,56,56]{2,1,0:T(8,128)} %param.17) | copy-start | bytes 112900
  10.6 7.1 %collective-permute-start = (f32[72,189]{1,0:T(8,128)S(1)}, f32[72,189]{1,0:T(8,128)S(1)}, u32[]{:S(2)}, u32[]{:S(2)}) collective-permute-start(f32[72,189]{1,0:T(8,128)S(1)} %get-tuple-element.55), channel_id=1, source_target_pairs={{0,1},{1,2},{2,3},{4,5},{5,6},{6,7},{8,9},{9,10},{10,11},{12,13},{... | collective-permute-start | bytes 163304 | tf_op jit(solution)/shard_map/ppermute | solution.py:45
  14.3 5.7 %collective-permute-start.1 = (f32[72,189]{1,0:T(8,128)S(1)}, f32[72,189]{1,0:T(8,128)S(1)}, u32[]{:S(2)}, u32[]{:S(2)}) collective-permute-start(f32[72,189]{1,0:T(8,128)S(1)} %get-tuple-element.56), channel_id=1, source_target_pairs={{1,0},{2,1},{3,2},{5,4},{6,5},{7,6},{9,8},{10,9},{11,10},{13,12},{... | collective-permute-start | bytes 163304 | tf_op jit(solution)/shard_map/ppermute | solution.py:45
  17.7 7.8 %copy-start.8 = (s32[1,1,8,24]{3,2,1,0:T(8,128)S(1)}, s32[1,1,8,24]{3,2,1,0:T(8,128)}, u32[]{:S(2)}) copy-start(s32[1,1,8,24]{3,2,1,0:T(8,128)} %param.29) | copy-start | bytes 2308
  20.0 5.6 %collective-permute-start.3 = (f32[72,189]{1,0:T(8,128)S(1)}, f32[72,189]{1,0:T(8,128)S(1)}, u32[]{:S(2)}, u32[]{:S(2)}) collective-permute-start(f32[72,189]{1,0:T(8,128)S(1)} %pad_maximum_fusion.1), channel_id=1, source_target_pairs={{4,0},{8,4},{12,8},{16,12},{20,16},{24,20},{28,24},{5,1},{9,5},{13... | collective-permute-start | bytes 163304 | tf_op jit(solution)/shard_map/ppermute | solution.py:45
  23.0 6.0 %collective-permute-start.2 = (f32[72,189]{1,0:T(8,128)S(1)}, f32[72,189]{1,0:T(8,128)S(1)}, u32[]{:S(2)}, u32[]{:S(2)}) collective-permute-start(f32[72,189]{1,0:T(8,128)S(1)} %pad_maximum_fusion), channel_id=1, source_target_pairs={{0,4},{4,8},{8,12},{12,16},{16,20},{20,24},{24,28},{1,5},{5,9},{9,... | collective-permute-start | bytes 163304 | tf_op jit(solution)/shard_map/ppermute | solution.py:45
  29.6 0.8 %copy-start.5 = (f32[3,21,21]{2,1,0:T(8,128)S(1)}, f32[3,21,21]{2,1,0:T(8,128)}, u32[]{:S(2)}) copy-start(f32[3,21,21]{2,1,0:T(8,128)} %param.20) | copy-start | bytes 15880
  31.3 0.8 %copy-start.4 = (f32[4,56,21]{1,0,2:T(4,128)S(1)}, f32[4,56,21]{1,0,2:T(4,128)}, u32[]{:S(2)}) copy-start(f32[4,56,21]{1,0,2:T(4,128)} %param.19) | copy-start | bytes 56452
  38.2 5.4 %collective-permute-start.4 = (f32[72,189]{1,0:T(8,128)S(1)}, f32[72,189]{1,0:T(8,128)S(1)}, u32[]{:S(2)}, u32[]{:S(2)}) collective-permute-start(f32[72,189]{1,0:T(8,128)S(1)} %get-tuple-element.51), channel_id=1, source_target_pairs={{0,1},{1,2},{2,3},{4,5},{5,6},{6,7},{8,9},{9,10},{10,11},{12,13},{... | collective-permute-start | bytes 163304 | tf_op jit(solution)/shard_map/ppermute | solution.py:45
  41.7 5.7 %collective-permute-start.5 = (f32[72,189]{1,0:T(8,128)S(1)}, f32[72,189]{1,0:T(8,128)S(1)}, u32[]{:S(2)}, u32[]{:S(2)}) collective-permute-start(f32[72,189]{1,0:T(8,128)S(1)} %get-tuple-element.52), channel_id=1, source_target_pairs={{1,0},{2,1},{3,2},{5,4},{6,5},{7,6},{9,8},{10,9},{11,10},{13,12},{... | collective-permute-start | bytes 163304 | tf_op jit(solution)/shard_map/ppermute | solution.py:45
  47.4 5.3 %collective-permute-start.7 = (f32[72,189]{1,0:T(8,128)S(1)}, f32[72,189]{1,0:T(8,128)S(1)}, u32[]{:S(2)}, u32[]{:S(2)}) collective-permute-start(f32[72,189]{1,0:T(8,128)S(1)} %pad_maximum_fusion.3), channel_id=1, source_target_pairs={{4,0},{8,4},{12,8},{16,12},{20,16},{24,20},{28,24},{5,1},{9,5},{13... | collective-permute-start | bytes 163304 | tf_op jit(solution)/shard_map/ppermute | solution.py:45
  49.3 6.0 %collective-permute-start.6 = (f32[72,189]{1,0:T(8,128)S(1)}, f32[72,189]{1,0:T(8,128)S(1)}, u32[]{:S(2)}, u32[]{:S(2)}) collective-permute-start(f32[72,189]{1,0:T(8,128)S(1)} %pad_maximum_fusion.2), channel_id=1, source_target_pairs={{0,4},{4,8},{8,12},{12,16},{16,20},{20,24},{24,28},{1,5},{5,9},{9,... | collective-permute-start | bytes 163304 | tf_op jit(solution)/shard_map/ppermute | solution.py:45

commit v9 on v4

--- a/solution.py
+++ b/solution.py
@@ -115,24 +115,24 @@
     return current + volume - lifted
 
 
-SEND_ORDER = (0, 3, 5, 2, 4, 7, 1, 6)
-RECV_ORDER = (4, 3, 6, 5, 7, 1, 0, 2)
+SEND_ORDER = (0, 1, 2, 5, 6, 7, 3, 4)
+RECV_ORDER = (4, 7, 2, 3, 5, 0, 6, 1)
 
 
 def deliver(outgoing, slot_total):
     group = 3 * slot_total
-    left = shifted(outgoing[:group], "pcol", -1)
-    right = shifted(outgoing[group : 2 * group], "pcol", 1)
-    up_bundle = jnp.concatenate(
-        [outgoing[2 * group : 2 * group + slot_total], right[:slot_total], left[:slot_total]], axis=0
-    )
-    down_bundle = jnp.concatenate(
-        [outgoing[2 * group + slot_total :], right[2 * slot_total :], left[2 * slot_total :]], axis=0
-    )
-    up = shifted(up_bundle, "prow", -1)
-    down = shifted(down_bundle, "prow", 1)
+    up = shifted(outgoing[:group], "prow", -1)
+    down = shifted(outgoing[group : 2 * group], "prow", 1)
+    left_bundle = jnp.concatenate(
+        [outgoing[2 * group : 2 * group + slot_total], up[:slot_total], down[:slot_total]], axis=0
+    )
+    right_bundle = jnp.concatenate(
+        [outgoing[2 * group + slot_total :], up[2 * slot_total :], down[2 * slot_total :]], axis=0
+    )
+    left = shifted(left_bundle, "pcol", -1)
+    right = shifted(right_bundle, "pcol", 1)
     return jnp.concatenate(
-        [left[slot_total : 2 * slot_total], right[slot_total : 2 * slot_total], up, down], axis=0
+        [left, right, up[slot_total : 2 * slot_total], down[slot_total : 2 * slot_total]], axis=0
     )
 
 

time: 58.8 us -> 59.9 us (1.019)
  starting transfers between devices: 21.6 us -> 22.7 us
    ppermute x8, starting transfers between devices: 21.6 us -> 22.7 us  [shifted(): return lax.ppermute(x, axis, pairs)]
where the time goes in v9:
time: 59.9 us; the launch traced here: 59.2 us
  starting transfers between devices  22.7 us (38%)
  matrix products  14 us (23%)
  waiting for transfers between devices  12 us (20%)
  local copies, waits for them, and re-layouts  5.52 us (9%)
  other arithmetic  3.65 us (6%)
  between operations  1.38 us (2%)
    ppermute x8, starting transfers between devices, shifted(): return lax.ppermute(x, axis, pairs)  22.7 us
    ppermute x8, waiting for transfers between devices, shifted(): return lax.ppermute(x, axis, pairs)  12 us
    dot_general x10, matrix products, predict(): jnp.einsum('dab,qbe->dqae', grad_matrix, derivative, precision=fast_mode)  6.46 us
    unnamed x28, local copies, waits for them, and re-layouts  2.98 us
    dot_general x2, matrix products, face_update(): jnp.einsum('fai,pife->pae', face_lift, flux_total, precision=fast_mode)  1.46 us
    dot_general x2, matrix products, face_update(): jnp.einsum('hil,qlfe->hqife', rotate, neighbour_data, precision=fast_mode)  1.36 us
    unnamed x112, other arithmetic  1.32 us
    dot_general x2, matrix products, per_device(): jnp.dot(flat_faces, gather_local, precision=exact_mode)  1.22 us
  transfers between devices with their start and end apart: 8, of which 4 were waited for; matrix products, arithmetic and copies ran while one was open for 3% of the time, Pallas kernels for 0%

profile of v9, /device:TPU:25, one launch (start us, length us, event | category | flops | bytes accessed | tf_op | source)
XLA Modules:
  0.0 59.2 jit_solution(4199583159171669972)
XLA Ops:
  0.0 0.7 %iota_compare_fusion.6 = pred[16,128]{1,0:T(8,128)(4,1)S(1)} fusion(s32[128]{0:T(128)} %param.22), kind=kLoop, calls=%fused_computation.545 | loop fusion | flops 2048 | bytes 2560 | tf_op jit(solution)/shard_map/eq | solution.py:50
  0.7 0.8 %select_reduce_fusion = f32[3,128]{1,0:T(4,128)S(1)} fusion(f32[16,3]{0,1:T(4,128)} %param.21, pred[16,128]{1,0:T(8,128)(4,1)S(1)} %iota_compare_fusion.6), kind=kLoop, calls=%fused_computation.543 | loop fusion | flops 11904 | bytes 3776 | tf_op jit(solution)/shard_map/reduce_sum | solution.py:51
  1.5 1.0 %slice_bitcast_fusion.11 = (s32[1,24]{1,0:T(1,128)S(1)}, s32[1,24]{1,0:T(1,128)S(1)}, s32[1,24]{1,0:T(1,128)S(1)}, s32[1,24]{1,0:T(1,128)S(1)}, s32[1,24]{1,0:T(...) fusion(s32[1,1,8,24]{3,2,1,0:T(8,128)} %param.28), kind=kLoop, calls=%fused_computation.566 | loop fusion | bytes 1536 | tf_op jit(solution)/shard_map/squeeze | solution.py:165
  2.6 0.8 %fusion.196 = (f32[3,1,128]{2,1,0:T(1,128)S(1)}, f32[3,1,128]{2,1,0:T(1,128)S(1)}, f32[3,1,128]{2,1,0:T(1,128)S(1)}) fusion(f32[3,3,128]{2,1,0:T(4,128)} %param.23), kind=kLoop, calls=%fused_computation.592 | loop fusion | bytes 9216 | tf_op jit(solution)/shard_map/slice | solution.py:69
  3.4 1.6 %multiply_reduce_fusion.33 = (f32[9,56,128]{2,1,0:T(8,128)S(1)}, f32[9,56,128]{2,1,0:T(8,128)S(1)}, f32[9,56,128]{2,1,0:T(8,128)S(1)}) fusion(f32[3,128]{1,0:T(4,128)S(1)} %get-tuple-element.96, f32[3,128]{1,0:T(4,128)S(1)} %get-tuple-element.97, f32[3,128]{1,0:T(4,128)S(1)} %bitcast.295, f32[3,56,56]{2,1,0:T(8,128)S(1)} %copy-done, f32[9,56,128]{2,1,0:T(8,128)} %param.15), kind=kOutput, calls=%fused_computation.63 | convolution fusion | flops 65995776 | bytes 1074432 | tf_op jit(solution)/shard_map/dab,qbe->dqae/dot_general | solution.py:78
  8.0 0.8 %copy-done.1 = f32[9,56,128]{2,1,0:T(8,128)S(1)} copy-done((f32[9,56,128]{2,1,0:T(8,128)S(1)}, f32[9,56,128]{2,1,0:T(8,128)}, u32[]{:S(2)}) %copy-start.1) | copy-done | bytes 258072
  9.0 0.6 %copy-done.3 = f32[4,21,56]{2,0,1:T(4,128)S(1)} copy-done((f32[4,21,56]{2,0,1:T(4,128)S(1)}, f32[4,21,56]{2,0,1:T(4,128)}, u32[]{:S(2)}) %copy-start.3) | copy-done | bytes 18840
  10.6 3.0 %collective-permute-start = (f32[72,189]{1,0:T(8,128)S(1)}, f32[72,189]{1,0:T(8,128)S(1)}, u32[]{:S(2)}, u32[]{:S(2)}) collective-permute-start(f32[72,189]{1,0:T(8,128)S(1)} %get-tuple-element.55), channel_id=1, source_target_pairs={{4,0},{8,4},{12,8},{16,12},{20,16},{24,20},{28,24},{5,1},{9,5},{13... | collective-permute-start | bytes 163304 | tf_op jit(solution)/shard_map/ppermute | solution.py:45
  13.6 2.3 %collective-permute-start.1 = (f32[72,189]{1,0:T(8,128)S(1)}, f32[72,189]{1,0:T(8,128)S(1)}, u32[]{:S(2)}, u32[]{:S(2)}) collective-permute-start(f32[72,189]{1,0:T(8,128)S(1)} %get-tuple-element.56), channel_id=1, source_target_pairs={{0,4},{4,8},{8,12},{12,16},{16,20},{20,24},{24,28},{1,5},{5,9},{9,... | collective-permute-start | bytes 163304 | tf_op jit(solution)/shard_map/ppermute | solution.py:45
  17.4 2.2 %collective-permute-done.1 = f32[72,189]{1,0:T(8,128)S(1)} collective-permute-done((f32[72,189]{1,0:T(8,128)S(1)}, f32[72,189]{1,0:T(8,128)S(1)}, u32[]{:S(2)}, u32[]{:S(2)}) %collective-permute-start.1) | collective-permute-done | bytes 54464 | tf_op jit(solution)/shard_map/ppermute | solution.py:45
  19.7 5.1 %collective-permute-start.3 = (f32[72,189]{1,0:T(8,128)S(1)}, f32[72,189]{1,0:T(8,128)S(1)}, u32[]{:S(2)}, u32[]{:S(2)}) collective-permute-start(f32[72,189]{1,0:T(8,128)S(1)} %pad_maximum_fusion.1), channel_id=1, source_target_pairs={{0,1},{1,2},{2,3},{4,5},{5,6},{6,7},{8,9},{9,10},{10,11},{12,13},{... | collective-permute-start | bytes 163304 | tf_op jit(solution)/shard_map/ppermute | solution.py:45
  24.8 2.1 %collective-permute-start.2 = (f32[72,189]{1,0:T(8,128)S(1)}, f32[72,189]{1,0:T(8,128)S(1)}, u32[]{:S(2)}, u32[]{:S(2)}) collective-permute-start(f32[72,189]{1,0:T(8,128)S(1)} %pad_maximum_fusion), channel_id=1, source_target_pairs={{1,0},{2,1},{3,2},{5,4},{6,5},{7,6},{9,8},{10,9},{11,10},{13,12},{... | collective-permute-start | bytes 163304 | tf_op jit(solution)/shard_map/ppermute | solution.py:45
  27.0 3.5 %collective-permute-done.2 = f32[72,189]{1,0:T(8,128)S(1)} collective-permute-done((f32[72,189]{1,0:T(8,128)S(1)}, f32[72,189]{1,0:T(8,128)S(1)}, u32[]{:S(2)}, u32[]{:S(2)}) %collective-permute-start.2) | collective-permute-done | bytes 54464 | tf_op jit(solution)/shard_map/ppermute | solution.py:45
  31.1 0.6 %copy-done.5 = f32[3,21,21]{2,1,0:T(8,128)S(1)} copy-done((f32[3,21,21]{2,1,0:T(8,128)S(1)}, f32[3,21,21]{2,1,0:T(8,128)}, u32[]{:S(2)}) %copy-start.5) | copy-done | bytes 5316
  31.7 0.7 %fusion.2 = f32[9,21,4,128]{3,1,2,0:T(8,128)S(1)} fusion(f32[3,4,128]{2,0,1:T(4,128)S(1)} %fusion.182, f32[9,21,4,128,1]{3,2,1,0,4:T(4,128)S(1)} %bitcast.290, f32[3,21,21]{2,1,0:T(8,128)S(1)} %copy-done.5), kind=kOutput, calls=%fused_computation.4 | convolution fusion | flops 37062144 | bytes 785580 | tf_op jit(solution)/shard_map/hil,qlfe->hqife/dot_general | solution.py:105
  32.8 0.7 %copy-done.4 = f32[4,56,21]{1,0,2:T(4,128)S(1)} copy-done((f32[4,56,21]{1,0,2:T(4,128)S(1)}, f32[4,56,21]{1,0,2:T(4,128)}, u32[]{:S(2)}) %copy-start.4) | copy-done | bytes 18840
  39.7 1.9 %collective-permute-start.4 = (f32[72,189]{1,0:T(8,128)S(1)}, f32[72,189]{1,0:T(8,128)S(1)}, u32[]{:S(2)}, u32[]{:S(2)}) collective-permute-start(f32[72,189]{1,0:T(8,128)S(1)} %get-tuple-element.51), channel_id=1, source_target_pairs={{4,0},{8,4},{12,8},{16,12},{20,16},{24,20},{28,24},{5,1},{9,5},{13... | collective-permute-start | bytes 163304 | tf_op jit(solution)/shard_map/ppermute | solution.py:45
  41.7 3.4 %collective-permute-start.5 = (f32[72,189]{1,0:T(8,128)S(1)}, f32[72,189]{1,0:T(8,128)S(1)}, u32[]{:S(2)}, u32[]{:S(2)}) collective-permute-start(f32[72,189]{1,0:T(8,128)S(1)} %get-tuple-element.52), channel_id=1, source_target_pairs={{0,4},{4,8},{8,12},{12,16},{16,20},{20,24},{24,28},{1,5},{5,9},{9,... | collective-permute-start | bytes 163304 | tf_op jit(solution)/shard_map/ppermute | solution.py:45
  45.1 2.6 %collective-permute-done.5 = f32[72,189]{1,0:T(8,128)S(1)} collective-permute-done((f32[72,189]{1,0:T(8,128)S(1)}, f32[72,189]{1,0:T(8,128)S(1)}, u32[]{:S(2)}, u32[]{:S(2)}) %collective-permute-start.5) | collective-permute-done | bytes 54464 | tf_op jit(solution)/shard_map/ppermute | solution.py:45
  47.8 3.0 %collective-permute-start.7 = (f32[72,189]{1,0:T(8,128)S(1)}, f32[72,189]{1,0:T(8,128)S(1)}, u32[]{:S(2)}, u32[]{:S(2)}) collective-permute-start(f32[72,189]{1,0:T(8,128)S(1)} %pad_maximum_fusion.3), channel_id=1, source_target_pairs={{0,1},{1,2},{2,3},{4,5},{5,6},{6,7},{8,9},{9,10},{10,11},{12,13},{... | collective-permute-start | bytes 163304 | tf_op jit(solution)/shard_map/ppermute | solution.py:45
  50.8 1.9 %collective-permute-start.6 = (f32[72,189]{1,0:T(8,128)S(1)}, f32[72,189]{1,0:T(8,128)S(1)}, u32[]{:S(2)}, u32[]{:S(2)}) collective-permute-start(f32[72,189]{1,0:T(8,128)S(1)} %pad_maximum_fusion.2), channel_id=1, source_target_pairs={{1,0},{2,1},{3,2},{5,4},{6,5},{7,6},{9,8},{10,9},{11,10},{13,12},{... | collective-permute-start | bytes 163304 | tf_op jit(solution)/shard_map/ppermute | solution.py:45
  52.8 3.7 %collective-permute-done.6 = f32[72,189]{1,0:T(8,128)S(1)} collective-permute-done((f32[72,189]{1,0:T(8,128)S(1)}, f32[72,189]{1,0:T(8,128)S(1)}, u32[]{:S(2)}, u32[]{:S(2)}) %collective-permute-start.6) | collective-permute-done | bytes 54464 | tf_op jit(solution)/shard_map/ppermute | solution.py:45
  57.1 0.7 %fusion.3 = f32[9,21,4,128]{3,1,2,0:T(8,128)S(1)} fusion(f32[3,4,128]{2,0,1:T(4,128)S(1)} %fusion.182, f32[9,21,4,128,1]{3,2,1,0,4:T(4,128)S(1)} %bitcast.289, f32[3,21,21]{2,1,0:T(8,128)S(1)} %copy-done.5), kind=kOutput, calls=%fused_computation.5 | convolution fusion | flops 37062144 | bytes 785580 | tf_op jit(solution)/shard_map/hil,qlfe->hqife/dot_general | solution.py:105
  58.2 1.1 %fusion.5 = f32[9,56,128]{2,1,0:T(8,128)} fusion(f32[9,21,4,128]{3,1,2,0:T(8,128)S(1)} %constant_dynamic-update-slice_fusion.117, f32[9,21,4,128]{3,1,2,0:T(8,128)S(1)} %convolution_bitcast_fusion.14, f32[9,21,4,128]{3,1,2,0:T(8,128)S(1)} %fusion.3, f32[9,56,128]{2,1,0:T(8,128)S(1)} %fusion.4, f32[9,56,128]{2,1,0:T(8,128)S(1)} %constant_dynamic-update-slice_fusion.108, ...), kind=kOutput, calls=%fused_computation.25 | convolution fusion | flops 33030144 | bytes 1956224 | tf_op jit(solution)/shard_map/fai,pife->pae/dot_general | solution.py:114
  (205 shorter events, 13.1 us)
Async XLA Ops:
  0.0 3.4 %copy-start = (f32[3,56,56]{2,1,0:T(8,128)S(1)}, f32[3,56,56]{2,1,0:T(8,128)}, u32[]{:S(2)}) copy-start(f32[3,56,56]{2,1,0:T(8,128)} %param.16) | copy-start | bytes 112900
  7.9 1.0 %copy-start.1 = (f32[9,56,128]{2,1,0:T(8,128)S(1)}, f32[9,56,128]{2,1,0:T(8,128)}, u32[]{:S(2)}) copy-start(f32[9,56,128]{2,1,0:T(8,128)} %param.15) | copy-start | bytes 774148
  8.8 0.8 %copy-start.3 = (f32[4,21,56]{2,0,1:T(4,128)S(1)}, f32[4,21,56]{2,0,1:T(4,128)}, u32[]{:S(2)}) copy-start(f32[4,21,56]{2,0,1:T(4,128)} %param.18) | copy-start | bytes 56452
  10.1 5.8 %copy-start.7 = (s32[4,128]{1,0:T(4,128)S(1)}, s32[4,128]{1,0:T(4,128)}, u32[]{:S(2)}) copy-start(s32[4,128]{1,0:T(4,128)} %param.26) | copy-start | bytes 6148
  10.2 5.8 %copy-start.9 = (s32[4,128]{1,0:T(4,128)S(1)}, s32[4,128]{1,0:T(4,128)}, u32[]{:S(2)}) copy-start(s32[4,128]{1,0:T(4,128)} %param.27) | copy-start | bytes 6148
  10.2 5.8 %copy-start.8 = (s32[1,1,8,24]{3,2,1,0:T(8,128)S(1)}, s32[1,1,8,24]{3,2,1,0:T(8,128)}, u32[]{:S(2)}) copy-start(s32[1,1,8,24]{3,2,1,0:T(8,128)} %param.29) | copy-start | bytes 2308
  10.2 5.8 %copy-start.6 = (f32[4,3,128]{2,0,1:T(4,128)S(1)}, f32[4,3,128]{2,0,1:T(4,128)}, u32[]{:S(2)}) copy-start(f32[4,3,128]{2,0,1:T(4,128)} %param.24) | copy-start | bytes 18436
  10.2 5.8 %copy-start.10 = (s32[4,128]{1,0:T(4,128)S(1)}, s32[4,128]{1,0:T(4,128)}, u32[]{:S(2)}) copy-start(s32[4,128]{1,0:T(4,128)} %param.25) | copy-start | bytes 6148
  10.2 5.9 %copy-start.2 = (f32[3,56,56]{2,1,0:T(8,128)S(1)}, f32[3,56,56]{2,1,0:T(8,128)}, u32[]{:S(2)}) copy-start(f32[3,56,56]{2,1,0:T(8,128)} %param.17) | copy-start | bytes 112900
  10.6 6.8 %collective-permute-start = (f32[72,189]{1,0:T(8,128)S(1)}, f32[72,189]{1,0:T(8,128)S(1)}, u32[]{:S(2)}, u32[]{:S(2)}) collective-permute-start(f32[72,189]{1,0:T(8,128)S(1)} %get-tuple-element.55), channel_id=1, source_target_pairs={{4,0},{8,4},{12,8},{16,12},{20,16},{24,20},{28,24},{5,1},{9,5},{13... | collective-permute-start | bytes 163304 | tf_op jit(solution)/shard_map/ppermute | solution.py:45
  13.6 6.0 %collective-permute-start.1 = (f32[72,189]{1,0:T(8,128)S(1)}, f32[72,189]{1,0:T(8,128)S(1)}, u32[]{:S(2)}, u32[]{:S(2)}) collective-permute-start(f32[72,189]{1,0:T(8,128)S(1)} %get-tuple-element.56), channel_id=1, source_target_pairs={{0,4},{4,8},{8,12},{12,16},{16,20},{20,24},{24,28},{1,5},{5,9},{9,... | collective-permute-start | bytes 163304 | tf_op jit(solution)/shard_map/ppermute | solution.py:45
  19.7 7.4 %collective-permute-start.3 = (f32[72,189]{1,0:T(8,128)S(1)}, f32[72,189]{1,0:T(8,128)S(1)}, u32[]{:S(2)}, u32[]{:S(2)}) collective-permute-start(f32[72,189]{1,0:T(8,128)S(1)} %pad_maximum_fusion.1), channel_id=1, source_target_pairs={{0,1},{1,2},{2,3},{4,5},{5,6},{6,7},{8,9},{9,10},{10,11},{12,13},{... | collective-permute-start | bytes 163304 | tf_op jit(solution)/shard_map/ppermute | solution.py:45
  24.8 5.7 %collective-permute-start.2 = (f32[72,189]{1,0:T(8,128)S(1)}, f32[72,189]{1,0:T(8,128)S(1)}, u32[]{:S(2)}, u32[]{:S(2)}) collective-permute-start(f32[72,189]{1,0:T(8,128)S(1)} %pad_maximum_fusion), channel_id=1, source_target_pairs={{1,0},{2,1},{3,2},{5,4},{6,5},{7,6},{9,8},{10,9},{11,10},{13,12},{... | collective-permute-start | bytes 163304 | tf_op jit(solution)/shard_map/ppermute | solution.py:45
  31.0 0.8 %copy-start.5 = (f32[3,21,21]{2,1,0:T(8,128)S(1)}, f32[3,21,21]{2,1,0:T(8,128)}, u32[]{:S(2)}) copy-start(f32[3,21,21]{2,1,0:T(8,128)} %param.20) | copy-start | bytes 15880
  32.7 0.8 %copy-start.4 = (f32[4,56,21]{1,0,2:T(4,128)S(1)}, f32[4,56,21]{1,0,2:T(4,128)}, u32[]{:S(2)}) copy-start(f32[4,56,21]{1,0,2:T(4,128)} %param.19) | copy-start | bytes 56452
  39.7 5.5 %collective-permute-start.4 = (f32[72,189]{1,0:T(8,128)S(1)}, f32[72,189]{1,0:T(8,128)S(1)}, u32[]{:S(2)}, u32[]{:S(2)}) collective-permute-start(f32[72,189]{1,0:T(8,128)S(1)} %get-tuple-element.51), channel_id=1, source_target_pairs={{4,0},{8,4},{12,8},{16,12},{20,16},{24,20},{28,24},{5,1},{9,5},{13... | collective-permute-start | bytes 163304 | tf_op jit(solution)/shard_map/ppermute | solution.py:45
  41.7 6.0 %collective-permute-start.5 = (f32[72,189]{1,0:T(8,128)S(1)}, f32[72,189]{1,0:T(8,128)S(1)}, u32[]{:S(2)}, u32[]{:S(2)}) collective-permute-start(f32[72,189]{1,0:T(8,128)S(1)} %get-tuple-element.52), channel_id=1, source_target_pairs={{0,4},{4,8},{8,12},{12,16},{16,20},{20,24},{24,28},{1,5},{5,9},{9,... | collective-permute-start | bytes 163304 | tf_op jit(solution)/shard_map/ppermute | solution.py:45
  47.8 5.0 %collective-permute-start.7 = (f32[72,189]{1,0:T(8,128)S(1)}, f32[72,189]{1,0:T(8,128)S(1)}, u32[]{:S(2)}, u32[]{:S(2)}) collective-permute-start(f32[72,189]{1,0:T(8,128)S(1)} %pad_maximum_fusion.3), channel_id=1, source_target_pairs={{0,1},{1,2},{2,3},{4,5},{5,6},{6,7},{8,9},{9,10},{10,11},{12,13},{... | collective-permute-start | bytes 163304 | tf_op jit(solution)/shard_map/ppermute | solution.py:45
  50.8 5.7 %collective-permute-start.6 = (f32[72,189]{1,0:T(8,128)S(1)}, f32[72,189]{1,0:T(8,128)S(1)}, u32[]{:S(2)}, u32[]{:S(2)}) collective-permute-start(f32[72,189]{1,0:T(8,128)S(1)} %pad_maximum_fusion.2), channel_id=1, source_target_pairs={{1,0},{2,1},{3,2},{5,4},{6,5},{7,6},{9,8},{10,9},{11,10},{13,12},{... | collective-permute-start | bytes 163304 | tf_op jit(solution)/shard_map/ppermute | solution.py:45

commit v10 on v8

--- a/solution.py
+++ b/solution.py
@@ -82,12 +82,10 @@
     return integrated
 
 
-def local_part(current, inv_jacobian, values, grad_matrix, stiff_matrix, face_proj):
+def local_part(current, inv_jacobian, values, grad_matrix, face_proj):
     integrated = predict(current, inv_jacobian, values, grad_matrix)
-    slopes = jnp.einsum("dab,qbe->dqae", stiff_matrix, integrated, precision=fast_mode)
-    volume = star_apply(slopes, inv_jacobian, values)
     face_data = jnp.einsum("fib,qbe->qife", face_proj, integrated, precision=fast_mode)
-    return (volume, face_data)
+    return (integrated, face_data)
 
 
 def face_update(
@@ -118,10 +116,12 @@
 SEND_ORDER = (0, 3, 5, 2, 4, 7, 1, 6)
 
 
-def deliver(outgoing, slot_total):
+def deliver(outgoing, slot_total, deferred, local_work):
     group = 3 * slot_total
     left = shifted(outgoing[:group], "pcol", -1)
     right = shifted(outgoing[group : 2 * group], "pcol", 1)
+    left, right, deferred = lax.optimization_barrier((left, right, deferred))
+    finished = local_work(*deferred)
     up_bundle = jnp.concatenate(
         [right[:slot_total], outgoing[2 * group : 2 * group + slot_total], left[:slot_total]], axis=0
     )
@@ -130,9 +130,10 @@
     )
     up = shifted(up_bundle, "prow", -1)
     down = shifted(down_bundle, "prow", 1)
+    up, down, finished = lax.optimization_barrier((up, down, finished))
     return jnp.concatenate(
         [down, right[slot_total : 2 * slot_total], left[slot_total : 2 * slot_total], up], axis=0
-    )
+    ), finished
 
 
 def per_device(
@@ -168,15 +169,24 @@
     scatter_in = ((targets[:, None] == face_ids[None, :]) & ~inside[None, :]).astype(dtype)
     current = dof_values
     for time_index in range(STEPS):
-        volume, face_data = local_part(
-            current, inv_jacobian, values, grad_matrix, stiff_matrix, face_proj
+        integrated, face_data = local_part(
+            current, inv_jacobian, values, grad_matrix, face_proj
         )
         flat_faces = face_data.reshape(9 * face_width, face_total)
         outgoing = lax.dot_general(
             gather_out, flat_faces, (((1,), (1,)), ((), ())), precision=exact_mode
         )
-        received = deliver(outgoing, slot_total)
-        neighbour_data = jnp.dot(flat_faces, gather_local, precision=exact_mode) + lax.dot_general(
+
+        def local_work(integrated, flat_faces):
+            slopes = jnp.einsum("dab,qbe->dqae", stiff_matrix, integrated, precision=fast_mode)
+            volume = star_apply(slopes, inv_jacobian, values)
+            local_data = jnp.dot(flat_faces, gather_local, precision=exact_mode)
+            return volume, local_data
+
+        received, (volume, local_data) = deliver(
+            outgoing, slot_total, (integrated, flat_faces), local_work
+        )
+        neighbour_data = local_data + lax.dot_general(
             received, scatter_in, (((0,), (0,)), ((), ())), precision=exact_mode
         )
         neighbour_data = neighbour_data.reshape(9, face_width, 4, elem_count)

time: 58.8 us -> 57.8 us (0.983)
  waiting for transfers between devices: 12 us -> 10.7 us
  other arithmetic: 3.65 us -> 4.54 us
  matrix products: 14 us -> 13.3 us
    ppermute x8, waiting for transfers between devices: 12 us -> 10.7 us  [shifted(): return lax.ppermute(x, axis, pairs)]
    sub x0 -> x2, other arithmetic: none -> 0.79 us  [face_update(): return current + volume - lifted]
    dot_general x2, matrix products: 1.46 us -> 0.75 us  [face_update(): jnp.einsum('fai,pife->pae', face_lift, flux_total, precision=fast_mode)]
  transfers between devices with their start and end apart: 8 -> 8, of which waited for: 4 -> 4; matrix products, arithmetic and copies ran while one was open for 3% -> 5% of each run, Pallas kernels for 0% -> 0%
where the time goes in v10:
time: 57.8 us; the launch traced here: 57.1 us
  starting transfers between devices  21.7 us (38%)
  matrix products  13.3 us (23%)
  waiting for transfers between devices  10.7 us (19%)
  local copies, waits for them, and re-layouts  5.5 us (10%)
  other arithmetic  4.54 us (8%)
  between operations  1.38 us (2%)
    ppermute x8, starting transfers between devices, shifted(): return lax.ppermute(x, axis, pairs)  21.7 us
    ppermute x8, waiting for transfers between devices, shifted(): return lax.ppermute(x, axis, pairs)  10.7 us
    dot_general x10, matrix products, predict(): jnp.einsum('dab,qbe->dqae', grad_matrix, derivative, precision=fast_mode)  6.45 us
    unnamed x28, local copies, waits for them, and re-layouts  2.98 us
    dot_general x2, matrix products, face_update(): jnp.einsum('hil,qlfe->hqife', rotate, neighbour_data, precision=fast_mode)  1.36 us
    unnamed x112, other arithmetic  1.34 us
    dot_general x2, matrix products, local_work(): local_data = jnp.dot(flat_faces, gather_local, precision=exact_mode)  1.22 us
  transfers between devices with their start and end apart: 8, of which 4 were waited for; matrix products, arithmetic and copies ran while one was open for 5% of the time, Pallas kernels for 0%

profile of v10, /device:TPU:25, one launch (start us, length us, event | category | flops | bytes accessed | tf_op | source)
XLA Modules:
  0.0 57.1 jit_solution(15700088127641921600)
XLA Ops:
  0.0 0.7 %iota_compare_fusion.6 = pred[16,128]{1,0:T(8,128)(4,1)S(1)} fusion(s32[128]{0:T(128)} %param.22), kind=kLoop, calls=%fused_computation.545 | loop fusion | flops 2048 | bytes 2560 | tf_op jit(solution)/shard_map/eq | solution.py:50
  0.7 0.8 %select_reduce_fusion = f32[3,128]{1,0:T(4,128)S(1)} fusion(f32[16,3]{0,1:T(4,128)} %param.21, pred[16,128]{1,0:T(8,128)(4,1)S(1)} %iota_compare_fusion.6), kind=kLoop, calls=%fused_computation.543 | loop fusion | flops 11904 | bytes 3776 | tf_op jit(solution)/shard_map/reduce_sum | solution.py:51
  1.5 1.0 %slice_bitcast_fusion.3 = (s32[1,24]{1,0:T(1,128)S(1)}, s32[1,24]{1,0:T(1,128)S(1)}, s32[1,24]{1,0:T(1,128)S(1)}, s32[1,24]{1,0:T(1,128)S(1)}, s32[1,24]{1,0:T(1...) fusion(s32[1,1,8,24]{3,2,1,0:T(8,128)} %param.28), kind=kLoop, calls=%fused_computation.563 | loop fusion | bytes 1536 | tf_op jit(solution)/shard_map/squeeze | solution.py:165
  2.6 0.8 %fusion.196 = (f32[3,1,128]{2,1,0:T(1,128)S(1)}, f32[3,1,128]{2,1,0:T(1,128)S(1)}, f32[3,1,128]{2,1,0:T(1,128)S(1)}) fusion(f32[3,3,128]{2,1,0:T(4,128)} %param.23), kind=kLoop, calls=%fused_computation.584 | loop fusion | bytes 9216 | tf_op jit(solution)/shard_map/slice | solution.py:69
  3.4 1.6 %multiply_reduce_fusion.33 = (f32[9,56,128]{2,1,0:T(8,128)S(1)}, f32[9,56,128]{2,1,0:T(8,128)S(1)}, f32[9,56,128]{2,1,0:T(8,128)S(1)}) fusion(f32[3,128]{1,0:T(4,128)S(1)} %get-tuple-element.120, f32[3,128]{1,0:T(4,128)S(1)} %get-tuple-element.121, f32[3,128]{1,0:T(4,128)S(1)} %bitcast.283, f32[3,56,56]{2,1,0:T(8,128)S(1)} %copy-done, f32[9,56,128]{2,1,0:T(8,128)} %param.15), kind=kOutput, calls=%fused_computation.59 | convolution fusion | flops 65995776 | bytes 1074432 | tf_op jit(solution)/shard_map/dab,qbe->dqae/dot_general | solution.py:78
  8.0 0.8 %copy-done.1 = f32[9,56,128]{2,1,0:T(8,128)S(1)} copy-done((f32[9,56,128]{2,1,0:T(8,128)S(1)}, f32[9,56,128]{2,1,0:T(8,128)}, u32[]{:S(2)}) %copy-start.1) | copy-done | bytes 258072
  9.0 0.6 %copy-done.4 = f32[4,21,56]{2,0,1:T(4,128)S(1)} copy-done((f32[4,21,56]{2,0,1:T(4,128)S(1)}, f32[4,21,56]{2,0,1:T(4,128)}, u32[]{:S(2)}) %copy-start.4) | copy-done | bytes 18840
  10.6 3.8 %collective-permute-start.1 = (f32[72,189]{1,0:T(8,128)S(1)}, f32[72,189]{1,0:T(8,128)S(1)}, u32[]{:S(2)}, u32[]{:S(2)}) collective-permute-start(f32[72,189]{1,0:T(8,128)S(1)} %get-tuple-element.87), channel_id=1, source_target_pairs={{0,1},{1,2},{2,3},{4,5},{5,6},{6,7},{8,9},{9,10},{10,11},{12,13},{... | collective-permute-start | bytes 163304 | tf_op jit(solution)/shard_map/ppermute | solution.py:45
  14.5 1.9 %collective-permute-start = (f32[72,189]{1,0:T(8,128)S(1)}, f32[72,189]{1,0:T(8,128)S(1)}, u32[]{:S(2)}, u32[]{:S(2)}) collective-permute-start(f32[72,189]{1,0:T(8,128)S(1)} %get-tuple-element.88), channel_id=1, source_target_pairs={{1,0},{2,1},{3,2},{5,4},{6,5},{7,6},{9,8},{10,9},{11,10},{13,12},{... | collective-permute-start | bytes 163304 | tf_op jit(solution)/shard_map/ppermute | solution.py:45
  16.6 3.5 %collective-permute-done = f32[72,189]{1,0:T(8,128)S(1)} collective-permute-done((f32[72,189]{1,0:T(8,128)S(1)}, f32[72,189]{1,0:T(8,128)S(1)}, u32[]{:S(2)}, u32[]{:S(2)}) %collective-permute-start) | collective-permute-done | bytes 54464 | tf_op jit(solution)/shard_map/ppermute | solution.py:45
  20.2 3.0 %collective-permute-start.2 = (f32[72,189]{1,0:T(8,128)S(1)}, f32[72,189]{1,0:T(8,128)S(1)}, u32[]{:S(2)}, u32[]{:S(2)}) collective-permute-start(f32[72,189]{1,0:T(8,128)S(1)} %pad_maximum_fusion), channel_id=1, source_target_pairs={{4,0},{8,4},{12,8},{16,12},{20,16},{24,20},{28,24},{5,1},{9,5},{13... | collective-permute-start | bytes 163304 | tf_op jit(solution)/shard_map/ppermute | solution.py:45
  23.2 2.3 %collective-permute-start.3 = (f32[72,189]{1,0:T(8,128)S(1)}, f32[72,189]{1,0:T(8,128)S(1)}, u32[]{:S(2)}, u32[]{:S(2)}) collective-permute-start(f32[72,189]{1,0:T(8,128)S(1)} %pad_maximum_fusion.1), channel_id=1, source_target_pairs={{0,4},{4,8},{8,12},{12,16},{16,20},{20,24},{24,28},{1,5},{5,9},{9,... | collective-permute-start | bytes 163304 | tf_op jit(solution)/shard_map/ppermute | solution.py:45
  26.8 2.4 %collective-permute-done.3 = f32[72,189]{1,0:T(8,128)S(1)} collective-permute-done((f32[72,189]{1,0:T(8,128)S(1)}, f32[72,189]{1,0:T(8,128)S(1)}, u32[]{:S(2)}, u32[]{:S(2)}) %collective-permute-start.3) | collective-permute-done | bytes 54464 | tf_op jit(solution)/shard_map/ppermute | solution.py:45
  29.9 0.6 %copy-done.5 = f32[3,21,21]{2,1,0:T(8,128)S(1)} copy-done((f32[3,21,21]{2,1,0:T(8,128)S(1)}, f32[3,21,21]{2,1,0:T(8,128)}, u32[]{:S(2)}) %copy-start.5) | copy-done | bytes 5316
  30.6 0.7 %fusion.2 = f32[9,21,4,128]{3,1,2,0:T(8,128)S(1)} fusion(f32[3,4,128]{2,0,1:T(4,128)S(1)} %fusion.182, f32[9,21,4,128,1]{3,2,1,0,4:T(4,128)S(1)} %bitcast.278, f32[3,21,21]{2,1,0:T(8,128)S(1)} %copy-done.5), kind=kOutput, calls=%fused_computation.4 | convolution fusion | flops 37062144 | bytes 785580 | tf_op jit(solution)/shard_map/hil,qlfe->hqife/dot_general | solution.py:103
  31.6 0.7 %copy-done.3 = f32[4,56,21]{1,0,2:T(4,128)S(1)} copy-done((f32[4,56,21]{1,0,2:T(4,128)S(1)}, f32[4,56,21]{1,0,2:T(4,128)}, u32[]{:S(2)}) %copy-start.3) | copy-done | bytes 18840
  37.3 3.3 %collective-permute-start.5 = (f32[72,189]{1,0:T(8,128)S(1)}, f32[72,189]{1,0:T(8,128)S(1)}, u32[]{:S(2)}, u32[]{:S(2)}) collective-permute-start(f32[72,189]{1,0:T(8,128)S(1)} %get-tuple-element.83), channel_id=1, source_target_pairs={{0,1},{1,2},{2,3},{4,5},{5,6},{6,7},{8,9},{9,10},{10,11},{12,13},{... | collective-permute-start | bytes 163304 | tf_op jit(solution)/shard_map/ppermute | solution.py:45
  40.6 1.9 %collective-permute-start.4 = (f32[72,189]{1,0:T(8,128)S(1)}, f32[72,189]{1,0:T(8,128)S(1)}, u32[]{:S(2)}, u32[]{:S(2)}) collective-permute-start(f32[72,189]{1,0:T(8,128)S(1)} %get-tuple-element.84), channel_id=1, source_target_pairs={{1,0},{2,1},{3,2},{5,4},{6,5},{7,6},{9,8},{10,9},{11,10},{13,12},{... | collective-permute-start | bytes 163304 | tf_op jit(solution)/shard_map/ppermute | solution.py:45
  42.5 3.7 %collective-permute-done.4 = f32[72,189]{1,0:T(8,128)S(1)} collective-permute-done((f32[72,189]{1,0:T(8,128)S(1)}, f32[72,189]{1,0:T(8,128)S(1)}, u32[]{:S(2)}, u32[]{:S(2)}) %collective-permute-start.4) | collective-permute-done | bytes 54464 | tf_op jit(solution)/shard_map/ppermute | solution.py:45
  46.3 1.9 %collective-permute-start.6 = (f32[72,189]{1,0:T(8,128)S(1)}, f32[72,189]{1,0:T(8,128)S(1)}, u32[]{:S(2)}, u32[]{:S(2)}) collective-permute-start(f32[72,189]{1,0:T(8,128)S(1)} %pad_maximum_fusion.2), channel_id=1, source_target_pairs={{4,0},{8,4},{12,8},{16,12},{20,16},{24,20},{28,24},{5,1},{9,5},{13... | collective-permute-start | bytes 163304 | tf_op jit(solution)/shard_map/ppermute | solution.py:45
  48.2 3.5 %collective-permute-start.7 = (f32[72,189]{1,0:T(8,128)S(1)}, f32[72,189]{1,0:T(8,128)S(1)}, u32[]{:S(2)}, u32[]{:S(2)}) collective-permute-start(f32[72,189]{1,0:T(8,128)S(1)} %pad_maximum_fusion.3), channel_id=1, source_target_pairs={{0,4},{4,8},{8,12},{12,16},{16,20},{20,24},{24,28},{1,5},{5,9},{9,... | collective-permute-start | bytes 163304 | tf_op jit(solution)/shard_map/ppermute | solution.py:45
  53.1 1.1 %collective-permute-done.7 = f32[72,189]{1,0:T(8,128)S(1)} collective-permute-done((f32[72,189]{1,0:T(8,128)S(1)}, f32[72,189]{1,0:T(8,128)S(1)}, u32[]{:S(2)}, u32[]{:S(2)}) %collective-permute-start.7) | collective-permute-done | bytes 54464 | tf_op jit(solution)/shard_map/ppermute | solution.py:45
  55.0 0.7 %fusion.3 = f32[9,21,4,128]{3,1,2,0:T(8,128)S(1)} fusion(f32[3,4,128]{2,0,1:T(4,128)S(1)} %fusion.182, f32[9,21,4,128,1]{3,2,1,0,4:T(4,128)S(1)} %bitcast.277, f32[3,21,21]{2,1,0:T(8,128)S(1)} %copy-done.5), kind=kOutput, calls=%fused_computation.5 | convolution fusion | flops 37062144 | bytes 785580 | tf_op jit(solution)/shard_map/hil,qlfe->hqife/dot_general | solution.py:103
  56.4 0.8 %add_subtract_fusion = f32[9,56,128]{2,1,0:T(8,128)} fusion(f32[9,56,128]{2,1,0:T(8,128)S(1)} %convolution_bitcast_fusion.16, f32[9,56,128]{2,1,0:T(8,128)S(1)} %add_subtract_fusion.1, f32[9,56,128]{2,1,0:T(8,128)S(1)} %constant_dynamic-update-slice_fusion.108), kind=kLoop, calls=%fused_computation.223 | loop fusion | flops 129024 | bytes 1032192 | tf_op jit(solution)/shard_map/sub | solution.py:113
  (208 shorter events, 13.6 us)
Async XLA Ops:
  0.0 3.4 %copy-start = (f32[3,56,56]{2,1,0:T(8,128)S(1)}, f32[3,56,56]{2,1,0:T(8,128)}, u32[]{:S(2)}) copy-start(f32[3,56,56]{2,1,0:T(8,128)} %param.16) | copy-start | bytes 112900
  7.9 1.0 %copy-start.1 = (f32[9,56,128]{2,1,0:T(8,128)S(1)}, f32[9,56,128]{2,1,0:T(8,128)}, u32[]{:S(2)}) copy-start(f32[9,56,128]{2,1,0:T(8,128)} %param.15) | copy-start | bytes 774148
  8.8 0.8 %copy-start.4 = (f32[4,21,56]{2,0,1:T(4,128)S(1)}, f32[4,21,56]{2,0,1:T(4,128)}, u32[]{:S(2)}) copy-start(f32[4,21,56]{2,0,1:T(4,128)} %param.18) | copy-start | bytes 56452
  10.2 6.3 %copy-start.6 = (f32[4,3,128]{2,0,1:T(4,128)S(1)}, f32[4,3,128]{2,0,1:T(4,128)}, u32[]{:S(2)}) copy-start(f32[4,3,128]{2,0,1:T(4,128)} %param.24) | copy-start | bytes 18436
  10.2 6.3 %copy-start.9 = (s32[4,128]{1,0:T(4,128)S(1)}, s32[4,128]{1,0:T(4,128)}, u32[]{:S(2)}) copy-start(s32[4,128]{1,0:T(4,128)} %param.25) | copy-start | bytes 6148
  10.2 6.3 %copy-start.7 = (s32[4,128]{1,0:T(4,128)S(1)}, s32[4,128]{1,0:T(4,128)}, u32[]{:S(2)}) copy-start(s32[4,128]{1,0:T(4,128)} %param.26) | copy-start | bytes 6148
  10.2 6.3 %copy-start.10 = (s32[4,128]{1,0:T(4,128)S(1)}, s32[4,128]{1,0:T(4,128)}, u32[]{:S(2)}) copy-start(s32[4,128]{1,0:T(4,128)} %param.27) | copy-start | bytes 6148
  10.2 6.3 %copy-start.8 = (s32[1,1,8,24]{3,2,1,0:T(8,128)S(1)}, s32[1,1,8,24]{3,2,1,0:T(8,128)}, u32[]{:S(2)}) copy-start(s32[1,1,8,24]{3,2,1,0:T(8,128)} %param.29) | copy-start | bytes 2308
  10.6 14.9 %copy-start.2 = (f32[3,56,56]{2,1,0:T(8,128)S(1)}, f32[3,56,56]{2,1,0:T(8,128)}, u32[]{:S(2)}) copy-start(f32[3,56,56]{2,1,0:T(8,128)} %param.17) | copy-start | bytes 112900
  10.6 6.0 %collective-permute-start.1 = (f32[72,189]{1,0:T(8,128)S(1)}, f32[72,189]{1,0:T(8,128)S(1)}, u32[]{:S(2)}, u32[]{:S(2)}) collective-permute-start(f32[72,189]{1,0:T(8,128)S(1)} %get-tuple-element.87), channel_id=1, source_target_pairs={{0,1},{1,2},{2,3},{4,5},{5,6},{6,7},{8,9},{9,10},{10,11},{12,13},{... | collective-permute-start | bytes 163304 | tf_op jit(solution)/shard_map/ppermute | solution.py:45
  14.5 5.7 %collective-permute-start = (f32[72,189]{1,0:T(8,128)S(1)}, f32[72,189]{1,0:T(8,128)S(1)}, u32[]{:S(2)}, u32[]{:S(2)}) collective-permute-start(f32[72,189]{1,0:T(8,128)S(1)} %get-tuple-element.88), channel_id=1, source_target_pairs={{1,0},{2,1},{3,2},{5,4},{6,5},{7,6},{9,8},{10,9},{11,10},{13,12},{... | collective-permute-start | bytes 163304 | tf_op jit(solution)/shard_map/ppermute | solution.py:45
  20.2 6.7 %collective-permute-start.2 = (f32[72,189]{1,0:T(8,128)S(1)}, f32[72,189]{1,0:T(8,128)S(1)}, u32[]{:S(2)}, u32[]{:S(2)}) collective-permute-start(f32[72,189]{1,0:T(8,128)S(1)} %pad_maximum_fusion), channel_id=1, source_target_pairs={{4,0},{8,4},{12,8},{16,12},{20,16},{24,20},{28,24},{5,1},{9,5},{13... | collective-permute-start | bytes 163304 | tf_op jit(solution)/shard_map/ppermute | solution.py:45
  23.2 6.0 %collective-permute-start.3 = (f32[72,189]{1,0:T(8,128)S(1)}, f32[72,189]{1,0:T(8,128)S(1)}, u32[]{:S(2)}, u32[]{:S(2)}) collective-permute-start(f32[72,189]{1,0:T(8,128)S(1)} %pad_maximum_fusion.1), channel_id=1, source_target_pairs={{0,4},{4,8},{8,12},{12,16},{16,20},{20,24},{24,28},{1,5},{5,9},{9,... | collective-permute-start | bytes 163304 | tf_op jit(solution)/shard_map/ppermute | solution.py:45
  29.8 0.8 %copy-start.5 = (f32[3,21,21]{2,1,0:T(8,128)S(1)}, f32[3,21,21]{2,1,0:T(8,128)}, u32[]{:S(2)}) copy-start(f32[3,21,21]{2,1,0:T(8,128)} %param.20) | copy-start | bytes 15880
  31.5 0.8 %copy-start.3 = (f32[4,56,21]{1,0,2:T(4,128)S(1)}, f32[4,56,21]{1,0,2:T(4,128)}, u32[]{:S(2)}) copy-start(f32[4,56,21]{1,0,2:T(4,128)} %param.19) | copy-start | bytes 56452
  37.3 5.2 %collective-permute-start.5 = (f32[72,189]{1,0:T(8,128)S(1)}, f32[72,189]{1,0:T(8,128)S(1)}, u32[]{:S(2)}, u32[]{:S(2)}) collective-permute-start(f32[72,189]{1,0:T(8,128)S(1)} %get-tuple-element.83), channel_id=1, source_target_pairs={{0,1},{1,2},{2,3},{4,5},{5,6},{6,7},{8,9},{9,10},{10,11},{12,13},{... | collective-permute-start | bytes 163304 | tf_op jit(solution)/shard_map/ppermute | solution.py:45
  40.6 5.7 %collective-permute-start.4 = (f32[72,189]{1,0:T(8,128)S(1)}, f32[72,189]{1,0:T(8,128)S(1)}, u32[]{:S(2)}, u32[]{:S(2)}) collective-permute-start(f32[72,189]{1,0:T(8,128)S(1)} %get-tuple-element.84), channel_id=1, source_target_pairs={{1,0},{2,1},{3,2},{5,4},{6,5},{7,6},{9,8},{10,9},{11,10},{13,12},{... | collective-permute-start | bytes 163304 | tf_op jit(solution)/shard_map/ppermute | solution.py:45
  46.3 6.8 %collective-permute-start.6 = (f32[72,189]{1,0:T(8,128)S(1)}, f32[72,189]{1,0:T(8,128)S(1)}, u32[]{:S(2)}, u32[]{:S(2)}) collective-permute-start(f32[72,189]{1,0:T(8,128)S(1)} %pad_maximum_fusion.2), channel_id=1, source_target_pairs={{4,0},{8,4},{12,8},{16,12},{20,16},{24,20},{28,24},{5,1},{9,5},{13... | collective-permute-start | bytes 163304 | tf_op jit(solution)/shard_map/ppermute | solution.py:45
  48.2 6.0 %collective-permute-start.7 = (f32[72,189]{1,0:T(8,128)S(1)}, f32[72,189]{1,0:T(8,128)S(1)}, u32[]{:S(2)}, u32[]{:S(2)}) collective-permute-start(f32[72,189]{1,0:T(8,128)S(1)} %pad_maximum_fusion.3), channel_id=1, source_target_pairs={{0,4},{4,8},{8,12},{12,16},{16,20},{20,24},{24,28},{1,5},{5,9},{9,... | collective-permute-start | bytes 163304 | tf_op jit(solution)/shard_map/ppermute | solution.py:45

commit v11 on v10

--- a/solution.py
+++ b/solution.py
@@ -97,19 +97,21 @@
     normals,
     values,
     wave_speed,
-    rotate,
-    face_lift,
+    rotate_negated,
+    half_lift,
 ):
-    turned = jnp.einsum("hil,qlfe->hqife", rotate, neighbour_data, precision=fast_mode)
+    turned_negated = jnp.einsum(
+        "hil,qlfe->hqife", rotate_negated, neighbour_data, precision=fast_mode
+    )
     chosen = (orientation[None] == jnp.arange(3, dtype=jnp.int32)[:, None, None]).astype(
         current.dtype
     )
-    turned = jnp.sum(turned * chosen[:, None, None, :, :], axis=0)
-    both = face_data + turned
-    apart = face_data - turned
+    turned_negated = jnp.sum(turned_negated * chosen[:, None, None, :, :], axis=0)
+    both = face_data - turned_negated
+    apart = face_data + turned_negated
     parts = [normals[:, k, :][None, None] * both for k in range(3)]
-    flux_total = 0.5 * (elastic_apply(parts, values) + wave_speed[None, None] * apart)
-    lifted = jnp.einsum("fai,pife->pae", face_lift, flux_total, precision=fast_mode)
+    flux_total = elastic_apply(parts, values) + wave_speed[None, None] * apart
+    lifted = jnp.einsum("fai,pife->pae", half_lift, flux_total, precision=fast_mode)
     return current + volume - lifted
 
 
@@ -168,6 +170,7 @@
     targets = recv_list[0, 0].reshape(-1)
     scatter_in = ((targets[:, None] == face_ids[None, :]) & ~inside[None, :]).astype(dtype)
     current = dof_values
+    rotate_negated, half_lift = rotate, face_lift
     for time_index in range(STEPS):
         integrated, face_data = local_part(
             current, inv_jacobian, values, grad_matrix, face_proj
@@ -177,14 +180,17 @@
             gather_out, flat_faces, (((1,), (1,)), ((), ())), precision=exact_mode
         )
 
-        def local_work(integrated, flat_faces):
+        def local_work(integrated, flat_faces, rotate_negated, half_lift):
             slopes = jnp.einsum("dab,qbe->dqae", stiff_matrix, integrated, precision=fast_mode)
             volume = star_apply(slopes, inv_jacobian, values)
             local_data = jnp.dot(flat_faces, gather_local, precision=exact_mode)
-            return volume, local_data
-
-        received, (volume, local_data) = deliver(
-            outgoing, slot_total, (integrated, flat_faces), local_work
+            if time_index == 0:
+                rotate_negated = -rotate_negated
+                half_lift = 0.5 * half_lift
+            return volume, local_data, rotate_negated, half_lift
+
+        received, (volume, local_data, rotate_negated, half_lift) = deliver(
+            outgoing, slot_total, (integrated, flat_faces, rotate_negated, half_lift), local_work
         )
         neighbour_data = local_data + lax.dot_general(
             received, scatter_in, (((0,), (0,)), ((), ())), precision=exact_mode
@@ -199,8 +205,8 @@
             normals,
             values,
             wave_speed,
-            rotate,
-            face_lift,
+            rotate_negated,
+            half_lift,
         )
     return current
 

time: 57.8 us -> 56.3 us (0.974)
  local copies, waits for them, and re-layouts: 5.5 us -> 4.33 us
  other arithmetic: 4.54 us -> 3.82 us
  matrix products: 13.3 us -> 13.9 us
    unnamed x28, local copies, waits for them, and re-layouts: 2.98 us -> 1.8 us
    sub x2 -> x0, other arithmetic: 0.79 us -> none  [face_update(): return current + volume - lifted]
    dot_general x4, matrix products: 2.1 us -> 2.75 us  [the longest x2 1.39 us: face_update(): jnp.einsum('fai,pife->pae', half_lift, flux_total, precision=fast_mode)]
where the time goes in v11:
time: 56.3 us; the launch traced here: 55.7 us
  starting transfers between devices  21.7 us (39%)
  matrix products  13.9 us (25%)
  waiting for transfers between devices  10.5 us (19%)
  local copies, waits for them, and re-layouts  4.33 us (8%)
  other arithmetic  3.82 us (7%)
  between operations  1.39 us (2%)
    ppermute x8, starting transfers between devices, shifted(): return lax.ppermute(x, axis, pairs)  21.7 us
    ppermute x8, waiting for transfers between devices, shifted(): return lax.ppermute(x, axis, pairs)  10.5 us
    dot_general x10, matrix products, predict(): jnp.einsum('dab,qbe->dqae', grad_matrix, derivative, precision=fast_mode)  6.46 us
    unnamed x28, local copies, waits for them, and re-layouts  1.8 us
    dot_general x2, matrix products, face_update(): jnp.einsum('fai,pife->pae', half_lift, flux_total, precision=fast_mode)  1.39 us
    dot_general x2, matrix products, face_update(): jnp.einsum('hil,qlfe->hqife', rotate_negated, neighbour_data, precision=f...  1.36 us
    unnamed x112, other arithmetic  1.34 us
    dot_general x2, matrix products, local_work(): local_data = jnp.dot(flat_faces, gather_local, precision=exact_mode)  1.22 us
  transfers between devices with their start and end apart: 8, of which 4 were waited for; matrix products, arithmetic and copies ran while one was open for 5% of the time, Pallas kernels for 0%

profile of v11, /device:TPU:25, one launch (start us, length us, event | category | flops | bytes accessed | tf_op | source)
XLA Modules:
  0.0 55.7 jit_solution(15362576817491834241)
XLA Ops:
  0.0 0.7 %iota_compare_fusion.6 = pred[16,128]{1,0:T(8,128)(4,1)S(1)} fusion(s32[128]{0:T(128)} %param.22), kind=kLoop, calls=%fused_computation.542 | loop fusion | flops 2048 | bytes 2560 | tf_op jit(solution)/shard_map/eq | solution.py:50
  0.7 0.8 %select_reduce_fusion = f32[3,128]{1,0:T(4,128)S(1)} fusion(f32[16,3]{0,1:T(4,128)} %param.21, pred[16,128]{1,0:T(8,128)(4,1)S(1)} %iota_compare_fusion.6), kind=kLoop, calls=%fused_computation.539 | loop fusion | flops 11904 | bytes 3776 | tf_op jit(solution)/shard_map/reduce_sum | solution.py:51
  1.5 1.0 %slice_bitcast_fusion.3 = (s32[1,24]{1,0:T(1,128)S(1)}, s32[1,24]{1,0:T(1,128)S(1)}, s32[1,24]{1,0:T(1,128)S(1)}, s32[1,24]{1,0:T(1,128)S(1)}, s32[1,24]{1,0:T(1...) fusion(s32[1,1,8,24]{3,2,1,0:T(8,128)} %param.28), kind=kLoop, calls=%fused_computation.560 | loop fusion | bytes 1536 | tf_op jit(solution)/shard_map/squeeze | solution.py:167
  2.6 0.8 %fusion.198 = (f32[3,1,128]{2,1,0:T(1,128)S(1)}, f32[3,1,128]{2,1,0:T(1,128)S(1)}, f32[3,1,128]{2,1,0:T(1,128)S(1)}) fusion(f32[3,3,128]{2,1,0:T(4,128)} %param.23), kind=kLoop, calls=%fused_computation.579 | loop fusion | bytes 9216 | tf_op jit(solution)/shard_map/slice | solution.py:69
  3.4 1.6 %multiply_reduce_fusion.33 = (f32[9,56,128]{2,1,0:T(8,128)S(1)}, f32[9,56,128]{2,1,0:T(8,128)S(1)}, f32[9,56,128]{2,1,0:T(8,128)S(1)}) fusion(f32[3,128]{1,0:T(4,128)S(1)} %get-tuple-element.136, f32[3,128]{1,0:T(4,128)S(1)} %get-tuple-element.137, f32[3,128]{1,0:T(4,128)S(1)} %bitcast.294, f32[3,56,56]{2,1,0:T(8,128)S(1)} %copy-done, f32[9,56,128]{2,1,0:T(8,128)} %param.15), kind=kOutput, calls=%fused_computation.59 | convolution fusion | flops 65995776 | bytes 1074432 | tf_op jit(solution)/shard_map/dab,qbe->dqae/dot_general | solution.py:78
  8.0 0.8 %copy-done.1 = f32[9,56,128]{2,1,0:T(8,128)S(1)} copy-done((f32[9,56,128]{2,1,0:T(8,128)S(1)}, f32[9,56,128]{2,1,0:T(8,128)}, u32[]{:S(2)}) %copy-start.1) | copy-done | bytes 258072
  9.0 0.6 %copy-done.3 = f32[4,21,56]{2,0,1:T(4,128)S(1)} copy-done((f32[4,21,56]{2,0,1:T(4,128)S(1)}, f32[4,21,56]{2,0,1:T(4,128)}, u32[]{:S(2)}) %copy-start.3) | copy-done | bytes 18840
  10.6 3.8 %collective-permute-start.1 = (f32[72,189]{1,0:T(8,128)S(1)}, f32[72,189]{1,0:T(8,128)S(1)}, u32[]{:S(2)}, u32[]{:S(2)}) collective-permute-start(f32[72,189]{1,0:T(8,128)S(1)} %get-tuple-element.103), channel_id=1, source_target_pairs={{0,1},{1,2},{2,3},{4,5},{5,6},{6,7},{8,9},{9,10},{10,11},{12,13},{... | collective-permute-start | bytes 163304 | tf_op jit(solution)/shard_map/ppermute | solution.py:45
  14.5 1.9 %collective-permute-start = (f32[72,189]{1,0:T(8,128)S(1)}, f32[72,189]{1,0:T(8,128)S(1)}, u32[]{:S(2)}, u32[]{:S(2)}) collective-permute-start(f32[72,189]{1,0:T(8,128)S(1)} %get-tuple-element.104), channel_id=1, source_target_pairs={{1,0},{2,1},{3,2},{5,4},{6,5},{7,6},{9,8},{10,9},{11,10},{13,12},{... | collective-permute-start | bytes 163304 | tf_op jit(solution)/shard_map/ppermute | solution.py:45
  16.6 3.5 %collective-permute-done = f32[72,189]{1,0:T(8,128)S(1)} collective-permute-done((f32[72,189]{1,0:T(8,128)S(1)}, f32[72,189]{1,0:T(8,128)S(1)}, u32[]{:S(2)}, u32[]{:S(2)}) %collective-permute-start) | collective-permute-done | bytes 54464 | tf_op jit(solution)/shard_map/ppermute | solution.py:45
  20.2 3.0 %collective-permute-start.2 = (f32[72,189]{1,0:T(8,128)S(1)}, f32[72,189]{1,0:T(8,128)S(1)}, u32[]{:S(2)}, u32[]{:S(2)}) collective-permute-start(f32[72,189]{1,0:T(8,128)S(1)} %pad_maximum_fusion), channel_id=1, source_target_pairs={{4,0},{8,4},{12,8},{16,12},{20,16},{24,20},{28,24},{5,1},{9,5},{13... | collective-permute-start | bytes 163304 | tf_op jit(solution)/shard_map/ppermute | solution.py:45
  23.2 2.3 %collective-permute-start.3 = (f32[72,189]{1,0:T(8,128)S(1)}, f32[72,189]{1,0:T(8,128)S(1)}, u32[]{:S(2)}, u32[]{:S(2)}) collective-permute-start(f32[72,189]{1,0:T(8,128)S(1)} %pad_maximum_fusion.1), channel_id=1, source_target_pairs={{0,4},{4,8},{8,12},{12,16},{16,20},{20,24},{24,28},{1,5},{5,9},{9,... | collective-permute-start | bytes 163304 | tf_op jit(solution)/shard_map/ppermute | solution.py:45
  26.2 0.6 %fusion.7 = f32[189,512]{1,0:T(8,128)S(1)} fusion(f32[189,512]{1,0:T(8,128)S(1)} %bitcast.285, s32[512]{0:T(512)S(1)} %add_bitcast_fusion, pred[512]{0:T(512)(128)(4,1)S(1)} %get-tuple-element.90), kind=kOutput, calls=%fused_computation.25 | convolution fusion | flops 595066880 | bytes 776704 | tf_op jit(solution)/shard_map/dot_general | solution.py:186
  27.0 2.2 %collective-permute-done.3 = f32[72,189]{1,0:T(8,128)S(1)} collective-permute-done((f32[72,189]{1,0:T(8,128)S(1)}, f32[72,189]{1,0:T(8,128)S(1)}, u32[]{:S(2)}, u32[]{:S(2)}) %collective-permute-start.3) | collective-permute-done | bytes 54464 | tf_op jit(solution)/shard_map/ppermute | solution.py:45
  29.9 0.7 %fusion.2 = f32[9,21,4,128]{3,1,2,0:T(8,128)S(1)} fusion(f32[3,4,128]{2,0,1:T(4,128)S(1)} %fusion.186, f32[9,21,4,128,1]{3,2,1,0,4:T(4,128)S(1)} %bitcast.289, f32[3,21,21]{2,1,0:T(8,128)S(1)} %neg.68), kind=kOutput, calls=%fused_computation.4 | convolution fusion | flops 37062144 | bytes 785580 | tf_op jit(solution)/shard_map/hil,qlfe->hqife/dot_general | solution.py:103
  36.0 3.3 %collective-permute-start.5 = (f32[72,189]{1,0:T(8,128)S(1)}, f32[72,189]{1,0:T(8,128)S(1)}, u32[]{:S(2)}, u32[]{:S(2)}) collective-permute-start(f32[72,189]{1,0:T(8,128)S(1)} %get-tuple-element.99), channel_id=1, source_target_pairs={{0,1},{1,2},{2,3},{4,5},{5,6},{6,7},{8,9},{9,10},{10,11},{12,13},{... | collective-permute-start | bytes 163304 | tf_op jit(solution)/shard_map/ppermute | solution.py:45
  39.3 1.9 %collective-permute-start.4 = (f32[72,189]{1,0:T(8,128)S(1)}, f32[72,189]{1,0:T(8,128)S(1)}, u32[]{:S(2)}, u32[]{:S(2)}) collective-permute-start(f32[72,189]{1,0:T(8,128)S(1)} %get-tuple-element.100), channel_id=1, source_target_pairs={{1,0},{2,1},{3,2},{5,4},{6,5},{7,6},{9,8},{10,9},{11,10},{13,12},{... | collective-permute-start | bytes 163304 | tf_op jit(solution)/shard_map/ppermute | solution.py:45
  41.2 3.7 %collective-permute-done.4 = f32[72,189]{1,0:T(8,128)S(1)} collective-permute-done((f32[72,189]{1,0:T(8,128)S(1)}, f32[72,189]{1,0:T(8,128)S(1)}, u32[]{:S(2)}, u32[]{:S(2)}) %collective-permute-start.4) | collective-permute-done | bytes 54464 | tf_op jit(solution)/shard_map/ppermute | solution.py:45
  45.0 1.9 %collective-permute-start.6 = (f32[72,189]{1,0:T(8,128)S(1)}, f32[72,189]{1,0:T(8,128)S(1)}, u32[]{:S(2)}, u32[]{:S(2)}) collective-permute-start(f32[72,189]{1,0:T(8,128)S(1)} %pad_maximum_fusion.2), channel_id=1, source_target_pairs={{4,0},{8,4},{12,8},{16,12},{20,16},{24,20},{28,24},{5,1},{9,5},{13... | collective-permute-start | bytes 163304 | tf_op jit(solution)/shard_map/ppermute | solution.py:45
  46.9 3.5 %collective-permute-start.7 = (f32[72,189]{1,0:T(8,128)S(1)}, f32[72,189]{1,0:T(8,128)S(1)}, u32[]{:S(2)}, u32[]{:S(2)}) collective-permute-start(f32[72,189]{1,0:T(8,128)S(1)} %pad_maximum_fusion.3), channel_id=1, source_target_pairs={{0,4},{4,8},{8,12},{12,16},{16,20},{20,24},{24,28},{1,5},{5,9},{9,... | collective-permute-start | bytes 163304 | tf_op jit(solution)/shard_map/ppermute | solution.py:45
  50.5 0.6 %fusion.5 = f32[189,512]{1,0:T(8,128)S(1)} fusion(f32[189,512]{1,0:T(8,128)S(1)} %bitcast.287, s32[512]{0:T(512)S(1)} %add_bitcast_fusion, pred[512]{0:T(512)(128)(4,1)S(1)} %get-tuple-element.90), kind=kOutput, calls=%fused_computation.24 | convolution fusion | flops 595066880 | bytes 776704 | tf_op jit(solution)/shard_map/dot_general | solution.py:186
  51.8 1.1 %collective-permute-done.7 = f32[72,189]{1,0:T(8,128)S(1)} collective-permute-done((f32[72,189]{1,0:T(8,128)S(1)}, f32[72,189]{1,0:T(8,128)S(1)}, u32[]{:S(2)}, u32[]{:S(2)}) %collective-permute-start.7) | collective-permute-done | bytes 54464 | tf_op jit(solution)/shard_map/ppermute | solution.py:45
  53.6 0.7 %fusion.3 = f32[9,21,4,128]{3,1,2,0:T(8,128)S(1)} fusion(f32[3,4,128]{2,0,1:T(4,128)S(1)} %fusion.186, f32[9,21,4,128,1]{3,2,1,0,4:T(4,128)S(1)} %bitcast.288, f32[3,21,21]{2,1,0:T(8,128)S(1)} %neg.68), kind=kOutput, calls=%fused_computation.5 | convolution fusion | flops 37062144 | bytes 785580 | tf_op jit(solution)/shard_map/hil,qlfe->hqife/dot_general | solution.py:103
  54.7 1.0 %add_subtract_fusion = f32[9,56,128]{2,1,0:T(8,128)} fusion(f32[9,56,128]{2,1,0:T(8,128)S(1)} %add_subtract_fusion.1, f32[9,56,128]{2,1,0:T(8,128)S(1)} %constant_dynamic-update-slice_fusion.108, f32[9,21,4,128]{3,1,2,0:T(8,128)S(1)} %constant_dynamic-update-slice_fusion.117, f32[9,21,4,128]{3,1,2,0:T(8,128)S(1)} %convolution_bitcast_fusion.14, ...), kind=kOutput, calls=%fused_computation.221 | convolution fusion | flops 32933376 | bytes 1956224 | tf_op jit(solution)/shard_map/fai,pife->pae/dot_general | solution.py:114
  (208 shorter events, 12.2 us)
Async XLA Ops:
  0.0 3.4 %copy-start = (f32[3,56,56]{2,1,0:T(8,128)S(1)}, f32[3,56,56]{2,1,0:T(8,128)}, u32[]{:S(2)}) copy-start(f32[3,56,56]{2,1,0:T(8,128)} %param.16) | copy-start | bytes 112900
  7.9 1.0 %copy-start.1 = (f32[9,56,128]{2,1,0:T(8,128)S(1)}, f32[9,56,128]{2,1,0:T(8,128)}, u32[]{:S(2)}) copy-start(f32[9,56,128]{2,1,0:T(8,128)} %param.15) | copy-start | bytes 774148
  8.8 0.8 %copy-start.3 = (f32[4,21,56]{2,0,1:T(4,128)S(1)}, f32[4,21,56]{2,0,1:T(4,128)}, u32[]{:S(2)}) copy-start(f32[4,21,56]{2,0,1:T(4,128)} %param.18) | copy-start | bytes 56452
  10.1 6.3 %copy-start.6 = (f32[4,3,128]{2,0,1:T(4,128)S(1)}, f32[4,3,128]{2,0,1:T(4,128)}, u32[]{:S(2)}) copy-start(f32[4,3,128]{2,0,1:T(4,128)} %param.24) | copy-start | bytes 18436
  10.2 6.3 %copy-start.9 = (s32[4,128]{1,0:T(4,128)S(1)}, s32[4,128]{1,0:T(4,128)}, u32[]{:S(2)}) copy-start(s32[4,128]{1,0:T(4,128)} %param.25) | copy-start | bytes 6148
  10.2 6.3 %copy-start.7 = (s32[4,128]{1,0:T(4,128)S(1)}, s32[4,128]{1,0:T(4,128)}, u32[]{:S(2)}) copy-start(s32[4,128]{1,0:T(4,128)} %param.26) | copy-start | bytes 6148
  10.2 6.3 %copy-start.10 = (s32[4,128]{1,0:T(4,128)S(1)}, s32[4,128]{1,0:T(4,128)}, u32[]{:S(2)}) copy-start(s32[4,128]{1,0:T(4,128)} %param.27) | copy-start | bytes 6148
  10.2 6.3 %copy-start.8 = (s32[1,1,8,24]{3,2,1,0:T(8,128)S(1)}, s32[1,1,8,24]{3,2,1,0:T(8,128)}, u32[]{:S(2)}) copy-start(s32[1,1,8,24]{3,2,1,0:T(8,128)} %param.29) | copy-start | bytes 2308
  10.6 14.9 %copy-start.2 = (f32[3,56,56]{2,1,0:T(8,128)S(1)}, f32[3,56,56]{2,1,0:T(8,128)}, u32[]{:S(2)}) copy-start(f32[3,56,56]{2,1,0:T(8,128)} %param.17) | copy-start | bytes 112900
  10.6 6.0 %collective-permute-start.1 = (f32[72,189]{1,0:T(8,128)S(1)}, f32[72,189]{1,0:T(8,128)S(1)}, u32[]{:S(2)}, u32[]{:S(2)}) collective-permute-start(f32[72,189]{1,0:T(8,128)S(1)} %get-tuple-element.103), channel_id=1, source_target_pairs={{0,1},{1,2},{2,3},{4,5},{5,6},{6,7},{8,9},{9,10},{10,11},{12,13},{... | collective-permute-start | bytes 163304 | tf_op jit(solution)/shard_map/ppermute | solution.py:45
  14.5 5.7 %collective-permute-start = (f32[72,189]{1,0:T(8,128)S(1)}, f32[72,189]{1,0:T(8,128)S(1)}, u32[]{:S(2)}, u32[]{:S(2)}) collective-permute-start(f32[72,189]{1,0:T(8,128)S(1)} %get-tuple-element.104), channel_id=1, source_target_pairs={{1,0},{2,1},{3,2},{5,4},{6,5},{7,6},{9,8},{10,9},{11,10},{13,12},{... | collective-permute-start | bytes 163304 | tf_op jit(solution)/shard_map/ppermute | solution.py:45
  20.2 6.8 %collective-permute-start.2 = (f32[72,189]{1,0:T(8,128)S(1)}, f32[72,189]{1,0:T(8,128)S(1)}, u32[]{:S(2)}, u32[]{:S(2)}) collective-permute-start(f32[72,189]{1,0:T(8,128)S(1)} %pad_maximum_fusion), channel_id=1, source_target_pairs={{4,0},{8,4},{12,8},{16,12},{20,16},{24,20},{28,24},{5,1},{9,5},{13... | collective-permute-start | bytes 163304 | tf_op jit(solution)/shard_map/ppermute | solution.py:45
  23.2 6.0 %collective-permute-start.3 = (f32[72,189]{1,0:T(8,128)S(1)}, f32[72,189]{1,0:T(8,128)S(1)}, u32[]{:S(2)}, u32[]{:S(2)}) collective-permute-start(f32[72,189]{1,0:T(8,128)S(1)} %pad_maximum_fusion.1), channel_id=1, source_target_pairs={{0,4},{4,8},{8,12},{12,16},{16,20},{20,24},{24,28},{1,5},{5,9},{9,... | collective-permute-start | bytes 163304 | tf_op jit(solution)/shard_map/ppermute | solution.py:45
  26.2 0.8 %copy-start.4 = (f32[4,56,21]{1,0,2:T(4,128)S(1)}, f32[4,56,21]{1,0,2:T(4,128)}, u32[]{:S(2)}) copy-start(f32[4,56,21]{1,0,2:T(4,128)} %param.19) | copy-start | bytes 56452
  26.2 0.8 %copy-start.5 = (f32[3,21,21]{2,1,0:T(8,128)S(1)}, f32[3,21,21]{2,1,0:T(8,128)}, u32[]{:S(2)}) copy-start(f32[3,21,21]{2,1,0:T(8,128)} %param.20) | copy-start | bytes 15880
  36.0 5.2 %collective-permute-start.5 = (f32[72,189]{1,0:T(8,128)S(1)}, f32[72,189]{1,0:T(8,128)S(1)}, u32[]{:S(2)}, u32[]{:S(2)}) collective-permute-start(f32[72,189]{1,0:T(8,128)S(1)} %get-tuple-element.99), channel_id=1, source_target_pairs={{0,1},{1,2},{2,3},{4,5},{5,6},{6,7},{8,9},{9,10},{10,11},{12,13},{... | collective-permute-start | bytes 163304 | tf_op jit(solution)/shard_map/ppermute | solution.py:45
  39.3 5.7 %collective-permute-start.4 = (f32[72,189]{1,0:T(8,128)S(1)}, f32[72,189]{1,0:T(8,128)S(1)}, u32[]{:S(2)}, u32[]{:S(2)}) collective-permute-start(f32[72,189]{1,0:T(8,128)S(1)} %get-tuple-element.100), channel_id=1, source_target_pairs={{1,0},{2,1},{3,2},{5,4},{6,5},{7,6},{9,8},{10,9},{11,10},{13,12},{... | collective-permute-start | bytes 163304 | tf_op jit(solution)/shard_map/ppermute | solution.py:45
  45.0 6.8 %collective-permute-start.6 = (f32[72,189]{1,0:T(8,128)S(1)}, f32[72,189]{1,0:T(8,128)S(1)}, u32[]{:S(2)}, u32[]{:S(2)}) collective-permute-start(f32[72,189]{1,0:T(8,128)S(1)} %pad_maximum_fusion.2), channel_id=1, source_target_pairs={{4,0},{8,4},{12,8},{16,12},{20,16},{24,20},{28,24},{5,1},{9,5},{13... | collective-permute-start | bytes 163304 | tf_op jit(solution)/shard_map/ppermute | solution.py:45
  46.9 6.0 %collective-permute-start.7 = (f32[72,189]{1,0:T(8,128)S(1)}, f32[72,189]{1,0:T(8,128)S(1)}, u32[]{:S(2)}, u32[]{:S(2)}) collective-permute-start(f32[72,189]{1,0:T(8,128)S(1)} %pad_maximum_fusion.3), channel_id=1, source_target_pairs={{0,4},{4,8},{8,12},{12,16},{16,20},{20,24},{24,28},{1,5},{5,9},{9,... | collective-permute-start | bytes 163304 | tf_op jit(solution)/shard_map/ppermute | solution.py:45

commit v12 on v11

--- a/solution.py
+++ b/solution.py
@@ -88,25 +88,33 @@
     return (integrated, face_data)
 
 
+def rotate_faces(neighbour_data, orientation, rotate_negated):
+    turned_negated = jnp.einsum(
+        "hil,qlfe->hqife", rotate_negated, neighbour_data, precision=fast_mode
+    )
+    chosen = (orientation[None] == jnp.arange(3, dtype=jnp.int32)[:, None, None]).astype(
+        neighbour_data.dtype
+    )
+    return jnp.sum(turned_negated * chosen[:, None, None, :, :], axis=0)
+
+
+def rotate_slots(received, slot_chosen, rotate_negated, face_width):
+    slots = received.reshape(received.shape[0], -1, face_width)
+    turned_negated = jnp.einsum("hil,sql->hsqi", rotate_negated, slots, precision=fast_mode)
+    turned_negated = jnp.sum(turned_negated * slot_chosen[:, :, None, None], axis=0)
+    return turned_negated.reshape(received.shape)
+
+
 def face_update(
     current,
     volume,
     face_data,
-    neighbour_data,
-    orientation,
+    turned_negated,
     normals,
     values,
     wave_speed,
-    rotate_negated,
     half_lift,
 ):
-    turned_negated = jnp.einsum(
-        "hil,qlfe->hqife", rotate_negated, neighbour_data, precision=fast_mode
-    )
-    chosen = (orientation[None] == jnp.arange(3, dtype=jnp.int32)[:, None, None]).astype(
-        current.dtype
-    )
-    turned_negated = jnp.sum(turned_negated * chosen[:, None, None, :, :], axis=0)
     both = face_data - turned_negated
     apart = face_data + turned_negated
     parts = [normals[:, k, :][None, None] * both for k in range(3)]
@@ -171,6 +179,7 @@
     scatter_in = ((targets[:, None] == face_ids[None, :]) & ~inside[None, :]).astype(dtype)
     current = dof_values
     rotate_negated, half_lift = rotate, face_lift
+    slot_chosen = jnp.zeros((3, scatter_in.shape[0]), dtype)
     for time_index in range(STEPS):
         integrated, face_data = local_part(
             current, inv_jacobian, values, grad_matrix, face_proj
@@ -180,32 +189,45 @@
             gather_out, flat_faces, (((1,), (1,)), ((), ())), precision=exact_mode
         )
 
-        def local_work(integrated, flat_faces, rotate_negated, half_lift):
+        def local_work(integrated, flat_faces, rotate_negated, half_lift, slot_chosen):
             slopes = jnp.einsum("dab,qbe->dqae", stiff_matrix, integrated, precision=fast_mode)
             volume = star_apply(slopes, inv_jacobian, values)
-            local_data = jnp.dot(flat_faces, gather_local, precision=exact_mode)
             if time_index == 0:
                 rotate_negated = -rotate_negated
                 half_lift = 0.5 * half_lift
-            return volume, local_data, rotate_negated, half_lift
-
-        received, (volume, local_data, rotate_negated, half_lift) = deliver(
-            outgoing, slot_total, (integrated, flat_faces, rotate_negated, half_lift), local_work
-        )
-        neighbour_data = local_data + lax.dot_general(
-            received, scatter_in, (((0,), (0,)), ((), ())), precision=exact_mode
-        )
-        neighbour_data = neighbour_data.reshape(9, face_width, 4, elem_count)
+                slot_orientation = jnp.dot(
+                    scatter_in, orientation.reshape(-1).astype(dtype), precision=exact_mode
+                )
+                slot_chosen = (
+                    slot_orientation[None, :] == jnp.arange(3, dtype=dtype)[:, None]
+                ).astype(dtype)
+            local_data = jnp.dot(flat_faces, gather_local, precision=exact_mode)
+            local_turned = rotate_faces(
+                local_data.reshape(9, face_width, 4, elem_count), orientation, rotate_negated
+            )
+            return volume, local_turned, rotate_negated, half_lift, slot_chosen
+
+        received, (volume, local_turned, rotate_negated, half_lift, slot_chosen) = deliver(
+            outgoing,
+            slot_total,
+            (integrated, flat_faces, rotate_negated, half_lift, slot_chosen),
+            local_work,
+        )
+        remote_turned = lax.dot_general(
+            rotate_slots(received, slot_chosen, rotate_negated, face_width),
+            scatter_in,
+            (((0,), (0,)), ((), ())),
+            precision=exact_mode,
+        )
+        turned_negated = local_turned + remote_turned.reshape(9, face_width, 4, elem_count)
         current = face_update(
             current,
             volume,
             face_data,
-            neighbour_data,
-            orientation,
+            turned_negated,
             normals,
             values,
             wave_speed,
-            rotate_negated,
             half_lift,
         )
     return current

time: 56.3 us -> 56.9 us (1.011)
  waiting for transfers between devices: 10.5 us -> 8.44 us
  local copies, waits for them, and re-layouts: 4.33 us -> 5.95 us
  matrix products: 13.9 us -> 15.2 us
    ppermute x8, waiting for transfers between devices: 10.5 us -> 8.44 us  [shifted(): return lax.ppermute(x, axis, pairs)]
    unnamed x28, local copies, waits for them, and re-layouts: 1.8 us -> 3.05 us
    dot_general x4 -> x7, matrix products: 2.37 us -> 3.51 us  [the longest x2 1.35 us: rotate_faces(): jnp.einsum('hil,qlfe->hqife', rotate_negated, neighbour_data, precision=f...]
  transfers between devices with their start and end apart: 8 -> 8, of which waited for: 4 -> 3; matrix products, arithmetic and copies ran while one was open for 5% -> 8% of each run, Pallas kernels for 0% -> 0%
where the time goes in v12:
time: 56.9 us; the launch traced here: 56.2 us
  starting transfers between devices  21.5 us (38%)
  matrix products  15.2 us (27%)
  waiting for transfers between devices  8.44 us (15%)
  local copies, waits for them, and re-layouts  5.95 us (10%)
  other arithmetic  3.64 us (6%)
  between operations  1.47 us (3%)
    ppermute x8, starting transfers between devices, shifted(): return lax.ppermute(x, axis, pairs)  21.5 us
    ppermute x8, waiting for transfers between devices, shifted(): return lax.ppermute(x, axis, pairs)  8.44 us
    dot_general x10, matrix products, predict(): jnp.einsum('dab,qbe->dqae', grad_matrix, derivative, precision=fast_mode)  6.46 us
    unnamed x28, local copies, waits for them, and re-layouts  3.05 us
    dot_general x2, matrix products, face_update(): jnp.einsum('fai,pife->pae', half_lift, flux_total, precision=fast_mode)  1.48 us
    unnamed x112, other arithmetic  1.36 us
    dot_general x2, matrix products, rotate_faces(): jnp.einsum('hil,qlfe->hqife', rotate_negated, neighbour_data, precision=f...  1.35 us
    dot_general x2, matrix products, local_work(): local_data = jnp.dot(flat_faces, gather_local, precision=exact_mode)  1.22 us
  transfers between devices with their start and end apart: 8, of which 3 were waited for; matrix products, arithmetic and copies ran while one was open for 8% of the time, Pallas kernels for 0%

profile of v12, /device:TPU:25, one launch (start us, length us, event | category | flops | bytes accessed | tf_op | source)
XLA Modules:
  0.0 56.2 jit_solution(527924609553691498)
XLA Ops:
  0.0 0.7 %iota_compare_fusion.6 = pred[16,128]{1,0:T(8,128)(4,1)S(1)} fusion(s32[128]{0:T(128)} %param.22), kind=kLoop, calls=%fused_computation.554 | loop fusion | flops 2048 | bytes 2560 | tf_op jit(solution)/shard_map/eq | solution.py:50
  0.7 0.8 %select_reduce_fusion = f32[3,128]{1,0:T(4,128)S(1)} fusion(f32[16,3]{0,1:T(4,128)} %param.21, pred[16,128]{1,0:T(8,128)(4,1)S(1)} %iota_compare_fusion.6), kind=kLoop, calls=%fused_computation.551 | loop fusion | flops 11904 | bytes 3776 | tf_op jit(solution)/shard_map/reduce_sum | solution.py:51
  1.5 1.0 %slice_bitcast_fusion.3 = (s32[1,24]{1,0:T(1,128)S(1)}, s32[1,24]{1,0:T(1,128)S(1)}, s32[1,24]{1,0:T(1,128)S(1)}, s32[1,24]{1,0:T(1,128)S(1)}, s32[1,24]{1,0:T(1...) fusion(s32[1,1,8,24]{3,2,1,0:T(8,128)} %param.28), kind=kLoop, calls=%fused_computation.575 | loop fusion | bytes 1536 | tf_op jit(solution)/shard_map/squeeze | solution.py:175
  2.6 0.8 %fusion.198 = (f32[3,1,128]{2,1,0:T(1,128)S(1)}, f32[3,1,128]{2,1,0:T(1,128)S(1)}, f32[3,1,128]{2,1,0:T(1,128)S(1)}) fusion(f32[3,3,128]{2,1,0:T(4,128)} %param.23), kind=kLoop, calls=%fused_computation.594 | loop fusion | bytes 9216 | tf_op jit(solution)/shard_map/slice | solution.py:69
  3.4 1.6 %multiply_reduce_fusion.33 = (f32[9,56,128]{2,1,0:T(8,128)S(1)}, f32[9,56,128]{2,1,0:T(8,128)S(1)}, f32[9,56,128]{2,1,0:T(8,128)S(1)}) fusion(f32[3,128]{1,0:T(4,128)S(1)} %get-tuple-element.146, f32[3,128]{1,0:T(4,128)S(1)} %get-tuple-element.147, f32[3,128]{1,0:T(4,128)S(1)} %bitcast.349, f32[3,56,56]{2,1,0:T(8,128)S(1)} %copy-done, f32[9,56,128]{2,1,0:T(8,128)} %param.15), kind=kOutput, calls=%fused_computation.65 | convolution fusion | flops 65995776 | bytes 1074432 | tf_op jit(solution)/shard_map/dab,qbe->dqae/dot_general | solution.py:78
  8.0 0.8 %copy-done.1 = f32[9,56,128]{2,1,0:T(8,128)S(1)} copy-done((f32[9,56,128]{2,1,0:T(8,128)S(1)}, f32[9,56,128]{2,1,0:T(8,128)}, u32[]{:S(2)}) %copy-start.1) | copy-done | bytes 258072
  8.9 0.6 %copy-done.3 = f32[4,21,56]{2,0,1:T(4,128)S(1)} copy-done((f32[4,21,56]{2,0,1:T(4,128)S(1)}, f32[4,21,56]{2,0,1:T(4,128)}, u32[]{:S(2)}) %copy-start.3) | copy-done | bytes 18840
  10.6 3.7 %collective-permute-start.1 = (f32[72,189]{1,0:T(8,128)S(1)}, f32[72,189]{1,0:T(8,128)S(1)}, u32[]{:S(2)}, u32[]{:S(2)}) collective-permute-start(f32[72,189]{1,0:T(8,128)S(1)} %get-tuple-element.111), channel_id=1, source_target_pairs={{0,1},{1,2},{2,3},{4,5},{5,6},{6,7},{8,9},{9,10},{10,11},{12,13},{... | collective-permute-start | bytes 163304 | tf_op jit(solution)/shard_map/ppermute | solution.py:45
  14.3 1.9 %collective-permute-start = (f32[72,189]{1,0:T(8,128)S(1)}, f32[72,189]{1,0:T(8,128)S(1)}, u32[]{:S(2)}, u32[]{:S(2)}) collective-permute-start(f32[72,189]{1,0:T(8,128)S(1)} %get-tuple-element.112), channel_id=1, source_target_pairs={{1,0},{2,1},{3,2},{5,4},{6,5},{7,6},{9,8},{10,9},{11,10},{13,12},{... | collective-permute-start | bytes 163304 | tf_op jit(solution)/shard_map/ppermute | solution.py:45
  16.9 3.1 %collective-permute-done = f32[72,189]{1,0:T(8,128)S(1)} collective-permute-done((f32[72,189]{1,0:T(8,128)S(1)}, f32[72,189]{1,0:T(8,128)S(1)}, u32[]{:S(2)}, u32[]{:S(2)}) %collective-permute-start) | collective-permute-done | bytes 54464 | tf_op jit(solution)/shard_map/ppermute | solution.py:45
  20.1 3.0 %collective-permute-start.2 = (f32[72,189]{1,0:T(8,128)S(1)}, f32[72,189]{1,0:T(8,128)S(1)}, u32[]{:S(2)}, u32[]{:S(2)}) collective-permute-start(f32[72,189]{1,0:T(8,128)S(1)} %pad_maximum_fusion.2), channel_id=1, source_target_pairs={{4,0},{8,4},{12,8},{16,12},{20,16},{24,20},{28,24},{5,1},{9,5},{13... | collective-permute-start | bytes 163304 | tf_op jit(solution)/shard_map/ppermute | solution.py:45
  23.1 2.5 %collective-permute-start.3 = (f32[72,189]{1,0:T(8,128)S(1)}, f32[72,189]{1,0:T(8,128)S(1)}, u32[]{:S(2)}, u32[]{:S(2)}) collective-permute-start(f32[72,189]{1,0:T(8,128)S(1)} %pad_maximum_fusion.3), channel_id=1, source_target_pairs={{0,4},{4,8},{8,12},{12,16},{16,20},{20,24},{24,28},{1,5},{5,9},{9,... | collective-permute-start | bytes 163304 | tf_op jit(solution)/shard_map/ppermute | solution.py:45
  25.6 0.6 %fusion.11 = f32[189,512]{1,0:T(8,128)S(1)} fusion(f32[189,512]{1,0:T(8,128)S(1)} %bitcast.338, s32[512]{0:T(512)S(1)} %add_bitcast_fusion, pred[512]{0:T(512)(128)(4,1)S(1)} %bitcast.361), kind=kOutput, calls=%fused_computation.31 | convolution fusion | flops 595066880 | bytes 776704 | tf_op jit(solution)/shard_map/dot_general | solution.py:204
  26.3 0.7 %copy-done.2 = f32[3,56,56]{2,1,0:T(8,128)S(1)} copy-done((f32[3,56,56]{2,1,0:T(8,128)S(1)}, f32[3,56,56]{2,1,0:T(8,128)}, u32[]{:S(2)}) %copy-start.2) | copy-done | bytes 37656
  27.8 0.6 %copy-done.4 = f32[3,21,21]{2,1,0:T(8,128)S(1)} copy-done((f32[3,21,21]{2,1,0:T(8,128)S(1)}, f32[3,21,21]{2,1,0:T(8,128)}, u32[]{:S(2)}) %copy-start.4) | copy-done | bytes 5316
  28.4 0.7 %fusion.2 = f32[9,21,4,128]{3,1,2,0:T(8,128)S(1)} fusion(f32[3,4,128]{2,0,1:T(4,128)S(1)} %fusion.186, f32[9,21,4,128,1]{3,2,1,0,4:T(4,128)S(1)} %bitcast.342, f32[3,21,21]{2,1,0:T(8,128)S(1)} %copy-done.4), kind=kOutput, calls=%fused_computation.4 | convolution fusion | flops 37063468 | bytes 785580 | tf_op jit(solution)/shard_map/hil,qlfe->hqife/dot_general | solution.py:92
  35.6 3.3 %collective-permute-start.5 = (f32[72,189]{1,0:T(8,128)S(1)}, f32[72,189]{1,0:T(8,128)S(1)}, u32[]{:S(2)}, u32[]{:S(2)}) collective-permute-start(f32[72,189]{1,0:T(8,128)S(1)} %get-tuple-element.107), channel_id=1, source_target_pairs={{0,1},{1,2},{2,3},{4,5},{5,6},{6,7},{8,9},{9,10},{10,11},{12,13},{... | collective-permute-start | bytes 163304 | tf_op jit(solution)/shard_map/ppermute | solution.py:45
  38.9 1.9 %collective-permute-start.4 = (f32[72,189]{1,0:T(8,128)S(1)}, f32[72,189]{1,0:T(8,128)S(1)}, u32[]{:S(2)}, u32[]{:S(2)}) collective-permute-start(f32[72,189]{1,0:T(8,128)S(1)} %get-tuple-element.108), channel_id=1, source_target_pairs={{1,0},{2,1},{3,2},{5,4},{6,5},{7,6},{9,8},{10,9},{11,10},{13,12},{... | collective-permute-start | bytes 163304 | tf_op jit(solution)/shard_map/ppermute | solution.py:45
  40.8 3.7 %collective-permute-done.4 = f32[72,189]{1,0:T(8,128)S(1)} collective-permute-done((f32[72,189]{1,0:T(8,128)S(1)}, f32[72,189]{1,0:T(8,128)S(1)}, u32[]{:S(2)}, u32[]{:S(2)}) %collective-permute-start.4) | collective-permute-done | bytes 54464 | tf_op jit(solution)/shard_map/ppermute | solution.py:45
  44.6 3.1 %collective-permute-start.6 = (f32[72,189]{1,0:T(8,128)S(1)}, f32[72,189]{1,0:T(8,128)S(1)}, u32[]{:S(2)}, u32[]{:S(2)}) collective-permute-start(f32[72,189]{1,0:T(8,128)S(1)} %pad_maximum_fusion.4), channel_id=1, source_target_pairs={{4,0},{8,4},{12,8},{16,12},{20,16},{24,20},{28,24},{5,1},{9,5},{13... | collective-permute-start | bytes 163304 | tf_op jit(solution)/shard_map/ppermute | solution.py:45
  47.7 2.2 %collective-permute-start.7 = (f32[72,189]{1,0:T(8,128)S(1)}, f32[72,189]{1,0:T(8,128)S(1)}, u32[]{:S(2)}, u32[]{:S(2)}) collective-permute-start(f32[72,189]{1,0:T(8,128)S(1)} %pad_maximum_fusion.5), channel_id=1, source_target_pairs={{0,4},{4,8},{8,12},{12,16},{16,20},{20,24},{24,28},{1,5},{5,9},{9,... | collective-permute-start | bytes 163304 | tf_op jit(solution)/shard_map/ppermute | solution.py:45
  51.4 0.7 %fusion.3 = f32[9,21,4,128]{3,1,2,0:T(8,128)S(1)} fusion(f32[3,4,128]{2,0,1:T(4,128)S(1)} %fusion.186, f32[9,21,4,128,1]{3,2,1,0,4:T(4,128)S(1)} %bitcast.341, f32[3,21,21]{2,1,0:T(8,128)S(1)} %neg.68), kind=kOutput, calls=%fused_computation.5 | convolution fusion | flops 37062144 | bytes 785580 | tf_op jit(solution)/shard_map/hil,qlfe->hqife/dot_general | solution.py:92
  52.1 1.6 %collective-permute-done.7 = f32[72,189]{1,0:T(8,128)S(1)} collective-permute-done((f32[72,189]{1,0:T(8,128)S(1)}, f32[72,189]{1,0:T(8,128)S(1)}, u32[]{:S(2)}, u32[]{:S(2)}) %collective-permute-start.7) | collective-permute-done | bytes 54464 | tf_op jit(solution)/shard_map/ppermute | solution.py:45
  55.1 1.1 %add_subtract_fusion = f32[9,56,128]{2,1,0:T(8,128)} fusion(f32[9,56,128]{2,1,0:T(8,128)S(1)} %add_subtract_fusion.1, f32[9,56,128]{2,1,0:T(8,128)S(1)} %constant_dynamic-update-slice_fusion.108, f32[9,21,4,128]{3,1,2,0:T(8,128)S(1)} %constant_dynamic-update-slice_fusion.117, f32[9,21,4,128]{3,1,2,0:T(8,128)S(1)} %convolution_bitcast_fusion.16, ...), kind=kOutput, calls=%fused_computation.231 | convolution fusion | flops 33030144 | bytes 2343296 | tf_op jit(solution)/shard_map/fai,pife->pae/dot_general | solution.py:122
  (223 shorter events, 14.1 us)
Async XLA Ops:
  0.0 3.4 %copy-start = (f32[3,56,56]{2,1,0:T(8,128)S(1)}, f32[3,56,56]{2,1,0:T(8,128)}, u32[]{:S(2)}) copy-start(f32[3,56,56]{2,1,0:T(8,128)} %param.16) | copy-start | bytes 112900
  7.9 1.0 %copy-start.1 = (f32[9,56,128]{2,1,0:T(8,128)S(1)}, f32[9,56,128]{2,1,0:T(8,128)}, u32[]{:S(2)}) copy-start(f32[9,56,128]{2,1,0:T(8,128)} %param.15) | copy-start | bytes 774148
  8.8 0.8 %copy-start.3 = (f32[4,21,56]{2,0,1:T(4,128)S(1)}, f32[4,21,56]{2,0,1:T(4,128)}, u32[]{:S(2)}) copy-start(f32[4,21,56]{2,0,1:T(4,128)} %param.18) | copy-start | bytes 56452
  10.1 6.1 %copy-start.6 = (f32[4,3,128]{2,0,1:T(4,128)S(1)}, f32[4,3,128]{2,0,1:T(4,128)}, u32[]{:S(2)}) copy-start(f32[4,3,128]{2,0,1:T(4,128)} %param.24) | copy-start | bytes 18436
  10.2 6.1 %copy-start.7 = (s32[4,128]{1,0:T(4,128)S(1)}, s32[4,128]{1,0:T(4,128)}, u32[]{:S(2)}) copy-start(s32[4,128]{1,0:T(4,128)} %param.25) | copy-start | bytes 6148
  10.2 6.2 %copy-start.9 = (s32[1,1,8,24]{3,2,1,0:T(8,128)S(1)}, s32[1,1,8,24]{3,2,1,0:T(8,128)}, u32[]{:S(2)}) copy-start(s32[1,1,8,24]{3,2,1,0:T(8,128)} %param.29) | copy-start | bytes 2308
  10.2 6.3 %copy-start.8 = (s32[4,128]{1,0:T(4,128)S(1)}, s32[4,128]{1,0:T(4,128)}, u32[]{:S(2)}) copy-start(s32[4,128]{1,0:T(4,128)} %param.26) | copy-start | bytes 6148
  10.2 6.3 %copy-start.10 = (s32[4,128]{1,0:T(4,128)S(1)}, s32[4,128]{1,0:T(4,128)}, u32[]{:S(2)}) copy-start(s32[4,128]{1,0:T(4,128)} %param.27) | copy-start | bytes 6148
  10.6 9.4 %copy-start.5 = (f32[4,56,21]{1,0,2:T(4,128)S(1)}, f32[4,56,21]{1,0,2:T(4,128)}, u32[]{:S(2)}) copy-start(f32[4,56,21]{1,0,2:T(4,128)} %param.19) | copy-start | bytes 56452
  10.6 6.3 %collective-permute-start.1 = (f32[72,189]{1,0:T(8,128)S(1)}, f32[72,189]{1,0:T(8,128)S(1)}, u32[]{:S(2)}, u32[]{:S(2)}) collective-permute-start(f32[72,189]{1,0:T(8,128)S(1)} %get-tuple-element.111), channel_id=1, source_target_pairs={{0,1},{1,2},{2,3},{4,5},{5,6},{6,7},{8,9},{9,10},{10,11},{12,13},{... | collective-permute-start | bytes 163304 | tf_op jit(solution)/shard_map/ppermute | solution.py:45
  14.3 5.7 %collective-permute-start = (f32[72,189]{1,0:T(8,128)S(1)}, f32[72,189]{1,0:T(8,128)S(1)}, u32[]{:S(2)}, u32[]{:S(2)}) collective-permute-start(f32[72,189]{1,0:T(8,128)S(1)} %get-tuple-element.112), channel_id=1, source_target_pairs={{1,0},{2,1},{3,2},{5,4},{6,5},{7,6},{9,8},{10,9},{11,10},{13,12},{... | collective-permute-start | bytes 163304 | tf_op jit(solution)/shard_map/ppermute | solution.py:45
  20.1 9.0 %collective-permute-start.2 = (f32[72,189]{1,0:T(8,128)S(1)}, f32[72,189]{1,0:T(8,128)S(1)}, u32[]{:S(2)}, u32[]{:S(2)}) collective-permute-start(f32[72,189]{1,0:T(8,128)S(1)} %pad_maximum_fusion.2), channel_id=1, source_target_pairs={{4,0},{8,4},{12,8},{16,12},{20,16},{24,20},{28,24},{5,1},{9,5},{13... | collective-permute-start | bytes 163304 | tf_op jit(solution)/shard_map/ppermute | solution.py:45
  23.1 6.0 %collective-permute-start.3 = (f32[72,189]{1,0:T(8,128)S(1)}, f32[72,189]{1,0:T(8,128)S(1)}, u32[]{:S(2)}, u32[]{:S(2)}) collective-permute-start(f32[72,189]{1,0:T(8,128)S(1)} %pad_maximum_fusion.3), channel_id=1, source_target_pairs={{0,4},{4,8},{8,12},{12,16},{16,20},{20,24},{24,28},{1,5},{5,9},{9,... | collective-permute-start | bytes 163304 | tf_op jit(solution)/shard_map/ppermute | solution.py:45
  26.2 0.9 %copy-start.2 = (f32[3,56,56]{2,1,0:T(8,128)S(1)}, f32[3,56,56]{2,1,0:T(8,128)}, u32[]{:S(2)}) copy-start(f32[3,56,56]{2,1,0:T(8,128)} %param.17) | copy-start | bytes 112900
  27.6 0.8 %copy-start.4 = (f32[3,21,21]{2,1,0:T(8,128)S(1)}, f32[3,21,21]{2,1,0:T(8,128)}, u32[]{:S(2)}) copy-start(f32[3,21,21]{2,1,0:T(8,128)} %param.20) | copy-start | bytes 15880
  35.6 5.2 %collective-permute-start.5 = (f32[72,189]{1,0:T(8,128)S(1)}, f32[72,189]{1,0:T(8,128)S(1)}, u32[]{:S(2)}, u32[]{:S(2)}) collective-permute-start(f32[72,189]{1,0:T(8,128)S(1)} %get-tuple-element.107), channel_id=1, source_target_pairs={{0,1},{1,2},{2,3},{4,5},{5,6},{6,7},{8,9},{9,10},{10,11},{12,13},{... | collective-permute-start | bytes 163304 | tf_op jit(solution)/shard_map/ppermute | solution.py:45
  38.9 5.7 %collective-permute-start.4 = (f32[72,189]{1,0:T(8,128)S(1)}, f32[72,189]{1,0:T(8,128)S(1)}, u32[]{:S(2)}, u32[]{:S(2)}) collective-permute-start(f32[72,189]{1,0:T(8,128)S(1)} %get-tuple-element.108), channel_id=1, source_target_pairs={{1,0},{2,1},{3,2},{5,4},{6,5},{7,6},{9,8},{10,9},{11,10},{13,12},{... | collective-permute-start | bytes 163304 | tf_op jit(solution)/shard_map/ppermute | solution.py:45
  44.6 7.5 %collective-permute-start.6 = (f32[72,189]{1,0:T(8,128)S(1)}, f32[72,189]{1,0:T(8,128)S(1)}, u32[]{:S(2)}, u32[]{:S(2)}) collective-permute-start(f32[72,189]{1,0:T(8,128)S(1)} %pad_maximum_fusion.4), channel_id=1, source_target_pairs={{4,0},{8,4},{12,8},{16,12},{20,16},{24,20},{28,24},{5,1},{9,5},{13... | collective-permute-start | bytes 163304 | tf_op jit(solution)/shard_map/ppermute | solution.py:45
  47.7 6.0 %collective-permute-start.7 = (f32[72,189]{1,0:T(8,128)S(1)}, f32[72,189]{1,0:T(8,128)S(1)}, u32[]{:S(2)}, u32[]{:S(2)}) collective-permute-start(f32[72,189]{1,0:T(8,128)S(1)} %pad_maximum_fusion.5), channel_id=1, source_target_pairs={{0,4},{4,8},{8,12},{12,16},{16,20},{20,24},{24,28},{1,5},{5,9},{9,... | collective-permute-start | bytes 163304 | tf_op jit(solution)/shard_map/ppermute | solution.py:45

commit v13 on v11

--- a/solution.py
+++ b/solution.py
@@ -164,9 +164,12 @@
     inside = (neighbour >= 0).reshape(-1)
     local_index = (neighbour_face * elem_count + jnp.maximum(neighbour, 0)).reshape(-1)
     gather_local = ((local_index[None, :] == face_ids[:, None]) & inside[None, :]).astype(dtype)
-    source_ids = jnp.concatenate([send_list[0, 0, d : d + 1] for d in SEND_ORDER], axis=0)
-    slot_total = source_ids.shape[1]
-    gather_out = (source_ids.reshape(-1)[:, None] == face_ids[None, :]).astype(dtype)
+    slot_total = send_list.shape[3]
+    natural_out = (send_list.reshape(-1)[:, None] == face_ids[None, :]).astype(dtype)
+    slot_ids = jnp.arange(8 * slot_total, dtype=jnp.int32)
+    send_slots = (jnp.array(SEND_ORDER, dtype=jnp.int32)[:, None] * slot_total + jnp.arange(slot_total, dtype=jnp.int32)[None, :]).reshape(-1)
+    reorder = (send_slots[:, None] == slot_ids[None, :]).astype(dtype)
+    gather_out = jnp.dot(reorder, natural_out, precision=exact_mode)
     targets = recv_list[0, 0].reshape(-1)
     scatter_in = ((targets[:, None] == face_ids[None, :]) & ~inside[None, :]).astype(dtype)
     current = dof_values

time: 56.3 us -> 58.8 us (1.044)
  the two profiles are of different devices: /device:TPU:25 before, /device:TPU:22 now
where the time goes in v13:
time: 58.8 us; the launch traced here: 58.2 us
  starting transfers between devices  20.7 us (35%)
  matrix products  14.5 us (25%)
  waiting for transfers between devices  13.9 us (24%)
  local copies, waits for them, and re-layouts  3.9 us (7%)
  other arithmetic  3.83 us (7%)
  between operations  1.45 us (2%)
    ppermute x8, starting transfers between devices, shifted(): return lax.ppermute(x, axis, pairs)  20.7 us
    ppermute x8, waiting for transfers between devices, shifted(): return lax.ppermute(x, axis, pairs)  13.9 us
    dot_general x10, matrix products, predict(): jnp.einsum('dab,qbe->dqae', grad_matrix, derivative, precision=fast_mode)  6.45 us
    unnamed x32, local copies, waits for them, and re-layouts  2.31 us
    dot_general x2, matrix products, face_update(): jnp.einsum('fai,pife->pae', half_lift, flux_total, precision=fast_mode)  1.4 us
    dot_general x2, matrix products, face_update(): jnp.einsum('hil,qlfe->hqife', rotate_negated, neighbour_data, precision=f...  1.36 us
    unnamed x112, other arithmetic  1.34 us
    dot_general x2, matrix products, local_work(): local_data = jnp.dot(flat_faces, gather_local, precision=exact_mode)  1.22 us
  transfers between devices with their start and end apart: 8, of which 4 were waited for; matrix products, arithmetic and copies ran while one was open for 2% of the time, Pallas kernels for 0%

profile of v13, /device:TPU:22, one launch (start us, length us, event | category | flops | bytes accessed | tf_op | source)
XLA Modules:
  0.0 58.2 jit_solution(15193846897504296797)
XLA Ops:
  0.0 0.8 %fusion.197 = (f32[3,1,128]{2,1,0:T(1,128)S(1)}, f32[3,1,128]{2,1,0:T(1,128)S(1)}, f32[3,1,128]{2,1,0:T(1,128)S(1)}) fusion(f32[3,3,128]{2,1,0:T(4,128)} %param.24), kind=kLoop, calls=%fused_computation.572 | loop fusion | bytes 9216 | tf_op jit(solution)/shard_map/slice | solution.py:69
  0.8 0.7 %iota_compare_fusion.7 = pred[16,128]{1,0:T(8,128)(4,1)S(1)} fusion(s32[128]{0:T(128)} %param.23), kind=kLoop, calls=%fused_computation.542 | loop fusion | flops 2048 | bytes 2560 | tf_op jit(solution)/shard_map/eq | solution.py:50
  1.5 0.8 %select_reduce_fusion = f32[3,128]{1,0:T(4,128)S(1)} fusion(f32[16,3]{0,1:T(4,128)} %param.22, pred[16,128]{1,0:T(8,128)(4,1)S(1)} %iota_compare_fusion.7), kind=kLoop, calls=%fused_computation.539 | loop fusion | flops 11904 | bytes 3776 | tf_op jit(solution)/shard_map/reduce_sum | solution.py:51
  2.3 1.6 %multiply_reduce_fusion.33 = (f32[9,56,128]{2,1,0:T(8,128)S(1)}, f32[9,56,128]{2,1,0:T(8,128)S(1)}, f32[9,56,128]{2,1,0:T(8,128)S(1)}) fusion(f32[3,128]{1,0:T(4,128)S(1)} %get-tuple-element.128, f32[3,128]{1,0:T(4,128)S(1)} %get-tuple-element.129, f32[3,128]{1,0:T(4,128)S(1)} %bitcast.282, f32[3,56,56]{2,1,0:T(8,128)S(1)} %copy-done, f32[9,56,128]{2,1,0:T(8,128)} %param.16), kind=kOutput, calls=%fused_computation.59 | convolution fusion | flops 65995776 | bytes 1074432 | tf_op jit(solution)/shard_map/dab,qbe->dqae/dot_general | solution.py:78
  6.9 0.8 %copy-done.1 = f32[9,56,128]{2,1,0:T(8,128)S(1)} copy-done((f32[9,56,128]{2,1,0:T(8,128)S(1)}, f32[9,56,128]{2,1,0:T(8,128)}, u32[]{:S(2)}) %copy-start.1) | copy-done | bytes 258072
  7.8 0.6 %copy-done.3 = f32[4,21,56]{2,0,1:T(4,128)S(1)} copy-done((f32[4,21,56]{2,0,1:T(4,128)S(1)}, f32[4,21,56]{2,0,1:T(4,128)}, u32[]{:S(2)}) %copy-start.3) | copy-done | bytes 18840
  9.0 0.6 %copy-done.12 = s32[8]{0:T(128)S(1)} copy-done((s32[8]{0:T(128)S(1)}, s32[8]{0:T(128)}, u32[]{:S(2)}) %copy-start.12) | copy-done | bytes 56
  10.8 2.1 %collective-permute-start = (f32[72,189]{1,0:T(8,128)S(1)}, f32[72,189]{1,0:T(8,128)S(1)}, u32[]{:S(2)}, u32[]{:S(2)}) collective-permute-start(f32[72,189]{1,0:T(8,128)S(1)} %get-tuple-element.104), channel_id=1, source_target_pairs={{1,0},{2,1},{3,2},{5,4},{6,5},{7,6},{9,8},{10,9},{11,10},{13,12},{... | collective-permute-start | bytes 163304 | tf_op jit(solution)/shard_map/ppermute | solution.py:45
  12.9 2.4 %collective-permute-start.1 = (f32[72,189]{1,0:T(8,128)S(1)}, f32[72,189]{1,0:T(8,128)S(1)}, u32[]{:S(2)}, u32[]{:S(2)}) collective-permute-start(f32[72,189]{1,0:T(8,128)S(1)} %get-tuple-element.103), channel_id=1, source_target_pairs={{0,1},{1,2},{2,3},{4,5},{5,6},{6,7},{8,9},{9,10},{10,11},{12,13},{... | collective-permute-start | bytes 163304 | tf_op jit(solution)/shard_map/ppermute | solution.py:45
  15.5 3.0 %collective-permute-done.1 = f32[72,189]{1,0:T(8,128)S(1)} collective-permute-done((f32[72,189]{1,0:T(8,128)S(1)}, f32[72,189]{1,0:T(8,128)S(1)}, u32[]{:S(2)}, u32[]{:S(2)}) %collective-permute-start.1) | collective-permute-done | bytes 54464 | tf_op jit(solution)/shard_map/ppermute | solution.py:45
  19.3 3.5 %collective-permute-start.3 = (f32[72,189]{1,0:T(8,128)S(1)}, f32[72,189]{1,0:T(8,128)S(1)}, u32[]{:S(2)}, u32[]{:S(2)}) collective-permute-start(f32[72,189]{1,0:T(8,128)S(1)} %pad_maximum_fusion.1), channel_id=1, source_target_pairs={{0,4},{4,8},{8,12},{12,16},{16,20},{20,24},{24,28},{1,5},{5,9},{9,... | collective-permute-start | bytes 163304 | tf_op jit(solution)/shard_map/ppermute | solution.py:45
  22.8 2.6 %collective-permute-start.2 = (f32[72,189]{1,0:T(8,128)S(1)}, f32[72,189]{1,0:T(8,128)S(1)}, u32[]{:S(2)}, u32[]{:S(2)}) collective-permute-start(f32[72,189]{1,0:T(8,128)S(1)} %pad_maximum_fusion), channel_id=1, source_target_pairs={{4,0},{8,4},{12,8},{16,12},{20,16},{24,20},{28,24},{5,1},{9,5},{13... | collective-permute-start | bytes 163304 | tf_op jit(solution)/shard_map/ppermute | solution.py:45
  25.4 0.6 %fusion.7 = f32[189,512]{1,0:T(8,128)S(1)} fusion(f32[189,512]{1,0:T(8,128)S(1)} %bitcast.273, s32[512]{0:T(512)S(1)} %add_bitcast_fusion, pred[512]{0:T(512)(128)(4,1)S(1)} %get-tuple-element.90), kind=kOutput, calls=%fused_computation.25 | convolution fusion | flops 595066880 | bytes 776704 | tf_op jit(solution)/shard_map/dot_general | solution.py:189
  26.1 3.9 %collective-permute-done.2 = f32[72,189]{1,0:T(8,128)S(1)} collective-permute-done((f32[72,189]{1,0:T(8,128)S(1)}, f32[72,189]{1,0:T(8,128)S(1)}, u32[]{:S(2)}, u32[]{:S(2)}) %collective-permute-start.2) | collective-permute-done | bytes 54464 | tf_op jit(solution)/shard_map/ppermute | solution.py:45
  30.7 0.7 %fusion.2 = f32[9,21,4,128]{3,1,2,0:T(8,128)S(1)} fusion(f32[3,4,128]{2,0,1:T(4,128)S(1)} %fusion.185, f32[9,21,4,128,1]{3,2,1,0,4:T(4,128)S(1)} %bitcast.277, f32[3,21,21]{2,1,0:T(8,128)S(1)} %neg.68), kind=kOutput, calls=%fused_computation.4 | convolution fusion | flops 37062144 | bytes 785580 | tf_op jit(solution)/shard_map/hil,qlfe->hqife/dot_general | solution.py:103
  36.8 1.9 %collective-permute-start.4 = (f32[72,189]{1,0:T(8,128)S(1)}, f32[72,189]{1,0:T(8,128)S(1)}, u32[]{:S(2)}, u32[]{:S(2)}) collective-permute-start(f32[72,189]{1,0:T(8,128)S(1)} %get-tuple-element.100), channel_id=1, source_target_pairs={{1,0},{2,1},{3,2},{5,4},{6,5},{7,6},{9,8},{10,9},{11,10},{13,12},{... | collective-permute-start | bytes 163304 | tf_op jit(solution)/shard_map/ppermute | solution.py:45
  38.7 2.4 %collective-permute-start.5 = (f32[72,189]{1,0:T(8,128)S(1)}, f32[72,189]{1,0:T(8,128)S(1)}, u32[]{:S(2)}, u32[]{:S(2)}) collective-permute-start(f32[72,189]{1,0:T(8,128)S(1)} %get-tuple-element.99), channel_id=1, source_target_pairs={{0,1},{1,2},{2,3},{4,5},{5,6},{6,7},{8,9},{9,10},{10,11},{12,13},{... | collective-permute-start | bytes 163304 | tf_op jit(solution)/shard_map/ppermute | solution.py:45
  41.2 3.2 %collective-permute-done.5 = f32[72,189]{1,0:T(8,128)S(1)} collective-permute-done((f32[72,189]{1,0:T(8,128)S(1)}, f32[72,189]{1,0:T(8,128)S(1)}, u32[]{:S(2)}, u32[]{:S(2)}) %collective-permute-start.5) | collective-permute-done | bytes 54464 | tf_op jit(solution)/shard_map/ppermute | solution.py:45
  45.1 2.5 %collective-permute-start.7 = (f32[72,189]{1,0:T(8,128)S(1)}, f32[72,189]{1,0:T(8,128)S(1)}, u32[]{:S(2)}, u32[]{:S(2)}) collective-permute-start(f32[72,189]{1,0:T(8,128)S(1)} %pad_maximum_fusion.3), channel_id=1, source_target_pairs={{0,4},{4,8},{8,12},{12,16},{16,20},{20,24},{24,28},{1,5},{5,9},{9,... | collective-permute-start | bytes 163304 | tf_op jit(solution)/shard_map/ppermute | solution.py:45
  47.6 0.6 %fusion.5 = f32[189,512]{1,0:T(8,128)S(1)} fusion(f32[189,512]{1,0:T(8,128)S(1)} %bitcast.275, s32[512]{0:T(512)S(1)} %add_bitcast_fusion, pred[512]{0:T(512)(128)(4,1)S(1)} %get-tuple-element.90), kind=kOutput, calls=%fused_computation.24 | convolution fusion | flops 595066880 | bytes 776704 | tf_op jit(solution)/shard_map/dot_general | solution.py:189
  48.3 3.4 %collective-permute-start.6 = (f32[72,189]{1,0:T(8,128)S(1)}, f32[72,189]{1,0:T(8,128)S(1)}, u32[]{:S(2)}, u32[]{:S(2)}) collective-permute-start(f32[72,189]{1,0:T(8,128)S(1)} %pad_maximum_fusion.2), channel_id=1, source_target_pairs={{4,0},{8,4},{12,8},{16,12},{20,16},{24,20},{28,24},{5,1},{9,5},{13... | collective-permute-start | bytes 163304 | tf_op jit(solution)/shard_map/ppermute | solution.py:45
  51.7 3.8 %collective-permute-done.6 = f32[72,189]{1,0:T(8,128)S(1)} collective-permute-done((f32[72,189]{1,0:T(8,128)S(1)}, f32[72,189]{1,0:T(8,128)S(1)}, u32[]{:S(2)}, u32[]{:S(2)}) %collective-permute-start.6) | collective-permute-done | bytes 54464 | tf_op jit(solution)/shard_map/ppermute | solution.py:45
  56.1 0.7 %fusion.3 = f32[9,21,4,128]{3,1,2,0:T(8,128)S(1)} fusion(f32[3,4,128]{2,0,1:T(4,128)S(1)} %fusion.185, f32[9,21,4,128,1]{3,2,1,0,4:T(4,128)S(1)} %bitcast.276, f32[3,21,21]{2,1,0:T(8,128)S(1)} %neg.68), kind=kOutput, calls=%fused_computation.5 | convolution fusion | flops 37062144 | bytes 785580 | tf_op jit(solution)/shard_map/hil,qlfe->hqife/dot_general | solution.py:103
  57.2 1.0 %add_subtract_fusion = f32[9,56,128]{2,1,0:T(8,128)} fusion(f32[9,56,128]{2,1,0:T(8,128)S(1)} %add_subtract_fusion.1, f32[9,56,128]{2,1,0:T(8,128)S(1)} %constant_dynamic-update-slice_fusion.108, f32[9,21,4,128]{3,1,2,0:T(8,128)S(1)} %constant_dynamic-update-slice_fusion.117, f32[9,21,4,128]{3,1,2,0:T(8,128)S(1)} %convolution_bitcast_fusion.14, ...), kind=kOutput, calls=%fused_computation.220 | convolution fusion | flops 32933376 | bytes 1956224 | tf_op jit(solution)/shard_map/fai,pife->pae/dot_general | solution.py:114
  (213 shorter events, 12.7 us)
Async XLA Ops:
  0.0 2.3 %copy-start = (f32[3,56,56]{2,1,0:T(8,128)S(1)}, f32[3,56,56]{2,1,0:T(8,128)}, u32[]{:S(2)}) copy-start(f32[3,56,56]{2,1,0:T(8,128)} %param.17) | copy-start | bytes 112900
  6.7 1.0 %copy-start.1 = (f32[9,56,128]{2,1,0:T(8,128)S(1)}, f32[9,56,128]{2,1,0:T(8,128)}, u32[]{:S(2)}) copy-start(f32[9,56,128]{2,1,0:T(8,128)} %param.16) | copy-start | bytes 774148
  7.7 0.8 %copy-start.3 = (f32[4,21,56]{2,0,1:T(4,128)S(1)}, f32[4,21,56]{2,0,1:T(4,128)}, u32[]{:S(2)}) copy-start(f32[4,21,56]{2,0,1:T(4,128)} %param.19) | copy-start | bytes 56452
  9.0 0.7 %copy-start.12 = (s32[8]{0:T(128)S(1)}, s32[8]{0:T(128)}, u32[]{:S(2)}) copy-start(s32[8]{0:T(128)} %constant.31) | copy-start | bytes 100
  9.0 0.8 %copy-start.8 = (s32[1,1,8,24]{3,2,1,0:T(8,128)S(1)}, s32[1,1,8,24]{3,2,1,0:T(8,128)}, u32[]{:S(2)}) copy-start(s32[1,1,8,24]{3,2,1,0:T(8,128)} %param.29) | copy-start | bytes 2308
  10.2 5.1 %copy-start.6 = (f32[4,3,128]{2,0,1:T(4,128)S(1)}, f32[4,3,128]{2,0,1:T(4,128)}, u32[]{:S(2)}) copy-start(f32[4,3,128]{2,0,1:T(4,128)} %param.25) | copy-start | bytes 18436
  10.2 5.1 %copy-start.10 = (s32[4,128]{1,0:T(4,128)S(1)}, s32[4,128]{1,0:T(4,128)}, u32[]{:S(2)}) copy-start(s32[4,128]{1,0:T(4,128)} %param.26) | copy-start | bytes 6148
  10.2 5.1 %copy-start.7 = (s32[4,128]{1,0:T(4,128)S(1)}, s32[4,128]{1,0:T(4,128)}, u32[]{:S(2)}) copy-start(s32[4,128]{1,0:T(4,128)} %param.27) | copy-start | bytes 6148
  10.2 5.1 %copy-start.11 = (s32[4,128]{1,0:T(4,128)S(1)}, s32[4,128]{1,0:T(4,128)}, u32[]{:S(2)}) copy-start(s32[4,128]{1,0:T(4,128)} %param.28) | copy-start | bytes 6148
  10.8 4.7 %copy-start.9 = (s32[1,1,8,24]{3,2,1,0:T(8,128)S(1)}, s32[1,1,8,24]{3,2,1,0:T(8,128)}, u32[]{:S(2)}) copy-start(s32[1,1,8,24]{3,2,1,0:T(8,128)} %param.30) | copy-start | bytes 2308
  10.8 7.8 %copy-start.2 = (f32[3,56,56]{2,1,0:T(8,128)S(1)}, f32[3,56,56]{2,1,0:T(8,128)}, u32[]{:S(2)}) copy-start(f32[3,56,56]{2,1,0:T(8,128)} %param.18) | copy-start | bytes 112900
  10.8 4.7 %collective-permute-start = (f32[72,189]{1,0:T(8,128)S(1)}, f32[72,189]{1,0:T(8,128)S(1)}, u32[]{:S(2)}, u32[]{:S(2)}) collective-permute-start(f32[72,189]{1,0:T(8,128)S(1)} %get-tuple-element.104), channel_id=1, source_target_pairs={{1,0},{2,1},{3,2},{5,4},{6,5},{7,6},{9,8},{10,9},{11,10},{13,12},{... | collective-permute-start | bytes 163304 | tf_op jit(solution)/shard_map/ppermute | solution.py:45
  12.9 5.7 %collective-permute-start.1 = (f32[72,189]{1,0:T(8,128)S(1)}, f32[72,189]{1,0:T(8,128)S(1)}, u32[]{:S(2)}, u32[]{:S(2)}) collective-permute-start(f32[72,189]{1,0:T(8,128)S(1)} %get-tuple-element.103), channel_id=1, source_target_pairs={{0,1},{1,2},{2,3},{4,5},{5,6},{6,7},{8,9},{9,10},{10,11},{12,13},{... | collective-permute-start | bytes 163304 | tf_op jit(solution)/shard_map/ppermute | solution.py:45
  19.3 6.8 %collective-permute-start.3 = (f32[72,189]{1,0:T(8,128)S(1)}, f32[72,189]{1,0:T(8,128)S(1)}, u32[]{:S(2)}, u32[]{:S(2)}) collective-permute-start(f32[72,189]{1,0:T(8,128)S(1)} %pad_maximum_fusion.1), channel_id=1, source_target_pairs={{0,4},{4,8},{8,12},{12,16},{16,20},{20,24},{24,28},{1,5},{5,9},{9,... | collective-permute-start | bytes 163304 | tf_op jit(solution)/shard_map/ppermute | solution.py:45
  22.8 3.2 %copy-start.4 = (f32[4,56,21]{1,0,2:T(4,128)S(1)}, f32[4,56,21]{1,0,2:T(4,128)}, u32[]{:S(2)}) copy-start(f32[4,56,21]{1,0,2:T(4,128)} %param.20) | copy-start | bytes 56452
  22.8 3.2 %copy-start.5 = (f32[3,21,21]{2,1,0:T(8,128)S(1)}, f32[3,21,21]{2,1,0:T(8,128)}, u32[]{:S(2)}) copy-start(f32[3,21,21]{2,1,0:T(8,128)} %param.21) | copy-start | bytes 15880
  22.8 7.1 %collective-permute-start.2 = (f32[72,189]{1,0:T(8,128)S(1)}, f32[72,189]{1,0:T(8,128)S(1)}, u32[]{:S(2)}, u32[]{:S(2)}) collective-permute-start(f32[72,189]{1,0:T(8,128)S(1)} %pad_maximum_fusion), channel_id=1, source_target_pairs={{4,0},{8,4},{12,8},{16,12},{20,16},{24,20},{28,24},{5,1},{9,5},{13... | collective-permute-start | bytes 163304 | tf_op jit(solution)/shard_map/ppermute | solution.py:45
  36.8 4.4 %collective-permute-start.4 = (f32[72,189]{1,0:T(8,128)S(1)}, f32[72,189]{1,0:T(8,128)S(1)}, u32[]{:S(2)}, u32[]{:S(2)}) collective-permute-start(f32[72,189]{1,0:T(8,128)S(1)} %get-tuple-element.100), channel_id=1, source_target_pairs={{1,0},{2,1},{3,2},{5,4},{6,5},{7,6},{9,8},{10,9},{11,10},{13,12},{... | collective-permute-start | bytes 163304 | tf_op jit(solution)/shard_map/ppermute | solution.py:45
  38.7 5.7 %collective-permute-start.5 = (f32[72,189]{1,0:T(8,128)S(1)}, f32[72,189]{1,0:T(8,128)S(1)}, u32[]{:S(2)}, u32[]{:S(2)}) collective-permute-start(f32[72,189]{1,0:T(8,128)S(1)} %get-tuple-element.99), channel_id=1, source_target_pairs={{0,1},{1,2},{2,3},{4,5},{5,6},{6,7},{8,9},{9,10},{10,11},{12,13},{... | collective-permute-start | bytes 163304 | tf_op jit(solution)/shard_map/ppermute | solution.py:45
  45.1 6.5 %collective-permute-start.7 = (f32[72,189]{1,0:T(8,128)S(1)}, f32[72,189]{1,0:T(8,128)S(1)}, u32[]{:S(2)}, u32[]{:S(2)}) collective-permute-start(f32[72,189]{1,0:T(8,128)S(1)} %pad_maximum_fusion.3), channel_id=1, source_target_pairs={{0,4},{4,8},{8,12},{12,16},{16,20},{20,24},{24,28},{1,5},{5,9},{9,... | collective-permute-start | bytes 163304 | tf_op jit(solution)/shard_map/ppermute | solution.py:45
  48.3 7.1 %collective-permute-start.6 = (f32[72,189]{1,0:T(8,128)S(1)}, f32[72,189]{1,0:T(8,128)S(1)}, u32[]{:S(2)}, u32[]{:S(2)}) collective-permute-start(f32[72,189]{1,0:T(8,128)S(1)} %pad_maximum_fusion.2), channel_id=1, source_target_pairs={{4,0},{8,4},{12,8},{16,12},{20,16},{24,20},{28,24},{5,1},{9,5},{13... | collective-permute-start | bytes 163304 | tf_op jit(solution)/shard_map/ppermute | solution.py:45

commit v14 on v11

--- a/solution.py
+++ b/solution.py
@@ -177,7 +177,7 @@
         )
         flat_faces = face_data.reshape(9 * face_width, face_total)
         outgoing = lax.dot_general(
-            gather_out, flat_faces, (((1,), (1,)), ((), ())), precision=exact_mode
+            gather_out, flat_faces, (((1,), (1,)), ((), ())), precision=fast_mode
         )
 
         def local_work(integrated, flat_faces, rotate_negated, half_lift):
@@ -193,7 +193,7 @@
             outgoing, slot_total, (integrated, flat_faces, rotate_negated, half_lift), local_work
         )
         neighbour_data = local_data + lax.dot_general(
-            received, scatter_in, (((0,), (0,)), ((), ())), precision=exact_mode
+            received, scatter_in, (((0,), (0,)), ((), ())), precision=fast_mode
         )
         neighbour_data = neighbour_data.reshape(9, face_width, 4, elem_count)
         current = face_update(

time: 56.3 us -> 56.1 us (level)
  no operation moved by 1% of the time
where the time goes in v14:
time: 56.1 us; the launch traced here: 55.4 us
  starting transfers between devices  21.7 us (39%)
  matrix products  13.6 us (24%)
  waiting for transfers between devices  10.5 us (19%)
  local copies, waits for them, and re-layouts  4.33 us (8%)
  other arithmetic  3.82 us (7%)
  between operations  1.39 us (2%)
    ppermute x8, starting transfers between devices, shifted(): return lax.ppermute(x, axis, pairs)  21.7 us
    ppermute x8, waiting for transfers between devices, shifted(): return lax.ppermute(x, axis, pairs)  10.5 us
    dot_general x10, matrix products, predict(): jnp.einsum('dab,qbe->dqae', grad_matrix, derivative, precision=fast_mode)  6.46 us
    unnamed x28, local copies, waits for them, and re-layouts  1.81 us
    dot_general x2, matrix products, face_update(): jnp.einsum('fai,pife->pae', half_lift, flux_total, precision=fast_mode)  1.39 us
    dot_general x2, matrix products, face_update(): jnp.einsum('hil,qlfe->hqife', rotate_negated, neighbour_data, precision=f...  1.36 us
    unnamed x112, other arithmetic  1.34 us
    dot_general x2, matrix products, local_work(): local_data = jnp.dot(flat_faces, gather_local, precision=exact_mode)  1.22 us
  transfers between devices with their start and end apart: 8, of which 4 were waited for; matrix products, arithmetic and copies ran while one was open for 5% of the time, Pallas kernels for 0%

profile of v14, /device:TPU:25, one launch (start us, length us, event | category | flops | bytes accessed | tf_op | source)
XLA Modules:
  0.0 55.4 jit_solution(16047677776256874047)
XLA Ops:
  0.0 0.7 %iota_compare_fusion.6 = pred[16,128]{1,0:T(8,128)(4,1)S(1)} fusion(s32[128]{0:T(128)} %param.22), kind=kLoop, calls=%fused_computation.542 | loop fusion | flops 2048 | bytes 2560 | tf_op jit(solution)/shard_map/eq | solution.py:50
  0.7 0.8 %select_reduce_fusion = f32[3,128]{1,0:T(4,128)S(1)} fusion(f32[16,3]{0,1:T(4,128)} %param.21, pred[16,128]{1,0:T(8,128)(4,1)S(1)} %iota_compare_fusion.6), kind=kLoop, calls=%fused_computation.539 | loop fusion | flops 11904 | bytes 3776 | tf_op jit(solution)/shard_map/reduce_sum | solution.py:51
  1.5 1.0 %slice_bitcast_fusion.3 = (s32[1,24]{1,0:T(1,128)S(1)}, s32[1,24]{1,0:T(1,128)S(1)}, s32[1,24]{1,0:T(1,128)S(1)}, s32[1,24]{1,0:T(1,128)S(1)}, s32[1,24]{1,0:T(1...) fusion(s32[1,1,8,24]{3,2,1,0:T(8,128)} %param.28), kind=kLoop, calls=%fused_computation.560 | loop fusion | bytes 1536 | tf_op jit(solution)/shard_map/squeeze | solution.py:167
  2.6 0.8 %fusion.198 = (f32[3,1,128]{2,1,0:T(1,128)S(1)}, f32[3,1,128]{2,1,0:T(1,128)S(1)}, f32[3,1,128]{2,1,0:T(1,128)S(1)}) fusion(f32[3,3,128]{2,1,0:T(4,128)} %param.23), kind=kLoop, calls=%fused_computation.579 | loop fusion | bytes 9216 | tf_op jit(solution)/shard_map/slice | solution.py:69
  3.4 1.6 %multiply_reduce_fusion.33 = (f32[9,56,128]{2,1,0:T(8,128)S(1)}, f32[9,56,128]{2,1,0:T(8,128)S(1)}, f32[9,56,128]{2,1,0:T(8,128)S(1)}) fusion(f32[3,128]{1,0:T(4,128)S(1)} %get-tuple-element.136, f32[3,128]{1,0:T(4,128)S(1)} %get-tuple-element.137, f32[3,128]{1,0:T(4,128)S(1)} %bitcast.294, f32[3,56,56]{2,1,0:T(8,128)S(1)} %copy-done, f32[9,56,128]{2,1,0:T(8,128)} %param.15), kind=kOutput, calls=%fused_computation.59 | convolution fusion | flops 65995776 | bytes 1074432 | tf_op jit(solution)/shard_map/dab,qbe->dqae/dot_general | solution.py:78
  8.0 0.8 %copy-done.1 = f32[9,56,128]{2,1,0:T(8,128)S(1)} copy-done((f32[9,56,128]{2,1,0:T(8,128)S(1)}, f32[9,56,128]{2,1,0:T(8,128)}, u32[]{:S(2)}) %copy-start.1) | copy-done | bytes 258072
  9.0 0.6 %copy-done.3 = f32[4,21,56]{2,0,1:T(4,128)S(1)} copy-done((f32[4,21,56]{2,0,1:T(4,128)S(1)}, f32[4,21,56]{2,0,1:T(4,128)}, u32[]{:S(2)}) %copy-start.3) | copy-done | bytes 18840
  10.6 3.8 %collective-permute-start.1 = (f32[72,189]{1,0:T(8,128)S(1)}, f32[72,189]{1,0:T(8,128)S(1)}, u32[]{:S(2)}, u32[]{:S(2)}) collective-permute-start(f32[72,189]{1,0:T(8,128)S(1)} %get-tuple-element.103), channel_id=1, source_target_pairs={{0,1},{1,2},{2,3},{4,5},{5,6},{6,7},{8,9},{9,10},{10,11},{12,13},{... | collective-permute-start | bytes 163304 | tf_op jit(solution)/shard_map/ppermute | solution.py:45
  14.4 1.9 %collective-permute-start = (f32[72,189]{1,0:T(8,128)S(1)}, f32[72,189]{1,0:T(8,128)S(1)}, u32[]{:S(2)}, u32[]{:S(2)}) collective-permute-start(f32[72,189]{1,0:T(8,128)S(1)} %get-tuple-element.104), channel_id=1, source_target_pairs={{1,0},{2,1},{3,2},{5,4},{6,5},{7,6},{9,8},{10,9},{11,10},{13,12},{... | collective-permute-start | bytes 163304 | tf_op jit(solution)/shard_map/ppermute | solution.py:45
  16.6 3.5 %collective-permute-done = f32[72,189]{1,0:T(8,128)S(1)} collective-permute-done((f32[72,189]{1,0:T(8,128)S(1)}, f32[72,189]{1,0:T(8,128)S(1)}, u32[]{:S(2)}, u32[]{:S(2)}) %collective-permute-start) | collective-permute-done | bytes 54464 | tf_op jit(solution)/shard_map/ppermute | solution.py:45
  20.1 3.0 %collective-permute-start.2 = (f32[72,189]{1,0:T(8,128)S(1)}, f32[72,189]{1,0:T(8,128)S(1)}, u32[]{:S(2)}, u32[]{:S(2)}) collective-permute-start(f32[72,189]{1,0:T(8,128)S(1)} %pad_maximum_fusion), channel_id=1, source_target_pairs={{4,0},{8,4},{12,8},{16,12},{20,16},{24,20},{28,24},{5,1},{9,5},{13... | collective-permute-start | bytes 163304 | tf_op jit(solution)/shard_map/ppermute | solution.py:45
  23.1 2.3 %collective-permute-start.3 = (f32[72,189]{1,0:T(8,128)S(1)}, f32[72,189]{1,0:T(8,128)S(1)}, u32[]{:S(2)}, u32[]{:S(2)}) collective-permute-start(f32[72,189]{1,0:T(8,128)S(1)} %pad_maximum_fusion.1), channel_id=1, source_target_pairs={{0,4},{4,8},{8,12},{12,16},{16,20},{20,24},{24,28},{1,5},{5,9},{9,... | collective-permute-start | bytes 163304 | tf_op jit(solution)/shard_map/ppermute | solution.py:45
  26.2 0.6 %fusion.7 = f32[189,512]{1,0:T(8,128)S(1)} fusion(f32[189,512]{1,0:T(8,128)S(1)} %bitcast.285, s32[512]{0:T(512)S(1)} %add_bitcast_fusion, pred[512]{0:T(512)(128)(4,1)S(1)} %get-tuple-element.90), kind=kOutput, calls=%fused_computation.25 | convolution fusion | flops 595066880 | bytes 776704 | tf_op jit(solution)/shard_map/dot_general | solution.py:186
  27.0 2.2 %collective-permute-done.3 = f32[72,189]{1,0:T(8,128)S(1)} collective-permute-done((f32[72,189]{1,0:T(8,128)S(1)}, f32[72,189]{1,0:T(8,128)S(1)}, u32[]{:S(2)}, u32[]{:S(2)}) %collective-permute-start.3) | collective-permute-done | bytes 54464 | tf_op jit(solution)/shard_map/ppermute | solution.py:45
  29.8 0.7 %fusion.2 = f32[9,21,4,128]{3,1,2,0:T(8,128)S(1)} fusion(f32[3,4,128]{2,0,1:T(4,128)S(1)} %fusion.186, f32[9,21,4,128,1]{3,2,1,0,4:T(4,128)S(1)} %bitcast.289, f32[3,21,21]{2,1,0:T(8,128)S(1)} %neg.68), kind=kOutput, calls=%fused_computation.4 | convolution fusion | flops 37062144 | bytes 785580 | tf_op jit(solution)/shard_map/hil,qlfe->hqife/dot_general | solution.py:103
  35.8 3.3 %collective-permute-start.5 = (f32[72,189]{1,0:T(8,128)S(1)}, f32[72,189]{1,0:T(8,128)S(1)}, u32[]{:S(2)}, u32[]{:S(2)}) collective-permute-start(f32[72,189]{1,0:T(8,128)S(1)} %get-tuple-element.99), channel_id=1, source_target_pairs={{0,1},{1,2},{2,3},{4,5},{5,6},{6,7},{8,9},{9,10},{10,11},{12,13},{... | collective-permute-start | bytes 163304 | tf_op jit(solution)/shard_map/ppermute | solution.py:45
  39.0 1.9 %collective-permute-start.4 = (f32[72,189]{1,0:T(8,128)S(1)}, f32[72,189]{1,0:T(8,128)S(1)}, u32[]{:S(2)}, u32[]{:S(2)}) collective-permute-start(f32[72,189]{1,0:T(8,128)S(1)} %get-tuple-element.100), channel_id=1, source_target_pairs={{1,0},{2,1},{3,2},{5,4},{6,5},{7,6},{9,8},{10,9},{11,10},{13,12},{... | collective-permute-start | bytes 163304 | tf_op jit(solution)/shard_map/ppermute | solution.py:45
  41.0 3.7 %collective-permute-done.4 = f32[72,189]{1,0:T(8,128)S(1)} collective-permute-done((f32[72,189]{1,0:T(8,128)S(1)}, f32[72,189]{1,0:T(8,128)S(1)}, u32[]{:S(2)}, u32[]{:S(2)}) %collective-permute-start.4) | collective-permute-done | bytes 54464 | tf_op jit(solution)/shard_map/ppermute | solution.py:45
  44.7 1.9 %collective-permute-start.6 = (f32[72,189]{1,0:T(8,128)S(1)}, f32[72,189]{1,0:T(8,128)S(1)}, u32[]{:S(2)}, u32[]{:S(2)}) collective-permute-start(f32[72,189]{1,0:T(8,128)S(1)} %pad_maximum_fusion.2), channel_id=1, source_target_pairs={{4,0},{8,4},{12,8},{16,12},{20,16},{24,20},{28,24},{5,1},{9,5},{13... | collective-permute-start | bytes 163304 | tf_op jit(solution)/shard_map/ppermute | solution.py:45
  46.7 3.5 %collective-permute-start.7 = (f32[72,189]{1,0:T(8,128)S(1)}, f32[72,189]{1,0:T(8,128)S(1)}, u32[]{:S(2)}, u32[]{:S(2)}) collective-permute-start(f32[72,189]{1,0:T(8,128)S(1)} %pad_maximum_fusion.3), channel_id=1, source_target_pairs={{0,4},{4,8},{8,12},{12,16},{16,20},{20,24},{24,28},{1,5},{5,9},{9,... | collective-permute-start | bytes 163304 | tf_op jit(solution)/shard_map/ppermute | solution.py:45
  50.2 0.6 %fusion.5 = f32[189,512]{1,0:T(8,128)S(1)} fusion(f32[189,512]{1,0:T(8,128)S(1)} %bitcast.287, s32[512]{0:T(512)S(1)} %add_bitcast_fusion, pred[512]{0:T(512)(128)(4,1)S(1)} %get-tuple-element.90), kind=kOutput, calls=%fused_computation.24 | convolution fusion | flops 595066880 | bytes 776704 | tf_op jit(solution)/shard_map/dot_general | solution.py:186
  51.6 1.1 %collective-permute-done.7 = f32[72,189]{1,0:T(8,128)S(1)} collective-permute-done((f32[72,189]{1,0:T(8,128)S(1)}, f32[72,189]{1,0:T(8,128)S(1)}, u32[]{:S(2)}, u32[]{:S(2)}) %collective-permute-start.7) | collective-permute-done | bytes 54464 | tf_op jit(solution)/shard_map/ppermute | solution.py:45
  53.3 0.7 %fusion.3 = f32[9,21,4,128]{3,1,2,0:T(8,128)S(1)} fusion(f32[3,4,128]{2,0,1:T(4,128)S(1)} %fusion.186, f32[9,21,4,128,1]{3,2,1,0,4:T(4,128)S(1)} %bitcast.288, f32[3,21,21]{2,1,0:T(8,128)S(1)} %neg.68), kind=kOutput, calls=%fused_computation.5 | convolution fusion | flops 37062144 | bytes 785580 | tf_op jit(solution)/shard_map/hil,qlfe->hqife/dot_general | solution.py:103
  54.4 1.0 %add_subtract_fusion = f32[9,56,128]{2,1,0:T(8,128)} fusion(f32[9,56,128]{2,1,0:T(8,128)S(1)} %add_subtract_fusion.1, f32[9,56,128]{2,1,0:T(8,128)S(1)} %constant_dynamic-update-slice_fusion.108, f32[9,21,4,128]{3,1,2,0:T(8,128)S(1)} %constant_dynamic-update-slice_fusion.117, f32[9,21,4,128]{3,1,2,0:T(8,128)S(1)} %convolution_bitcast_fusion.14, ...), kind=kOutput, calls=%fused_computation.221 | convolution fusion | flops 32933376 | bytes 1956224 | tf_op jit(solution)/shard_map/fai,pife->pae/dot_general | solution.py:114
  (208 shorter events, 11.9 us)
Async XLA Ops:
  0.0 3.4 %copy-start = (f32[3,56,56]{2,1,0:T(8,128)S(1)}, f32[3,56,56]{2,1,0:T(8,128)}, u32[]{:S(2)}) copy-start(f32[3,56,56]{2,1,0:T(8,128)} %param.16) | copy-start | bytes 112900
  7.9 1.0 %copy-start.1 = (f32[9,56,128]{2,1,0:T(8,128)S(1)}, f32[9,56,128]{2,1,0:T(8,128)}, u32[]{:S(2)}) copy-start(f32[9,56,128]{2,1,0:T(8,128)} %param.15) | copy-start | bytes 774148
  8.8 0.8 %copy-start.3 = (f32[4,21,56]{2,0,1:T(4,128)S(1)}, f32[4,21,56]{2,0,1:T(4,128)}, u32[]{:S(2)}) copy-start(f32[4,21,56]{2,0,1:T(4,128)} %param.18) | copy-start | bytes 56452
  10.1 6.2 %copy-start.6 = (f32[4,3,128]{2,0,1:T(4,128)S(1)}, f32[4,3,128]{2,0,1:T(4,128)}, u32[]{:S(2)}) copy-start(f32[4,3,128]{2,0,1:T(4,128)} %param.24) | copy-start | bytes 18436
  10.2 6.2 %copy-start.9 = (s32[4,128]{1,0:T(4,128)S(1)}, s32[4,128]{1,0:T(4,128)}, u32[]{:S(2)}) copy-start(s32[4,128]{1,0:T(4,128)} %param.25) | copy-start | bytes 6148
  10.2 6.2 %copy-start.7 = (s32[4,128]{1,0:T(4,128)S(1)}, s32[4,128]{1,0:T(4,128)}, u32[]{:S(2)}) copy-start(s32[4,128]{1,0:T(4,128)} %param.26) | copy-start | bytes 6148
  10.2 6.2 %copy-start.10 = (s32[4,128]{1,0:T(4,128)S(1)}, s32[4,128]{1,0:T(4,128)}, u32[]{:S(2)}) copy-start(s32[4,128]{1,0:T(4,128)} %param.27) | copy-start | bytes 6148
  10.2 6.3 %copy-start.8 = (s32[1,1,8,24]{3,2,1,0:T(8,128)S(1)}, s32[1,1,8,24]{3,2,1,0:T(8,128)}, u32[]{:S(2)}) copy-start(s32[1,1,8,24]{3,2,1,0:T(8,128)} %param.29) | copy-start | bytes 2308
  10.5 14.9 %copy-start.2 = (f32[3,56,56]{2,1,0:T(8,128)S(1)}, f32[3,56,56]{2,1,0:T(8,128)}, u32[]{:S(2)}) copy-start(f32[3,56,56]{2,1,0:T(8,128)} %param.17) | copy-start | bytes 112900
  10.6 6.0 %collective-permute-start.1 = (f32[72,189]{1,0:T(8,128)S(1)}, f32[72,189]{1,0:T(8,128)S(1)}, u32[]{:S(2)}, u32[]{:S(2)}) collective-permute-start(f32[72,189]{1,0:T(8,128)S(1)} %get-tuple-element.103), channel_id=1, source_target_pairs={{0,1},{1,2},{2,3},{4,5},{5,6},{6,7},{8,9},{9,10},{10,11},{12,13},{... | collective-permute-start | bytes 163304 | tf_op jit(solution)/shard_map/ppermute | solution.py:45
  14.4 5.7 %collective-permute-start = (f32[72,189]{1,0:T(8,128)S(1)}, f32[72,189]{1,0:T(8,128)S(1)}, u32[]{:S(2)}, u32[]{:S(2)}) collective-permute-start(f32[72,189]{1,0:T(8,128)S(1)} %get-tuple-element.104), channel_id=1, source_target_pairs={{1,0},{2,1},{3,2},{5,4},{6,5},{7,6},{9,8},{10,9},{11,10},{13,12},{... | collective-permute-start | bytes 163304 | tf_op jit(solution)/shard_map/ppermute | solution.py:45
  20.1 6.8 %collective-permute-start.2 = (f32[72,189]{1,0:T(8,128)S(1)}, f32[72,189]{1,0:T(8,128)S(1)}, u32[]{:S(2)}, u32[]{:S(2)}) collective-permute-start(f32[72,189]{1,0:T(8,128)S(1)} %pad_maximum_fusion), channel_id=1, source_target_pairs={{4,0},{8,4},{12,8},{16,12},{20,16},{24,20},{28,24},{5,1},{9,5},{13... | collective-permute-start | bytes 163304 | tf_op jit(solution)/shard_map/ppermute | solution.py:45
  23.1 6.0 %collective-permute-start.3 = (f32[72,189]{1,0:T(8,128)S(1)}, f32[72,189]{1,0:T(8,128)S(1)}, u32[]{:S(2)}, u32[]{:S(2)}) collective-permute-start(f32[72,189]{1,0:T(8,128)S(1)} %pad_maximum_fusion.1), channel_id=1, source_target_pairs={{0,4},{4,8},{8,12},{12,16},{16,20},{20,24},{24,28},{1,5},{5,9},{9,... | collective-permute-start | bytes 163304 | tf_op jit(solution)/shard_map/ppermute | solution.py:45
  26.1 0.8 %copy-start.4 = (f32[4,56,21]{1,0,2:T(4,128)S(1)}, f32[4,56,21]{1,0,2:T(4,128)}, u32[]{:S(2)}) copy-start(f32[4,56,21]{1,0,2:T(4,128)} %param.19) | copy-start | bytes 56452
  26.2 0.8 %copy-start.5 = (f32[3,21,21]{2,1,0:T(8,128)S(1)}, f32[3,21,21]{2,1,0:T(8,128)}, u32[]{:S(2)}) copy-start(f32[3,21,21]{2,1,0:T(8,128)} %param.20) | copy-start | bytes 15880
  35.8 5.2 %collective-permute-start.5 = (f32[72,189]{1,0:T(8,128)S(1)}, f32[72,189]{1,0:T(8,128)S(1)}, u32[]{:S(2)}, u32[]{:S(2)}) collective-permute-start(f32[72,189]{1,0:T(8,128)S(1)} %get-tuple-element.99), channel_id=1, source_target_pairs={{0,1},{1,2},{2,3},{4,5},{5,6},{6,7},{8,9},{9,10},{10,11},{12,13},{... | collective-permute-start | bytes 163304 | tf_op jit(solution)/shard_map/ppermute | solution.py:45
  39.0 5.7 %collective-permute-start.4 = (f32[72,189]{1,0:T(8,128)S(1)}, f32[72,189]{1,0:T(8,128)S(1)}, u32[]{:S(2)}, u32[]{:S(2)}) collective-permute-start(f32[72,189]{1,0:T(8,128)S(1)} %get-tuple-element.100), channel_id=1, source_target_pairs={{1,0},{2,1},{3,2},{5,4},{6,5},{7,6},{9,8},{10,9},{11,10},{13,12},{... | collective-permute-start | bytes 163304 | tf_op jit(solution)/shard_map/ppermute | solution.py:45
  44.7 6.8 %collective-permute-start.6 = (f32[72,189]{1,0:T(8,128)S(1)}, f32[72,189]{1,0:T(8,128)S(1)}, u32[]{:S(2)}, u32[]{:S(2)}) collective-permute-start(f32[72,189]{1,0:T(8,128)S(1)} %pad_maximum_fusion.2), channel_id=1, source_target_pairs={{4,0},{8,4},{12,8},{16,12},{20,16},{24,20},{28,24},{5,1},{9,5},{13... | collective-permute-start | bytes 163304 | tf_op jit(solution)/shard_map/ppermute | solution.py:45
  46.7 6.0 %collective-permute-start.7 = (f32[72,189]{1,0:T(8,128)S(1)}, f32[72,189]{1,0:T(8,128)S(1)}, u32[]{:S(2)}, u32[]{:S(2)}) collective-permute-start(f32[72,189]{1,0:T(8,128)S(1)} %pad_maximum_fusion.3), channel_id=1, source_target_pairs={{0,4},{4,8},{8,12},{12,16},{16,20},{20,24},{24,28},{1,5},{5,9},{9,... | collective-permute-start | bytes 163304 | tf_op jit(solution)/shard_map/ppermute | solution.py:45

commit v15 on v14

--- a/solution.py
+++ b/solution.py
@@ -192,10 +192,13 @@
         received, (volume, local_data, rotate_negated, half_lift) = deliver(
             outgoing, slot_total, (integrated, flat_faces, rotate_negated, half_lift), local_work
         )
-        neighbour_data = local_data + lax.dot_general(
-            received, scatter_in, (((0,), (0,)), ((), ())), precision=fast_mode
-        )
-        neighbour_data = neighbour_data.reshape(9, face_width, 4, elem_count)
+        remote_data = jnp.einsum(
+            "sqi,sfe->qife",
+            received.reshape(-1, 9, face_width),
+            scatter_in.reshape(-1, 4, elem_count),
+            precision=fast_mode,
+        )
+        neighbour_data = local_data.reshape(9, face_width, 4, elem_count) + remote_data
         current = face_update(
             current,
             volume,

time: 56.1 us -> 56.2 us (level)
  no operation moved by 1% of the time
where the time goes in v15:
time: 56.2 us; the launch traced here: 55.6 us
  starting transfers between devices  21.7 us (39%)
  matrix products  13.6 us (24%)
  waiting for transfers between devices  10.5 us (19%)
  local copies, waits for them, and re-layouts  4.63 us (8%)
  other arithmetic  3.75 us (7%)
  between operations  1.38 us (2%)
    ppermute x8, starting transfers between devices, shifted(): return lax.ppermute(x, axis, pairs)  21.7 us
    ppermute x8, waiting for transfers between devices, shifted(): return lax.ppermute(x, axis, pairs)  10.5 us
    dot_general x10, matrix products, predict(): jnp.einsum('dab,qbe->dqae', grad_matrix, derivative, precision=fast_mode)  6.44 us
    unnamed x28, local copies, waits for them, and re-layouts  1.83 us
    dot_general x2, matrix products, face_update(): jnp.einsum('fai,pife->pae', half_lift, flux_total, precision=fast_mode)  1.4 us
    unnamed x112, other arithmetic  1.37 us
    dot_general x2, matrix products, face_update(): jnp.einsum('hil,qlfe->hqife', rotate_negated, neighbour_data, precision=f...  1.36 us
    dot_general x2, matrix products, local_work(): local_data = jnp.dot(flat_faces, gather_local, precision=exact_mode)  1.22 us
  transfers between devices with their start and end apart: 8, of which 4 were waited for; matrix products, arithmetic and copies ran while one was open for 5% of the time, Pallas kernels for 0%

profile of v15, /device:TPU:25, one launch (start us, length us, event | category | flops | bytes accessed | tf_op | source)
XLA Modules:
  0.0 55.6 jit_solution(3478130071281042148)
XLA Ops:
  0.0 0.7 %iota_compare_fusion.5 = pred[16,128]{1,0:T(8,128)(4,1)S(1)} fusion(s32[128]{0:T(128)} %param.22), kind=kLoop, calls=%fused_computation.537 | loop fusion | flops 2048 | bytes 2560 | tf_op jit(solution)/shard_map/eq | solution.py:50
  0.7 0.8 %select_reduce_fusion = f32[3,128]{1,0:T(4,128)S(1)} fusion(f32[16,3]{0,1:T(4,128)} %param.21, pred[16,128]{1,0:T(8,128)(4,1)S(1)} %iota_compare_fusion.5), kind=kLoop, calls=%fused_computation.534 | loop fusion | flops 11904 | bytes 3776 | tf_op jit(solution)/shard_map/reduce_sum | solution.py:51
  1.5 1.0 %slice_bitcast_fusion.3 = (s32[1,24]{1,0:T(1,128)S(1)}, s32[1,24]{1,0:T(1,128)S(1)}, s32[1,24]{1,0:T(1,128)S(1)}, s32[1,24]{1,0:T(1,128)S(1)}, s32[1,24]{1,0:T(1...) fusion(s32[1,1,8,24]{3,2,1,0:T(8,128)} %param.28), kind=kLoop, calls=%fused_computation.556 | loop fusion | bytes 1536 | tf_op jit(solution)/shard_map/squeeze | solution.py:167
  2.6 0.8 %fusion.185 = (f32[3,1,128]{2,1,0:T(1,128)S(1)}, f32[3,1,128]{2,1,0:T(1,128)S(1)}, f32[3,1,128]{2,1,0:T(1,128)S(1)}) fusion(f32[3,3,128]{2,1,0:T(4,128)} %param.23), kind=kLoop, calls=%fused_computation.573 | loop fusion | bytes 9216 | tf_op jit(solution)/shard_map/slice | solution.py:69
  3.4 1.6 %multiply_reduce_fusion.33 = (f32[9,56,128]{2,1,0:T(8,128)S(1)}, f32[9,56,128]{2,1,0:T(8,128)S(1)}, f32[9,56,128]{2,1,0:T(8,128)S(1)}) fusion(f32[3,128]{1,0:T(4,128)S(1)} %get-tuple-element.136, f32[3,128]{1,0:T(4,128)S(1)} %get-tuple-element.137, f32[3,128]{1,0:T(4,128)S(1)} %bitcast.313, f32[3,56,56]{2,1,0:T(8,128)S(1)} %copy-done, f32[9,56,128]{2,1,0:T(8,128)} %param.15), kind=kOutput, calls=%fused_computation.59 | convolution fusion | flops 65995776 | bytes 1074432 | tf_op jit(solution)/shard_map/dab,qbe->dqae/dot_general | solution.py:78
  8.0 0.8 %copy-done.1 = f32[9,56,128]{2,1,0:T(8,128)S(1)} copy-done((f32[9,56,128]{2,1,0:T(8,128)S(1)}, f32[9,56,128]{2,1,0:T(8,128)}, u32[]{:S(2)}) %copy-start.1) | copy-done | bytes 258072
  8.9 0.6 %copy-done.3 = f32[4,21,56]{2,0,1:T(4,128)S(1)} copy-done((f32[4,21,56]{2,0,1:T(4,128)S(1)}, f32[4,21,56]{2,0,1:T(4,128)}, u32[]{:S(2)}) %copy-start.3) | copy-done | bytes 18840
  10.6 3.8 %collective-permute-start.1 = (f32[72,189]{1,0:T(8,128)S(1)}, f32[72,189]{1,0:T(8,128)S(1)}, u32[]{:S(2)}, u32[]{:S(2)}) collective-permute-start(f32[72,189]{1,0:T(8,128)S(1)} %get-tuple-element.103), channel_id=1, source_target_pairs={{0,1},{1,2},{2,3},{4,5},{5,6},{6,7},{8,9},{9,10},{10,11},{12,13},{... | collective-permute-start | bytes 163304 | tf_op jit(solution)/shard_map/ppermute | solution.py:45
  14.4 1.9 %collective-permute-start = (f32[72,189]{1,0:T(8,128)S(1)}, f32[72,189]{1,0:T(8,128)S(1)}, u32[]{:S(2)}, u32[]{:S(2)}) collective-permute-start(f32[72,189]{1,0:T(8,128)S(1)} %get-tuple-element.104), channel_id=1, source_target_pairs={{1,0},{2,1},{3,2},{5,4},{6,5},{7,6},{9,8},{10,9},{11,10},{13,12},{... | collective-permute-start | bytes 163304 | tf_op jit(solution)/shard_map/ppermute | solution.py:45
  16.6 3.5 %collective-permute-done = f32[72,189]{1,0:T(8,128)S(1)} collective-permute-done((f32[72,189]{1,0:T(8,128)S(1)}, f32[72,189]{1,0:T(8,128)S(1)}, u32[]{:S(2)}, u32[]{:S(2)}) %collective-permute-start) | collective-permute-done | bytes 54464 | tf_op jit(solution)/shard_map/ppermute | solution.py:45
  20.1 3.0 %collective-permute-start.2 = (f32[72,189]{1,0:T(8,128)S(1)}, f32[72,189]{1,0:T(8,128)S(1)}, u32[]{:S(2)}, u32[]{:S(2)}) collective-permute-start(f32[72,189]{1,0:T(8,128)S(1)} %pad_maximum_fusion.2), channel_id=1, source_target_pairs={{4,0},{8,4},{12,8},{16,12},{20,16},{24,20},{28,24},{5,1},{9,5},{13... | collective-permute-start | bytes 163304 | tf_op jit(solution)/shard_map/ppermute | solution.py:45
  23.1 2.3 %collective-permute-start.3 = (f32[72,189]{1,0:T(8,128)S(1)}, f32[72,189]{1,0:T(8,128)S(1)}, u32[]{:S(2)}, u32[]{:S(2)}) collective-permute-start(f32[72,189]{1,0:T(8,128)S(1)} %pad_maximum_fusion.3), channel_id=1, source_target_pairs={{0,4},{4,8},{8,12},{12,16},{16,20},{20,24},{24,28},{1,5},{5,9},{9,... | collective-permute-start | bytes 163304 | tf_op jit(solution)/shard_map/ppermute | solution.py:45
  26.2 0.6 %fusion.7 = f32[189,512]{1,0:T(8,128)S(1)} fusion(f32[189,512]{1,0:T(8,128)S(1)} %bitcast.306, s32[512]{0:T(512)S(1)} %add_bitcast_fusion, pred[512]{0:T(512)(128)(4,1)S(1)} %bitcast.325), kind=kOutput, calls=%fused_computation.25 | convolution fusion | flops 595066880 | bytes 776704 | tf_op jit(solution)/shard_map/dot_general | solution.py:186
  27.0 2.2 %collective-permute-done.3 = f32[72,189]{1,0:T(8,128)S(1)} collective-permute-done((f32[72,189]{1,0:T(8,128)S(1)}, f32[72,189]{1,0:T(8,128)S(1)}, u32[]{:S(2)}, u32[]{:S(2)}) %collective-permute-start.3) | collective-permute-done | bytes 54464 | tf_op jit(solution)/shard_map/ppermute | solution.py:45
  29.9 0.7 %fusion.2 = f32[9,21,4,128]{3,1,2,0:T(8,128)S(1)} fusion(f32[3,4,128]{2,0,1:T(4,128)S(1)} %fusion.175, f32[9,21,4,128]{3,1,2,0:T(8,128)S(1)} %fusion.25, f32[9,21,4,128]{3,2,1,0:T(4,128)S(1)} %reshape.1870, f32[3,21,21]{2,1,0:T(8,128)S(1)} %neg.68), kind=kOutput, calls=%fused_computation.4 | convolution fusion | flops 37158912 | bytes 1172652 | tf_op jit(solution)/shard_map/hil,qlfe->hqife/dot_general | solution.py:103
  35.8 3.3 %collective-permute-start.5 = (f32[72,189]{1,0:T(8,128)S(1)}, f32[72,189]{1,0:T(8,128)S(1)}, u32[]{:S(2)}, u32[]{:S(2)}) collective-permute-start(f32[72,189]{1,0:T(8,128)S(1)} %get-tuple-element.99), channel_id=1, source_target_pairs={{0,1},{1,2},{2,3},{4,5},{5,6},{6,7},{8,9},{9,10},{10,11},{12,13},{... | collective-permute-start | bytes 163304 | tf_op jit(solution)/shard_map/ppermute | solution.py:45
  39.1 1.9 %collective-permute-start.4 = (f32[72,189]{1,0:T(8,128)S(1)}, f32[72,189]{1,0:T(8,128)S(1)}, u32[]{:S(2)}, u32[]{:S(2)}) collective-permute-start(f32[72,189]{1,0:T(8,128)S(1)} %get-tuple-element.100), channel_id=1, source_target_pairs={{1,0},{2,1},{3,2},{5,4},{6,5},{7,6},{9,8},{10,9},{11,10},{13,12},{... | collective-permute-start | bytes 163304 | tf_op jit(solution)/shard_map/ppermute | solution.py:45
  41.1 3.7 %collective-permute-done.4 = f32[72,189]{1,0:T(8,128)S(1)} collective-permute-done((f32[72,189]{1,0:T(8,128)S(1)}, f32[72,189]{1,0:T(8,128)S(1)}, u32[]{:S(2)}, u32[]{:S(2)}) %collective-permute-start.4) | collective-permute-done | bytes 54464 | tf_op jit(solution)/shard_map/ppermute | solution.py:45
  44.8 1.9 %collective-permute-start.6 = (f32[72,189]{1,0:T(8,128)S(1)}, f32[72,189]{1,0:T(8,128)S(1)}, u32[]{:S(2)}, u32[]{:S(2)}) collective-permute-start(f32[72,189]{1,0:T(8,128)S(1)} %pad_maximum_fusion.4), channel_id=1, source_target_pairs={{4,0},{8,4},{12,8},{16,12},{20,16},{24,20},{28,24},{5,1},{9,5},{13... | collective-permute-start | bytes 163304 | tf_op jit(solution)/shard_map/ppermute | solution.py:45
  46.8 3.5 %collective-permute-start.7 = (f32[72,189]{1,0:T(8,128)S(1)}, f32[72,189]{1,0:T(8,128)S(1)}, u32[]{:S(2)}, u32[]{:S(2)}) collective-permute-start(f32[72,189]{1,0:T(8,128)S(1)} %pad_maximum_fusion.5), channel_id=1, source_target_pairs={{0,4},{4,8},{8,12},{12,16},{16,20},{20,24},{24,28},{1,5},{5,9},{9,... | collective-permute-start | bytes 163304 | tf_op jit(solution)/shard_map/ppermute | solution.py:45
  50.3 0.6 %fusion.5 = f32[189,512]{1,0:T(8,128)S(1)} fusion(f32[189,512]{1,0:T(8,128)S(1)} %bitcast.308, s32[512]{0:T(512)S(1)} %add_bitcast_fusion, pred[512]{0:T(512)(128)(4,1)S(1)} %bitcast.326), kind=kOutput, calls=%fused_computation.24 | convolution fusion | flops 595066880 | bytes 776704 | tf_op jit(solution)/shard_map/dot_general | solution.py:186
  51.6 1.1 %collective-permute-done.7 = f32[72,189]{1,0:T(8,128)S(1)} collective-permute-done((f32[72,189]{1,0:T(8,128)S(1)}, f32[72,189]{1,0:T(8,128)S(1)}, u32[]{:S(2)}, u32[]{:S(2)}) %collective-permute-start.7) | collective-permute-done | bytes 54464 | tf_op jit(solution)/shard_map/ppermute | solution.py:45
  53.5 0.7 %fusion.3 = f32[9,21,4,128]{3,1,2,0:T(8,128)S(1)} fusion(f32[3,4,128]{2,0,1:T(4,128)S(1)} %fusion.175, f32[9,21,4,128]{3,1,2,0:T(8,128)S(1)} %fusion.23, f32[9,21,4,128]{3,2,1,0:T(4,128)S(1)} %reshape.1873, f32[3,21,21]{2,1,0:T(8,128)S(1)} %neg.68), kind=kOutput, calls=%fused_computation.5 | convolution fusion | flops 37158912 | bytes 1172652 | tf_op jit(solution)/shard_map/hil,qlfe->hqife/dot_general | solution.py:103
  54.5 1.0 %add_subtract_fusion = f32[9,56,128]{2,1,0:T(8,128)} fusion(f32[9,56,128]{2,1,0:T(8,128)S(1)} %add_subtract_fusion.1, f32[9,56,128]{2,1,0:T(8,128)S(1)} %constant_dynamic-update-slice_fusion.108, f32[9,21,4,128]{3,1,2,0:T(8,128)S(1)} %constant_dynamic-update-slice_fusion.117, f32[9,21,4,128]{3,1,2,0:T(8,128)S(1)} %convolution_bitcast_fusion.14, ...), kind=kOutput, calls=%fused_computation.224 | convolution fusion | flops 32933376 | bytes 1956224 | tf_op jit(solution)/shard_map/fai,pife->pae/dot_general | solution.py:114
  (213 shorter events, 12.0 us)
Async XLA Ops:
  0.0 3.4 %copy-start = (f32[3,56,56]{2,1,0:T(8,128)S(1)}, f32[3,56,56]{2,1,0:T(8,128)}, u32[]{:S(2)}) copy-start(f32[3,56,56]{2,1,0:T(8,128)} %param.16) | copy-start | bytes 112900
  7.8 1.0 %copy-start.1 = (f32[9,56,128]{2,1,0:T(8,128)S(1)}, f32[9,56,128]{2,1,0:T(8,128)}, u32[]{:S(2)}) copy-start(f32[9,56,128]{2,1,0:T(8,128)} %param.15) | copy-start | bytes 774148
  8.8 0.8 %copy-start.3 = (f32[4,21,56]{2,0,1:T(4,128)S(1)}, f32[4,21,56]{2,0,1:T(4,128)}, u32[]{:S(2)}) copy-start(f32[4,21,56]{2,0,1:T(4,128)} %param.18) | copy-start | bytes 56452
  10.1 6.2 %copy-start.6 = (f32[4,3,128]{2,0,1:T(4,128)S(1)}, f32[4,3,128]{2,0,1:T(4,128)}, u32[]{:S(2)}) copy-start(f32[4,3,128]{2,0,1:T(4,128)} %param.24) | copy-start | bytes 18436
  10.1 6.2 %copy-start.7 = (s32[4,128]{1,0:T(4,128)S(1)}, s32[4,128]{1,0:T(4,128)}, u32[]{:S(2)}) copy-start(s32[4,128]{1,0:T(4,128)} %param.26) | copy-start | bytes 6148
  10.2 6.3 %copy-start.9 = (s32[4,128]{1,0:T(4,128)S(1)}, s32[4,128]{1,0:T(4,128)}, u32[]{:S(2)}) copy-start(s32[4,128]{1,0:T(4,128)} %param.27) | copy-start | bytes 6148
  10.2 6.3 %copy-start.10 = (s32[4,128]{1,0:T(4,128)S(1)}, s32[4,128]{1,0:T(4,128)}, u32[]{:S(2)}) copy-start(s32[4,128]{1,0:T(4,128)} %param.25) | copy-start | bytes 6148
  10.2 6.3 %copy-start.8 = (s32[1,1,8,24]{3,2,1,0:T(8,128)S(1)}, s32[1,1,8,24]{3,2,1,0:T(8,128)}, u32[]{:S(2)}) copy-start(s32[1,1,8,24]{3,2,1,0:T(8,128)} %param.29) | copy-start | bytes 2308
  10.5 14.9 %copy-start.2 = (f32[3,56,56]{2,1,0:T(8,128)S(1)}, f32[3,56,56]{2,1,0:T(8,128)}, u32[]{:S(2)}) copy-start(f32[3,56,56]{2,1,0:T(8,128)} %param.17) | copy-start | bytes 112900
  10.6 6.0 %collective-permute-start.1 = (f32[72,189]{1,0:T(8,128)S(1)}, f32[72,189]{1,0:T(8,128)S(1)}, u32[]{:S(2)}, u32[]{:S(2)}) collective-permute-start(f32[72,189]{1,0:T(8,128)S(1)} %get-tuple-element.103), channel_id=1, source_target_pairs={{0,1},{1,2},{2,3},{4,5},{5,6},{6,7},{8,9},{9,10},{10,11},{12,13},{... | collective-permute-start | bytes 163304 | tf_op jit(solution)/shard_map/ppermute | solution.py:45
  14.4 5.7 %collective-permute-start = (f32[72,189]{1,0:T(8,128)S(1)}, f32[72,189]{1,0:T(8,128)S(1)}, u32[]{:S(2)}, u32[]{:S(2)}) collective-permute-start(f32[72,189]{1,0:T(8,128)S(1)} %get-tuple-element.104), channel_id=1, source_target_pairs={{1,0},{2,1},{3,2},{5,4},{6,5},{7,6},{9,8},{10,9},{11,10},{13,12},{... | collective-permute-start | bytes 163304 | tf_op jit(solution)/shard_map/ppermute | solution.py:45
  20.1 6.8 %collective-permute-start.2 = (f32[72,189]{1,0:T(8,128)S(1)}, f32[72,189]{1,0:T(8,128)S(1)}, u32[]{:S(2)}, u32[]{:S(2)}) collective-permute-start(f32[72,189]{1,0:T(8,128)S(1)} %pad_maximum_fusion.2), channel_id=1, source_target_pairs={{4,0},{8,4},{12,8},{16,12},{20,16},{24,20},{28,24},{5,1},{9,5},{13... | collective-permute-start | bytes 163304 | tf_op jit(solution)/shard_map/ppermute | solution.py:45
  23.1 6.0 %collective-permute-start.3 = (f32[72,189]{1,0:T(8,128)S(1)}, f32[72,189]{1,0:T(8,128)S(1)}, u32[]{:S(2)}, u32[]{:S(2)}) collective-permute-start(f32[72,189]{1,0:T(8,128)S(1)} %pad_maximum_fusion.3), channel_id=1, source_target_pairs={{0,4},{4,8},{8,12},{12,16},{16,20},{20,24},{24,28},{1,5},{5,9},{9,... | collective-permute-start | bytes 163304 | tf_op jit(solution)/shard_map/ppermute | solution.py:45
  26.1 0.8 %copy-start.4 = (f32[4,56,21]{1,0,2:T(4,128)S(1)}, f32[4,56,21]{1,0,2:T(4,128)}, u32[]{:S(2)}) copy-start(f32[4,56,21]{1,0,2:T(4,128)} %param.19) | copy-start | bytes 56452
  26.2 0.8 %copy-start.5 = (f32[3,21,21]{2,1,0:T(8,128)S(1)}, f32[3,21,21]{2,1,0:T(8,128)}, u32[]{:S(2)}) copy-start(f32[3,21,21]{2,1,0:T(8,128)} %param.20) | copy-start | bytes 15880
  35.8 5.2 %collective-permute-start.5 = (f32[72,189]{1,0:T(8,128)S(1)}, f32[72,189]{1,0:T(8,128)S(1)}, u32[]{:S(2)}, u32[]{:S(2)}) collective-permute-start(f32[72,189]{1,0:T(8,128)S(1)} %get-tuple-element.99), channel_id=1, source_target_pairs={{0,1},{1,2},{2,3},{4,5},{5,6},{6,7},{8,9},{9,10},{10,11},{12,13},{... | collective-permute-start | bytes 163304 | tf_op jit(solution)/shard_map/ppermute | solution.py:45
  39.1 5.7 %collective-permute-start.4 = (f32[72,189]{1,0:T(8,128)S(1)}, f32[72,189]{1,0:T(8,128)S(1)}, u32[]{:S(2)}, u32[]{:S(2)}) collective-permute-start(f32[72,189]{1,0:T(8,128)S(1)} %get-tuple-element.100), channel_id=1, source_target_pairs={{1,0},{2,1},{3,2},{5,4},{6,5},{7,6},{9,8},{10,9},{11,10},{13,12},{... | collective-permute-start | bytes 163304 | tf_op jit(solution)/shard_map/ppermute | solution.py:45
  44.8 6.8 %collective-permute-start.6 = (f32[72,189]{1,0:T(8,128)S(1)}, f32[72,189]{1,0:T(8,128)S(1)}, u32[]{:S(2)}, u32[]{:S(2)}) collective-permute-start(f32[72,189]{1,0:T(8,128)S(1)} %pad_maximum_fusion.4), channel_id=1, source_target_pairs={{4,0},{8,4},{12,8},{16,12},{20,16},{24,20},{28,24},{5,1},{9,5},{13... | collective-permute-start | bytes 163304 | tf_op jit(solution)/shard_map/ppermute | solution.py:45
  46.8 6.0 %collective-permute-start.7 = (f32[72,189]{1,0:T(8,128)S(1)}, f32[72,189]{1,0:T(8,128)S(1)}, u32[]{:S(2)}, u32[]{:S(2)}) collective-permute-start(f32[72,189]{1,0:T(8,128)S(1)} %pad_maximum_fusion.5), channel_id=1, source_target_pairs={{0,4},{4,8},{8,12},{12,16},{16,20},{20,24},{24,28},{1,5},{5,9},{9,... | collective-permute-start | bytes 163304 | tf_op jit(solution)/shard_map/ppermute | solution.py:45

commit v16 on v14

--- a/solution.py
+++ b/solution.py
@@ -47,8 +47,8 @@
 
 def element_params(material, material_id, normals):
     id_range = jnp.arange(material.shape[0], dtype=jnp.int32)
-    chosen = material_id[None, None, :] == id_range[:, None, None]
-    params = jnp.sum(jnp.where(chosen, material[:, :, None], 0.0), axis=0)
+    onehot = (material_id[None, :] == id_range[:, None]).astype(material.dtype)
+    params = jnp.dot(material.T, onehot, precision=fast_mode)
     density, lame_first, shear_modulus = (params[0], params[1], params[2])
     values = (-(lame_first + 2.0 * shear_modulus), -lame_first, -shear_modulus, -1.0 / density)
     wave_speed = jnp.sqrt((lame_first + 2.0 * shear_modulus) / density) * jnp.sum(

time: 56.1 us -> 55.4 us (0.988)
  other arithmetic: 3.82 us -> 2.36 us
  matrix products: 13.6 us -> 14.5 us
    dot_general x0 -> x1, matrix products: none -> 0.85 us  [element_params(): params = jnp.dot(material.T, onehot, precision=fast_mode)]
    reduce_sum x1 -> x0, other arithmetic: 0.77 us -> none  [element_params(): params = jnp.sum(jnp.where(chosen, material[:, :, None], 0.0), axis=0)]
    eq x1 -> x0, other arithmetic: 0.69 us -> none  [element_params(): chosen = material_id[None, None, :] == id_range[:, None, None]]
where the time goes in v16:
time: 55.4 us; the launch traced here: 54.8 us
  starting transfers between devices  21.7 us (39%)
  matrix products  14.5 us (26%)
  waiting for transfers between devices  10.5 us (19%)
  local copies, waits for them, and re-layouts  4.33 us (8%)
  other arithmetic  2.36 us (4%)
  between operations  1.39 us (3%)
    ppermute x8, starting transfers between devices, shifted(): return lax.ppermute(x, axis, pairs)  21.7 us
    ppermute x8, waiting for transfers between devices, shifted(): return lax.ppermute(x, axis, pairs)  10.5 us
    dot_general x10, matrix products, predict(): jnp.einsum('dab,qbe->dqae', grad_matrix, derivative, precision=fast_mode)  6.46 us
    unnamed x28, local copies, waits for them, and re-layouts  1.81 us
    dot_general x2, matrix products, face_update(): jnp.einsum('fai,pife->pae', half_lift, flux_total, precision=fast_mode)  1.39 us
    dot_general x2, matrix products, face_update(): jnp.einsum('hil,qlfe->hqife', rotate_negated, neighbour_data, precision=f...  1.36 us
    unnamed x112, other arithmetic  1.34 us
    dot_general x2, matrix products, local_work(): local_data = jnp.dot(flat_faces, gather_local, precision=exact_mode)  1.22 us
  transfers between devices with their start and end apart: 8, of which 4 were waited for; matrix products, arithmetic and copies ran while one was open for 5% of the time, Pallas kernels for 0%

profile of v16, /device:TPU:25, one launch (start us, length us, event | category | flops | bytes accessed | tf_op | source)
XLA Modules:
  0.0 54.8 jit_solution(10634549699344610368)
XLA Ops:
  0.0 0.9 %convolution_bitcast_fusion.18 = f32[3,128]{1,0:T(4,128)S(1)} fusion(f32[16,3]{0,1:T(4,128)} %param.21, s32[128]{0:T(128)} %param.22), kind=kOutput, calls=%fused_computation.22 | convolution fusion | flops 38912 | bytes 2240 | tf_op jit(solution)/shard_map/dot_general | solution.py:51
  0.9 1.0 %slice_bitcast_fusion.3 = (s32[1,24]{1,0:T(1,128)S(1)}, s32[1,24]{1,0:T(1,128)S(1)}, s32[1,24]{1,0:T(1,128)S(1)}, s32[1,24]{1,0:T(1,128)S(1)}, s32[1,24]{1,0:T(1...) fusion(s32[1,1,8,24]{3,2,1,0:T(8,128)} %param.28), kind=kLoop, calls=%fused_computation.561 | loop fusion | bytes 1536 | tf_op jit(solution)/shard_map/squeeze | solution.py:167
  2.0 0.8 %fusion.199 = (f32[3,1,128]{2,1,0:T(1,128)S(1)}, f32[3,1,128]{2,1,0:T(1,128)S(1)}, f32[3,1,128]{2,1,0:T(1,128)S(1)}) fusion(f32[3,3,128]{2,1,0:T(4,128)} %param.23), kind=kLoop, calls=%fused_computation.580 | loop fusion | bytes 9216 | tf_op jit(solution)/shard_map/slice | solution.py:69
  2.8 1.6 %multiply_reduce_fusion.33 = (f32[9,56,128]{2,1,0:T(8,128)S(1)}, f32[9,56,128]{2,1,0:T(8,128)S(1)}, f32[9,56,128]{2,1,0:T(8,128)S(1)}) fusion(f32[3,128]{1,0:T(4,128)S(1)} %get-tuple-element.136, f32[3,128]{1,0:T(4,128)S(1)} %get-tuple-element.137, f32[3,128]{1,0:T(4,128)S(1)} %bitcast.297, f32[3,56,56]{2,1,0:T(8,128)S(1)} %copy-done, f32[9,56,128]{2,1,0:T(8,128)} %param.15), kind=kOutput, calls=%fused_computation.60 | convolution fusion | flops 65995776 | bytes 1074432 | tf_op jit(solution)/shard_map/dab,qbe->dqae/dot_general | solution.py:78
  7.4 0.8 %copy-done.1 = f32[9,56,128]{2,1,0:T(8,128)S(1)} copy-done((f32[9,56,128]{2,1,0:T(8,128)S(1)}, f32[9,56,128]{2,1,0:T(8,128)}, u32[]{:S(2)}) %copy-start.1) | copy-done | bytes 258072
  8.4 0.6 %copy-done.3 = f32[4,21,56]{2,0,1:T(4,128)S(1)} copy-done((f32[4,21,56]{2,0,1:T(4,128)S(1)}, f32[4,21,56]{2,0,1:T(4,128)}, u32[]{:S(2)}) %copy-start.3) | copy-done | bytes 18840
  9.9 3.8 %collective-permute-start.1 = (f32[72,189]{1,0:T(8,128)S(1)}, f32[72,189]{1,0:T(8,128)S(1)}, u32[]{:S(2)}, u32[]{:S(2)}) collective-permute-start(f32[72,189]{1,0:T(8,128)S(1)} %get-tuple-element.103), channel_id=1, source_target_pairs={{0,1},{1,2},{2,3},{4,5},{5,6},{6,7},{8,9},{9,10},{10,11},{12,13},{... | collective-permute-start | bytes 163304 | tf_op jit(solution)/shard_map/ppermute | solution.py:45
  13.8 1.9 %collective-permute-start = (f32[72,189]{1,0:T(8,128)S(1)}, f32[72,189]{1,0:T(8,128)S(1)}, u32[]{:S(2)}, u32[]{:S(2)}) collective-permute-start(f32[72,189]{1,0:T(8,128)S(1)} %get-tuple-element.104), channel_id=1, source_target_pairs={{1,0},{2,1},{3,2},{5,4},{6,5},{7,6},{9,8},{10,9},{11,10},{13,12},{... | collective-permute-start | bytes 163304 | tf_op jit(solution)/shard_map/ppermute | solution.py:45
  15.9 3.5 %collective-permute-done = f32[72,189]{1,0:T(8,128)S(1)} collective-permute-done((f32[72,189]{1,0:T(8,128)S(1)}, f32[72,189]{1,0:T(8,128)S(1)}, u32[]{:S(2)}, u32[]{:S(2)}) %collective-permute-start) | collective-permute-done | bytes 54464 | tf_op jit(solution)/shard_map/ppermute | solution.py:45
  19.5 3.0 %collective-permute-start.2 = (f32[72,189]{1,0:T(8,128)S(1)}, f32[72,189]{1,0:T(8,128)S(1)}, u32[]{:S(2)}, u32[]{:S(2)}) collective-permute-start(f32[72,189]{1,0:T(8,128)S(1)} %pad_maximum_fusion), channel_id=1, source_target_pairs={{4,0},{8,4},{12,8},{16,12},{20,16},{24,20},{28,24},{5,1},{9,5},{13... | collective-permute-start | bytes 163304 | tf_op jit(solution)/shard_map/ppermute | solution.py:45
  22.5 2.3 %collective-permute-start.3 = (f32[72,189]{1,0:T(8,128)S(1)}, f32[72,189]{1,0:T(8,128)S(1)}, u32[]{:S(2)}, u32[]{:S(2)}) collective-permute-start(f32[72,189]{1,0:T(8,128)S(1)} %pad_maximum_fusion.1), channel_id=1, source_target_pairs={{0,4},{4,8},{8,12},{12,16},{16,20},{20,24},{24,28},{1,5},{5,9},{9,... | collective-permute-start | bytes 163304 | tf_op jit(solution)/shard_map/ppermute | solution.py:45
  25.6 0.6 %fusion.7 = f32[189,512]{1,0:T(8,128)S(1)} fusion(f32[189,512]{1,0:T(8,128)S(1)} %bitcast.288, s32[512]{0:T(512)S(1)} %add_bitcast_fusion, pred[512]{0:T(512)(128)(4,1)S(1)} %get-tuple-element.90), kind=kOutput, calls=%fused_computation.26 | convolution fusion | flops 595066880 | bytes 776704 | tf_op jit(solution)/shard_map/dot_general | solution.py:186
  26.3 2.2 %collective-permute-done.3 = f32[72,189]{1,0:T(8,128)S(1)} collective-permute-done((f32[72,189]{1,0:T(8,128)S(1)}, f32[72,189]{1,0:T(8,128)S(1)}, u32[]{:S(2)}, u32[]{:S(2)}) %collective-permute-start.3) | collective-permute-done | bytes 54464 | tf_op jit(solution)/shard_map/ppermute | solution.py:45
  29.2 0.7 %fusion.2 = f32[9,21,4,128]{3,1,2,0:T(8,128)S(1)} fusion(f32[3,4,128]{2,0,1:T(4,128)S(1)} %fusion.186, f32[9,21,4,128,1]{3,2,1,0,4:T(4,128)S(1)} %bitcast.292, f32[3,21,21]{2,1,0:T(8,128)S(1)} %neg.68), kind=kOutput, calls=%fused_computation.4 | convolution fusion | flops 37062144 | bytes 785580 | tf_op jit(solution)/shard_map/hil,qlfe->hqife/dot_general | solution.py:103
  33.4 0.5 %multiply_reduce_fusion.3 = (f32[9,56,128]{2,1,0:T(8,128)S(1)}, f32[9,56,128]{2,1,0:T(8,128)S(1)}, f32[9,56,128]{2,1,0:T(8,128)S(1)}) fusion(f32[3,128]{1,0:T(4,128)S(1)} %get-tuple-element.136, f32[3,128]{1,0:T(4,128)S(1)} %get-tuple-element.137, f32[3,128]{1,0:T(4,128)S(1)} %bitcast.307, f32[3,56,56]{2,1,0:T(8,128)S(1)} %copy-done, ...), kind=kOutput, calls=%fused_computation.30 | convolution fusion | flops 66060288 | bytes 1074432 | tf_op jit(solution)/shard_map/dab,qbe->dqae/dot_general | solution.py:78
  35.1 3.3 %collective-permute-start.5 = (f32[72,189]{1,0:T(8,128)S(1)}, f32[72,189]{1,0:T(8,128)S(1)}, u32[]{:S(2)}, u32[]{:S(2)}) collective-permute-start(f32[72,189]{1,0:T(8,128)S(1)} %get-tuple-element.99), channel_id=1, source_target_pairs={{0,1},{1,2},{2,3},{4,5},{5,6},{6,7},{8,9},{9,10},{10,11},{12,13},{... | collective-permute-start | bytes 163304 | tf_op jit(solution)/shard_map/ppermute | solution.py:45
  38.4 1.9 %collective-permute-start.4 = (f32[72,189]{1,0:T(8,128)S(1)}, f32[72,189]{1,0:T(8,128)S(1)}, u32[]{:S(2)}, u32[]{:S(2)}) collective-permute-start(f32[72,189]{1,0:T(8,128)S(1)} %get-tuple-element.100), channel_id=1, source_target_pairs={{1,0},{2,1},{3,2},{5,4},{6,5},{7,6},{9,8},{10,9},{11,10},{13,12},{... | collective-permute-start | bytes 163304 | tf_op jit(solution)/shard_map/ppermute | solution.py:45
  40.4 3.7 %collective-permute-done.4 = f32[72,189]{1,0:T(8,128)S(1)} collective-permute-done((f32[72,189]{1,0:T(8,128)S(1)}, f32[72,189]{1,0:T(8,128)S(1)}, u32[]{:S(2)}, u32[]{:S(2)}) %collective-permute-start.4) | collective-permute-done | bytes 54464 | tf_op jit(solution)/shard_map/ppermute | solution.py:45
  44.1 1.9 %collective-permute-start.6 = (f32[72,189]{1,0:T(8,128)S(1)}, f32[72,189]{1,0:T(8,128)S(1)}, u32[]{:S(2)}, u32[]{:S(2)}) collective-permute-start(f32[72,189]{1,0:T(8,128)S(1)} %pad_maximum_fusion.2), channel_id=1, source_target_pairs={{4,0},{8,4},{12,8},{16,12},{20,16},{24,20},{28,24},{5,1},{9,5},{13... | collective-permute-start | bytes 163304 | tf_op jit(solution)/shard_map/ppermute | solution.py:45
  46.1 3.5 %collective-permute-start.7 = (f32[72,189]{1,0:T(8,128)S(1)}, f32[72,189]{1,0:T(8,128)S(1)}, u32[]{:S(2)}, u32[]{:S(2)}) collective-permute-start(f32[72,189]{1,0:T(8,128)S(1)} %pad_maximum_fusion.3), channel_id=1, source_target_pairs={{0,4},{4,8},{8,12},{12,16},{16,20},{20,24},{24,28},{1,5},{5,9},{9,... | collective-permute-start | bytes 163304 | tf_op jit(solution)/shard_map/ppermute | solution.py:45
  49.6 0.6 %fusion.5 = f32[189,512]{1,0:T(8,128)S(1)} fusion(f32[189,512]{1,0:T(8,128)S(1)} %bitcast.290, s32[512]{0:T(512)S(1)} %add_bitcast_fusion, pred[512]{0:T(512)(128)(4,1)S(1)} %get-tuple-element.90), kind=kOutput, calls=%fused_computation.25 | convolution fusion | flops 595066880 | bytes 776704 | tf_op jit(solution)/shard_map/dot_general | solution.py:186
  51.0 1.1 %collective-permute-done.7 = f32[72,189]{1,0:T(8,128)S(1)} collective-permute-done((f32[72,189]{1,0:T(8,128)S(1)}, f32[72,189]{1,0:T(8,128)S(1)}, u32[]{:S(2)}, u32[]{:S(2)}) %collective-permute-start.7) | collective-permute-done | bytes 54464 | tf_op jit(solution)/shard_map/ppermute | solution.py:45
  52.7 0.7 %fusion.3 = f32[9,21,4,128]{3,1,2,0:T(8,128)S(1)} fusion(f32[3,4,128]{2,0,1:T(4,128)S(1)} %fusion.186, f32[9,21,4,128,1]{3,2,1,0,4:T(4,128)S(1)} %bitcast.291, f32[3,21,21]{2,1,0:T(8,128)S(1)} %neg.68), kind=kOutput, calls=%fused_computation.5 | convolution fusion | flops 37062144 | bytes 785580 | tf_op jit(solution)/shard_map/hil,qlfe->hqife/dot_general | solution.py:103
  53.8 1.0 %add_subtract_fusion = f32[9,56,128]{2,1,0:T(8,128)} fusion(f32[9,56,128]{2,1,0:T(8,128)S(1)} %add_subtract_fusion.1, f32[9,56,128]{2,1,0:T(8,128)S(1)} %constant_dynamic-update-slice_fusion.108, f32[9,21,4,128]{3,1,2,0:T(8,128)S(1)} %constant_dynamic-update-slice_fusion.117, f32[9,21,4,128]{3,1,2,0:T(8,128)S(1)} %convolution_bitcast_fusion.14, ...), kind=kOutput, calls=%fused_computation.222 | convolution fusion | flops 32933376 | bytes 1956224 | tf_op jit(solution)/shard_map/fai,pife->pae/dot_general | solution.py:114
  (207 shorter events, 11.4 us)
Async XLA Ops:
  0.0 2.8 %copy-start = (f32[3,56,56]{2,1,0:T(8,128)S(1)}, f32[3,56,56]{2,1,0:T(8,128)}, u32[]{:S(2)}) copy-start(f32[3,56,56]{2,1,0:T(8,128)} %param.16) | copy-start | bytes 112900
  7.2 1.0 %copy-start.1 = (f32[9,56,128]{2,1,0:T(8,128)S(1)}, f32[9,56,128]{2,1,0:T(8,128)}, u32[]{:S(2)}) copy-start(f32[9,56,128]{2,1,0:T(8,128)} %param.15) | copy-start | bytes 774148
  8.2 0.8 %copy-start.3 = (f32[4,21,56]{2,0,1:T(4,128)S(1)}, f32[4,21,56]{2,0,1:T(4,128)}, u32[]{:S(2)}) copy-start(f32[4,21,56]{2,0,1:T(4,128)} %param.18) | copy-start | bytes 56452
  9.5 6.2 %copy-start.6 = (f32[4,3,128]{2,0,1:T(4,128)S(1)}, f32[4,3,128]{2,0,1:T(4,128)}, u32[]{:S(2)}) copy-start(f32[4,3,128]{2,0,1:T(4,128)} %param.24) | copy-start | bytes 18436
  9.5 6.2 %copy-start.9 = (s32[4,128]{1,0:T(4,128)S(1)}, s32[4,128]{1,0:T(4,128)}, u32[]{:S(2)}) copy-start(s32[4,128]{1,0:T(4,128)} %param.25) | copy-start | bytes 6148
  9.6 6.2 %copy-start.7 = (s32[4,128]{1,0:T(4,128)S(1)}, s32[4,128]{1,0:T(4,128)}, u32[]{:S(2)}) copy-start(s32[4,128]{1,0:T(4,128)} %param.26) | copy-start | bytes 6148
  9.6 6.2 %copy-start.10 = (s32[4,128]{1,0:T(4,128)S(1)}, s32[4,128]{1,0:T(4,128)}, u32[]{:S(2)}) copy-start(s32[4,128]{1,0:T(4,128)} %param.27) | copy-start | bytes 6148
  9.6 6.3 %copy-start.8 = (s32[1,1,8,24]{3,2,1,0:T(8,128)S(1)}, s32[1,1,8,24]{3,2,1,0:T(8,128)}, u32[]{:S(2)}) copy-start(s32[1,1,8,24]{3,2,1,0:T(8,128)} %param.29) | copy-start | bytes 2308
  9.9 14.9 %copy-start.2 = (f32[3,56,56]{2,1,0:T(8,128)S(1)}, f32[3,56,56]{2,1,0:T(8,128)}, u32[]{:S(2)}) copy-start(f32[3,56,56]{2,1,0:T(8,128)} %param.17) | copy-start | bytes 112900
  9.9 6.0 %collective-permute-start.1 = (f32[72,189]{1,0:T(8,128)S(1)}, f32[72,189]{1,0:T(8,128)S(1)}, u32[]{:S(2)}, u32[]{:S(2)}) collective-permute-start(f32[72,189]{1,0:T(8,128)S(1)} %get-tuple-element.103), channel_id=1, source_target_pairs={{0,1},{1,2},{2,3},{4,5},{5,6},{6,7},{8,9},{9,10},{10,11},{12,13},{... | collective-permute-start | bytes 163304 | tf_op jit(solution)/shard_map/ppermute | solution.py:45
  13.8 5.7 %collective-permute-start = (f32[72,189]{1,0:T(8,128)S(1)}, f32[72,189]{1,0:T(8,128)S(1)}, u32[]{:S(2)}, u32[]{:S(2)}) collective-permute-start(f32[72,189]{1,0:T(8,128)S(1)} %get-tuple-element.104), channel_id=1, source_target_pairs={{1,0},{2,1},{3,2},{5,4},{6,5},{7,6},{9,8},{10,9},{11,10},{13,12},{... | collective-permute-start | bytes 163304 | tf_op jit(solution)/shard_map/ppermute | solution.py:45
  19.5 6.8 %collective-permute-start.2 = (f32[72,189]{1,0:T(8,128)S(1)}, f32[72,189]{1,0:T(8,128)S(1)}, u32[]{:S(2)}, u32[]{:S(2)}) collective-permute-start(f32[72,189]{1,0:T(8,128)S(1)} %pad_maximum_fusion), channel_id=1, source_target_pairs={{4,0},{8,4},{12,8},{16,12},{20,16},{24,20},{28,24},{5,1},{9,5},{13... | collective-permute-start | bytes 163304 | tf_op jit(solution)/shard_map/ppermute | solution.py:45
  22.5 6.0 %collective-permute-start.3 = (f32[72,189]{1,0:T(8,128)S(1)}, f32[72,189]{1,0:T(8,128)S(1)}, u32[]{:S(2)}, u32[]{:S(2)}) collective-permute-start(f32[72,189]{1,0:T(8,128)S(1)} %pad_maximum_fusion.1), channel_id=1, source_target_pairs={{0,4},{4,8},{8,12},{12,16},{16,20},{20,24},{24,28},{1,5},{5,9},{9,... | collective-permute-start | bytes 163304 | tf_op jit(solution)/shard_map/ppermute | solution.py:45
  25.5 0.8 %copy-start.4 = (f32[4,56,21]{1,0,2:T(4,128)S(1)}, f32[4,56,21]{1,0,2:T(4,128)}, u32[]{:S(2)}) copy-start(f32[4,56,21]{1,0,2:T(4,128)} %param.19) | copy-start | bytes 56452
  25.5 0.8 %copy-start.5 = (f32[3,21,21]{2,1,0:T(8,128)S(1)}, f32[3,21,21]{2,1,0:T(8,128)}, u32[]{:S(2)}) copy-start(f32[3,21,21]{2,1,0:T(8,128)} %param.20) | copy-start | bytes 15880
  35.1 5.2 %collective-permute-start.5 = (f32[72,189]{1,0:T(8,128)S(1)}, f32[72,189]{1,0:T(8,128)S(1)}, u32[]{:S(2)}, u32[]{:S(2)}) collective-permute-start(f32[72,189]{1,0:T(8,128)S(1)} %get-tuple-element.99), channel_id=1, source_target_pairs={{0,1},{1,2},{2,3},{4,5},{5,6},{6,7},{8,9},{9,10},{10,11},{12,13},{... | collective-permute-start | bytes 163304 | tf_op jit(solution)/shard_map/ppermute | solution.py:45
  38.4 5.7 %collective-permute-start.4 = (f32[72,189]{1,0:T(8,128)S(1)}, f32[72,189]{1,0:T(8,128)S(1)}, u32[]{:S(2)}, u32[]{:S(2)}) collective-permute-start(f32[72,189]{1,0:T(8,128)S(1)} %get-tuple-element.100), channel_id=1, source_target_pairs={{1,0},{2,1},{3,2},{5,4},{6,5},{7,6},{9,8},{10,9},{11,10},{13,12},{... | collective-permute-start | bytes 163304 | tf_op jit(solution)/shard_map/ppermute | solution.py:45
  44.1 6.8 %collective-permute-start.6 = (f32[72,189]{1,0:T(8,128)S(1)}, f32[72,189]{1,0:T(8,128)S(1)}, u32[]{:S(2)}, u32[]{:S(2)}) collective-permute-start(f32[72,189]{1,0:T(8,128)S(1)} %pad_maximum_fusion.2), channel_id=1, source_target_pairs={{4,0},{8,4},{12,8},{16,12},{20,16},{24,20},{28,24},{5,1},{9,5},{13... | collective-permute-start | bytes 163304 | tf_op jit(solution)/shard_map/ppermute | solution.py:45
  46.1 6.0 %collective-permute-start.7 = (f32[72,189]{1,0:T(8,128)S(1)}, f32[72,189]{1,0:T(8,128)S(1)}, u32[]{:S(2)}, u32[]{:S(2)}) collective-permute-start(f32[72,189]{1,0:T(8,128)S(1)} %pad_maximum_fusion.3), channel_id=1, source_target_pairs={{0,4},{4,8},{8,12},{12,16},{16,20},{20,24},{24,28},{1,5},{5,9},{9,... | collective-permute-start | bytes 163304 | tf_op jit(solution)/shard_map/ppermute | solution.py:45

commit v17 on v16

--- a/solution.py
+++ b/solution.py
@@ -164,9 +164,14 @@
     inside = (neighbour >= 0).reshape(-1)
     local_index = (neighbour_face * elem_count + jnp.maximum(neighbour, 0)).reshape(-1)
     gather_local = ((local_index[None, :] == face_ids[:, None]) & inside[None, :]).astype(dtype)
-    source_ids = jnp.concatenate([send_list[0, 0, d : d + 1] for d in SEND_ORDER], axis=0)
-    slot_total = source_ids.shape[1]
-    gather_out = (source_ids.reshape(-1)[:, None] == face_ids[None, :]).astype(dtype)
+    slot_total = send_list.shape[3]
+    slot_ids = jnp.arange(8 * slot_total, dtype=jnp.int32)
+    send_slots = jnp.array(
+        [d * slot_total + m for d in SEND_ORDER for m in range(slot_total)], dtype=jnp.int32
+    )
+    reorder = (send_slots[:, None] == slot_ids[None, :]).astype(dtype)
+    source_ids = jnp.dot(reorder, send_list.reshape(-1).astype(dtype), precision=exact_mode)
+    gather_out = (source_ids[:, None] == face_ids.astype(dtype)[None, :]).astype(dtype)
     targets = recv_list[0, 0].reshape(-1)
     scatter_in = ((targets[:, None] == face_ids[None, :]) & ~inside[None, :]).astype(dtype)
     current = dof_values

time: 55.4 us -> 56 us (1.011)
  other arithmetic: 2.36 us -> 3.05 us
    squeeze x1 -> x0, local copies, waits for them, and re-layouts: 0.99 us -> none  [per_device(): send_list[0, 0, d:d + 1]]
    unnamed x28 -> x30, local copies, waits for them, and re-layouts: 1.81 us -> 2.52 us
    convert_element_type x0 -> x2, other arithmetic: none -> 0.7 us  [the longest x1 0.69 us: per_device(): send_list.reshape(-1).astype(dtype)]
where the time goes in v17:
time: 56 us; the launch traced here: 55.4 us
  starting transfers between devices  21.7 us (39%)
  matrix products  14.7 us (26%)
  waiting for transfers between devices  10.5 us (19%)
  local copies, waits for them, and re-layouts  4.03 us (7%)
  other arithmetic  3.05 us (5%)
  between operations  1.38 us (2%)
    ppermute x8, starting transfers between devices, shifted(): return lax.ppermute(x, axis, pairs)  21.7 us
    ppermute x8, waiting for transfers between devices, shifted(): return lax.ppermute(x, axis, pairs)  10.5 us
    dot_general x10, matrix products, predict(): jnp.einsum('dab,qbe->dqae', grad_matrix, derivative, precision=fast_mode)  6.45 us
    unnamed x30, local copies, waits for them, and re-layouts  2.52 us
    dot_general x2, matrix products, face_update(): jnp.einsum('fai,pife->pae', half_lift, flux_total, precision=fast_mode)  1.39 us
    dot_general x2, matrix products, face_update(): jnp.einsum('hil,qlfe->hqife', rotate_negated, neighbour_data, precision=f...  1.36 us
    unnamed x112, other arithmetic  1.34 us
    dot_general x2, matrix products, local_work(): local_data = jnp.dot(flat_faces, gather_local, precision=exact_mode)  1.22 us
  transfers between devices with their start and end apart: 8, of which 4 were waited for; matrix products, arithmetic and copies ran while one was open for 5% of the time, Pallas kernels for 0%

profile of v17, /device:TPU:25, one launch (start us, length us, event | category | flops | bytes accessed | tf_op | source)
XLA Modules:
  0.0 55.4 jit_solution(9188365515552710589)
XLA Ops:
  0.0 0.9 %convolution_bitcast_fusion.18 = f32[3,128]{1,0:T(4,128)S(1)} fusion(f32[16,3]{0,1:T(4,128)} %param.22, s32[128]{0:T(128)} %param.23), kind=kOutput, calls=%fused_computation.22 | convolution fusion | flops 38912 | bytes 2240 | tf_op jit(solution)/shard_map/dot_general | solution.py:51
  0.9 0.7 %convert_element_type.26 = f32[1,1,8,24]{3,2,1,0:T(8,128)S(1)} convert(s32[1,1,8,24]{3,2,1,0:T(8,128)} %param.29) | non-fusion elementwise | flops 192 | bytes 1536 | tf_op jit(solution)/shard_map/convert_element_type | solution.py:173
  1.7 0.8 %fusion.205 = (f32[3,1,128]{2,1,0:T(1,128)S(1)}, f32[3,1,128]{2,1,0:T(1,128)S(1)}, f32[3,1,128]{2,1,0:T(1,128)S(1)}) fusion(f32[3,3,128]{2,1,0:T(4,128)} %param.24), kind=kLoop, calls=%fused_computation.579 | loop fusion | bytes 9216 | tf_op jit(solution)/shard_map/slice | solution.py:69
  2.5 1.6 %multiply_reduce_fusion.33 = (f32[9,56,128]{2,1,0:T(8,128)S(1)}, f32[9,56,128]{2,1,0:T(8,128)S(1)}, f32[9,56,128]{2,1,0:T(8,128)S(1)}) fusion(f32[3,128]{1,0:T(4,128)S(1)} %get-tuple-element.128, f32[3,128]{1,0:T(4,128)S(1)} %get-tuple-element.129, f32[3,128]{1,0:T(4,128)S(1)} %bitcast.285, f32[3,56,56]{2,1,0:T(8,128)S(1)} %copy-done, f32[9,56,128]{2,1,0:T(8,128)} %param.16), kind=kOutput, calls=%fused_computation.60 | convolution fusion | flops 65995776 | bytes 1074432 | tf_op jit(solution)/shard_map/dab,qbe->dqae/dot_general | solution.py:78
  7.1 0.8 %copy-done.1 = f32[9,56,128]{2,1,0:T(8,128)S(1)} copy-done((f32[9,56,128]{2,1,0:T(8,128)S(1)}, f32[9,56,128]{2,1,0:T(8,128)}, u32[]{:S(2)}) %copy-start.1) | copy-done | bytes 258072
  8.0 0.6 %copy-done.3 = f32[4,21,56]{2,0,1:T(4,128)S(1)} copy-done((f32[4,21,56]{2,0,1:T(4,128)S(1)}, f32[4,21,56]{2,0,1:T(4,128)}, u32[]{:S(2)}) %copy-start.3) | copy-done | bytes 18840
  9.2 0.6 %copy-done.11 = s32[192]{0:T(256)S(1)} copy-done((s32[192]{0:T(256)S(1)}, s32[192]{0:T(256)}, u32[]{:S(2)}) %copy-start.11) | copy-done | bytes 792
  10.5 3.8 %collective-permute-start.1 = (f32[72,189]{1,0:T(8,128)S(1)}, f32[72,189]{1,0:T(8,128)S(1)}, u32[]{:S(2)}, u32[]{:S(2)}) collective-permute-start(f32[72,189]{1,0:T(8,128)S(1)} %get-tuple-element.103), channel_id=1, source_target_pairs={{0,1},{1,2},{2,3},{4,5},{5,6},{6,7},{8,9},{9,10},{10,11},{12,13},{... | collective-permute-start | bytes 163304 | tf_op jit(solution)/shard_map/ppermute | solution.py:45
  14.4 1.9 %collective-permute-start = (f32[72,189]{1,0:T(8,128)S(1)}, f32[72,189]{1,0:T(8,128)S(1)}, u32[]{:S(2)}, u32[]{:S(2)}) collective-permute-start(f32[72,189]{1,0:T(8,128)S(1)} %get-tuple-element.104), channel_id=1, source_target_pairs={{1,0},{2,1},{3,2},{5,4},{6,5},{7,6},{9,8},{10,9},{11,10},{13,12},{... | collective-permute-start | bytes 163304 | tf_op jit(solution)/shard_map/ppermute | solution.py:45
  16.5 3.5 %collective-permute-done = f32[72,189]{1,0:T(8,128)S(1)} collective-permute-done((f32[72,189]{1,0:T(8,128)S(1)}, f32[72,189]{1,0:T(8,128)S(1)}, u32[]{:S(2)}, u32[]{:S(2)}) %collective-permute-start) | collective-permute-done | bytes 54464 | tf_op jit(solution)/shard_map/ppermute | solution.py:45
  20.1 3.0 %collective-permute-start.2 = (f32[72,189]{1,0:T(8,128)S(1)}, f32[72,189]{1,0:T(8,128)S(1)}, u32[]{:S(2)}, u32[]{:S(2)}) collective-permute-start(f32[72,189]{1,0:T(8,128)S(1)} %pad_maximum_fusion), channel_id=1, source_target_pairs={{4,0},{8,4},{12,8},{16,12},{20,16},{24,20},{28,24},{5,1},{9,5},{13... | collective-permute-start | bytes 163304 | tf_op jit(solution)/shard_map/ppermute | solution.py:45
  23.1 2.3 %collective-permute-start.3 = (f32[72,189]{1,0:T(8,128)S(1)}, f32[72,189]{1,0:T(8,128)S(1)}, u32[]{:S(2)}, u32[]{:S(2)}) collective-permute-start(f32[72,189]{1,0:T(8,128)S(1)} %pad_maximum_fusion.1), channel_id=1, source_target_pairs={{0,4},{4,8},{8,12},{12,16},{16,20},{20,24},{24,28},{1,5},{5,9},{9,... | collective-permute-start | bytes 163304 | tf_op jit(solution)/shard_map/ppermute | solution.py:45
  26.1 0.6 %fusion.7 = f32[189,512]{1,0:T(8,128)S(1)} fusion(f32[189,512]{1,0:T(8,128)S(1)} %bitcast.276, s32[512]{0:T(512)S(1)} %add_bitcast_fusion, pred[512]{0:T(512)(128)(4,1)S(1)} %get-tuple-element.90), kind=kOutput, calls=%fused_computation.26 | convolution fusion | flops 595066880 | bytes 776704 | tf_op jit(solution)/shard_map/dot_general | solution.py:191
  26.9 2.2 %collective-permute-done.3 = f32[72,189]{1,0:T(8,128)S(1)} collective-permute-done((f32[72,189]{1,0:T(8,128)S(1)}, f32[72,189]{1,0:T(8,128)S(1)}, u32[]{:S(2)}, u32[]{:S(2)}) %collective-permute-start.3) | collective-permute-done | bytes 54464 | tf_op jit(solution)/shard_map/ppermute | solution.py:45
  29.8 0.7 %fusion.2 = f32[9,21,4,128]{3,1,2,0:T(8,128)S(1)} fusion(f32[3,4,128]{2,0,1:T(4,128)S(1)} %fusion.192, f32[9,21,4,128,1]{3,2,1,0,4:T(4,128)S(1)} %bitcast.280, f32[3,21,21]{2,1,0:T(8,128)S(1)} %neg.68), kind=kOutput, calls=%fused_computation.4 | convolution fusion | flops 37062144 | bytes 785580 | tf_op jit(solution)/shard_map/hil,qlfe->hqife/dot_general | solution.py:103
  35.7 3.3 %collective-permute-start.5 = (f32[72,189]{1,0:T(8,128)S(1)}, f32[72,189]{1,0:T(8,128)S(1)}, u32[]{:S(2)}, u32[]{:S(2)}) collective-permute-start(f32[72,189]{1,0:T(8,128)S(1)} %get-tuple-element.99), channel_id=1, source_target_pairs={{0,1},{1,2},{2,3},{4,5},{5,6},{6,7},{8,9},{9,10},{10,11},{12,13},{... | collective-permute-start | bytes 163304 | tf_op jit(solution)/shard_map/ppermute | solution.py:45
  39.0 1.9 %collective-permute-start.4 = (f32[72,189]{1,0:T(8,128)S(1)}, f32[72,189]{1,0:T(8,128)S(1)}, u32[]{:S(2)}, u32[]{:S(2)}) collective-permute-start(f32[72,189]{1,0:T(8,128)S(1)} %get-tuple-element.100), channel_id=1, source_target_pairs={{1,0},{2,1},{3,2},{5,4},{6,5},{7,6},{9,8},{10,9},{11,10},{13,12},{... | collective-permute-start | bytes 163304 | tf_op jit(solution)/shard_map/ppermute | solution.py:45
  41.0 3.7 %collective-permute-done.4 = f32[72,189]{1,0:T(8,128)S(1)} collective-permute-done((f32[72,189]{1,0:T(8,128)S(1)}, f32[72,189]{1,0:T(8,128)S(1)}, u32[]{:S(2)}, u32[]{:S(2)}) %collective-permute-start.4) | collective-permute-done | bytes 54464 | tf_op jit(solution)/shard_map/ppermute | solution.py:45
  44.7 1.9 %collective-permute-start.6 = (f32[72,189]{1,0:T(8,128)S(1)}, f32[72,189]{1,0:T(8,128)S(1)}, u32[]{:S(2)}, u32[]{:S(2)}) collective-permute-start(f32[72,189]{1,0:T(8,128)S(1)} %pad_maximum_fusion.2), channel_id=1, source_target_pairs={{4,0},{8,4},{12,8},{16,12},{20,16},{24,20},{28,24},{5,1},{9,5},{13... | collective-permute-start | bytes 163304 | tf_op jit(solution)/shard_map/ppermute | solution.py:45
  46.7 3.5 %collective-permute-start.7 = (f32[72,189]{1,0:T(8,128)S(1)}, f32[72,189]{1,0:T(8,128)S(1)}, u32[]{:S(2)}, u32[]{:S(2)}) collective-permute-start(f32[72,189]{1,0:T(8,128)S(1)} %pad_maximum_fusion.3), channel_id=1, source_target_pairs={{0,4},{4,8},{8,12},{12,16},{16,20},{20,24},{24,28},{1,5},{5,9},{9,... | collective-permute-start | bytes 163304 | tf_op jit(solution)/shard_map/ppermute | solution.py:45
  50.2 0.6 %fusion.5 = f32[189,512]{1,0:T(8,128)S(1)} fusion(f32[189,512]{1,0:T(8,128)S(1)} %bitcast.278, s32[512]{0:T(512)S(1)} %add_bitcast_fusion, pred[512]{0:T(512)(128)(4,1)S(1)} %get-tuple-element.90), kind=kOutput, calls=%fused_computation.25 | convolution fusion | flops 595066880 | bytes 776704 | tf_op jit(solution)/shard_map/dot_general | solution.py:191
  51.6 1.1 %collective-permute-done.7 = f32[72,189]{1,0:T(8,128)S(1)} collective-permute-done((f32[72,189]{1,0:T(8,128)S(1)}, f32[72,189]{1,0:T(8,128)S(1)}, u32[]{:S(2)}, u32[]{:S(2)}) %collective-permute-start.7) | collective-permute-done | bytes 54464 | tf_op jit(solution)/shard_map/ppermute | solution.py:45
  53.3 0.7 %fusion.3 = f32[9,21,4,128]{3,1,2,0:T(8,128)S(1)} fusion(f32[3,4,128]{2,0,1:T(4,128)S(1)} %fusion.192, f32[9,21,4,128,1]{3,2,1,0,4:T(4,128)S(1)} %bitcast.279, f32[3,21,21]{2,1,0:T(8,128)S(1)} %neg.68), kind=kOutput, calls=%fused_computation.5 | convolution fusion | flops 37062144 | bytes 785580 | tf_op jit(solution)/shard_map/hil,qlfe->hqife/dot_general | solution.py:103
  54.4 1.0 %add_subtract_fusion = f32[9,56,128]{2,1,0:T(8,128)} fusion(f32[9,56,128]{2,1,0:T(8,128)S(1)} %add_subtract_fusion.1, f32[9,56,128]{2,1,0:T(8,128)S(1)} %constant_dynamic-update-slice_fusion.108, f32[9,21,4,128]{3,1,2,0:T(8,128)S(1)} %constant_dynamic-update-slice_fusion.117, f32[9,21,4,128]{3,1,2,0:T(8,128)S(1)} %convolution_bitcast_fusion.14, ...), kind=kOutput, calls=%fused_computation.223 | convolution fusion | flops 32933376 | bytes 1956224 | tf_op jit(solution)/shard_map/fai,pife->pae/dot_general | solution.py:114
  (210 shorter events, 12.2 us)
Async XLA Ops:
  0.0 2.5 %copy-start = (f32[3,56,56]{2,1,0:T(8,128)S(1)}, f32[3,56,56]{2,1,0:T(8,128)}, u32[]{:S(2)}) copy-start(f32[3,56,56]{2,1,0:T(8,128)} %param.17) | copy-start | bytes 112900
  6.9 1.0 %copy-start.1 = (f32[9,56,128]{2,1,0:T(8,128)S(1)}, f32[9,56,128]{2,1,0:T(8,128)}, u32[]{:S(2)}) copy-start(f32[9,56,128]{2,1,0:T(8,128)} %param.16) | copy-start | bytes 774148
  7.9 0.8 %copy-start.3 = (f32[4,21,56]{2,0,1:T(4,128)S(1)}, f32[4,21,56]{2,0,1:T(4,128)}, u32[]{:S(2)}) copy-start(f32[4,21,56]{2,0,1:T(4,128)} %param.19) | copy-start | bytes 56452
  9.2 0.7 %copy-start.11 = (s32[192]{0:T(256)S(1)}, s32[192]{0:T(256)}, u32[]{:S(2)}) copy-start(s32[192]{0:T(256)} %constant.26.clone) | copy-start | bytes 2308
  10.1 6.3 %copy-start.6 = (f32[4,3,128]{2,0,1:T(4,128)S(1)}, f32[4,3,128]{2,0,1:T(4,128)}, u32[]{:S(2)}) copy-start(f32[4,3,128]{2,0,1:T(4,128)} %param.25) | copy-start | bytes 18436
  10.1 6.3 %copy-start.9 = (s32[4,128]{1,0:T(4,128)S(1)}, s32[4,128]{1,0:T(4,128)}, u32[]{:S(2)}) copy-start(s32[4,128]{1,0:T(4,128)} %param.26) | copy-start | bytes 6148
  10.1 6.3 %copy-start.7 = (s32[4,128]{1,0:T(4,128)S(1)}, s32[4,128]{1,0:T(4,128)}, u32[]{:S(2)}) copy-start(s32[4,128]{1,0:T(4,128)} %param.27) | copy-start | bytes 6148
  10.2 6.2 %copy-start.10 = (s32[4,128]{1,0:T(4,128)S(1)}, s32[4,128]{1,0:T(4,128)}, u32[]{:S(2)}) copy-start(s32[4,128]{1,0:T(4,128)} %param.28) | copy-start | bytes 6148
  10.2 6.3 %copy-start.8 = (s32[1,1,8,24]{3,2,1,0:T(8,128)S(1)}, s32[1,1,8,24]{3,2,1,0:T(8,128)}, u32[]{:S(2)}) copy-start(s32[1,1,8,24]{3,2,1,0:T(8,128)} %param.30) | copy-start | bytes 2308
  10.5 14.9 %copy-start.2 = (f32[3,56,56]{2,1,0:T(8,128)S(1)}, f32[3,56,56]{2,1,0:T(8,128)}, u32[]{:S(2)}) copy-start(f32[3,56,56]{2,1,0:T(8,128)} %param.18) | copy-start | bytes 112900
  10.5 6.0 %collective-permute-start.1 = (f32[72,189]{1,0:T(8,128)S(1)}, f32[72,189]{1,0:T(8,128)S(1)}, u32[]{:S(2)}, u32[]{:S(2)}) collective-permute-start(f32[72,189]{1,0:T(8,128)S(1)} %get-tuple-element.103), channel_id=1, source_target_pairs={{0,1},{1,2},{2,3},{4,5},{5,6},{6,7},{8,9},{9,10},{10,11},{12,13},{... | collective-permute-start | bytes 163304 | tf_op jit(solution)/shard_map/ppermute | solution.py:45
  14.4 5.7 %collective-permute-start = (f32[72,189]{1,0:T(8,128)S(1)}, f32[72,189]{1,0:T(8,128)S(1)}, u32[]{:S(2)}, u32[]{:S(2)}) collective-permute-start(f32[72,189]{1,0:T(8,128)S(1)} %get-tuple-element.104), channel_id=1, source_target_pairs={{1,0},{2,1},{3,2},{5,4},{6,5},{7,6},{9,8},{10,9},{11,10},{13,12},{... | collective-permute-start | bytes 163304 | tf_op jit(solution)/shard_map/ppermute | solution.py:45
  20.1 6.8 %collective-permute-start.2 = (f32[72,189]{1,0:T(8,128)S(1)}, f32[72,189]{1,0:T(8,128)S(1)}, u32[]{:S(2)}, u32[]{:S(2)}) collective-permute-start(f32[72,189]{1,0:T(8,128)S(1)} %pad_maximum_fusion), channel_id=1, source_target_pairs={{4,0},{8,4},{12,8},{16,12},{20,16},{24,20},{28,24},{5,1},{9,5},{13... | collective-permute-start | bytes 163304 | tf_op jit(solution)/shard_map/ppermute | solution.py:45
  23.1 6.0 %collective-permute-start.3 = (f32[72,189]{1,0:T(8,128)S(1)}, f32[72,189]{1,0:T(8,128)S(1)}, u32[]{:S(2)}, u32[]{:S(2)}) collective-permute-start(f32[72,189]{1,0:T(8,128)S(1)} %pad_maximum_fusion.1), channel_id=1, source_target_pairs={{0,4},{4,8},{8,12},{12,16},{16,20},{20,24},{24,28},{1,5},{5,9},{9,... | collective-permute-start | bytes 163304 | tf_op jit(solution)/shard_map/ppermute | solution.py:45
  26.1 0.8 %copy-start.4 = (f32[4,56,21]{1,0,2:T(4,128)S(1)}, f32[4,56,21]{1,0,2:T(4,128)}, u32[]{:S(2)}) copy-start(f32[4,56,21]{1,0,2:T(4,128)} %param.20) | copy-start | bytes 56452
  26.1 0.8 %copy-start.5 = (f32[3,21,21]{2,1,0:T(8,128)S(1)}, f32[3,21,21]{2,1,0:T(8,128)}, u32[]{:S(2)}) copy-start(f32[3,21,21]{2,1,0:T(8,128)} %param.21) | copy-start | bytes 15880
  35.7 5.2 %collective-permute-start.5 = (f32[72,189]{1,0:T(8,128)S(1)}, f32[72,189]{1,0:T(8,128)S(1)}, u32[]{:S(2)}, u32[]{:S(2)}) collective-permute-start(f32[72,189]{1,0:T(8,128)S(1)} %get-tuple-element.99), channel_id=1, source_target_pairs={{0,1},{1,2},{2,3},{4,5},{5,6},{6,7},{8,9},{9,10},{10,11},{12,13},{... | collective-permute-start | bytes 163304 | tf_op jit(solution)/shard_map/ppermute | solution.py:45
  39.0 5.7 %collective-permute-start.4 = (f32[72,189]{1,0:T(8,128)S(1)}, f32[72,189]{1,0:T(8,128)S(1)}, u32[]{:S(2)}, u32[]{:S(2)}) collective-permute-start(f32[72,189]{1,0:T(8,128)S(1)} %get-tuple-element.100), channel_id=1, source_target_pairs={{1,0},{2,1},{3,2},{5,4},{6,5},{7,6},{9,8},{10,9},{11,10},{13,12},{... | collective-permute-start | bytes 163304 | tf_op jit(solution)/shard_map/ppermute | solution.py:45
  44.7 6.8 %collective-permute-start.6 = (f32[72,189]{1,0:T(8,128)S(1)}, f32[72,189]{1,0:T(8,128)S(1)}, u32[]{:S(2)}, u32[]{:S(2)}) collective-permute-start(f32[72,189]{1,0:T(8,128)S(1)} %pad_maximum_fusion.2), channel_id=1, source_target_pairs={{4,0},{8,4},{12,8},{16,12},{20,16},{24,20},{28,24},{5,1},{9,5},{13... | collective-permute-start | bytes 163304 | tf_op jit(solution)/shard_map/ppermute | solution.py:45
  46.7 6.0 %collective-permute-start.7 = (f32[72,189]{1,0:T(8,128)S(1)}, f32[72,189]{1,0:T(8,128)S(1)}, u32[]{:S(2)}, u32[]{:S(2)}) collective-permute-start(f32[72,189]{1,0:T(8,128)S(1)} %pad_maximum_fusion.3), channel_id=1, source_target_pairs={{0,4},{4,8},{8,12},{12,16},{16,20},{20,24},{24,28},{1,5},{5,9},{9,... | collective-permute-start | bytes 163304 | tf_op jit(solution)/shard_map/ppermute | solution.py:45
